TPU v7x, 32 devices: a whole 2x2x4 slice. The times are simulated.
32 devices in a mesh: runs: 2 (over x), depth: 8 (over z, y), screen: 2 (over core).
Axes of the slice: x: 2, y: 2, z: 4, core: 2. Of those that a mesh axis runs over, the one named last changes fastest.
Arguments:
- density: float32 [16, 2, 128, 128, 128], P(('runs', 'depth'), 'screen'), parts along dimension 0, may hold values from -6 to 6
- foot_start: int32 [16, 2], P(('runs', 'depth'), 'screen'), parts along dimension 0, may hold values from 0 to 1920, as said below
- foot_rows: int32 [16, 2], P(('runs', 'depth'), 'screen'), parts along dimension 0, may hold values from 32 to 128, as said below
- extinction: float32 [2], P('runs'), parts along dimension 0, may hold values from 0.4 to 1.6
- colour_slope: float32 [3], replicated, may hold values from 0.5 to 2.5
- colour_offset: float32 [3], replicated, may hold values from -1 to 1
- tile_source: int32 [8192], P('runs'), parts along dimension 0, may hold values from 0 to 4095, as said below
Outputs:
- frame: float32 [8192, 4, 128], P(('runs', 'depth', 'screen')), parts along dimension 0
There are 2 independent parts, one for each index of `runs`. A program takes and returns all parts, laid end to end along the dimension named above; an argument that names none is the same for every part. Nothing has to cross between parts.
Inputs may be any that keep to these rules, and one draw needn't show every extreme that they name: `foot_start`: in each screen half the first rows of the bricks go from one end of the range to the other as depth grows, with a jitter; the rows of a brick meet only those of the bricks next to it along depth in the same screen half. `foot_rows`: some brick of every group shows all 128 of its rows. `tile_source`: a permutation of the image rows; each aligned block of 256 entries takes exactly 32 rows from each of 8 of the image's aligned blocks of 256 rows, and none from the others.
All inputs are finite; a program needn't handle non-finite values.
Results may differ from a plain program's by a relative error of at most 0.0003.
Values sent between devices are 32-bit elements; how exact they have to be, the bound alone decides.
No kernel may reach another device: no remote copies, remote signals or barrier semaphores. Data moves between devices by JAX's collectives and lax.ppermute only.
A program may use at most 128 MiB of HBM per device.

v0:
```python
import jax
import jax.numpy as jnp
from jax import lax
from jax.sharding import PartitionSpec as P

BLK = 256


def partner(x, axis, apart):
    return lax.ppermute(x, axis, [(i, i ^ 1 << apart) for i in range(lax.axis_size(axis))])


def render_layers(density_block, shown_rows, absorb, colour_slope, colour_offset):
    brick_rows, sample_count, pixels = density_block.shape
    optical = absorb * jax.nn.softplus(density_block) / sample_count
    below_mask = (
        lax.broadcasted_iota(jnp.int32, (sample_count, sample_count), 0)
        > lax.broadcasted_iota(jnp.int32, (sample_count, sample_count), 1)
    ).astype(jnp.float32)
    ahead_sum = jnp.einsum("kj,rjp->rkp", below_mask, optical, precision=lax.Precision.HIGHEST)
    depth_sum = jnp.sum(optical, axis=1)
    weight = jnp.exp(-ahead_sum) * (1.0 - jnp.exp(-optical))
    colours = [
        jnp.sum(
            weight * jax.nn.sigmoid(colour_slope[channel] * density_block + colour_offset[channel]),
            axis=1,
        )
        for channel in range(3)
    ]
    layers = jnp.stack(colours + [depth_sum], axis=1)
    visible = (jnp.arange(brick_rows) < shown_rows)[:, None, None]
    return jnp.where(visible, layers, jnp.zeros_like(layers))


def place_canvas(layers, start_row, canvas_rows):
    canvas = jnp.zeros((canvas_rows, 4, layers.shape[2]), jnp.float32)
    return lax.dynamic_update_slice(canvas, layers, (start_row, jnp.int32(0), jnp.int32(0)))


def blend_over(front_part, back_part):
    front_depth = front_part[:, 3:4, :]
    colours = front_part[:, :3, :] + jnp.exp(-front_depth) * back_part[:, :3, :]
    return jnp.concatenate([colours, front_depth + back_part[:, 3:4, :]], axis=1)


def reverse_bits(values, bit_count):
    result = jnp.zeros_like(values)
    for bit_number in range(bit_count):
        result = result + (values >> bit_number & 1) * (1 << bit_count - 1 - bit_number)
    return result


def on_device(density, foot_start, foot_rows, extinction, colour_slope, colour_offset, tile_source):
    depth_count = lax.axis_size("depth")
    screen_count = lax.axis_size("screen")
    depth_index = lax.axis_index("depth")
    screen_index = lax.axis_index("screen")
    canvas_rows = BLK * depth_count
    bit_count = depth_count.bit_length() - 1
    layers = render_layers(
        density[0, 0], foot_rows[0, 0], extinction[0], colour_slope, colour_offset
    )
    start_row = foot_start[0, 0]
    image_block = tile_source % canvas_rows // BLK
    holding = place_canvas(layers, start_row, canvas_rows)
    for bit_number in range(bit_count):
        middle_row = holding.shape[0] // 2
        low_half = holding[:middle_row]
        high_half = holding[middle_row:]
        upper_side = depth_index >> bit_number & 1 == 1
        kept_half = jnp.where(upper_side, high_half, low_half)
        given_half = jnp.where(upper_side, low_half, high_half)
        partner_half = partner(given_half, "depth", bit_number)
        mine_front = jnp.logical_not(upper_side)
        front_part = jnp.where(mine_front, kept_half, partner_half)
        back_part = jnp.where(mine_front, partner_half, kept_half)
        holding = blend_over(front_part, back_part)
    block_index = reverse_bits(depth_index, bit_count)
    holder_depth = reverse_bits(image_block, bit_count)
    finished = jnp.concatenate([holding[:, :3, :], 1.0 - jnp.exp(-holding[:, 3:4, :])], axis=1)
    holders = holder_depth * screen_count + tile_source // canvas_rows
    self_index = depth_index * screen_count + screen_index
    device_count = depth_count * screen_count
    own_holders = lax.dynamic_slice_in_dim(holders, self_index * BLK, BLK)
    slots = BLK // depth_count
    image_total = tile_source.shape[0]
    first_row = screen_index * canvas_rows + block_index * BLK
    owner_holders = holders.reshape(device_count, BLK)
    column_order = jnp.arange(BLK)
    earlier = (owner_holders[:, :, None] == owner_holders[:, None, :]) & (
        column_order[None, None, :] < column_order[None, :, None]
    )
    slot_rank = jnp.sum(earlier.astype(jnp.int32), axis=2)
    is_mine = owner_holders == self_index
    local_row = jnp.where(is_mine, tile_source.reshape(device_count, BLK) - first_row, 0)
    matches = is_mine[:, :, None] & (slot_rank[:, :, None] == jnp.arange(slots)[None, None, :])
    send_rows = jnp.sum(jnp.where(matches, local_row[:, :, None], 0), axis=1)
    outgoing = jnp.take(finished, send_rows.reshape(-1), axis=0).reshape(
        device_count, slots, 4, finished.shape[2]
    )
    incoming = lax.all_to_all(
        outgoing, ("depth", "screen"), split_axis=0, concat_axis=0, tiled=True
    )
    own_rank = lax.dynamic_slice_in_dim(slot_rank.reshape(image_total), self_index * BLK, BLK)
    position = own_holders * slots + own_rank
    frame = jnp.take(incoming.reshape(device_count * slots, 4, finished.shape[2]), position, axis=0)
    return frame


def solution(mesh):
    return jax.shard_map(
        on_device,
        mesh=mesh,
        in_specs=(
            P(("runs", "depth"), "screen", None, None, None),
            P(("runs", "depth"), "screen"),
            P(("runs", "depth"), "screen"),
            P("runs"),
            P(),
            P(),
            P("runs"),
        ),
        out_specs=P(("runs", "depth", "screen"), None, None),
        check_vma=False,
    )
```

profile of v0, /device:TPU:0, one launch (start us, length us, event | category | flops | bytes accessed | tf_op | source)
XLA Modules:
  0.0 178.9 jit_solution(663727104819705850)
XLA Ops:
  0.0 1.4 fusion.47
  1.4 1.4 fusion.48
  4.8 29.9 %fusion.25 = (f32[128,128]{1,0:T(8,128)S(1)}, f32[128,128]{1,0:T(8,128)S(1)}, f32[128,128]{1,0:T(8,128)S(1)}, f32[128,128]{1,0:T(8,128)S(1)}) fusion(f32[1,1,128,128,128]{4,3,2,1,0:T(8,128)} %param.7, f32[]{:T(128)} %bitcast.6, f32[]{:T(128)} %bitcast.5, f32[]{:T(128)} %bitcast.12, f32[]{:T(128)} %bitcast.11, f32[]{:T(128)} %bitcast.9, f32[]{:T(128)} %bitcast.8, ...), kind=kOutput, calls=%fused_computation.34 | convolution fusion | flops 3309256704 | bytes 8650780 | tf_op jit(solution)/shard_map/kj,rjp->rkp/dot_general | solution.py:20
  34.7 0.1 maximum_select_fusion
  34.8 2.2 %broadcast_in_dim.64 = f32[2048,4,128]{2,0,1:T(8,128)} broadcast(f32[]{:T(128)} %constant.97.clone.1), dimensions={} | broadcast | bytes 4194308 | tf_op jit(solution)/shard_map/broadcast_in_dim | solution.py:36
  37.0 1.7 dynamic_update_slice.3
  38.7 2.4 %slice_select_fusion = f32[1024,4,128]{2,0,1:T(8,128)S(1)} fusion(f32[2048,4,128]{2,0,1:T(8,128)} %dynamic_update_slice.3, pred[]{:T(512)S(6)} %eq.63), kind=kLoop, calls=%fused_computation.40 | loop fusion | flops 524288 | bytes 6291457 | tf_op jit(solution)/shard_map/jit(_where)/select_n | solution.py:72
  41.2 3.2 %collective-permute-start = (f32[1024,4,128]{2,0,1:T(8,128)S(1)}, f32[1024,4,128]{2,0,1:T(8,128)}, u32[]{:S(2)}, u32[]{:S(2)}) collective-permute-start(f32[1024,4,128]{2,0,1:T(8,128)S(1)} %slice_select_fusion), channel_id=1, source_target_pairs={{0,2},{2,0},{4,6},{6,4},{8,10},{10,8},{12,14},{14,12},{1,3},{3,1},... | collective-permute-start | bytes 6291464 | tf_op jit(solution)/shard_map/ppermute | solution.py:10
  44.3 45.7 %collective-permute-done = f32[1024,4,128]{2,0,1:T(8,128)} collective-permute-done((f32[1024,4,128]{2,0,1:T(8,128)S(1)}, f32[1024,4,128]{2,0,1:T(8,128)}, u32[]{:S(2)}, u32[]{:S(2)}) %collective-permute-start) | collective-permute-done | bytes 2097184 | tf_op jit(solution)/shard_map/ppermute | solution.py:10
  90.0 3.2 %broadcast_select_fusion.1 = (f32[1024,4,128]{2,0,1:T(8,128)S(1)}, f32[1024,4,128]{2,0,1:T(8,128)S(1)}) fusion(f32[1024,4,128]{2,0,1:T(8,128)} %collective-permute-done, pred[]{:T(512)S(6)} %not.11, f32[2048,4,128]{2,0,1:T(8,128)} %dynamic_update_slice.3, pred[]{:T(512)S(6)} %eq.63), kind=kLoop, calls=%fused_computation.49 | loop fusion | flops 1572864 | bytes 10485762 | tf_op jit(solution)/shard_map/jit(_where)/select_n | solution.py:75
  93.3 0.1 exponential_bitcast_fusion
  93.4 0.2 fusion.29
  93.6 0.1 broadcast_select_fusion.3
  93.7 1.9 %collective-permute-start.1 = (f32[512,4,128]{2,0,1:T(8,128)S(1)}, f32[512,4,128]{2,0,1:T(8,128)}, u32[]{:S(2)}, u32[]{:S(2)}) collective-permute-start(f32[512,4,128]{2,0,1:T(8,128)S(1)} %broadcast_select_fusion.3), channel_id=1, source_target_pairs={{0,4},{2,6},{4,0},{6,2},{8,12},{10,14},{12,8},{14,10},{1,5},{3,7},... | collective-permute-start | bytes 3145736 | tf_op jit(solution)/shard_map/ppermute | solution.py:10
  95.7 1.3 convert_reduce_fusion
  97.0 0.4 select_reduce_fusion
  97.4 0.1 reshape.92
  97.5 20.7 %collective-permute-done.1 = f32[512,4,128]{2,0,1:T(8,128)} collective-permute-done((f32[512,4,128]{2,0,1:T(8,128)S(1)}, f32[512,4,128]{2,0,1:T(8,128)}, u32[]{:S(2)}, u32[]{:S(2)}) %collective-permute-start.1) | collective-permute-done | bytes 1048608 | tf_op jit(solution)/shard_map/ppermute | solution.py:10
  118.2 1.4 broadcast_select_fusion.6
  119.7 0.1 fusion.31
  119.8 0.1 broadcast_select_fusion.8
  119.9 2.5 %collective-permute-start.2 = (f32[256,4,128]{2,0,1:T(8,128)S(1)}, f32[256,4,128]{2,0,1:T(8,128)S(1)}, u32[]{:S(2)}, u32[]{:S(2)}) collective-permute-start(f32[256,4,128]{2,0,1:T(8,128)S(1)} %broadcast_select_fusion.8), channel_id=1, source_target_pairs={{0,8},{2,10},{4,12},{6,14},{8,0},{10,2},{12,4},{14,6},{1,9},{3,11}... | collective-permute-start | bytes 1572872 | tf_op jit(solution)/shard_map/ppermute | solution.py:10
  122.4 21.8 %collective-permute-done.2 = f32[256,4,128]{2,0,1:T(8,128)S(1)} collective-permute-done((f32[256,4,128]{2,0,1:T(8,128)S(1)}, f32[256,4,128]{2,0,1:T(8,128)S(1)}, u32[]{:S(2)}, u32[]{:S(2)}) %collective-permute-start.2) | collective-permute-done | bytes 524320 | tf_op jit(solution)/shard_map/ppermute | solution.py:10
  144.2 0.1 broadcast_select_fusion.11
  144.5 0.3 copy.9
  144.8 2.1 %gather_fusion = f32[512,4,128]{2,1,0:T(4,128)S(1)} fusion(f32[256,4,128]{2,1,0:T(4,128)S(1)} %copy.9, s32[1024]{0:T(1024)S(1)} %pad_clamp_fusion.1), kind=kCustom, calls=%fused_computation | custom fusion | bytes 2099200 | tf_op jit(solution)/shard_map/jit(_take)/gather | solution.py:98
  146.9 1.5 broadcast_select_fusion.2
  148.4 5.4 %all-to-all-start = ((f32[16,32,4,128]{3,2,1,0:T(4,128)}), f32[16,32,4,128]{3,2,1,0:T(4,128)S(1)}, u32[]{:S(2)}, u32[]{:S(2)}) async-start(f32[16,32,4,128]{3,2,1,0:T(4,128)} %broadcast_select_fusion.2), calls=%async_computation | async-start | bytes 2097152 | tf_op jit(solution)/shard_map/all_to_all | solution.py:101
  153.8 0.1 compare_and_fusion.1
  153.9 22.8 %all-to-all-done = f32[16,32,4,128]{3,2,1,0:T(4,128)S(1)} async-done(((f32[16,32,4,128]{3,2,1,0:T(4,128)}), f32[16,32,4,128]{3,2,1,0:T(4,128)S(1)}, u32[]{:S(2)}, u32[]{:S(2)}) %all-to-all-start) | async-done | bytes 1048608 | tf_op jit(solution)/shard_map/all_to_all | solution.py:101
  176.8 1.0 gather_fusion.1
  177.8 1.1 broadcast_select_fusion.7
  (17 shorter events, 0.3 us)
Async XLA Ops:
  41.2 48.9 %collective-permute-start = (f32[1024,4,128]{2,0,1:T(8,128)S(1)}, f32[1024,4,128]{2,0,1:T(8,128)}, u32[]{:S(2)}, u32[]{:S(2)}) collective-permute-start(f32[1024,4,128]{2,0,1:T(8,128)S(1)} %slice_select_fusion), channel_id=1, source_target_pairs={{0,2},{2,0},{4,6},{6,4},{8,10},{10,8},{12,14},{14,12},{1,3},{3,1},... | collective-permute-start | bytes 6291464 | tf_op jit(solution)/shard_map/ppermute | solution.py:10
  44.3 51.3 %copy-start = (s32[4096]{0:T(1024)S(1)}, s32[4096]{0:T(1024)}, u32[]{:S(2)}) copy-start(s32[4096]{0:T(1024)} %param.13) | copy-start | bytes 49156
  93.7 24.5 %collective-permute-start.1 = (f32[512,4,128]{2,0,1:T(8,128)S(1)}, f32[512,4,128]{2,0,1:T(8,128)}, u32[]{:S(2)}, u32[]{:S(2)}) collective-permute-start(f32[512,4,128]{2,0,1:T(8,128)S(1)} %broadcast_select_fusion.3), channel_id=1, source_target_pairs={{0,4},{2,6},{4,0},{6,2},{8,12},{10,14},{12,8},{14,10},{1,5},{3,7},... | collective-permute-start | bytes 3145736 | tf_op jit(solution)/shard_map/ppermute | solution.py:10
  119.9 24.4 %collective-permute-start.2 = (f32[256,4,128]{2,0,1:T(8,128)S(1)}, f32[256,4,128]{2,0,1:T(8,128)S(1)}, u32[]{:S(2)}, u32[]{:S(2)}) collective-permute-start(f32[256,4,128]{2,0,1:T(8,128)S(1)} %broadcast_select_fusion.8), channel_id=1, source_target_pairs={{0,8},{2,10},{4,12},{6,14},{8,0},{10,2},{12,4},{14,6},{1,9},{3,11}... | collective-permute-start | bytes 1572872 | tf_op jit(solution)/shard_map/ppermute | solution.py:10
  148.4 28.4 %all-to-all-start = ((f32[16,32,4,128]{3,2,1,0:T(4,128)}), f32[16,32,4,128]{3,2,1,0:T(4,128)S(1)}, u32[]{:S(2)}, u32[]{:S(2)}) async-start(f32[16,32,4,128]{3,2,1,0:T(4,128)} %broadcast_select_fusion.2), calls=%async_computation | async-start | bytes 2097152 | tf_op jit(solution)/shard_map/all_to_all | solution.py:101
where the time goes:
time: 180 us; the launch traced here: 179 us
  waiting for transfers between devices  111 us (62%)
  matrix products  29.9 us (17%)
  starting transfers between devices  13 us (7%)
  other arithmetic  12.5 us (7%)
  local copies, waits for them, and re-layouts  10.2 us (6%)
  between operations  2.15 us (1%)
    ppermute x3, waiting for transfers between devices, partner(): lax.ppermute(x, axis, [(i, i ^ 1 << apart) for i in range(lax.axis_size(a...  88.2 us
    dot_general x1, matrix products, render_layers(): jnp.einsum('kj,rjp->rkp', below_mask, optical, precision=lax.Precision.HI...  29.9 us
    all_to_all x1, waiting for transfers between devices, on_device(): lax.all_to_all(outgoing, ('depth', 'screen'), split_axis=0, concat_axis=0...  22.8 us
    ppermute x3, starting transfers between devices, partner(): lax.ppermute(x, axis, [(i, i ^ 1 << apart) for i in range(lax.axis_size(a...  7.59 us
    all_to_all x1, starting transfers between devices, on_device(): lax.all_to_all(outgoing, ('depth', 'screen'), split_axis=0, concat_axis=0...  5.41 us
    select_n x3, other arithmetic, on_device(): front_part = jnp.where(mine_front, kept_half, partner_half)  4.72 us
  transfers between devices with their start and end apart: 4, of which 4 were waited for; matrix products, arithmetic and copies ran while one was open for 1% of the time, Pallas kernels for 0%

commit v1 on v0

v1 whole, which is shorter than its diff:
```python
import jax
import jax.numpy as jnp
from jax import lax
from jax.sharding import PartitionSpec as P

BLK = 256


def render_layers(density_block, shown_rows, absorb, colour_slope, colour_offset):
    brick_rows, sample_count, pixels = density_block.shape
    optical = absorb * jax.nn.softplus(density_block) / sample_count
    below_mask = (
        lax.broadcasted_iota(jnp.int32, (sample_count, sample_count), 0)
        > lax.broadcasted_iota(jnp.int32, (sample_count, sample_count), 1)
    ).astype(jnp.float32)
    ahead_sum = jnp.einsum("kj,rjp->rkp", below_mask, optical, precision=lax.Precision.HIGHEST)
    depth_sum = jnp.sum(optical, axis=1)
    weight = jnp.exp(-ahead_sum) * (1.0 - jnp.exp(-optical))
    colours = [
        jnp.sum(
            weight * jax.nn.sigmoid(colour_slope[channel] * density_block + colour_offset[channel]),
            axis=1,
        )
        for channel in range(3)
    ]
    layers = jnp.stack(colours + [depth_sum], axis=1)
    visible = (jnp.arange(brick_rows) < shown_rows)[:, None, None]
    return jnp.where(visible, layers, jnp.zeros_like(layers))


def composite_rows(bricks, starts, counts, image_rows):
    depth_count, brick_rows = bricks.shape[0], bricks.shape[1]
    flat = bricks.reshape((depth_count * brick_rows,) + bricks.shape[2:])
    offset = image_rows[:, None] - starts[None, :]
    covered = (offset >= 0) & (offset < counts[None, :])
    depth_ids = jnp.arange(depth_count)[None, :]
    back = jnp.max(jnp.where(covered, depth_ids, -1), axis=1)
    any_back = back >= 0
    back_c = jnp.maximum(back, 0)
    front_c = jnp.maximum(back - 1, 0)
    back_off = jnp.take_along_axis(offset, back_c[:, None], axis=1)[:, 0]
    front_off = jnp.take_along_axis(offset, front_c[:, None], axis=1)[:, 0]
    front_cov = jnp.take_along_axis(covered, front_c[:, None], axis=1)[:, 0] & (back >= 1)
    back_idx = back_c * brick_rows + jnp.clip(back_off, 0, brick_rows - 1)
    front_idx = front_c * brick_rows + jnp.clip(front_off, 0, brick_rows - 1)
    back_rows = jnp.take(flat, back_idx, axis=0)
    front_rows = jnp.take(flat, front_idx, axis=0)
    back_rows = jnp.where(any_back[:, None, None], back_rows, 0.0)
    front_rows = jnp.where(front_cov[:, None, None], front_rows, 0.0)
    front_depth = front_rows[:, 3:4, :]
    colours = front_rows[:, :3, :] + jnp.exp(-front_depth) * back_rows[:, :3, :]
    opacity = 1.0 - jnp.exp(-(front_depth + back_rows[:, 3:4, :]))
    return jnp.concatenate([colours, opacity], axis=1)


def on_device(density, foot_start, foot_rows, extinction, colour_slope, colour_offset, tile_source):
    depth_count = lax.axis_size("depth")
    screen_count = lax.axis_size("screen")
    depth_index = lax.axis_index("depth")
    screen_index = lax.axis_index("screen")
    image_total = tile_source.shape[0]
    half_rows = image_total // screen_count
    owner_rows = image_total // (depth_count * screen_count)
    my_starts = foot_start.reshape(depth_count, screen_count)
    my_counts = foot_rows.reshape(depth_count, screen_count)
    shown = my_counts[depth_index, screen_index]
    layers = render_layers(density[0, 0], shown, extinction[0], colour_slope, colour_offset)
    bricks = lax.all_gather(layers, "depth")
    starts = lax.dynamic_index_in_dim(my_starts, screen_index, axis=1, keepdims=False)
    counts = lax.dynamic_index_in_dim(my_counts, screen_index, axis=1, keepdims=False)
    self_owner = depth_index * screen_count + screen_index
    partner_owner = depth_index * screen_count + (1 - screen_index)
    wanted_self = lax.dynamic_slice_in_dim(tile_source, self_owner * owner_rows, owner_rows)
    wanted_partner = lax.dynamic_slice_in_dim(tile_source, partner_owner * owner_rows, owner_rows)
    wanted = jnp.concatenate([wanted_self, wanted_partner])
    rows = composite_rows(bricks, starts, counts, wanted % half_rows)
    mine = rows[:owner_rows]
    for_partner = rows[owner_rows:]
    received = lax.ppermute(for_partner, "screen", [(0, 1), (1, 0)])
    in_my_half = (wanted_self // half_rows) == screen_index
    return jnp.where(in_my_half[:, None, None], mine, received)


def solution(mesh):
    return jax.shard_map(
        on_device,
        mesh=mesh,
        in_specs=(
            P(("runs", "depth"), "screen", None, None, None),
            P("runs", None),
            P("runs", None),
            P("runs"),
            P(),
            P(),
            P("runs"),
        ),
        out_specs=P(("runs", "depth", "screen"), None, None),
        check_vma=False,
    )
```

time: 180 us -> 127 us (0.71)
  waiting for transfers between devices: 111 us -> 34.3 us
  local copies, waits for them, and re-layouts: 10.2 us -> 28.2 us
  blocking collectives: 0 us -> 13.9 us
  between operations: 2.15 us -> 15.6 us
  starting transfers between devices: 13 us -> 0.07 us
  other arithmetic: 12.5 us -> 4.58 us
    ppermute x3 -> x1, waiting for transfers between devices: 88.2 us -> 1.9 us  [on_device(): received = lax.ppermute(for_partner, 'screen', [(0, 1), (1, 0)])]
    all_gather x0 -> x1, waiting for transfers between devices: none -> 32.4 us  [on_device(): bricks = lax.all_gather(layers, 'depth')]
    all_to_all x1 -> x0, waiting for transfers between devices: 22.8 us -> none  [on_device(): lax.all_to_all(outgoing, ('depth', 'screen'), split_axis=0, concat_axis=0...]
    gather x2 -> x5, local copies, waits for them, and re-layouts: 3.07 us -> 17 us  [the longest x1 4.79 us: composite_rows(): jnp.take_along_axis(covered, front_c[:, None], axis=1)[:, 0] & (back >= 1)]
    unnamed x0 -> x1, blocking collectives: none -> 13.9 us
    select_n x10 -> x4, other arithmetic: 9.98 us -> 1.76 us  [the longest x1 1.43 us: composite_rows(): front_rows = jnp.where(front_cov[:, None, None], front_rows, 0.0)]
    ppermute x3 -> x1, starting transfers between devices: 7.59 us -> 0.07 us  [on_device(): received = lax.ppermute(for_partner, 'screen', [(0, 1), (1, 0)])]
    all_to_all x1 -> x0, starting transfers between devices: 5.41 us -> none  [on_device(): lax.all_to_all(outgoing, ('depth', 'screen'), split_axis=0, concat_axis=0...]
  transfers between devices with their start and end apart: 4 -> 2, of which waited for: 4 -> 2; matrix products, arithmetic and copies ran while one was open for 1% -> 12% of each run, Pallas kernels for 0% -> 0%
where the time goes in v1:
time: 127 us
  waiting for transfers between devices  34.3 us (27%)
  matrix products  30 us (24%)
  local copies, waits for them, and re-layouts  28.2 us (22%)
  between operations  15.6 us (12%)
  blocking collectives  13.9 us (11%)
  other arithmetic  4.58 us (4%)
    all_gather x1, waiting for transfers between devices, on_device(): bricks = lax.all_gather(layers, 'depth')  32.4 us
    dot_general x1, matrix products, render_layers(): jnp.einsum('kj,rjp->rkp', below_mask, optical, precision=lax.Precision.HI...  30 us
    unnamed x1, blocking collectives  13.9 us
    gather x1, local copies, waits for them, and re-layouts, composite_rows(): jnp.take_along_axis(covered, front_c[:, None], axis=1)[:, 0] & (back >= 1)  4.79 us
    gather x1, local copies, waits for them, and re-layouts, composite_rows(): front_off = jnp.take_along_axis(offset, front_c[:, None], axis=1)[:, 0]  3.77 us
    gather x1, local copies, waits for them, and re-layouts, composite_rows(): back_off = jnp.take_along_axis(offset, back_c[:, None], axis=1)[:, 0]  3.77 us
    all_gather x1, local copies, waits for them, and re-layouts, on_device(): bricks = lax.all_gather(layers, 'depth')  2.94 us
    gather x1, local copies, waits for them, and re-layouts, composite_rows(): front_rows = jnp.take(flat, front_idx, axis=0)  2.64 us
  transfers between devices with their start and end apart: 2, of which 2 were waited for; matrix products, arithmetic and copies ran while one was open for 12% of the time, Pallas kernels for 0%

profile of v1, /device:TPU:0, one launch (start us, length us, event | category | flops | bytes accessed | tf_op | source)
XLA Modules:
  0.0 126.6 jit_solution(757611200806304633)
XLA Ops:
  6.5 1.4 %fusion.60 = (f32[1]{0:T(128)}, f32[1]{0:T(128)}, f32[1]{0:T(128)}) fusion(f32[3]{0:T(128)} %param.16), kind=kLoop, calls=%fused_computation.118 | loop fusion | bytes 24 | tf_op jit(solution)/shard_map/slice | solution.py:21
  7.9 1.4 %fusion.59 = (f32[1]{0:T(128)}, f32[1]{0:T(128)}, f32[1]{0:T(128)}) fusion(f32[3]{0:T(128)} %param.15), kind=kLoop, calls=%fused_computation.117 | loop fusion | bytes 24 | tf_op jit(solution)/shard_map/slice | solution.py:21
  10.6 1.3 dynamic-slice.8
  11.8 0.6 bitcast_dynamic-update-slice_fusion.1
  12.5 0.1 reshape.219
  12.6 0.6 bitcast_dynamic-update-slice_fusion
  13.9 13.9 %all-reduce.3 = (s32[16]{0:T(128)S(1)}, s32[8,2,1,1]{1,0,3,2:T(8,128)S(1)}) all-reduce(s32[16]{0:T(128)S(1)} %bitcast_dynamic-update-slice_fusion, s32[8,2,1,1]{1,0,3,2:T(8,128)S(1)} %reshape.219), channel_id=5, replica_groups=[2,16]<=[32], use_global_device_ids=true, to_apply=%add.1 | all-reduce | flops 32 | bytes 256
  27.8 0.1 reshape.226
  27.9 0.6 dynamic_slice.20
  28.5 0.6 iota_compare_fusion.1
  29.0 30.0 %fusion.25 = (f32[128,128]{1,0:T(8,128)S(1)}, f32[128,128]{1,0:T(8,128)S(1)}, f32[128,128]{1,0:T(8,128)S(1)}, f32[128,128]{1,0:T(8,128)S(1)}) fusion(f32[1,1,128,128,128]{4,3,2,1,0:T(8,128)} %param.11, f32[]{:T(128)} %bitcast.18, f32[]{:T(128)} %bitcast.17, f32[]{:T(128)} %bitcast.24, f32[]{:T(128)} %bitcast.23, f32[]{:T(128)} %bitcast.21, f32[]{:T(128)} %bitcast.20, ...), kind=kOutput, calls=%fused_computation.37 | convolution fusion | flops 3309256704 | bytes 8650780 | tf_op jit(solution)/shard_map/kj,rjp->rkp/dot_general | solution.py:16
  59.0 0.8 maximum_select_fusion
  59.8 0.1 reshape.225
  59.9 0.8 dynamic_slice.17
  60.7 0.2 dynamic-slice_reduce_fusion
  60.9 0.8 fusion.54
  61.7 0.2 select_reduce_fusion
  62.0 3.8 %gather_fusion.1 = s32[512]{0:T(512)S(1)} fusion(s32[512,8]{1,0:T(8,128)S(1)} %get-tuple-element.22, s32[512]{0:T(512)S(1)} %bitcast.118), kind=kCustom, calls=%fused_computation.clone | custom fusion | bytes 8192 | tf_op jit(solution)/shard_map/jit(take_along_axis)/gather | solution.py:42
  65.8 3.8 %gather_fusion.3 = s32[512]{0:T(512)S(1)} fusion(s32[512,8]{1,0:T(8,128)S(1)} %get-tuple-element.22, s32[512]{0:T(512)S(1)} %bitcast.119), kind=kCustom, calls=%fused_computation.2.clone | custom fusion | bytes 8192 | tf_op jit(solution)/shard_map/jit(take_along_axis)/gather | solution.py:41
  69.6 0.1 compare_and_fusion
  69.7 4.8 %gather_fusion = pred[512]{0:T(512)(128)(4,1)S(1)} fusion(pred[512,8]{1,0:T(8,128)(4,1)S(1)} %compare_and_fusion, s32[512]{0:T(512)S(1)} %bitcast.117), kind=kCustom, calls=%fused_computation.4 | custom fusion | bytes 5120 | tf_op jit(solution)/shard_map/jit(take_along_axis)/gather | solution.py:43
  74.6 32.4 %all-gather.6.cloned.1.call-done = f32[8,128,4,128]{3,1,2,0:T(8,128)} async-done(((f32[1,128,4,128]{3,1,2,0:T(8,128)}), f32[8,128,4,128]{3,1,2,0:T(8,128)}) %all-gather.6.cloned.1.call-update) | async-done | bytes 2097168 | tf_op jit(solution)/shard_map/all_gather | solution.py:68
  107.0 2.9 %copy.9 = f32[8,128,4,128]{3,2,1,0:T(4,128)S(1)} copy(f32[8,128,4,128]{3,1,2,0:T(8,128)} %all-gather.6.cloned.1.call-done) | data formatting | bytes 4194304 | tf_op jit(solution)/shard_map/all_gather | solution.py:68
  110.0 2.6 %gather_fusion.2 = f32[512,4,128]{2,1,0:T(4,128)} fusion(f32[1024,4,128]{2,1,0:T(4,128)S(1)} %bitcast.120, s32[1024]{0:T(1024)S(1)} %pad_clamp_fusion.1), kind=kCustom, calls=%fused_computation.1.clone | custom fusion | bytes 2099200 | tf_op jit(solution)/shard_map/jit(_take)/gather | solution.py:47
  112.6 2.1 %gather_fusion.4 = f32[512,4,128]{2,1,0:T(4,128)S(1)} fusion(f32[1024,4,128]{2,1,0:T(4,128)S(1)} %bitcast.121, s32[1024]{0:T(1024)S(1)} %pad_clamp_fusion), kind=kCustom, calls=%fused_computation.3.clone | custom fusion | bytes 2099200 | tf_op jit(solution)/shard_map/jit(_take)/gather | solution.py:46
  114.7 1.4 %fusion.30 = f32[512,4,128]{2,0,1:T(8,128)S(1)} fusion(f32[512,4,128]{2,1,0:T(4,128)} %gather_fusion.2, pred[512]{0:T(512)(128)(4,1)S(1)} %get-tuple-element.15, pred[512]{0:T(512)(128)(4,1)S(1)} %get-tuple-element.27), kind=kLoop, calls=%fused_computation.45 | loop fusion | flops 524288 | bytes 2098176 | tf_op jit(solution)/shard_map/jit(_where)/select_n | solution.py:49
  116.1 0.2 fusion.29
  116.3 0.1 exponential_bitcast_fusion
  116.4 0.1 fusion.31
  116.6 1.9 %collective-permute-done = f32[256,4,128]{2,0,1:T(8,128)S(1)} collective-permute-done((f32[256,4,128]{2,0,1:T(8,128)S(1)}, f32[256,4,128]{2,0,1:T(8,128)S(1)}, u32[]{:S(2)}, u32[]{:S(2)}) %collective-permute-start) | collective-permute-done | bytes 524320 | tf_op jit(solution)/shard_map/ppermute | solution.py:79
  118.5 0.1 fusion.33
  118.7 1.1 copy.12
  (20 shorter events, 0.3 us)
Async XLA Ops:
  6.5 100.5 %all-gather.6.cloned.1.call-start = ((), (), s32[]{:S(2)}) async-start(), calls=%async_computation | async-start | bytes 2359296 | tf_op jit(solution)/shard_map/all_gather | solution.py:68
  116.6 2.0 %collective-permute-start = (f32[256,4,128]{2,0,1:T(8,128)S(1)}, f32[256,4,128]{2,0,1:T(8,128)S(1)}, u32[]{:S(2)}, u32[]{:S(2)}) collective-permute-start(f32[256,4,128]{2,0,1:T(8,128)S(1)} %pad_maximum_fusion), channel_id=1, source_target_pairs={{0,1},{1,0},{2,3},{3,2},{4,5},{5,4},{6,7},{7,6},{8,9},{9,8},{10,11... | collective-permute-start | bytes 1572872 | tf_op jit(solution)/shard_map/ppermute | solution.py:79
Sparse Core Ops, SparseCore 0:
  59.9 47.0 all-gather.5

commit v2 on v1

--- a/solution.py
+++ b/solution.py
@@ -28,25 +28,24 @@
     return jnp.where(visible, layers, jnp.zeros_like(layers))
 
 
-def composite_rows(bricks, starts, counts, image_rows):
-    depth_count, brick_rows = bricks.shape[0], bricks.shape[1]
-    flat = bricks.reshape((depth_count * brick_rows,) + bricks.shape[2:])
+def composite_rows(flat, starts, counts, stride, image_rows):
+    depth_count = starts.shape[0]
     offset = image_rows[:, None] - starts[None, :]
     covered = (offset >= 0) & (offset < counts[None, :])
-    depth_ids = jnp.arange(depth_count)[None, :]
+    depth_ids = jnp.arange(depth_count, dtype=jnp.int32)[None, :]
     back = jnp.max(jnp.where(covered, depth_ids, -1), axis=1)
-    any_back = back >= 0
-    back_c = jnp.maximum(back, 0)
-    front_c = jnp.maximum(back - 1, 0)
-    back_off = jnp.take_along_axis(offset, back_c[:, None], axis=1)[:, 0]
-    front_off = jnp.take_along_axis(offset, front_c[:, None], axis=1)[:, 0]
-    front_cov = jnp.take_along_axis(covered, front_c[:, None], axis=1)[:, 0] & (back >= 1)
-    back_idx = back_c * brick_rows + jnp.clip(back_off, 0, brick_rows - 1)
-    front_idx = front_c * brick_rows + jnp.clip(front_off, 0, brick_rows - 1)
-    back_rows = jnp.take(flat, back_idx, axis=0)
-    front_rows = jnp.take(flat, front_idx, axis=0)
-    back_rows = jnp.where(any_back[:, None, None], back_rows, 0.0)
-    front_rows = jnp.where(front_cov[:, None, None], front_rows, 0.0)
+    is_back = depth_ids == back[:, None]
+    is_front = (depth_ids == back[:, None] - 1) & covered
+    back_off = jnp.sum(jnp.where(is_back, offset, 0), axis=1)
+    front_off = jnp.sum(jnp.where(is_front, offset, 0), axis=1)
+    has_front = jnp.any(is_front, axis=1)
+    has_back = back >= 0
+    back_idx = jnp.where(has_back, back * stride + back_off, 0)
+    front_idx = jnp.where(has_front, (back - 1) * stride + front_off, 0)
+    back_rows = jnp.take(flat, back_idx, axis=0, mode="clip")
+    front_rows = jnp.take(flat, front_idx, axis=0, mode="clip")
+    back_rows = jnp.where(has_back[:, None, None], back_rows, 0.0)
+    front_rows = jnp.where(has_front[:, None, None], front_rows, 0.0)
     front_depth = front_rows[:, 3:4, :]
     colours = front_rows[:, :3, :] + jnp.exp(-front_depth) * back_rows[:, :3, :]
     opacity = 1.0 - jnp.exp(-(front_depth + back_rows[:, 3:4, :]))
@@ -61,19 +60,23 @@
     image_total = tile_source.shape[0]
     half_rows = image_total // screen_count
     owner_rows = image_total // (depth_count * screen_count)
-    my_starts = foot_start.reshape(depth_count, screen_count)
-    my_counts = foot_rows.reshape(depth_count, screen_count)
-    shown = my_counts[depth_index, screen_index]
+    start = foot_start[0, 0]
+    shown = foot_rows[0, 0]
     layers = render_layers(density[0, 0], shown, extinction[0], colour_slope, colour_offset)
-    bricks = lax.all_gather(layers, "depth")
-    starts = lax.dynamic_index_in_dim(my_starts, screen_index, axis=1, keepdims=False)
-    counts = lax.dynamic_index_in_dim(my_counts, screen_index, axis=1, keepdims=False)
+    brick_rows, channels, pixels = layers.shape
+    lane = lax.broadcasted_iota(jnp.int32, (1, channels, pixels), 2)
+    meta = jnp.where(lane == 0, start, jnp.where(lane == 1, shown, 0)).astype(jnp.float32)
+    stride = brick_rows + 1
+    flat = lax.all_gather(jnp.concatenate([layers, meta], axis=0), "depth", tiled=True)
+    meta_rows = flat.reshape(depth_count, stride, channels, pixels)[:, brick_rows, 0, :2]
+    starts = meta_rows[:, 0].astype(jnp.int32)
+    counts = meta_rows[:, 1].astype(jnp.int32)
     self_owner = depth_index * screen_count + screen_index
     partner_owner = depth_index * screen_count + (1 - screen_index)
     wanted_self = lax.dynamic_slice_in_dim(tile_source, self_owner * owner_rows, owner_rows)
     wanted_partner = lax.dynamic_slice_in_dim(tile_source, partner_owner * owner_rows, owner_rows)
     wanted = jnp.concatenate([wanted_self, wanted_partner])
-    rows = composite_rows(bricks, starts, counts, wanted % half_rows)
+    rows = composite_rows(flat, starts, counts, stride, wanted % half_rows)
     mine = rows[:owner_rows]
     for_partner = rows[owner_rows:]
     received = lax.ppermute(for_partner, "screen", [(0, 1), (1, 0)])
@@ -87,8 +90,8 @@
         mesh=mesh,
         in_specs=(
             P(("runs", "depth"), "screen", None, None, None),
-            P("runs", None),
-            P("runs", None),
+            P(("runs", "depth"), "screen"),
+            P(("runs", "depth"), "screen"),
             P("runs"),
             P(),
             P(),

time: 127 us -> 113 us (0.89)
  waiting for transfers between devices: 34.3 us -> 52.8 us
  local copies, waits for them, and re-layouts: 28.2 us -> 11.7 us
  blocking collectives: 13.9 us -> 0 us
  other arithmetic: 4.58 us -> 2.79 us
    all_gather x1, waiting for transfers between devices: 32.4 us -> 50.9 us  [on_device(): lax.all_gather(jnp.concatenate([layers, meta], axis=0), 'depth', tiled=True)]
    unnamed x1 -> x0, blocking collectives: 13.9 us -> none
    gather x5 -> x2, local copies, waits for them, and re-layouts: 17 us -> 6.21 us  [the longest x1 3.1 us: composite_rows(): back_rows = jnp.take(flat, back_idx, axis=0, mode='clip')]
    all_gather x1 -> x0, local copies, waits for them, and re-layouts: 2.94 us -> none  [on_device(): bricks = lax.all_gather(layers, 'depth')]
    unnamed x6 -> x1, local copies, waits for them, and re-layouts: 2.55 us -> 0.72 us
    select_n x3 -> x5, other arithmetic: 1.65 us -> 0.34 us  [the longest x1 0.16 us: composite_rows(): front_rows = jnp.where(has_front[:, None, None], front_rows, 0.0)]
  transfers between devices with their start and end apart: 2 -> 2, of which waited for: 2 -> 2; matrix products, arithmetic and copies ran while one was open for 12% -> 1% of each run, Pallas kernels for 0% -> 0%
where the time goes in v2:
time: 113 us
  waiting for transfers between devices  52.8 us (47%)
  matrix products  29.9 us (26%)
  between operations  15.5 us (14%)
  local copies, waits for them, and re-layouts  11.7 us (10%)
  other arithmetic  2.79 us (2%)
    all_gather x1, waiting for transfers between devices, on_device(): lax.all_gather(jnp.concatenate([layers, meta], axis=0), 'depth', tiled=True)  50.9 us
    dot_general x1, matrix products, render_layers(): jnp.einsum('kj,rjp->rkp', below_mask, optical, precision=lax.Precision.HI...  29.9 us
    gather x1, local copies, waits for them, and re-layouts, composite_rows(): back_rows = jnp.take(flat, back_idx, axis=0, mode='clip')  3.1 us
    gather x1, local copies, waits for them, and re-layouts, composite_rows(): front_rows = jnp.take(flat, front_idx, axis=0, mode='clip')  3.1 us
  transfers between devices with their start and end apart: 2, of which 2 were waited for; matrix products, arithmetic and copies ran while one was open for 1% of the time, Pallas kernels for 0%

profile of v2, /device:TPU:0, one launch (start us, length us, event | category | flops | bytes accessed | tf_op | source)
XLA Modules:
  0.0 112.8 jit_solution(2861600345667408798)
XLA Ops:
  6.5 0.0 all-gather.2.cloned.1.call-start
  8.5 1.4 %fusion.46 = (f32[1]{0:T(128)}, f32[1]{0:T(128)}, f32[1]{0:T(128)}) fusion(f32[3]{0:T(128)} %param.11), kind=kLoop, calls=%fused_computation.91 | loop fusion | bytes 24 | tf_op jit(solution)/shard_map/slice | solution.py:21
  9.9 1.4 %fusion.47 = (f32[1]{0:T(128)}, f32[1]{0:T(128)}, f32[1]{0:T(128)}) fusion(f32[3]{0:T(128)} %param.12), kind=kLoop, calls=%fused_computation.92 | loop fusion | bytes 24 | tf_op jit(solution)/shard_map/slice | solution.py:21
  11.3 29.9 %fusion.25 = (f32[128,128]{1,0:T(8,128)S(1)}, f32[128,128]{1,0:T(8,128)S(1)}, f32[128,128]{1,0:T(8,128)S(1)}, f32[128,128]{1,0:T(8,128)S(1)}) fusion(f32[1,1,128,128,128]{4,3,2,1,0:T(8,128)} %param.7, f32[]{:T(128)} %bitcast.6, f32[]{:T(128)} %bitcast.5, f32[]{:T(128)} %bitcast.12, f32[]{:T(128)} %bitcast.11, f32[]{:T(128)} %bitcast.9, f32[]{:T(128)} %bitcast.8, ...), kind=kOutput, calls=%fused_computation.34 | convolution fusion | flops 3309256704 | bytes 8650780 | tf_op jit(solution)/shard_map/kj,rjp->rkp/dot_general | solution.py:16
  41.2 0.3 maximum_select_fusion
  41.5 0.8 pad_maximum_fusion.1
  42.3 0.0 all-gather.2.cloned.1.call-update
  42.3 0.8 dynamic_slice.7
  43.1 0.8 fusion.43
  43.9 50.9 %all-gather.2.cloned.1.call-done = f32[1032,4,128]{2,1,0:T(4,128)} async-done(((f32[129,4,128]{2,1,0:T(4,128)}), f32[1032,4,128]{2,1,0:T(4,128)}) %all-gather.2.cloned.1.call-update) | async-done | bytes 2113552 | tf_op jit(solution)/shard_map/all_gather | solution.py:70
  94.8 0.7 slice_bitcast_fusion
  95.5 0.1 copy.15
  95.6 0.1 select_reduce_fusion
  95.7 0.1 fusion.41
  95.8 0.1 fusion.37
  95.9 3.1 %gather_fusion = f32[512,4,128]{2,1,0:T(4,128)S(1)} fusion(f32[1032,4,128]{2,1,0:T(4,128)} %all-gather.2.cloned.1.call-done, s32[1024]{0:T(1024)S(1)} %get-tuple-element.26), kind=kCustom, calls=%fused_computation | custom fusion | bytes 2099200 | tf_op jit(solution)/shard_map/jit(_take)/gather | solution.py:46
  99.0 0.2 copy_select_fusion.1
  99.2 3.1 %gather_fusion.1 = f32[512,4,128]{2,1,0:T(4,128)S(1)} fusion(f32[1032,4,128]{2,1,0:T(4,128)} %all-gather.2.cloned.1.call-done, s32[1024]{0:T(1024)S(1)} %get-tuple-element.25), kind=kCustom, calls=%fused_computation.1 | custom fusion | bytes 2099200 | tf_op jit(solution)/shard_map/jit(_take)/gather | solution.py:45
  102.3 0.2 copy_select_fusion
  102.5 0.1 exponential_bitcast_fusion
  102.6 0.1 fusion.29
  102.7 0.1 collective-permute-start
  102.8 1.9 %collective-permute-done = f32[256,4,128]{2,0,1:T(8,128)S(1)} collective-permute-done((f32[256,4,128]{2,0,1:T(8,128)S(1)}, f32[256,4,128]{2,0,1:T(8,128)S(1)}, u32[]{:S(2)}, u32[]{:S(2)}) %collective-permute-start) | collective-permute-done | bytes 524320 | tf_op jit(solution)/shard_map/ppermute | solution.py:82
  104.7 0.1 fusion.31
  104.8 1.1 %copy.18 = f32[256,4,128]{2,1,0:T(4,128)} copy(f32[256,4,128]{2,0,1:T(8,128)S(1)} %fusion.31) | data formatting | bytes 1048576 | tf_op jit(solution)/shard_map/jit(_where)/select_n | solution.py:84
  (11 shorter events, 0.1 us)
Async XLA Ops:
  6.5 88.2 %all-gather.2.cloned.1.call-start = ((), (), s32[]{:S(2)}) async-start(), calls=%async_computation | async-start | bytes 2377728 | tf_op jit(solution)/shard_map/all_gather | solution.py:70
  102.7 2.0 %collective-permute-start = (f32[256,4,128]{2,0,1:T(8,128)S(1)}, f32[256,4,128]{2,0,1:T(8,128)S(1)}, u32[]{:S(2)}, u32[]{:S(2)}) collective-permute-start(f32[256,4,128]{2,0,1:T(8,128)S(1)} %pad_maximum_fusion), channel_id=1, source_target_pairs={{0,1},{1,0},{2,3},{3,2},{4,5},{5,4},{6,7},{7,6},{8,9},{9,8},{10,11... | collective-permute-start | bytes 1572872 | tf_op jit(solution)/shard_map/ppermute | solution.py:82
Sparse Core Ops, SparseCore 0:
  42.4 52.2 all-gather.1

commit v3 on v2

--- a/solution.py
+++ b/solution.py
@@ -28,20 +28,23 @@
     return jnp.where(visible, layers, jnp.zeros_like(layers))
 
 
-def composite_rows(flat, starts, counts, stride, image_rows):
-    depth_count = starts.shape[0]
+def composite_rows(flat, starts, counts, brick_ids, stride, image_rows):
+    slot_count = starts.shape[0]
     offset = image_rows[:, None] - starts[None, :]
     covered = (offset >= 0) & (offset < counts[None, :])
-    depth_ids = jnp.arange(depth_count, dtype=jnp.int32)[None, :]
+    depth_ids = brick_ids[None, :]
+    slot_ids = jnp.arange(slot_count, dtype=jnp.int32)[None, :]
     back = jnp.max(jnp.where(covered, depth_ids, -1), axis=1)
-    is_back = depth_ids == back[:, None]
+    is_back = (depth_ids == back[:, None]) & covered
     is_front = (depth_ids == back[:, None] - 1) & covered
     back_off = jnp.sum(jnp.where(is_back, offset, 0), axis=1)
     front_off = jnp.sum(jnp.where(is_front, offset, 0), axis=1)
+    back_slot = jnp.sum(jnp.where(is_back, slot_ids, 0), axis=1)
+    front_slot = jnp.sum(jnp.where(is_front, slot_ids, 0), axis=1)
     has_front = jnp.any(is_front, axis=1)
     has_back = back >= 0
-    back_idx = jnp.where(has_back, back * stride + back_off, 0)
-    front_idx = jnp.where(has_front, (back - 1) * stride + front_off, 0)
+    back_idx = jnp.where(has_back, back_slot * stride + back_off, 0)
+    front_idx = jnp.where(has_front, front_slot * stride + front_off, 0)
     back_rows = jnp.take(flat, back_idx, axis=0, mode="clip")
     front_rows = jnp.take(flat, front_idx, axis=0, mode="clip")
     back_rows = jnp.where(has_back[:, None, None], back_rows, 0.0)
@@ -50,6 +53,26 @@
     colours = front_rows[:, :3, :] + jnp.exp(-front_depth) * back_rows[:, :3, :]
     opacity = 1.0 - jnp.exp(-(front_depth + back_rows[:, 3:4, :]))
     return jnp.concatenate([colours, opacity], axis=1)
+
+
+def ring_order(count):
+    return list(range(0, count, 2)) + list(range(count - 1 - count % 2, 0, -2))
+
+
+def ring_gather(own, count):
+    order = ring_order(count)
+    forward = [(order[k], order[(k + 1) % count]) for k in range(count)]
+    backward = [(b, a) for a, b in forward]
+    slots = [own]
+    ahead = own
+    behind = own
+    for step in range(1, count // 2 + 1):
+        ahead = lax.ppermute(ahead, "depth", forward)
+        slots.append(ahead)
+        if 2 * step < count:
+            behind = lax.ppermute(behind, "depth", backward)
+            slots.append(behind)
+    return jnp.concatenate(slots, axis=0)
 
 
 def on_device(density, foot_start, foot_rows, extinction, colour_slope, colour_offset, tile_source):
@@ -65,18 +88,20 @@
     layers = render_layers(density[0, 0], shown, extinction[0], colour_slope, colour_offset)
     brick_rows, channels, pixels = layers.shape
     lane = lax.broadcasted_iota(jnp.int32, (1, channels, pixels), 2)
-    meta = jnp.where(lane == 0, start, jnp.where(lane == 1, shown, 0)).astype(jnp.float32)
+    meta = jnp.where(lane == 0, start, jnp.where(lane == 1, shown, jnp.where(lane == 2, depth_index, 0)))
     stride = brick_rows + 1
-    flat = lax.all_gather(jnp.concatenate([layers, meta], axis=0), "depth", tiled=True)
-    meta_rows = flat.reshape(depth_count, stride, channels, pixels)[:, brick_rows, 0, :2]
+    own = jnp.concatenate([layers, meta.astype(jnp.float32)], axis=0)
+    flat = ring_gather(own, depth_count)
+    meta_rows = flat.reshape(depth_count, stride, channels, pixels)[:, brick_rows, 0, :3]
     starts = meta_rows[:, 0].astype(jnp.int32)
     counts = meta_rows[:, 1].astype(jnp.int32)
+    brick_ids = meta_rows[:, 2].astype(jnp.int32)
     self_owner = depth_index * screen_count + screen_index
     partner_owner = depth_index * screen_count + (1 - screen_index)
     wanted_self = lax.dynamic_slice_in_dim(tile_source, self_owner * owner_rows, owner_rows)
     wanted_partner = lax.dynamic_slice_in_dim(tile_source, partner_owner * owner_rows, owner_rows)
     wanted = jnp.concatenate([wanted_self, wanted_partner])
-    rows = composite_rows(flat, starts, counts, stride, wanted % half_rows)
+    rows = composite_rows(flat, starts, counts, brick_ids, stride, wanted % half_rows)
     mine = rows[:owner_rows]
     for_partner = rows[owner_rows:]
     received = lax.ppermute(for_partner, "screen", [(0, 1), (1, 0)])

time: 113 us -> 74.8 us (0.66)
  waiting for transfers between devices: 52.8 us -> 21.1 us
  between operations: 15.5 us -> 2.16 us
  starting transfers between devices: 0.07 us -> 8.96 us
  local copies, waits for them, and re-layouts: 11.7 us -> 10.2 us
    all_gather x1 -> x0, waiting for transfers between devices: 50.9 us -> none  [on_device(): lax.all_gather(jnp.concatenate([layers, meta], axis=0), 'depth', tiled=True)]
    ppermute x0 -> x7, waiting for transfers between devices: none -> 19.2 us  [the longest x4 17.2 us: ring_gather(): ahead = lax.ppermute(ahead, 'depth', forward)]
    ppermute x0 -> x7, starting transfers between devices: none -> 8.89 us  [the longest x4 8.03 us: ring_gather(): ahead = lax.ppermute(ahead, 'depth', forward)]
  transfers between devices with their start and end apart: 2 -> 8, of which waited for: 2 -> 7; matrix products, arithmetic and copies ran while one was open for 1% -> 2% of each run, Pallas kernels for 0% -> 0%
where the time goes in v3:
time: 74.8 us; the launch traced here: 74.5 us
  matrix products  30 us (40%)
  waiting for transfers between devices  21.1 us (28%)
  local copies, waits for them, and re-layouts  10.2 us (14%)
  starting transfers between devices  8.96 us (12%)
  between operations  2.16 us (3%)
  other arithmetic  2.13 us (3%)
    dot_general x1, matrix products, render_layers(): jnp.einsum('kj,rjp->rkp', below_mask, optical, precision=lax.Precision.HI...  30 us
    ppermute x4, waiting for transfers between devices, ring_gather(): ahead = lax.ppermute(ahead, 'depth', forward)  17.2 us
    ppermute x4, starting transfers between devices, ring_gather(): ahead = lax.ppermute(ahead, 'depth', forward)  8.03 us
    gather x1, local copies, waits for them, and re-layouts, composite_rows(): front_rows = jnp.take(flat, front_idx, axis=0, mode='clip')  3.1 us
    gather x1, local copies, waits for them, and re-layouts, composite_rows(): back_rows = jnp.take(flat, back_idx, axis=0, mode='clip')  2.07 us
    ppermute x3, waiting for transfers between devices, ring_gather(): behind = lax.ppermute(behind, 'depth', backward)  1.99 us
    ppermute x1, waiting for transfers between devices, on_device(): received = lax.ppermute(for_partner, 'screen', [(0, 1), (1, 0)])  1.9 us
  transfers between devices with their start and end apart: 8, of which 7 were waited for; matrix products, arithmetic and copies ran while one was open for 2% of the time, Pallas kernels for 0%

profile of v3, /device:TPU:0, one launch (start us, length us, event | category | flops | bytes accessed | tf_op | source)
XLA Modules:
  0.0 74.5 jit_solution(566342907595654219)
XLA Ops:
  0.0 1.4 %fusion.45 = (f32[1]{0:T(128)}, f32[1]{0:T(128)}, f32[1]{0:T(128)}) fusion(f32[3]{0:T(128)} %param.11), kind=kLoop, calls=%fused_computation.103 | loop fusion | bytes 24 | tf_op jit(solution)/shard_map/slice | solution.py:21
  1.4 1.4 %fusion.46 = (f32[1]{0:T(128)}, f32[1]{0:T(128)}, f32[1]{0:T(128)}) fusion(f32[3]{0:T(128)} %param.12), kind=kLoop, calls=%fused_computation.104 | loop fusion | bytes 24 | tf_op jit(solution)/shard_map/slice | solution.py:21
  4.7 30.0 %fusion.25 = (f32[128,128]{1,0:T(8,128)S(1)}, f32[128,128]{1,0:T(8,128)S(1)}, f32[128,128]{1,0:T(8,128)S(1)}, f32[128,128]{1,0:T(8,128)S(1)}) fusion(f32[1,1,128,128,128]{4,3,2,1,0:T(8,128)} %param.7, f32[]{:T(128)} %bitcast.6, f32[]{:T(128)} %bitcast.5, f32[]{:T(128)} %bitcast.12, f32[]{:T(128)} %bitcast.11, f32[]{:T(128)} %bitcast.9, f32[]{:T(128)} %bitcast.8, ...), kind=kOutput, calls=%fused_computation.34 | convolution fusion | flops 3309256704 | bytes 8650780 | tf_op jit(solution)/shard_map/kj,rjp->rkp/dot_general | solution.py:16
  34.7 0.3 constant_dynamic-update-slice_fusion.8
  35.1 3.1 %collective-permute-start = (f32[129,4,128]{2,1,0:T(4,128)S(1)}, f32[129,4,128]{2,1,0:T(4,128)S(1)}, u32[]{:S(2)}, u32[]{:S(2)}) collective-permute-start(f32[129,4,128]{2,1,0:T(4,128)S(1)} %pad_maximum_fusion.1), channel_id=1, source_target_pairs={{0,4},{4,8},{8,12},{12,14},{14,10},{10,6},{6,2},{2,0},{1,5},{5,9},... | collective-permute-start | bytes 792584 | tf_op jit(solution)/shard_map/ppermute | solution.py:70
  38.2 6.3 %collective-permute-done = f32[129,4,128]{2,1,0:T(4,128)S(1)} collective-permute-done((f32[129,4,128]{2,1,0:T(4,128)S(1)}, f32[129,4,128]{2,1,0:T(4,128)S(1)}, u32[]{:S(2)}, u32[]{:S(2)}) %collective-permute-start) | collective-permute-done | bytes 264224 | tf_op jit(solution)/shard_map/ppermute | solution.py:70
  44.5 1.8 %collective-permute-start.2 = (f32[129,4,128]{2,1,0:T(4,128)S(1)}, f32[129,4,128]{2,1,0:T(4,128)S(1)}, u32[]{:S(2)}, u32[]{:S(2)}) collective-permute-start(f32[129,4,128]{2,1,0:T(4,128)S(1)} %collective-permute-done), channel_id=1, source_target_pairs={{0,4},{4,8},{8,12},{12,14},{14,10},{10,6},{6,2},{2,0},{1,5},{5,9},... | collective-permute-start | bytes 792584 | tf_op jit(solution)/shard_map/ppermute | solution.py:70
  46.3 0.8 %dynamic_slice.7 = s32[256]{0:T(256)S(1)} dynamic-slice(s32[4096]{0:T(1024)} %param.13, s32[]{:T(128)S(6)} %select_n.120), dynamic_slice_sizes={256} | dynamic-slice | bytes 2052 | tf_op jit(solution)/shard_map/dynamic_slice | solution.py:102
  47.0 0.8 %fusion.41 = (pred[256]{0:T(512)(128)(4,1)S(1)}, s32[256]{0:T(256)S(1)}) fusion(s32[]{:T(128)S(6)} %axis_index.25, s32[4096]{0:T(1024)} %param.13, s32[]{:T(128)S(6)} %select_n.113), kind=kLoop, calls=%fused_computation.93 | loop fusion | flops 4096 | bytes 2312 | tf_op jit(solution)/shard_map/eq | solution.py:108
  47.8 0.3 collective-permute-start.3
  48.1 3.9 %collective-permute-done.2 = f32[129,4,128]{2,1,0:T(4,128)S(1)} collective-permute-done((f32[129,4,128]{2,1,0:T(4,128)S(1)}, f32[129,4,128]{2,1,0:T(4,128)S(1)}, u32[]{:S(2)}, u32[]{:S(2)}) %collective-permute-start.2) | collective-permute-done | bytes 264224 | tf_op jit(solution)/shard_map/ppermute | solution.py:70
  52.0 1.5 %collective-permute-start.4 = (f32[129,4,128]{2,1,0:T(4,128)S(1)}, f32[129,4,128]{2,1,0:T(4,128)S(1)}, u32[]{:S(2)}, u32[]{:S(2)}) collective-permute-start(f32[129,4,128]{2,1,0:T(4,128)S(1)} %collective-permute-done.2), channel_id=1, source_target_pairs={{0,4},{4,8},{8,12},{12,14},{14,10},{10,6},{6,2},{2,0},{1,5},{5,9},... | collective-permute-start | bytes 792584 | tf_op jit(solution)/shard_map/ppermute | solution.py:70
  53.6 1.2 %collective-permute-done.3 = f32[129,4,128]{2,1,0:T(4,128)S(1)} collective-permute-done((f32[129,4,128]{2,1,0:T(4,128)S(1)}, f32[129,4,128]{2,1,0:T(4,128)S(1)}, u32[]{:S(2)}, u32[]{:S(2)}) %collective-permute-start.3) | collective-permute-done | bytes 264224 | tf_op jit(solution)/shard_map/ppermute | solution.py:73
  54.8 0.6 collective-permute-start.5
  55.4 3.2 %collective-permute-done.4 = f32[129,4,128]{2,1,0:T(4,128)S(1)} collective-permute-done((f32[129,4,128]{2,1,0:T(4,128)S(1)}, f32[129,4,128]{2,1,0:T(4,128)S(1)}, u32[]{:S(2)}, u32[]{:S(2)}) %collective-permute-start.4) | collective-permute-done | bytes 264224 | tf_op jit(solution)/shard_map/ppermute | solution.py:70
  58.6 1.7 %collective-permute-start.6 = (f32[129,4,128]{2,1,0:T(4,128)S(1)}, f32[129,4,128]{2,1,0:T(4,128)S(1)}, u32[]{:S(2)}, u32[]{:S(2)}) collective-permute-start(f32[129,4,128]{2,1,0:T(4,128)S(1)} %collective-permute-done.4), channel_id=1, source_target_pairs={{0,4},{4,8},{8,12},{12,14},{14,10},{10,6},{6,2},{2,0},{1,5},{5,9},... | collective-permute-start | bytes 792584 | tf_op jit(solution)/shard_map/ppermute | solution.py:70
  60.4 0.8 %collective-permute-done.5 = f32[129,4,128]{2,1,0:T(4,128)S(1)} collective-permute-done((f32[129,4,128]{2,1,0:T(4,128)S(1)}, f32[129,4,128]{2,1,0:T(4,128)S(1)}, u32[]{:S(2)}, u32[]{:S(2)}) %collective-permute-start.5) | collective-permute-done | bytes 264224 | tf_op jit(solution)/shard_map/ppermute | solution.py:73
  61.2 3.8 %collective-permute-done.6 = f32[129,4,128]{2,1,0:T(4,128)S(1)} collective-permute-done((f32[129,4,128]{2,1,0:T(4,128)S(1)}, f32[129,4,128]{2,1,0:T(4,128)S(1)}, u32[]{:S(2)}, u32[]{:S(2)}) %collective-permute-start.6) | collective-permute-done | bytes 264224 | tf_op jit(solution)/shard_map/ppermute | solution.py:70
  65.1 0.1 copy.13
  65.2 0.1 select_reduce_fusion.2
  65.3 0.1 fusion.44
  65.4 0.1 select_reduce_fusion.1
  65.5 2.1 %gather_fusion.1 = f32[512,4,128]{2,1,0:T(4,128)S(1)} fusion(f32[1032,4,128]{2,1,0:T(4,128)S(1)} %constant_dynamic-update-slice_fusion, s32[1024]{0:T(1024)S(1)} %pad_clamp_fusion), kind=kCustom, calls=%fused_computation.1 | custom fusion | bytes 2099200 | tf_op jit(solution)/shard_map/jit(_take)/gather | solution.py:48
  67.6 3.1 %gather_fusion = f32[512,4,128]{2,1,0:T(4,128)S(1)} fusion(f32[1032,4,128]{2,1,0:T(4,128)} %copy-done, s32[1024]{0:T(1024)S(1)} %pad_clamp_fusion.1), kind=kCustom, calls=%fused_computation | custom fusion | bytes 2099200 | tf_op jit(solution)/shard_map/jit(_take)/gather | solution.py:49
  70.7 0.2 copy_select_fusion.1
  70.9 0.2 copy_select_fusion
  71.1 0.1 exponential_bitcast_fusion
  71.1 0.1 fusion.29
  71.3 0.1 collective-permute-start.7
  71.4 1.9 %collective-permute-done.7 = f32[256,4,128]{2,0,1:T(8,128)S(1)} collective-permute-done((f32[256,4,128]{2,0,1:T(8,128)S(1)}, f32[256,4,128]{2,0,1:T(8,128)S(1)}, u32[]{:S(2)}, u32[]{:S(2)}) %collective-permute-start.7) | collective-permute-done | bytes 524320 | tf_op jit(solution)/shard_map/ppermute | solution.py:107
  73.3 0.1 fusion.31
  73.4 1.1 %copy.16 = f32[256,4,128]{2,1,0:T(4,128)} copy(f32[256,4,128]{2,0,1:T(8,128)S(1)} %fusion.31) | data formatting | bytes 1048576 | tf_op jit(solution)/shard_map/jit(_where)/select_n | solution.py:109
  (25 shorter events, 0.5 us)
Async XLA Ops:
  35.1 9.4 %collective-permute-start = (f32[129,4,128]{2,1,0:T(4,128)S(1)}, f32[129,4,128]{2,1,0:T(4,128)S(1)}, u32[]{:S(2)}, u32[]{:S(2)}) collective-permute-start(f32[129,4,128]{2,1,0:T(4,128)S(1)} %pad_maximum_fusion.1), channel_id=1, source_target_pairs={{0,4},{4,8},{8,12},{12,14},{14,10},{10,6},{6,2},{2,0},{1,5},{5,9},... | collective-permute-start | bytes 792584 | tf_op jit(solution)/shard_map/ppermute | solution.py:70
  38.2 9.6 %collective-permute-start.1 = (f32[129,4,128]{2,1,0:T(4,128)S(1)}, f32[129,4,128]{2,1,0:T(4,128)S(1)}, u32[]{:S(2)}, u32[]{:S(2)}) collective-permute-start(f32[129,4,128]{2,1,0:T(4,128)S(1)} %pad_maximum_fusion.1), channel_id=1, source_target_pairs={{4,0},{8,4},{12,8},{14,12},{10,14},{6,10},{2,6},{0,2},{5,1},{9,5},... | collective-permute-start | bytes 792584 | tf_op jit(solution)/shard_map/ppermute | solution.py:73
  44.5 7.5 %collective-permute-start.2 = (f32[129,4,128]{2,1,0:T(4,128)S(1)}, f32[129,4,128]{2,1,0:T(4,128)S(1)}, u32[]{:S(2)}, u32[]{:S(2)}) collective-permute-start(f32[129,4,128]{2,1,0:T(4,128)S(1)} %collective-permute-done), channel_id=1, source_target_pairs={{0,4},{4,8},{8,12},{12,14},{14,10},{10,6},{6,2},{2,0},{1,5},{5,9},... | collective-permute-start | bytes 792584 | tf_op jit(solution)/shard_map/ppermute | solution.py:70
  47.8 7.0 %collective-permute-start.3 = (f32[129,4,128]{2,1,0:T(4,128)S(1)}, f32[129,4,128]{2,1,0:T(4,128)S(1)}, u32[]{:S(2)}, u32[]{:S(2)}) collective-permute-start(f32[129,4,128]{2,1,0:T(4,128)S(1)} %collective-permute-done.1), channel_id=1, source_target_pairs={{4,0},{8,4},{12,8},{14,12},{10,14},{6,10},{2,6},{0,2},{5,1},{9,5},... | collective-permute-start | bytes 792584 | tf_op jit(solution)/shard_map/ppermute | solution.py:73
  52.0 6.6 %collective-permute-start.4 = (f32[129,4,128]{2,1,0:T(4,128)S(1)}, f32[129,4,128]{2,1,0:T(4,128)S(1)}, u32[]{:S(2)}, u32[]{:S(2)}) collective-permute-start(f32[129,4,128]{2,1,0:T(4,128)S(1)} %collective-permute-done.2), channel_id=1, source_target_pairs={{0,4},{4,8},{8,12},{12,14},{14,10},{10,6},{6,2},{2,0},{1,5},{5,9},... | collective-permute-start | bytes 792584 | tf_op jit(solution)/shard_map/ppermute | solution.py:70
  54.8 6.4 %collective-permute-start.5 = (f32[129,4,128]{2,1,0:T(4,128)S(1)}, f32[129,4,128]{2,1,0:T(4,128)S(1)}, u32[]{:S(2)}, u32[]{:S(2)}) collective-permute-start(f32[129,4,128]{2,1,0:T(4,128)S(1)} %collective-permute-done.3), channel_id=1, source_target_pairs={{4,0},{8,4},{12,8},{14,12},{10,14},{6,10},{2,6},{0,2},{5,1},{9,5},... | collective-permute-start | bytes 792584 | tf_op jit(solution)/shard_map/ppermute | solution.py:73
  58.6 6.4 %collective-permute-start.6 = (f32[129,4,128]{2,1,0:T(4,128)S(1)}, f32[129,4,128]{2,1,0:T(4,128)S(1)}, u32[]{:S(2)}, u32[]{:S(2)}) collective-permute-start(f32[129,4,128]{2,1,0:T(4,128)S(1)} %collective-permute-done.4), channel_id=1, source_target_pairs={{0,4},{4,8},{8,12},{12,14},{14,10},{10,6},{6,2},{2,0},{1,5},{5,9},... | collective-permute-start | bytes 792584 | tf_op jit(solution)/shard_map/ppermute | solution.py:70
  65.1 2.5 %copy-start = (f32[1032,4,128]{2,1,0:T(4,128)}, f32[1032,4,128]{2,1,0:T(4,128)S(1)}, u32[]{:S(2)}) copy-start(f32[1032,4,128]{2,1,0:T(4,128)S(1)} %constant_dynamic-update-slice_fusion) | copy-start | bytes 6340612
  71.3 2.0 %collective-permute-start.7 = (f32[256,4,128]{2,0,1:T(8,128)S(1)}, f32[256,4,128]{2,0,1:T(8,128)S(1)}, u32[]{:S(2)}, u32[]{:S(2)}) collective-permute-start(f32[256,4,128]{2,0,1:T(8,128)S(1)} %pad_maximum_fusion), channel_id=1, source_target_pairs={{0,1},{1,0},{2,3},{3,2},{4,5},{5,4},{6,7},{7,6},{8,9},{9,8},{10,11... | collective-permute-start | bytes 1572872 | tf_op jit(solution)/shard_map/ppermute | solution.py:107

commit v4 on v3

--- a/solution.py
+++ b/solution.py
@@ -2,30 +2,58 @@
 import jax.numpy as jnp
 from jax import lax
 from jax.sharding import PartitionSpec as P
+from jax.experimental import pallas as pl
+from jax.experimental.pallas import tpu as pltpu
 
 BLK = 256
 
 
-def render_layers(density_block, shown_rows, absorb, colour_slope, colour_offset):
-    brick_rows, sample_count, pixels = density_block.shape
-    optical = absorb * jax.nn.softplus(density_block) / sample_count
+def render_kernel(params_ref, density_ref, out_ref):
+    block_rows, sample_count, pixels = density_ref.shape
+    absorb = params_ref[0]
+    shown = params_ref[7]
     below_mask = (
         lax.broadcasted_iota(jnp.int32, (sample_count, sample_count), 0)
         > lax.broadcasted_iota(jnp.int32, (sample_count, sample_count), 1)
     ).astype(jnp.float32)
-    ahead_sum = jnp.einsum("kj,rjp->rkp", below_mask, optical, precision=lax.Precision.HIGHEST)
-    depth_sum = jnp.sum(optical, axis=1)
-    weight = jnp.exp(-ahead_sum) * (1.0 - jnp.exp(-optical))
-    colours = [
-        jnp.sum(
-            weight * jax.nn.sigmoid(colour_slope[channel] * density_block + colour_offset[channel]),
-            axis=1,
-        )
-        for channel in range(3)
-    ]
-    layers = jnp.stack(colours + [depth_sum], axis=1)
-    visible = (jnp.arange(brick_rows) < shown_rows)[:, None, None]
-    return jnp.where(visible, layers, jnp.zeros_like(layers))
+    first_row = pl.program_id(0) * block_rows
+
+    def one_row(row, carry):
+        values = density_ref[row]
+        optical = absorb * jax.nn.softplus(values) / sample_count
+        ahead_sum = jnp.dot(below_mask, optical, precision=lax.Precision.HIGHEST,
+                            preferred_element_type=jnp.float32)
+        weight = jnp.exp(-ahead_sum) * (1.0 - jnp.exp(-optical))
+        parts = [
+            jnp.sum(weight * jax.nn.sigmoid(params_ref[1 + channel] * values + params_ref[4 + channel]),
+                    axis=0, keepdims=True)
+            for channel in range(3)
+        ]
+        parts.append(jnp.sum(optical, axis=0, keepdims=True))
+        layer = jnp.concatenate(parts, axis=0)
+        visible = (first_row + row).astype(jnp.float32) < shown
+        out_ref[row] = jnp.where(visible, layer, 0.0)
+        return carry
+
+    lax.fori_loop(0, block_rows, one_row, 0)
+
+
+def render_layers(density_block, shown_rows, absorb, colour_slope, colour_offset, block_rows=8):
+    brick_rows, sample_count, pixels = density_block.shape
+    params = jnp.concatenate([
+        absorb.reshape(1), colour_slope, colour_offset,
+        shown_rows.astype(jnp.float32).reshape(1),
+    ])
+    return pl.pallas_call(
+        render_kernel,
+        grid=(brick_rows // block_rows,),
+        in_specs=[
+            pl.BlockSpec(memory_space=pltpu.SMEM),
+            pl.BlockSpec((block_rows, sample_count, pixels), lambda i: (i, 0, 0)),
+        ],
+        out_specs=pl.BlockSpec((block_rows, 4, pixels), lambda i: (i, 0, 0)),
+        out_shape=jax.ShapeDtypeStruct((brick_rows, 4, pixels), jnp.float32),
+    )(params, density_block)
 
 
 def composite_rows(flat, starts, counts, brick_ids, stride, image_rows):

time: 74.8 us -> 87.2 us (1.17)
  Pallas kernels: 0 us -> 37.5 us
  matrix products: 30 us -> 0 us
  other arithmetic: 2.13 us -> 9.96 us
  local copies, waits for them, and re-layouts: 10.2 us -> 7.26 us
    pallas_call x0 -> x1, Pallas kernels: none -> 37.5 us  [render_layers(): pl.pallas_call(render_kernel, grid=(brick_rows // block_rows,), in_specs=...]
    dot_general x1 -> x0, matrix products: 30 us -> none  [render_layers(): jnp.einsum('kj,rjp->rkp', below_mask, optical, precision=lax.Precision.HI...]
    slice x2 -> x0, local copies, waits for them, and re-layouts: 2.74 us -> none  [the longest x1 1.38 us: render_layers(): colour_slope[channel] * density_block + colour_offset[channel]]
    select_n x1, other arithmetic: 0.16 us -> 1.75 us  [composite_rows(): back_rows = jnp.where(has_back[:, None, None], back_rows, 0.0)]
    select_n x1, other arithmetic: 0.16 us -> 1.75 us  [composite_rows(): front_rows = jnp.where(has_front[:, None, None], front_rows, 0.0)]
    select_n x1, other arithmetic: 0.11 us -> 1.63 us  [on_device(): return jnp.where(in_my_half[:, None, None], mine, received)]
    concatenate x0 -> x1, other arithmetic: none -> 1.25 us  [render_layers(): jnp.concatenate([absorb.reshape(1), colour_slope, colour_offset, shown_ro...]
    select_n x1 -> x0, local copies, waits for them, and re-layouts: 1.13 us -> none  [on_device(): return jnp.where(in_my_half[:, None, None], mine, received)]
where the time goes in v4:
time: 87.2 us; the launch traced here: 86.9 us
  Pallas kernels  37.5 us (43%)
  waiting for transfers between devices  21.1 us (24%)
  other arithmetic  9.96 us (11%)
  starting transfers between devices  8.96 us (10%)
  local copies, waits for them, and re-layouts  7.26 us (8%)
  between operations  2.14 us (2%)
    pallas_call x1, Pallas kernels, render_layers(): pl.pallas_call(render_kernel, grid=(brick_rows // block_rows,), in_specs=...  37.5 us
    ppermute x4, waiting for transfers between devices, ring_gather(): ahead = lax.ppermute(ahead, 'depth', forward)  17.2 us
    ppermute x4, starting transfers between devices, ring_gather(): ahead = lax.ppermute(ahead, 'depth', forward)  8.05 us
    gather x1, local copies, waits for them, and re-layouts, composite_rows(): front_rows = jnp.take(flat, front_idx, axis=0, mode='clip')  3.1 us
    gather x1, local copies, waits for them, and re-layouts, composite_rows(): back_rows = jnp.take(flat, back_idx, axis=0, mode='clip')  2.07 us
    ppermute x3, waiting for transfers between devices, ring_gather(): behind = lax.ppermute(behind, 'depth', backward)  1.99 us
    ppermute x1, waiting for transfers between devices, on_device(): received = lax.ppermute(for_partner, 'screen', [(0, 1), (1, 0)])  1.9 us
    select_n x1, other arithmetic, composite_rows(): front_rows = jnp.where(has_front[:, None, None], front_rows, 0.0)  1.75 us
  transfers between devices with their start and end apart: 8, of which 7 were waited for; matrix products, arithmetic and copies ran while one was open for 2% of the time, Pallas kernels for 0%

profile of v4, /device:TPU:0, one launch (start us, length us, event | category | flops | bytes accessed | tf_op | source)
XLA Modules:
  0.0 86.9 jit_solution(4765773895578899542)
XLA Ops:
  1.3 1.3 %pad_maximum_fusion.2.params_ref = f32[8]{0:T(128)} fusion(f32[1]{0:T(128)} %bitcast.1, f32[3]{0:T(128)} %param.12, f32[3]{0:T(128)} %param.11, f32[1]{0:T(128)S(6)} %copy.23), kind=kLoop, calls=%fused_computation.54 | loop fusion | flops 24 | bytes 64 | tf_op jit(solution)/shard_map/concatenate | solution.py:43
  2.6 37.5 %shard_map.73 = f32[128,4,128]{2,1,0:T(4,128)} custom-call(f32[8]{0:T(128)} %pad_maximum_fusion.2.params_ref, f32[128,128,128]{2,1,0:T(8,128)} %bitcast.17), custom_call_target="tpu_custom_call" | custom-call | tf_op jit(solution)/shard_map/pallas_call | solution.py:47
  40.0 1.0 %constant_dynamic-update-slice_fusion.8 = f32[1032,4,128]{2,1,0:T(4,128)S(1)} fusion(f32[128,4,128]{2,1,0:T(4,128)} %shard_map.73), kind=kLoop, calls=%fused_computation.28 | loop fusion | bytes 524288
  41.7 1.0 %pad_maximum_fusion.1 = f32[129,4,128]{2,1,0:T(4,128)S(1)} fusion(f32[1,4,128]{2,1,0:T(4,128)S(1)} %get-tuple-element.18, f32[128,4,128]{2,1,0:T(4,128)} %shard_map.73), kind=kLoop, calls=%fused_computation.11 | loop fusion | flops 66048 | bytes 528384 | tf_op jit(solution)/shard_map/concatenate | solution.py:121
  42.7 3.1 %collective-permute-start = (f32[129,4,128]{2,1,0:T(4,128)S(1)}, f32[129,4,128]{2,1,0:T(4,128)S(1)}, u32[]{:S(2)}, u32[]{:S(2)}) collective-permute-start(f32[129,4,128]{2,1,0:T(4,128)S(1)} %pad_maximum_fusion.1), channel_id=1, source_target_pairs={{0,4},{4,8},{8,12},{12,14},{14,10},{10,6},{6,2},{2,0},{1,5},{5,9},... | collective-permute-start | bytes 792584 | tf_op jit(solution)/shard_map/ppermute | solution.py:98
  45.8 6.3 %collective-permute-done = f32[129,4,128]{2,1,0:T(4,128)S(1)} collective-permute-done((f32[129,4,128]{2,1,0:T(4,128)S(1)}, f32[129,4,128]{2,1,0:T(4,128)S(1)}, u32[]{:S(2)}, u32[]{:S(2)}) %collective-permute-start) | collective-permute-done | bytes 264224 | tf_op jit(solution)/shard_map/ppermute | solution.py:98
  52.0 1.8 %collective-permute-start.2 = (f32[129,4,128]{2,1,0:T(4,128)S(1)}, f32[129,4,128]{2,1,0:T(4,128)S(1)}, u32[]{:S(2)}, u32[]{:S(2)}) collective-permute-start(f32[129,4,128]{2,1,0:T(4,128)S(1)} %collective-permute-done), channel_id=1, source_target_pairs={{0,4},{4,8},{8,12},{12,14},{14,10},{10,6},{6,2},{2,0},{1,5},{5,9},... | collective-permute-start | bytes 792584 | tf_op jit(solution)/shard_map/ppermute | solution.py:98
  53.8 0.8 dynamic_slice.7
  54.6 0.8 fusion.8
  55.4 0.3 collective-permute-start.3
  55.7 3.9 %collective-permute-done.2 = f32[129,4,128]{2,1,0:T(4,128)S(1)} collective-permute-done((f32[129,4,128]{2,1,0:T(4,128)S(1)}, f32[129,4,128]{2,1,0:T(4,128)S(1)}, u32[]{:S(2)}, u32[]{:S(2)}) %collective-permute-start.2) | collective-permute-done | bytes 264224 | tf_op jit(solution)/shard_map/ppermute | solution.py:98
  59.6 1.5 %collective-permute-start.4 = (f32[129,4,128]{2,1,0:T(4,128)S(1)}, f32[129,4,128]{2,1,0:T(4,128)S(1)}, u32[]{:S(2)}, u32[]{:S(2)}) collective-permute-start(f32[129,4,128]{2,1,0:T(4,128)S(1)} %collective-permute-done.2), channel_id=1, source_target_pairs={{0,4},{4,8},{8,12},{12,14},{14,10},{10,6},{6,2},{2,0},{1,5},{5,9},... | collective-permute-start | bytes 792584 | tf_op jit(solution)/shard_map/ppermute | solution.py:98
  61.1 1.2 %collective-permute-done.3 = f32[129,4,128]{2,1,0:T(4,128)S(1)} collective-permute-done((f32[129,4,128]{2,1,0:T(4,128)S(1)}, f32[129,4,128]{2,1,0:T(4,128)S(1)}, u32[]{:S(2)}, u32[]{:S(2)}) %collective-permute-start.3) | collective-permute-done | bytes 264224 | tf_op jit(solution)/shard_map/ppermute | solution.py:101
  62.4 0.6 collective-permute-start.5
  63.0 3.2 %collective-permute-done.4 = f32[129,4,128]{2,1,0:T(4,128)S(1)} collective-permute-done((f32[129,4,128]{2,1,0:T(4,128)S(1)}, f32[129,4,128]{2,1,0:T(4,128)S(1)}, u32[]{:S(2)}, u32[]{:S(2)}) %collective-permute-start.4) | collective-permute-done | bytes 264224 | tf_op jit(solution)/shard_map/ppermute | solution.py:98
  66.2 1.7 %collective-permute-start.6 = (f32[129,4,128]{2,1,0:T(4,128)S(1)}, f32[129,4,128]{2,1,0:T(4,128)S(1)}, u32[]{:S(2)}, u32[]{:S(2)}) collective-permute-start(f32[129,4,128]{2,1,0:T(4,128)S(1)} %collective-permute-done.4), channel_id=1, source_target_pairs={{0,4},{4,8},{8,12},{12,14},{14,10},{10,6},{6,2},{2,0},{1,5},{5,9},... | collective-permute-start | bytes 792584 | tf_op jit(solution)/shard_map/ppermute | solution.py:98
  68.0 0.8 collective-permute-done.5
  68.8 3.8 %collective-permute-done.6 = f32[129,4,128]{2,1,0:T(4,128)S(1)} collective-permute-done((f32[129,4,128]{2,1,0:T(4,128)S(1)}, f32[129,4,128]{2,1,0:T(4,128)S(1)}, u32[]{:S(2)}, u32[]{:S(2)}) %collective-permute-start.6) | collective-permute-done | bytes 264224 | tf_op jit(solution)/shard_map/ppermute | solution.py:98
  72.7 0.1 copy.12
  72.7 0.1 select_reduce_fusion.2
  72.8 0.1 fusion.9
  72.9 0.1 select_reduce_fusion.1
  73.1 2.1 %gather_fusion.1 = f32[512,4,128]{2,1,0:T(4,128)S(1)} fusion(f32[1032,4,128]{2,1,0:T(4,128)S(1)} %constant_dynamic-update-slice_fusion, s32[1024]{0:T(1024)S(1)} %pad_clamp_fusion), kind=kCustom, calls=%fused_computation.1 | custom fusion | bytes 2099200 | tf_op jit(solution)/shard_map/jit(_take)/gather | solution.py:76
  75.2 3.1 %gather_fusion = f32[512,4,128]{2,1,0:T(4,128)S(1)} fusion(f32[1032,4,128]{2,1,0:T(4,128)} %copy-done, s32[1024]{0:T(1024)S(1)} %pad_clamp_fusion.1), kind=kCustom, calls=%fused_computation | custom fusion | bytes 2099200 | tf_op jit(solution)/shard_map/jit(_take)/gather | solution.py:77
  78.3 1.8 %broadcast_select_fusion.1 = f32[512,4,128]{2,1,0:T(4,128)S(1)} fusion(f32[512,4,128]{2,1,0:T(4,128)S(1)} %gather_fusion, pred[512]{0:T(512)(128)(4,1)S(1)} %get-tuple-element.13), kind=kLoop, calls=%fused_computation.10 | loop fusion | flops 262144 | bytes 2097664 | tf_op jit(solution)/shard_map/jit(_where)/select_n | solution.py:79
  80.0 1.8 %broadcast_select_fusion = f32[512,4,128]{2,1,0:T(4,128)S(1)} fusion(f32[512,4,128]{2,1,0:T(4,128)S(1)} %gather_fusion.1, pred[512]{0:T(512)(128)(4,1)S(1)} %get-tuple-element.16), kind=kLoop, calls=%fused_computation.9 | loop fusion | flops 262144 | bytes 2097664 | tf_op jit(solution)/shard_map/jit(_where)/select_n | solution.py:78
  81.8 0.8 negate_exponential_fusion
  82.7 0.4 fusion
  83.1 0.2 pad_maximum_fusion
  83.3 0.1 collective-permute-start.7
  83.4 1.9 %collective-permute-done.7 = f32[256,4,128]{2,1,0:T(4,128)S(1)} collective-permute-done((f32[256,4,128]{2,1,0:T(4,128)S(1)}, f32[256,4,128]{2,1,0:T(4,128)S(1)}, u32[]{:S(2)}, u32[]{:S(2)}) %collective-permute-start.7) | collective-permute-done | bytes 524320 | tf_op jit(solution)/shard_map/ppermute | solution.py:135
  85.3 1.6 %fusion.2 = f32[256,4,128]{2,1,0:T(4,128)} fusion(f32[256,4,128]{2,1,0:T(4,128)S(1)} %collective-permute-done.7, f32[512,3,128]{2,1,0:T(4,128)S(1)} %fusion, f32[512,1,128]{2,1,0:T(1,128)S(1)} %get-tuple-element.20, pred[256]{0:T(512)(128)(4,1)S(1)} %get-tuple-element.11), kind=kLoop, calls=%fused_computation.7 | loop fusion | flops 262144 | bytes 2097408 | tf_op jit(solution)/shard_map/jit(_where)/select_n | solution.py:137
  (23 shorter events, 0.4 us)
Async XLA Ops:
  42.7 9.4 %collective-permute-start = (f32[129,4,128]{2,1,0:T(4,128)S(1)}, f32[129,4,128]{2,1,0:T(4,128)S(1)}, u32[]{:S(2)}, u32[]{:S(2)}) collective-permute-start(f32[129,4,128]{2,1,0:T(4,128)S(1)} %pad_maximum_fusion.1), channel_id=1, source_target_pairs={{0,4},{4,8},{8,12},{12,14},{14,10},{10,6},{6,2},{2,0},{1,5},{5,9},... | collective-permute-start | bytes 792584 | tf_op jit(solution)/shard_map/ppermute | solution.py:98
  45.8 9.6 %collective-permute-start.1 = (f32[129,4,128]{2,1,0:T(4,128)S(1)}, f32[129,4,128]{2,1,0:T(4,128)S(1)}, u32[]{:S(2)}, u32[]{:S(2)}) collective-permute-start(f32[129,4,128]{2,1,0:T(4,128)S(1)} %pad_maximum_fusion.1), channel_id=1, source_target_pairs={{4,0},{8,4},{12,8},{14,12},{10,14},{6,10},{2,6},{0,2},{5,1},{9,5},... | collective-permute-start | bytes 792584 | tf_op jit(solution)/shard_map/ppermute | solution.py:101
  52.0 7.5 %collective-permute-start.2 = (f32[129,4,128]{2,1,0:T(4,128)S(1)}, f32[129,4,128]{2,1,0:T(4,128)S(1)}, u32[]{:S(2)}, u32[]{:S(2)}) collective-permute-start(f32[129,4,128]{2,1,0:T(4,128)S(1)} %collective-permute-done), channel_id=1, source_target_pairs={{0,4},{4,8},{8,12},{12,14},{14,10},{10,6},{6,2},{2,0},{1,5},{5,9},... | collective-permute-start | bytes 792584 | tf_op jit(solution)/shard_map/ppermute | solution.py:98
  55.4 7.0 %collective-permute-start.3 = (f32[129,4,128]{2,1,0:T(4,128)S(1)}, f32[129,4,128]{2,1,0:T(4,128)S(1)}, u32[]{:S(2)}, u32[]{:S(2)}) collective-permute-start(f32[129,4,128]{2,1,0:T(4,128)S(1)} %collective-permute-done.1), channel_id=1, source_target_pairs={{4,0},{8,4},{12,8},{14,12},{10,14},{6,10},{2,6},{0,2},{5,1},{9,5},... | collective-permute-start | bytes 792584 | tf_op jit(solution)/shard_map/ppermute | solution.py:101
  59.6 6.6 %collective-permute-start.4 = (f32[129,4,128]{2,1,0:T(4,128)S(1)}, f32[129,4,128]{2,1,0:T(4,128)S(1)}, u32[]{:S(2)}, u32[]{:S(2)}) collective-permute-start(f32[129,4,128]{2,1,0:T(4,128)S(1)} %collective-permute-done.2), channel_id=1, source_target_pairs={{0,4},{4,8},{8,12},{12,14},{14,10},{10,6},{6,2},{2,0},{1,5},{5,9},... | collective-permute-start | bytes 792584 | tf_op jit(solution)/shard_map/ppermute | solution.py:98
  62.4 6.4 %collective-permute-start.5 = (f32[129,4,128]{2,1,0:T(4,128)S(1)}, f32[129,4,128]{2,1,0:T(4,128)S(1)}, u32[]{:S(2)}, u32[]{:S(2)}) collective-permute-start(f32[129,4,128]{2,1,0:T(4,128)S(1)} %collective-permute-done.3), channel_id=1, source_target_pairs={{4,0},{8,4},{12,8},{14,12},{10,14},{6,10},{2,6},{0,2},{5,1},{9,5},... | collective-permute-start | bytes 792584 | tf_op jit(solution)/shard_map/ppermute | solution.py:101
  66.2 6.4 %collective-permute-start.6 = (f32[129,4,128]{2,1,0:T(4,128)S(1)}, f32[129,4,128]{2,1,0:T(4,128)S(1)}, u32[]{:S(2)}, u32[]{:S(2)}) collective-permute-start(f32[129,4,128]{2,1,0:T(4,128)S(1)} %collective-permute-done.4), channel_id=1, source_target_pairs={{0,4},{4,8},{8,12},{12,14},{14,10},{10,6},{6,2},{2,0},{1,5},{5,9},... | collective-permute-start | bytes 792584 | tf_op jit(solution)/shard_map/ppermute | solution.py:98
  72.6 2.5 %copy-start = (f32[1032,4,128]{2,1,0:T(4,128)}, f32[1032,4,128]{2,1,0:T(4,128)S(1)}, u32[]{:S(2)}) copy-start(f32[1032,4,128]{2,1,0:T(4,128)S(1)} %constant_dynamic-update-slice_fusion) | copy-start | bytes 6340612
  83.3 2.0 %collective-permute-start.7 = (f32[256,4,128]{2,1,0:T(4,128)S(1)}, f32[256,4,128]{2,1,0:T(4,128)S(1)}, u32[]{:S(2)}, u32[]{:S(2)}) collective-permute-start(f32[256,4,128]{2,1,0:T(4,128)S(1)} %pad_maximum_fusion), channel_id=1, source_target_pairs={{0,1},{1,0},{2,3},{3,2},{4,5},{5,4},{6,7},{7,6},{8,9},{9,8},{10,11... | collective-permute-start | bytes 1572872 | tf_op jit(solution)/shard_map/ppermute | solution.py:135

commit v5 on v4

--- a/solution.py
+++ b/solution.py
@@ -9,33 +9,34 @@
 
 
 def render_kernel(params_ref, density_ref, out_ref):
-    block_rows, sample_count, pixels = density_ref.shape
+    block_rows = out_ref.shape[1]
+    pixels = out_ref.shape[2]
+    sample_count = density_ref.shape[0] // block_rows
     absorb = params_ref[0]
+    slopes = [params_ref[1 + channel] for channel in range(3)]
+    offsets = [params_ref[4 + channel] for channel in range(3)]
     shown = params_ref[7]
-    below_mask = (
-        lax.broadcasted_iota(jnp.int32, (sample_count, sample_count), 0)
-        > lax.broadcasted_iota(jnp.int32, (sample_count, sample_count), 1)
-    ).astype(jnp.float32)
-    first_row = pl.program_id(0) * block_rows
 
-    def one_row(row, carry):
-        values = density_ref[row]
+    def one_step(step, carry):
+        transmit, depth_sum = carry[0], carry[1]
+        values = density_ref[pl.ds(step, block_rows, stride=sample_count), :]
         optical = absorb * jax.nn.softplus(values) / sample_count
-        ahead_sum = jnp.dot(below_mask, optical, precision=lax.Precision.HIGHEST,
-                            preferred_element_type=jnp.float32)
-        weight = jnp.exp(-ahead_sum) * (1.0 - jnp.exp(-optical))
-        parts = [
-            jnp.sum(weight * jax.nn.sigmoid(params_ref[1 + channel] * values + params_ref[4 + channel]),
-                    axis=0, keepdims=True)
+        passed = jnp.exp(-optical)
+        weight = transmit * (1.0 - passed)
+        colours = tuple(
+            carry[2 + channel] + weight * jax.nn.sigmoid(slopes[channel] * values + offsets[channel])
             for channel in range(3)
-        ]
-        parts.append(jnp.sum(optical, axis=0, keepdims=True))
-        layer = jnp.concatenate(parts, axis=0)
-        visible = (first_row + row).astype(jnp.float32) < shown
-        out_ref[row] = jnp.where(visible, layer, 0.0)
-        return carry
+        )
+        return (transmit * passed, depth_sum + optical) + colours
 
-    lax.fori_loop(0, block_rows, one_row, 0)
+    zeros = jnp.zeros((block_rows, pixels), jnp.float32)
+    carry = (jnp.ones((block_rows, pixels), jnp.float32), zeros, zeros, zeros, zeros)
+    carry = lax.fori_loop(0, sample_count, one_step, carry, unroll=8)
+    row_ids = pl.program_id(0) * block_rows + lax.broadcasted_iota(jnp.int32, (block_rows, pixels), 0)
+    visible = row_ids.astype(jnp.float32) < shown
+    for channel in range(3):
+        out_ref[channel] = jnp.where(visible, carry[2 + channel], 0.0)
+    out_ref[3] = jnp.where(visible, carry[1], 0.0)
 
 
 def render_layers(density_block, shown_rows, absorb, colour_slope, colour_offset, block_rows=8):
@@ -44,16 +45,17 @@
         absorb.reshape(1), colour_slope, colour_offset,
         shown_rows.astype(jnp.float32).reshape(1),
     ])
-    return pl.pallas_call(
+    planes = pl.pallas_call(
         render_kernel,
         grid=(brick_rows // block_rows,),
         in_specs=[
             pl.BlockSpec(memory_space=pltpu.SMEM),
-            pl.BlockSpec((block_rows, sample_count, pixels), lambda i: (i, 0, 0)),
+            pl.BlockSpec((block_rows * sample_count, pixels), lambda i: (i, 0)),
         ],
-        out_specs=pl.BlockSpec((block_rows, 4, pixels), lambda i: (i, 0, 0)),
-        out_shape=jax.ShapeDtypeStruct((brick_rows, 4, pixels), jnp.float32),
-    )(params, density_block)
+        out_specs=pl.BlockSpec((4, block_rows, pixels), lambda i: (0, i, 0)),
+        out_shape=jax.ShapeDtypeStruct((4, brick_rows, pixels), jnp.float32),
+    )(params, density_block.reshape(brick_rows * sample_count, pixels))
+    return jnp.transpose(planes, (1, 0, 2))
 
 
 def composite_rows(flat, starts, counts, brick_ids, stride, image_rows):

time: 87.2 us -> 77.2 us (0.89)
  Pallas kernels: 37.5 us -> 20.1 us
  local copies, waits for them, and re-layouts: 7.26 us -> 19.7 us
  other arithmetic: 9.96 us -> 3.98 us
    pallas_call x1, Pallas kernels: 37.5 us -> 20.1 us  [render_layers(): pl.pallas_call(render_kernel, grid=(brick_rows // block_rows,), in_specs=...]
    concatenate x1 -> x2, local copies, waits for them, and re-layouts: 0.04 us -> 8.61 us  [ring_gather(): return jnp.concatenate(slots, axis=0)]
    ppermute x4, waiting for transfers between devices: 17.2 us -> 20 us  [ring_gather(): ahead = lax.ppermute(ahead, 'depth', forward)]
    ppermute x3, waiting for transfers between devices: 1.99 us -> 0.01 us  [ring_gather(): behind = lax.ppermute(behind, 'depth', backward)]
    select_n x1, other arithmetic: 1.75 us -> 0.16 us  [composite_rows(): back_rows = jnp.where(has_back[:, None, None], back_rows, 0.0)]
    select_n x1, other arithmetic: 1.75 us -> 0.16 us  [composite_rows(): front_rows = jnp.where(has_front[:, None, None], front_rows, 0.0)]
    select_n x1, other arithmetic: 1.63 us -> 0.11 us  [on_device(): return jnp.where(in_my_half[:, None, None], mine, received)]
    reshape x0 -> x1, local copies, waits for them, and re-layouts: none -> 1.48 us  [on_device(): flat.reshape(depth_count, stride, channels, pixels)[:, brick_rows, 0, :3]]
  transfers between devices with their start and end apart: 8 -> 8, of which waited for: 7 -> 5; matrix products, arithmetic and copies ran while one was open for 2% -> 2% of each run, Pallas kernels for 0% -> 0%
where the time goes in v5:
time: 77.2 us; the launch traced here: 76.7 us
  waiting for transfers between devices  21.9 us (28%)
  Pallas kernels  20.1 us (26%)
  local copies, waits for them, and re-layouts  19.7 us (26%)
  starting transfers between devices  8.87 us (11%)
  other arithmetic  3.98 us (5%)
  between operations  2.09 us (3%)
    pallas_call x1, Pallas kernels, render_layers(): pl.pallas_call(render_kernel, grid=(brick_rows // block_rows,), in_specs=...  20.1 us
    ppermute x4, waiting for transfers between devices, ring_gather(): ahead = lax.ppermute(ahead, 'depth', forward)  20 us
    concatenate x2, local copies, waits for them, and re-layouts, ring_gather(): return jnp.concatenate(slots, axis=0)  8.61 us
    ppermute x4, starting transfers between devices, ring_gather(): ahead = lax.ppermute(ahead, 'depth', forward)  8.01 us
    gather x1, local copies, waits for them, and re-layouts, composite_rows(): back_rows = jnp.take(flat, back_idx, axis=0, mode='clip')  3.1 us
    gather x1, local copies, waits for them, and re-layouts, composite_rows(): front_rows = jnp.take(flat, front_idx, axis=0, mode='clip')  3.1 us
    ppermute x1, waiting for transfers between devices, on_device(): received = lax.ppermute(for_partner, 'screen', [(0, 1), (1, 0)])  1.9 us
  transfers between devices with their start and end apart: 8, of which 5 were waited for; matrix products, arithmetic and copies ran while one was open for 2% of the time, Pallas kernels for 0%

profile of v5, /device:TPU:0, one launch (start us, length us, event | category | flops | bytes accessed | tf_op | source)
XLA Modules:
  0.0 76.7 jit_solution(13244924279667155187)
XLA Ops:
  2.0 1.3 %pad_maximum_fusion.2.params_ref = f32[8]{0:T(128)} fusion(f32[1]{0:T(128)} %bitcast.1, f32[3]{0:T(128)} %param.12, f32[3]{0:T(128)} %param.11, f32[1]{0:T(128)S(6)} %copy.26), kind=kLoop, calls=%fused_computation.48 | loop fusion | flops 24 | bytes 64 | tf_op jit(solution)/shard_map/concatenate | solution.py:44
  3.2 20.1 %shard_map.73 = f32[4,128,128]{2,1,0:T(8,128)} custom-call(f32[8]{0:T(128)} %pad_maximum_fusion.2.params_ref, f32[16384,128]{1,0:T(8,128)} %bitcast.19), custom_call_target="tpu_custom_call" | custom-call | tf_op jit(solution)/shard_map/pallas_call | solution.py:48
  23.3 1.0 %pad_maximum_fusion.1 = f32[129,4,128]{2,0,1:T(8,128)S(1)} fusion(f32[1,4,128]{2,0,1:T(1,128)S(1)} %fusion.10, f32[128,4,128]{2,0,1:T(8,128)} %bitcast.20), kind=kLoop, calls=%fused_computation.11 | loop fusion | flops 66048 | bytes 528384 | tf_op jit(solution)/shard_map/concatenate | solution.py:123
  24.3 3.1 %collective-permute-start = (f32[129,4,128]{2,0,1:T(8,128)S(1)}, f32[129,4,128]{2,0,1:T(8,128)S(1)}, u32[]{:S(2)}, u32[]{:S(2)}) collective-permute-start(f32[129,4,128]{2,0,1:T(8,128)S(1)} %pad_maximum_fusion.1), channel_id=1, source_target_pairs={{0,4},{4,8},{8,12},{12,14},{14,10},{10,6},{6,2},{2,0},{1,5},{5,9},... | collective-permute-start | bytes 792584 | tf_op jit(solution)/shard_map/ppermute | solution.py:100
  27.4 6.6 %collective-permute-done = f32[129,4,128]{2,0,1:T(8,128)S(1)} collective-permute-done((f32[129,4,128]{2,0,1:T(8,128)S(1)}, f32[129,4,128]{2,0,1:T(8,128)S(1)}, u32[]{:S(2)}, u32[]{:S(2)}) %collective-permute-start) | collective-permute-done | bytes 264224 | tf_op jit(solution)/shard_map/ppermute | solution.py:100
  34.0 1.8 %collective-permute-start.2 = (f32[129,4,128]{2,0,1:T(8,128)S(1)}, f32[129,4,128]{2,0,1:T(8,128)S(1)}, u32[]{:S(2)}, u32[]{:S(2)}) collective-permute-start(f32[129,4,128]{2,0,1:T(8,128)S(1)} %collective-permute-done), channel_id=1, source_target_pairs={{0,4},{4,8},{8,12},{12,14},{14,10},{10,6},{6,2},{2,0},{1,5},{5,9},... | collective-permute-start | bytes 792584 | tf_op jit(solution)/shard_map/ppermute | solution.py:100
  35.8 0.2 collective-permute-start.3
  36.0 5.8 %collective-permute-done.2 = f32[129,4,128]{2,0,1:T(8,128)S(1)} collective-permute-done((f32[129,4,128]{2,0,1:T(8,128)S(1)}, f32[129,4,128]{2,0,1:T(8,128)S(1)}, u32[]{:S(2)}, u32[]{:S(2)}) %collective-permute-start.2) | collective-permute-done | bytes 264224 | tf_op jit(solution)/shard_map/ppermute | solution.py:100
  41.8 1.5 %collective-permute-start.4 = (f32[129,4,128]{2,0,1:T(8,128)S(1)}, f32[129,4,128]{2,0,1:T(8,128)S(1)}, u32[]{:S(2)}, u32[]{:S(2)}) collective-permute-start(f32[129,4,128]{2,0,1:T(8,128)S(1)} %collective-permute-done.2), channel_id=1, source_target_pairs={{0,4},{4,8},{8,12},{12,14},{14,10},{10,6},{6,2},{2,0},{1,5},{5,9},... | collective-permute-start | bytes 792584 | tf_op jit(solution)/shard_map/ppermute | solution.py:100
  43.3 0.5 collective-permute-start.5
  43.8 4.9 %collective-permute-done.4 = f32[129,4,128]{2,0,1:T(8,128)S(1)} collective-permute-done((f32[129,4,128]{2,0,1:T(8,128)S(1)}, f32[129,4,128]{2,0,1:T(8,128)S(1)}, u32[]{:S(2)}, u32[]{:S(2)}) %collective-permute-start.4) | collective-permute-done | bytes 264224 | tf_op jit(solution)/shard_map/ppermute | solution.py:100
  48.7 1.7 %collective-permute-start.6 = (f32[129,4,128]{2,0,1:T(8,128)S(1)}, f32[129,4,128]{2,0,1:T(8,128)}, u32[]{:S(2)}, u32[]{:S(2)}) collective-permute-start(f32[129,4,128]{2,0,1:T(8,128)S(1)} %collective-permute-done.4), channel_id=1, source_target_pairs={{0,4},{4,8},{8,12},{12,14},{14,10},{10,6},{6,2},{2,0},{1,5},{5,9},... | collective-permute-start | bytes 792584 | tf_op jit(solution)/shard_map/ppermute | solution.py:100
  50.4 0.8 dynamic_slice.7
  51.2 0.8 %fusion.11 = (pred[256]{0:T(512)(128)(4,1)S(1)}, s32[256]{0:T(256)S(1)}) fusion(s32[]{:T(128)S(6)} %axis_index.25, s32[4096]{0:T(1024)} %param.13, s32[]{:T(128)S(6)} %select_n.105), kind=kLoop, calls=%fused_computation.47 | loop fusion | flops 4096 | bytes 2312 | tf_op jit(solution)/shard_map/eq | solution.py:138
  52.0 0.7 copy-done
  52.7 2.7 %collective-permute-done.6 = f32[129,4,128]{2,0,1:T(8,128)} collective-permute-done((f32[129,4,128]{2,0,1:T(8,128)S(1)}, f32[129,4,128]{2,0,1:T(8,128)}, u32[]{:S(2)}, u32[]{:S(2)}) %collective-permute-start.6) | collective-permute-done | bytes 264224 | tf_op jit(solution)/shard_map/ppermute | solution.py:100
  55.4 4.4 %concatenate.28 = f32[1032,4,128]{2,0,1:T(8,128)S(1)} concatenate(f32[128,4,128]{2,0,1:T(8,128)} %bitcast.21, f32[1,4,128]{2,0,1:T(1,128)S(1)} %fusion.10, f32[129,4,128]{2,0,1:T(8,128)S(1)} %collective-permute-done, f32[129,4,128]{2,0,1:T(8,128)S(1)} %collective-permute-done.1, f32[129,4,128]{2,0,1:T(8,128)S(1)} %collective-permute-done.2, ...), dimensions={0} | concatenate | bytes 4227072 | tf_op jit(solution)/shard_map/concatenate | solution.py:105
  59.8 1.5 %reshape.213 = f32[8,129,4,128]{3,1,0,2:T(8,128)} reshape(f32[1032,4,128]{2,0,1:T(8,128)S(1)} %concatenate.28) | data formatting | bytes 4227072 | tf_op jit(solution)/shard_map/reshape | solution.py:125
  61.3 4.2 %copy.17 = f32[1032,4,128]{2,1,0:T(4,128)} copy(f32[1032,4,128]{2,0,1:T(8,128)S(1)} %concatenate.28) | data formatting | bytes 4227072 | tf_op jit(solution)/shard_map/concatenate | solution.py:105
  65.5 0.8 slice.44
  66.3 0.1 copy.16
  66.3 0.1 select_reduce_fusion.2
  66.4 0.1 fusion.12
  66.5 0.1 select_reduce_fusion.1
  66.7 3.1 %gather_fusion.1 = f32[512,4,128]{2,1,0:T(4,128)S(1)} fusion(f32[1032,4,128]{2,1,0:T(4,128)} %copy.17, s32[1024]{0:T(1024)S(1)} %pad_clamp_fusion), kind=kCustom, calls=%fused_computation.1 | custom fusion | bytes 2099200 | tf_op jit(solution)/shard_map/jit(_take)/gather | solution.py:78
  69.8 3.1 %gather_fusion = f32[512,4,128]{2,1,0:T(4,128)S(1)} fusion(f32[1032,4,128]{2,1,0:T(4,128)} %copy.17, s32[1024]{0:T(1024)S(1)} %pad_clamp_fusion.1), kind=kCustom, calls=%fused_computation | custom fusion | bytes 2099200 | tf_op jit(solution)/shard_map/jit(_take)/gather | solution.py:79
  72.9 0.2 copy_select_fusion.1
  73.1 0.2 copy_select_fusion
  73.3 0.1 fusion
  73.6 1.9 %collective-permute-done.7 = f32[256,4,128]{2,0,1:T(8,128)S(1)} collective-permute-done((f32[256,4,128]{2,0,1:T(8,128)S(1)}, f32[256,4,128]{2,0,1:T(8,128)S(1)}, u32[]{:S(2)}, u32[]{:S(2)}) %collective-permute-start.7) | collective-permute-done | bytes 524320 | tf_op jit(solution)/shard_map/ppermute | solution.py:137
  75.4 0.1 fusion.2
  75.6 1.1 %copy.21 = f32[256,4,128]{2,1,0:T(4,128)} copy(f32[256,4,128]{2,0,1:T(8,128)S(1)} %fusion.2) | data formatting | bytes 1048576 | tf_op jit(solution)/shard_map/jit(_where)/select_n | solution.py:139
  (18 shorter events, 0.3 us)
Async XLA Ops:
  24.3 9.7 %collective-permute-start = (f32[129,4,128]{2,0,1:T(8,128)S(1)}, f32[129,4,128]{2,0,1:T(8,128)S(1)}, u32[]{:S(2)}, u32[]{:S(2)}) collective-permute-start(f32[129,4,128]{2,0,1:T(8,128)S(1)} %pad_maximum_fusion.1), channel_id=1, source_target_pairs={{0,4},{4,8},{8,12},{12,14},{14,10},{10,6},{6,2},{2,0},{1,5},{5,9},... | collective-permute-start | bytes 792584 | tf_op jit(solution)/shard_map/ppermute | solution.py:100
  27.4 8.4 %collective-permute-start.1 = (f32[129,4,128]{2,0,1:T(8,128)S(1)}, f32[129,4,128]{2,0,1:T(8,128)S(1)}, u32[]{:S(2)}, u32[]{:S(2)}) collective-permute-start(f32[129,4,128]{2,0,1:T(8,128)S(1)} %pad_maximum_fusion.1), channel_id=1, source_target_pairs={{4,0},{8,4},{12,8},{14,12},{10,14},{6,10},{2,6},{0,2},{5,1},{9,5},... | collective-permute-start | bytes 792584 | tf_op jit(solution)/shard_map/ppermute | solution.py:103
  34.0 7.8 %collective-permute-start.2 = (f32[129,4,128]{2,0,1:T(8,128)S(1)}, f32[129,4,128]{2,0,1:T(8,128)S(1)}, u32[]{:S(2)}, u32[]{:S(2)}) collective-permute-start(f32[129,4,128]{2,0,1:T(8,128)S(1)} %collective-permute-done), channel_id=1, source_target_pairs={{0,4},{4,8},{8,12},{12,14},{14,10},{10,6},{6,2},{2,0},{1,5},{5,9},... | collective-permute-start | bytes 792584 | tf_op jit(solution)/shard_map/ppermute | solution.py:100
  35.8 7.5 %collective-permute-start.3 = (f32[129,4,128]{2,0,1:T(8,128)S(1)}, f32[129,4,128]{2,0,1:T(8,128)S(1)}, u32[]{:S(2)}, u32[]{:S(2)}) collective-permute-start(f32[129,4,128]{2,0,1:T(8,128)S(1)} %collective-permute-done.1), channel_id=1, source_target_pairs={{4,0},{8,4},{12,8},{14,12},{10,14},{6,10},{2,6},{0,2},{5,1},{9,5},... | collective-permute-start | bytes 792584 | tf_op jit(solution)/shard_map/ppermute | solution.py:103
  41.8 6.9 %collective-permute-start.4 = (f32[129,4,128]{2,0,1:T(8,128)S(1)}, f32[129,4,128]{2,0,1:T(8,128)S(1)}, u32[]{:S(2)}, u32[]{:S(2)}) collective-permute-start(f32[129,4,128]{2,0,1:T(8,128)S(1)} %collective-permute-done.2), channel_id=1, source_target_pairs={{0,4},{4,8},{8,12},{12,14},{14,10},{10,6},{6,2},{2,0},{1,5},{5,9},... | collective-permute-start | bytes 792584 | tf_op jit(solution)/shard_map/ppermute | solution.py:100
  43.3 8.6 %collective-permute-start.5 = (f32[129,4,128]{2,0,1:T(8,128)S(1)}, f32[129,4,128]{2,0,1:T(8,128)S(1)}, u32[]{:S(2)}, u32[]{:S(2)}) collective-permute-start(f32[129,4,128]{2,0,1:T(8,128)S(1)} %collective-permute-done.3), channel_id=1, source_target_pairs={{4,0},{8,4},{12,8},{14,12},{10,14},{6,10},{2,6},{0,2},{5,1},{9,5},... | collective-permute-start | bytes 792584 | tf_op jit(solution)/shard_map/ppermute | solution.py:103
  48.7 6.7 %collective-permute-start.6 = (f32[129,4,128]{2,0,1:T(8,128)S(1)}, f32[129,4,128]{2,0,1:T(8,128)}, u32[]{:S(2)}, u32[]{:S(2)}) collective-permute-start(f32[129,4,128]{2,0,1:T(8,128)S(1)} %collective-permute-done.4), channel_id=1, source_target_pairs={{0,4},{4,8},{8,12},{12,14},{14,10},{10,6},{6,2},{2,0},{1,5},{5,9},... | collective-permute-start | bytes 792584 | tf_op jit(solution)/shard_map/ppermute | solution.py:100
  51.9 0.7 copy-start
  73.5 2.0 %collective-permute-start.7 = (f32[256,4,128]{2,0,1:T(8,128)S(1)}, f32[256,4,128]{2,0,1:T(8,128)S(1)}, u32[]{:S(2)}, u32[]{:S(2)}) collective-permute-start(f32[256,4,128]{2,0,1:T(8,128)S(1)} %pad_maximum_fusion), channel_id=1, source_target_pairs={{0,1},{1,0},{2,3},{3,2},{4,5},{5,4},{6,7},{7,6},{8,9},{9,8},{10,11... | collective-permute-start | bytes 1572872 | tf_op jit(solution)/shard_map/ppermute | solution.py:137

commit v6 on v5

--- a/solution.py
+++ b/solution.py
@@ -9,7 +9,7 @@
 
 
 def render_kernel(params_ref, density_ref, out_ref):
-    block_rows = out_ref.shape[1]
+    block_rows = out_ref.shape[0]
     pixels = out_ref.shape[2]
     sample_count = density_ref.shape[0] // block_rows
     absorb = params_ref[0]
@@ -35,8 +35,8 @@
     row_ids = pl.program_id(0) * block_rows + lax.broadcasted_iota(jnp.int32, (block_rows, pixels), 0)
     visible = row_ids.astype(jnp.float32) < shown
     for channel in range(3):
-        out_ref[channel] = jnp.where(visible, carry[2 + channel], 0.0)
-    out_ref[3] = jnp.where(visible, carry[1], 0.0)
+        out_ref[:, channel, :] = jnp.where(visible, carry[2 + channel], 0.0)
+    out_ref[:, 3, :] = jnp.where(visible, carry[1], 0.0)
 
 
 def render_layers(density_block, shown_rows, absorb, colour_slope, colour_offset, block_rows=8):
@@ -45,17 +45,16 @@
         absorb.reshape(1), colour_slope, colour_offset,
         shown_rows.astype(jnp.float32).reshape(1),
     ])
-    planes = pl.pallas_call(
+    return pl.pallas_call(
         render_kernel,
         grid=(brick_rows // block_rows,),
         in_specs=[
             pl.BlockSpec(memory_space=pltpu.SMEM),
             pl.BlockSpec((block_rows * sample_count, pixels), lambda i: (i, 0)),
         ],
-        out_specs=pl.BlockSpec((4, block_rows, pixels), lambda i: (0, i, 0)),
-        out_shape=jax.ShapeDtypeStruct((4, brick_rows, pixels), jnp.float32),
+        out_specs=pl.BlockSpec((block_rows, 4, pixels), lambda i: (i, 0, 0)),
+        out_shape=jax.ShapeDtypeStruct((brick_rows, 4, pixels), jnp.float32),
     )(params, density_block.reshape(brick_rows * sample_count, pixels))
-    return jnp.transpose(planes, (1, 0, 2))
 
 
 def composite_rows(flat, starts, counts, brick_ids, stride, image_rows):

time: 77.2 us -> 70 us (0.907)
  local copies, waits for them, and re-layouts: 19.7 us -> 7.26 us
  other arithmetic: 3.98 us -> 9.96 us
  waiting for transfers between devices: 21.9 us -> 21.1 us
    concatenate x2 -> x1, local copies, waits for them, and re-layouts: 8.61 us -> 0.04 us  [ring_gather(): return jnp.concatenate(slots, axis=0)]
    ppermute x4, waiting for transfers between devices: 20 us -> 17.2 us  [ring_gather(): ahead = lax.ppermute(ahead, 'depth', forward)]
    ppermute x3, waiting for transfers between devices: 0.01 us -> 2 us  [ring_gather(): behind = lax.ppermute(behind, 'depth', backward)]
    select_n x1, other arithmetic: 0.16 us -> 1.75 us  [composite_rows(): back_rows = jnp.where(has_back[:, None, None], back_rows, 0.0)]
    select_n x1, other arithmetic: 0.16 us -> 1.75 us  [composite_rows(): front_rows = jnp.where(has_front[:, None, None], front_rows, 0.0)]
    select_n x1, other arithmetic: 0.11 us -> 1.63 us  [on_device(): return jnp.where(in_my_half[:, None, None], mine, received)]
    reshape x1 -> x0, local copies, waits for them, and re-layouts: 1.48 us -> none  [on_device(): flat.reshape(depth_count, stride, channels, pixels)[:, brick_rows, 0, :3]]
    select_n x1 -> x0, local copies, waits for them, and re-layouts: 1.13 us -> none  [on_device(): return jnp.where(in_my_half[:, None, None], mine, received)]
  transfers between devices with their start and end apart: 8 -> 8, of which waited for: 5 -> 7; matrix products, arithmetic and copies ran while one was open for 2% -> 3% of each run, Pallas kernels for 0% -> 0%
where the time goes in v6:
time: 70 us; the launch traced here: 69.7 us
  waiting for transfers between devices  21.1 us (30%)
  Pallas kernels  20.3 us (29%)
  other arithmetic  9.96 us (14%)
  starting transfers between devices  8.96 us (13%)
  local copies, waits for them, and re-layouts  7.26 us (10%)
  between operations  2.14 us (3%)
    pallas_call x1, Pallas kernels, render_layers(): pl.pallas_call(render_kernel, grid=(brick_rows // block_rows,), in_specs=...  20.3 us
    ppermute x4, waiting for transfers between devices, ring_gather(): ahead = lax.ppermute(ahead, 'depth', forward)  17.2 us
    ppermute x4, starting transfers between devices, ring_gather(): ahead = lax.ppermute(ahead, 'depth', forward)  8.05 us
    gather x1, local copies, waits for them, and re-layouts, composite_rows(): front_rows = jnp.take(flat, front_idx, axis=0, mode='clip')  3.1 us
    gather x1, local copies, waits for them, and re-layouts, composite_rows(): back_rows = jnp.take(flat, back_idx, axis=0, mode='clip')  2.07 us
    ppermute x3, waiting for transfers between devices, ring_gather(): behind = lax.ppermute(behind, 'depth', backward)  2 us
    ppermute x1, waiting for transfers between devices, on_device(): received = lax.ppermute(for_partner, 'screen', [(0, 1), (1, 0)])  1.9 us
    select_n x1, other arithmetic, composite_rows(): front_rows = jnp.where(has_front[:, None, None], front_rows, 0.0)  1.75 us
  transfers between devices with their start and end apart: 8, of which 7 were waited for; matrix products, arithmetic and copies ran while one was open for 3% of the time, Pallas kernels for 0%

profile of v6, /device:TPU:0, one launch (start us, length us, event | category | flops | bytes accessed | tf_op | source)
XLA Modules:
  0.0 69.7 jit_solution(13997316313460323160)
XLA Ops:
  1.3 1.3 %pad_maximum_fusion.2.params_ref = f32[8]{0:T(128)} fusion(f32[1]{0:T(128)} %bitcast.1, f32[3]{0:T(128)} %param.12, f32[3]{0:T(128)} %param.11, f32[1]{0:T(128)S(6)} %copy.23), kind=kLoop, calls=%fused_computation.54 | loop fusion | flops 24 | bytes 64 | tf_op jit(solution)/shard_map/concatenate | solution.py:44
  2.6 20.3 %shard_map.73 = f32[128,4,128]{2,1,0:T(4,128)} custom-call(f32[8]{0:T(128)} %pad_maximum_fusion.2.params_ref, f32[16384,128]{1,0:T(8,128)} %bitcast.17), custom_call_target="tpu_custom_call" | custom-call | tf_op jit(solution)/shard_map/pallas_call | solution.py:48
  22.8 1.0 %constant_dynamic-update-slice_fusion.8 = f32[1032,4,128]{2,1,0:T(4,128)S(1)} fusion(f32[128,4,128]{2,1,0:T(4,128)} %shard_map.73), kind=kLoop, calls=%fused_computation.28 | loop fusion | bytes 524288
  24.5 1.0 %pad_maximum_fusion.1 = f32[129,4,128]{2,1,0:T(4,128)S(1)} fusion(f32[1,4,128]{2,1,0:T(4,128)S(1)} %get-tuple-element.18, f32[128,4,128]{2,1,0:T(4,128)} %shard_map.73), kind=kLoop, calls=%fused_computation.11 | loop fusion | flops 66048 | bytes 528384 | tf_op jit(solution)/shard_map/concatenate | solution.py:122
  25.5 3.1 %collective-permute-start = (f32[129,4,128]{2,1,0:T(4,128)S(1)}, f32[129,4,128]{2,1,0:T(4,128)S(1)}, u32[]{:S(2)}, u32[]{:S(2)}) collective-permute-start(f32[129,4,128]{2,1,0:T(4,128)S(1)} %pad_maximum_fusion.1), channel_id=1, source_target_pairs={{0,4},{4,8},{8,12},{12,14},{14,10},{10,6},{6,2},{2,0},{1,5},{5,9},... | collective-permute-start | bytes 792584 | tf_op jit(solution)/shard_map/ppermute | solution.py:99
  28.6 6.3 %collective-permute-done = f32[129,4,128]{2,1,0:T(4,128)S(1)} collective-permute-done((f32[129,4,128]{2,1,0:T(4,128)S(1)}, f32[129,4,128]{2,1,0:T(4,128)S(1)}, u32[]{:S(2)}, u32[]{:S(2)}) %collective-permute-start) | collective-permute-done | bytes 264224 | tf_op jit(solution)/shard_map/ppermute | solution.py:99
  34.8 1.8 %collective-permute-start.2 = (f32[129,4,128]{2,1,0:T(4,128)S(1)}, f32[129,4,128]{2,1,0:T(4,128)S(1)}, u32[]{:S(2)}, u32[]{:S(2)}) collective-permute-start(f32[129,4,128]{2,1,0:T(4,128)S(1)} %collective-permute-done), channel_id=1, source_target_pairs={{0,4},{4,8},{8,12},{12,14},{14,10},{10,6},{6,2},{2,0},{1,5},{5,9},... | collective-permute-start | bytes 792584 | tf_op jit(solution)/shard_map/ppermute | solution.py:99
  36.6 0.8 %dynamic_slice.7 = s32[256]{0:T(256)S(1)} dynamic-slice(s32[4096]{0:T(1024)} %param.13, s32[]{:T(128)S(6)} %select_n.110), dynamic_slice_sizes={256} | dynamic-slice | bytes 2052 | tf_op jit(solution)/shard_map/dynamic_slice | solution.py:131
  37.4 0.8 %fusion.8 = (pred[256]{0:T(512)(128)(4,1)S(1)}, s32[256]{0:T(256)S(1)}) fusion(s32[]{:T(128)S(6)} %axis_index.25, s32[4096]{0:T(1024)} %param.13, s32[]{:T(128)S(6)} %select_n.105), kind=kLoop, calls=%fused_computation.53 | loop fusion | flops 4096 | bytes 2312 | tf_op jit(solution)/shard_map/eq | solution.py:137
  38.2 0.3 collective-permute-start.3
  38.5 3.9 %collective-permute-done.2 = f32[129,4,128]{2,1,0:T(4,128)S(1)} collective-permute-done((f32[129,4,128]{2,1,0:T(4,128)S(1)}, f32[129,4,128]{2,1,0:T(4,128)S(1)}, u32[]{:S(2)}, u32[]{:S(2)}) %collective-permute-start.2) | collective-permute-done | bytes 264224 | tf_op jit(solution)/shard_map/ppermute | solution.py:99
  42.4 1.5 %collective-permute-start.4 = (f32[129,4,128]{2,1,0:T(4,128)S(1)}, f32[129,4,128]{2,1,0:T(4,128)S(1)}, u32[]{:S(2)}, u32[]{:S(2)}) collective-permute-start(f32[129,4,128]{2,1,0:T(4,128)S(1)} %collective-permute-done.2), channel_id=1, source_target_pairs={{0,4},{4,8},{8,12},{12,14},{14,10},{10,6},{6,2},{2,0},{1,5},{5,9},... | collective-permute-start | bytes 792584 | tf_op jit(solution)/shard_map/ppermute | solution.py:99
  43.9 1.2 %collective-permute-done.3 = f32[129,4,128]{2,1,0:T(4,128)S(1)} collective-permute-done((f32[129,4,128]{2,1,0:T(4,128)S(1)}, f32[129,4,128]{2,1,0:T(4,128)S(1)}, u32[]{:S(2)}, u32[]{:S(2)}) %collective-permute-start.3) | collective-permute-done | bytes 264224 | tf_op jit(solution)/shard_map/ppermute | solution.py:102
  45.2 0.5 collective-permute-start.5
  45.8 3.2 %collective-permute-done.4 = f32[129,4,128]{2,1,0:T(4,128)S(1)} collective-permute-done((f32[129,4,128]{2,1,0:T(4,128)S(1)}, f32[129,4,128]{2,1,0:T(4,128)S(1)}, u32[]{:S(2)}, u32[]{:S(2)}) %collective-permute-start.4) | collective-permute-done | bytes 264224 | tf_op jit(solution)/shard_map/ppermute | solution.py:99
  49.0 1.7 %collective-permute-start.6 = (f32[129,4,128]{2,1,0:T(4,128)S(1)}, f32[129,4,128]{2,1,0:T(4,128)S(1)}, u32[]{:S(2)}, u32[]{:S(2)}) collective-permute-start(f32[129,4,128]{2,1,0:T(4,128)S(1)} %collective-permute-done.4), channel_id=1, source_target_pairs={{0,4},{4,8},{8,12},{12,14},{14,10},{10,6},{6,2},{2,0},{1,5},{5,9},... | collective-permute-start | bytes 792584 | tf_op jit(solution)/shard_map/ppermute | solution.py:99
  50.8 0.8 %collective-permute-done.5 = f32[129,4,128]{2,1,0:T(4,128)S(1)} collective-permute-done((f32[129,4,128]{2,1,0:T(4,128)S(1)}, f32[129,4,128]{2,1,0:T(4,128)S(1)}, u32[]{:S(2)}, u32[]{:S(2)}) %collective-permute-start.5) | collective-permute-done | bytes 264224 | tf_op jit(solution)/shard_map/ppermute | solution.py:102
  51.6 3.8 %collective-permute-done.6 = f32[129,4,128]{2,1,0:T(4,128)S(1)} collective-permute-done((f32[129,4,128]{2,1,0:T(4,128)S(1)}, f32[129,4,128]{2,1,0:T(4,128)S(1)}, u32[]{:S(2)}, u32[]{:S(2)}) %collective-permute-start.6) | collective-permute-done | bytes 264224 | tf_op jit(solution)/shard_map/ppermute | solution.py:99
  55.5 0.1 copy.12
  55.5 0.1 select_reduce_fusion.2
  55.6 0.1 fusion.9
  55.7 0.1 select_reduce_fusion.1
  55.9 2.1 %gather_fusion.1 = f32[512,4,128]{2,1,0:T(4,128)S(1)} fusion(f32[1032,4,128]{2,1,0:T(4,128)S(1)} %constant_dynamic-update-slice_fusion, s32[1024]{0:T(1024)S(1)} %pad_clamp_fusion), kind=kCustom, calls=%fused_computation.1 | custom fusion | bytes 2099200 | tf_op jit(solution)/shard_map/jit(_take)/gather | solution.py:77
  58.0 3.1 %gather_fusion = f32[512,4,128]{2,1,0:T(4,128)S(1)} fusion(f32[1032,4,128]{2,1,0:T(4,128)} %copy-done, s32[1024]{0:T(1024)S(1)} %pad_clamp_fusion.1), kind=kCustom, calls=%fused_computation | custom fusion | bytes 2099200 | tf_op jit(solution)/shard_map/jit(_take)/gather | solution.py:78
  61.1 1.8 %broadcast_select_fusion.1 = f32[512,4,128]{2,1,0:T(4,128)S(1)} fusion(f32[512,4,128]{2,1,0:T(4,128)S(1)} %gather_fusion, pred[512]{0:T(512)(128)(4,1)S(1)} %get-tuple-element.13), kind=kLoop, calls=%fused_computation.10 | loop fusion | flops 262144 | bytes 2097664 | tf_op jit(solution)/shard_map/jit(_where)/select_n | solution.py:80
  62.9 1.8 %broadcast_select_fusion = f32[512,4,128]{2,1,0:T(4,128)S(1)} fusion(f32[512,4,128]{2,1,0:T(4,128)S(1)} %gather_fusion.1, pred[512]{0:T(512)(128)(4,1)S(1)} %get-tuple-element.16), kind=kLoop, calls=%fused_computation.9 | loop fusion | flops 262144 | bytes 2097664 | tf_op jit(solution)/shard_map/jit(_where)/select_n | solution.py:79
  64.6 0.8 %negate_exponential_fusion = (f32[512,1,128]{2,1,0:T(1,128)S(1)}, f32[512,1,128]{2,1,0:T(1,128)S(1)}) fusion(f32[512,4,128]{2,1,0:T(4,128)S(1)} %broadcast_select_fusion.1, f32[512,1,128]{2,1,0:T(1,128)S(1)} %bitcast.19, f32[512,4,128]{2,1,0:T(4,128)S(1)} %broadcast_select_fusion), kind=kLoop, calls=%fused_computation.15 | loop fusion | flops 262144 | bytes 1310720 | tf_op jit(solution)/shard_map/exp | solution.py:82
  65.5 0.4 fusion
  65.9 0.2 pad_maximum_fusion
  66.1 0.1 collective-permute-start.7
  66.2 1.9 %collective-permute-done.7 = f32[256,4,128]{2,1,0:T(4,128)S(1)} collective-permute-done((f32[256,4,128]{2,1,0:T(4,128)S(1)}, f32[256,4,128]{2,1,0:T(4,128)S(1)}, u32[]{:S(2)}, u32[]{:S(2)}) %collective-permute-start.7) | collective-permute-done | bytes 524320 | tf_op jit(solution)/shard_map/ppermute | solution.py:136
  68.1 1.6 %fusion.2 = f32[256,4,128]{2,1,0:T(4,128)} fusion(f32[256,4,128]{2,1,0:T(4,128)S(1)} %collective-permute-done.7, f32[512,3,128]{2,1,0:T(4,128)S(1)} %fusion, f32[512,1,128]{2,1,0:T(1,128)S(1)} %get-tuple-element.20, pred[256]{0:T(512)(128)(4,1)S(1)} %get-tuple-element.11), kind=kLoop, calls=%fused_computation.7 | loop fusion | flops 262144 | bytes 2097408 | tf_op jit(solution)/shard_map/jit(_where)/select_n | solution.py:138
  (23 shorter events, 0.4 us)
Async XLA Ops:
  25.5 9.4 %collective-permute-start = (f32[129,4,128]{2,1,0:T(4,128)S(1)}, f32[129,4,128]{2,1,0:T(4,128)S(1)}, u32[]{:S(2)}, u32[]{:S(2)}) collective-permute-start(f32[129,4,128]{2,1,0:T(4,128)S(1)} %pad_maximum_fusion.1), channel_id=1, source_target_pairs={{0,4},{4,8},{8,12},{12,14},{14,10},{10,6},{6,2},{2,0},{1,5},{5,9},... | collective-permute-start | bytes 792584 | tf_op jit(solution)/shard_map/ppermute | solution.py:99
  28.6 9.6 %collective-permute-start.1 = (f32[129,4,128]{2,1,0:T(4,128)S(1)}, f32[129,4,128]{2,1,0:T(4,128)S(1)}, u32[]{:S(2)}, u32[]{:S(2)}) collective-permute-start(f32[129,4,128]{2,1,0:T(4,128)S(1)} %pad_maximum_fusion.1), channel_id=1, source_target_pairs={{4,0},{8,4},{12,8},{14,12},{10,14},{6,10},{2,6},{0,2},{5,1},{9,5},... | collective-permute-start | bytes 792584 | tf_op jit(solution)/shard_map/ppermute | solution.py:102
  34.8 7.5 %collective-permute-start.2 = (f32[129,4,128]{2,1,0:T(4,128)S(1)}, f32[129,4,128]{2,1,0:T(4,128)S(1)}, u32[]{:S(2)}, u32[]{:S(2)}) collective-permute-start(f32[129,4,128]{2,1,0:T(4,128)S(1)} %collective-permute-done), channel_id=1, source_target_pairs={{0,4},{4,8},{8,12},{12,14},{14,10},{10,6},{6,2},{2,0},{1,5},{5,9},... | collective-permute-start | bytes 792584 | tf_op jit(solution)/shard_map/ppermute | solution.py:99
  38.2 7.0 %collective-permute-start.3 = (f32[129,4,128]{2,1,0:T(4,128)S(1)}, f32[129,4,128]{2,1,0:T(4,128)S(1)}, u32[]{:S(2)}, u32[]{:S(2)}) collective-permute-start(f32[129,4,128]{2,1,0:T(4,128)S(1)} %collective-permute-done.1), channel_id=1, source_target_pairs={{4,0},{8,4},{12,8},{14,12},{10,14},{6,10},{2,6},{0,2},{5,1},{9,5},... | collective-permute-start | bytes 792584 | tf_op jit(solution)/shard_map/ppermute | solution.py:102
  42.4 6.6 %collective-permute-start.4 = (f32[129,4,128]{2,1,0:T(4,128)S(1)}, f32[129,4,128]{2,1,0:T(4,128)S(1)}, u32[]{:S(2)}, u32[]{:S(2)}) collective-permute-start(f32[129,4,128]{2,1,0:T(4,128)S(1)} %collective-permute-done.2), channel_id=1, source_target_pairs={{0,4},{4,8},{8,12},{12,14},{14,10},{10,6},{6,2},{2,0},{1,5},{5,9},... | collective-permute-start | bytes 792584 | tf_op jit(solution)/shard_map/ppermute | solution.py:99
  45.2 6.4 %collective-permute-start.5 = (f32[129,4,128]{2,1,0:T(4,128)S(1)}, f32[129,4,128]{2,1,0:T(4,128)S(1)}, u32[]{:S(2)}, u32[]{:S(2)}) collective-permute-start(f32[129,4,128]{2,1,0:T(4,128)S(1)} %collective-permute-done.3), channel_id=1, source_target_pairs={{4,0},{8,4},{12,8},{14,12},{10,14},{6,10},{2,6},{0,2},{5,1},{9,5},... | collective-permute-start | bytes 792584 | tf_op jit(solution)/shard_map/ppermute | solution.py:102
  49.0 6.4 %collective-permute-start.6 = (f32[129,4,128]{2,1,0:T(4,128)S(1)}, f32[129,4,128]{2,1,0:T(4,128)S(1)}, u32[]{:S(2)}, u32[]{:S(2)}) collective-permute-start(f32[129,4,128]{2,1,0:T(4,128)S(1)} %collective-permute-done.4), channel_id=1, source_target_pairs={{0,4},{4,8},{8,12},{12,14},{14,10},{10,6},{6,2},{2,0},{1,5},{5,9},... | collective-permute-start | bytes 792584 | tf_op jit(solution)/shard_map/ppermute | solution.py:99
  55.4 2.5 %copy-start = (f32[1032,4,128]{2,1,0:T(4,128)}, f32[1032,4,128]{2,1,0:T(4,128)S(1)}, u32[]{:S(2)}) copy-start(f32[1032,4,128]{2,1,0:T(4,128)S(1)} %constant_dynamic-update-slice_fusion) | copy-start | bytes 6340612
  66.1 2.0 %collective-permute-start.7 = (f32[256,4,128]{2,1,0:T(4,128)S(1)}, f32[256,4,128]{2,1,0:T(4,128)S(1)}, u32[]{:S(2)}, u32[]{:S(2)}) collective-permute-start(f32[256,4,128]{2,1,0:T(4,128)S(1)} %pad_maximum_fusion), channel_id=1, source_target_pairs={{0,1},{1,0},{2,3},{3,2},{4,5},{5,4},{6,7},{7,6},{8,9},{9,8},{10,11... | collective-permute-start | bytes 1572872 | tf_op jit(solution)/shard_map/ppermute | solution.py:136

commit v7 on v6

--- a/solution.py
+++ b/solution.py
@@ -1,3 +1,5 @@
+import functools
+
 import jax
 import jax.numpy as jnp
 from jax import lax
@@ -8,7 +10,7 @@
 BLK = 256
 
 
-def render_kernel(params_ref, density_ref, out_ref):
+def render_kernel(first_block, params_ref, density_ref, out_ref):
     block_rows = out_ref.shape[0]
     pixels = out_ref.shape[2]
     sample_count = density_ref.shape[0] // block_rows
@@ -32,32 +34,34 @@
     zeros = jnp.zeros((block_rows, pixels), jnp.float32)
     carry = (jnp.ones((block_rows, pixels), jnp.float32), zeros, zeros, zeros, zeros)
     carry = lax.fori_loop(0, sample_count, one_step, carry, unroll=8)
-    row_ids = pl.program_id(0) * block_rows + lax.broadcasted_iota(jnp.int32, (block_rows, pixels), 0)
+    row_ids = (pl.program_id(0) + first_block) * block_rows + lax.broadcasted_iota(jnp.int32, (block_rows, pixels), 0)
     visible = row_ids.astype(jnp.float32) < shown
     for channel in range(3):
         out_ref[:, channel, :] = jnp.where(visible, carry[2 + channel], 0.0)
     out_ref[:, 3, :] = jnp.where(visible, carry[1], 0.0)
 
 
-def render_layers(density_block, shown_rows, absorb, colour_slope, colour_offset, block_rows=8):
+def render_layers(density_block, shown_rows, absorb, colour_slope, colour_offset, first_row, row_count,
+                  block_rows=8):
     brick_rows, sample_count, pixels = density_block.shape
+    first_block = first_row // block_rows
     params = jnp.concatenate([
         absorb.reshape(1), colour_slope, colour_offset,
         shown_rows.astype(jnp.float32).reshape(1),
     ])
     return pl.pallas_call(
-        render_kernel,
-        grid=(brick_rows // block_rows,),
+        functools.partial(render_kernel, first_block),
+        grid=(row_count // block_rows,),
         in_specs=[
             pl.BlockSpec(memory_space=pltpu.SMEM),
-            pl.BlockSpec((block_rows * sample_count, pixels), lambda i: (i, 0)),
+            pl.BlockSpec((block_rows * sample_count, pixels), lambda i: (i + first_block, 0)),
         ],
         out_specs=pl.BlockSpec((block_rows, 4, pixels), lambda i: (i, 0, 0)),
-        out_shape=jax.ShapeDtypeStruct((brick_rows, 4, pixels), jnp.float32),
+        out_shape=jax.ShapeDtypeStruct((row_count, 4, pixels), jnp.float32),
     )(params, density_block.reshape(brick_rows * sample_count, pixels))
 
 
-def composite_rows(flat, starts, counts, brick_ids, stride, image_rows):
+def composite_rows(flat, starts, counts, brick_ids, stride, split, image_rows):
     slot_count = starts.shape[0]
     offset = image_rows[:, None] - starts[None, :]
     covered = (offset >= 0) & (offset < counts[None, :])
@@ -72,6 +76,8 @@
     front_slot = jnp.sum(jnp.where(is_front, slot_ids, 0), axis=1)
     has_front = jnp.any(is_front, axis=1)
     has_back = back >= 0
+    back_off = back_off + (back_off >= split).astype(jnp.int32)
+    front_off = front_off + (front_off >= split).astype(jnp.int32)
     back_idx = jnp.where(has_back, back_slot * stride + back_off, 0)
     front_idx = jnp.where(has_front, front_slot * stride + front_off, 0)
     back_rows = jnp.take(flat, back_idx, axis=0, mode="clip")
@@ -101,7 +107,7 @@
         if 2 * step < count:
             behind = lax.ppermute(behind, "depth", backward)
             slots.append(behind)
-    return jnp.concatenate(slots, axis=0)
+    return slots
 
 
 def on_device(density, foot_start, foot_rows, extinction, colour_slope, colour_offset, tile_source):
@@ -114,14 +120,19 @@
     owner_rows = image_total // (depth_count * screen_count)
     start = foot_start[0, 0]
     shown = foot_rows[0, 0]
-    layers = render_layers(density[0, 0], shown, extinction[0], colour_slope, colour_offset)
-    brick_rows, channels, pixels = layers.shape
+    brick_rows, pixels = density.shape[2], density.shape[4]
+    channels = 4
+    split = brick_rows // 2
     lane = lax.broadcasted_iota(jnp.int32, (1, channels, pixels), 2)
     meta = jnp.where(lane == 0, start, jnp.where(lane == 1, shown, jnp.where(lane == 2, depth_index, 0)))
     stride = brick_rows + 1
-    own = jnp.concatenate([layers, meta.astype(jnp.float32)], axis=0)
-    flat = ring_gather(own, depth_count)
-    meta_rows = flat.reshape(depth_count, stride, channels, pixels)[:, brick_rows, 0, :3]
+    front_half = render_layers(density[0, 0], shown, extinction[0], colour_slope, colour_offset, 0, split)
+    front_slots = ring_gather(jnp.concatenate([front_half, meta.astype(jnp.float32)], axis=0), depth_count)
+    back_half = render_layers(density[0, 0], shown, extinction[0], colour_slope, colour_offset, split,
+                              brick_rows - split)
+    back_slots = ring_gather(back_half, depth_count)
+    flat = jnp.concatenate([part for pair in zip(front_slots, back_slots) for part in pair], axis=0)
+    meta_rows = flat.reshape(depth_count, stride, channels, pixels)[:, split, 0, :3]
     starts = meta_rows[:, 0].astype(jnp.int32)
     counts = meta_rows[:, 1].astype(jnp.int32)
     brick_ids = meta_rows[:, 2].astype(jnp.int32)
@@ -130,7 +141,7 @@
     wanted_self = lax.dynamic_slice_in_dim(tile_source, self_owner * owner_rows, owner_rows)
     wanted_partner = lax.dynamic_slice_in_dim(tile_source, partner_owner * owner_rows, owner_rows)
     wanted = jnp.concatenate([wanted_self, wanted_partner])
-    rows = composite_rows(flat, starts, counts, brick_ids, stride, wanted % half_rows)
+    rows = composite_rows(flat, starts, counts, brick_ids, stride, split, wanted % half_rows)
     mine = rows[:owner_rows]
     for_partner = rows[owner_rows:]
     received = lax.ppermute(for_partner, "screen", [(0, 1), (1, 0)])

time: 70 us -> 72.5 us (1.036)
  waiting for transfers between devices: 21.1 us -> 10.8 us
  starting transfers between devices: 8.96 us -> 17.1 us
  local copies, waits for them, and re-layouts: 7.26 us -> 10.1 us
  Pallas kernels: 20.3 us -> 22 us
    ppermute x4 -> x8, waiting for transfers between devices: 17.2 us -> 8.88 us  [ring_gather(): ahead = lax.ppermute(ahead, 'depth', forward)]
    ppermute x4 -> x8, starting transfers between devices: 8.05 us -> 16.3 us  [ring_gather(): ahead = lax.ppermute(ahead, 'depth', forward)]
    ppermute x3 -> x6, waiting for transfers between devices: 2 us -> 0.02 us  [ring_gather(): behind = lax.ppermute(behind, 'depth', backward)]
    unnamed x10 -> x18, local copies, waits for them, and re-layouts: 1.27 us -> 3.09 us
    pallas_call x1 -> x2, Pallas kernels: 20.3 us -> 22 us  [render_layers(): pl.pallas_call(functools.partial(render_kernel, first_block), grid=(row_c...]
    gather x1, local copies, waits for them, and re-layouts: 2.07 us -> 3.1 us  [composite_rows(): back_rows = jnp.take(flat, back_idx, axis=0, mode='clip')]
  transfers between devices with their start and end apart: 8 -> 15, of which waited for: 7 -> 7; matrix products, arithmetic and copies ran while one was open for 3% -> 4% of each run, Pallas kernels for 0% -> 15%
where the time goes in v7:
time: 72.5 us; the launch traced here: 72.1 us
  Pallas kernels  22 us (30%)
  starting transfers between devices  17.1 us (24%)
  waiting for transfers between devices  10.8 us (15%)
  local copies, waits for them, and re-layouts  10.1 us (14%)
  other arithmetic  9.95 us (14%)
  between operations  2.23 us (3%)
    pallas_call x2, Pallas kernels, render_layers(): pl.pallas_call(functools.partial(render_kernel, first_block), grid=(row_c...  22 us
    ppermute x8, starting transfers between devices, ring_gather(): ahead = lax.ppermute(ahead, 'depth', forward)  16.3 us
    ppermute x8, waiting for transfers between devices, ring_gather(): ahead = lax.ppermute(ahead, 'depth', forward)  8.88 us
    gather x1, local copies, waits for them, and re-layouts, composite_rows(): front_rows = jnp.take(flat, front_idx, axis=0, mode='clip')  3.1 us
    gather x1, local copies, waits for them, and re-layouts, composite_rows(): back_rows = jnp.take(flat, back_idx, axis=0, mode='clip')  3.1 us
    unnamed x18, local copies, waits for them, and re-layouts  3.09 us
    ppermute x1, waiting for transfers between devices, on_device(): received = lax.ppermute(for_partner, 'screen', [(0, 1), (1, 0)])  1.9 us
    select_n x1, other arithmetic, composite_rows(): front_rows = jnp.where(has_front[:, None, None], front_rows, 0.0)  1.75 us
  transfers between devices with their start and end apart: 15, of which 7 were waited for; matrix products, arithmetic and copies ran while one was open for 4% of the time, Pallas kernels for 15%

profile of v7, /device:TPU:0, one launch (start us, length us, event | category | flops | bytes accessed | tf_op | source)
XLA Modules:
  0.0 72.1 jit_solution(18060486179749252649)
XLA Ops:
  1.3 1.3 %pad_maximum_fusion.2.params_ref = f32[8]{0:T(128)} fusion(f32[1]{0:T(128)} %bitcast.1, f32[3]{0:T(128)} %param.12, f32[3]{0:T(128)} %param.11, f32[1]{0:T(128)S(6)} %copy.32), kind=kLoop, calls=%fused_computation.70 | loop fusion | flops 24 | bytes 64 | tf_op jit(solution)/shard_map/concatenate | solution.py:48
  2.6 10.9 %shard_map.73 = f32[64,4,128]{2,1,0:T(4,128)} custom-call(f32[8]{0:T(128)} %pad_maximum_fusion.2.params_ref, f32[16384,128]{1,0:T(8,128)} %bitcast.23), custom_call_target="tpu_custom_call" | custom-call | tf_op jit(solution)/shard_map/pallas_call | solution.py:52
  13.5 0.9 %constant_dynamic-update-slice_fusion.16 = f32[1032,4,128]{2,1,0:T(4,128)S(1)} fusion(f32[64,4,128]{2,1,0:T(4,128)} %shard_map.73), kind=kLoop, calls=%fused_computation.36 | loop fusion | bytes 262144
  15.1 0.9 %pad_maximum_fusion.1 = f32[65,4,128]{2,1,0:T(4,128)S(1)} fusion(f32[1,4,128]{2,1,0:T(4,128)S(1)} %get-tuple-element.16, f32[64,4,128]{2,1,0:T(4,128)} %shard_map.73), kind=kLoop, calls=%fused_computation.15 | loop fusion | flops 33280 | bytes 266240 | tf_op jit(solution)/shard_map/concatenate | solution.py:130
  16.0 3.1 %collective-permute-start = (f32[65,4,128]{2,1,0:T(4,128)S(1)}, f32[65,4,128]{2,1,0:T(4,128)S(1)}, u32[]{:S(2)}, u32[]{:S(2)}) collective-permute-start(f32[65,4,128]{2,1,0:T(4,128)S(1)} %pad_maximum_fusion.1), channel_id=1, source_target_pairs={{0,4},{4,8},{8,12},{12,14},{14,10},{10,6},{6,2},{2,0},{1,5},{5,9},... | collective-permute-start | bytes 399368 | tf_op jit(solution)/shard_map/ppermute | solution.py:105
  19.1 11.0 %shard_map.74 = f32[64,4,128]{2,1,0:T(4,128)} custom-call(f32[8]{0:T(128)} %pad_maximum_fusion.2.params_ref, f32[16384,128]{1,0:T(8,128)} %bitcast.24), custom_call_target="tpu_custom_call" | custom-call | tf_op jit(solution)/shard_map/pallas_call | solution.py:52
  30.1 2.0 %collective-permute-start.1 = (f32[64,4,128]{2,1,0:T(4,128)}, f32[64,4,128]{2,1,0:T(4,128)S(1)}, u32[]{:S(2)}, u32[]{:S(2)}) collective-permute-start(f32[64,4,128]{2,1,0:T(4,128)} %shard_map.74), channel_id=1, source_target_pairs={{0,4},{4,8},{8,12},{12,14},{14,10},{10,6},{6,2},{2,0},{1,5},{5,9},... | collective-permute-start | bytes 393224 | tf_op jit(solution)/shard_map/ppermute | solution.py:105
  32.2 0.8 %fusion.12 = (pred[256]{0:T(512)(128)(4,1)S(1)}, s32[256]{0:T(256)S(1)}) fusion(s32[]{:T(128)S(6)} %axis_index.25, s32[4096]{0:T(1024)} %param.13, s32[]{:T(128)S(6)} %select_n.99), kind=kLoop, calls=%fused_computation.69 | loop fusion | flops 4096 | bytes 2312 | tf_op jit(solution)/shard_map/eq | solution.py:148
  32.9 0.8 %dynamic_slice.7 = s32[256]{0:T(256)S(1)} dynamic-slice(s32[4096]{0:T(1024)} %param.13, s32[]{:T(128)S(6)} %select_n.104), dynamic_slice_sizes={256} | dynamic-slice | bytes 2052 | tf_op jit(solution)/shard_map/dynamic_slice | solution.py:142
  33.7 0.9 %constant_dynamic-update-slice_fusion.14 = f32[1032,4,128]{2,1,0:T(4,128)S(1)} fusion(f32[1032,4,128]{2,1,0:T(4,128)S(1)} %get-tuple-element.15, f32[64,4,128]{2,1,0:T(4,128)} %shard_map.74), kind=kLoop, calls=%fused_computation.34 | loop fusion | bytes 262144
  34.6 0.7 collective-permute-done.1
  35.3 2.0 %collective-permute-start.5 = (f32[64,4,128]{2,1,0:T(4,128)S(1)}, f32[64,4,128]{2,1,0:T(4,128)S(1)}, u32[]{:S(2)}, u32[]{:S(2)}) collective-permute-start(f32[64,4,128]{2,1,0:T(4,128)S(1)} %collective-permute-done.1), channel_id=1, source_target_pairs={{0,4},{4,8},{8,12},{12,14},{14,10},{10,6},{6,2},{2,0},{1,5},{5,9},... | collective-permute-start | bytes 393224 | tf_op jit(solution)/shard_map/ppermute | solution.py:105
  37.4 2.0 %collective-permute-start.4 = (f32[65,4,128]{2,1,0:T(4,128)S(1)}, f32[65,4,128]{2,1,0:T(4,128)S(1)}, u32[]{:S(2)}, u32[]{:S(2)}) collective-permute-start(f32[65,4,128]{2,1,0:T(4,128)S(1)} %collective-permute-done), channel_id=1, source_target_pairs={{0,4},{4,8},{8,12},{12,14},{14,10},{10,6},{6,2},{2,0},{1,5},{5,9},... | collective-permute-start | bytes 399368 | tf_op jit(solution)/shard_map/ppermute | solution.py:105
  39.6 2.0 %collective-permute-done.5 = f32[64,4,128]{2,1,0:T(4,128)S(1)} collective-permute-done((f32[64,4,128]{2,1,0:T(4,128)S(1)}, f32[64,4,128]{2,1,0:T(4,128)S(1)}, u32[]{:S(2)}, u32[]{:S(2)}) %collective-permute-start.5) | collective-permute-done | bytes 131104 | tf_op jit(solution)/shard_map/ppermute | solution.py:105
  41.6 1.8 %collective-permute-start.9 = (f32[64,4,128]{2,1,0:T(4,128)S(1)}, f32[64,4,128]{2,1,0:T(4,128)S(1)}, u32[]{:S(2)}, u32[]{:S(2)}) collective-permute-start(f32[64,4,128]{2,1,0:T(4,128)S(1)} %collective-permute-done.5), channel_id=1, source_target_pairs={{0,4},{4,8},{8,12},{12,14},{14,10},{10,6},{6,2},{2,0},{1,5},{5,9},... | collective-permute-start | bytes 393224 | tf_op jit(solution)/shard_map/ppermute | solution.py:105
  43.6 0.8 %collective-permute-done.4 = f32[65,4,128]{2,1,0:T(4,128)S(1)} collective-permute-done((f32[65,4,128]{2,1,0:T(4,128)S(1)}, f32[65,4,128]{2,1,0:T(4,128)S(1)}, u32[]{:S(2)}, u32[]{:S(2)}) %collective-permute-start.4) | collective-permute-done | bytes 133152 | tf_op jit(solution)/shard_map/ppermute | solution.py:105
  44.4 1.8 %collective-permute-start.8 = (f32[65,4,128]{2,1,0:T(4,128)S(1)}, f32[65,4,128]{2,1,0:T(4,128)S(1)}, u32[]{:S(2)}, u32[]{:S(2)}) collective-permute-start(f32[65,4,128]{2,1,0:T(4,128)S(1)} %collective-permute-done.4), channel_id=1, source_target_pairs={{0,4},{4,8},{8,12},{12,14},{14,10},{10,6},{6,2},{2,0},{1,5},{5,9},... | collective-permute-start | bytes 399368 | tf_op jit(solution)/shard_map/ppermute | solution.py:105
  46.3 0.3 collective-permute-start.10
  46.6 0.8 %collective-permute-done.9 = f32[64,4,128]{2,1,0:T(4,128)S(1)} collective-permute-done((f32[64,4,128]{2,1,0:T(4,128)S(1)}, f32[64,4,128]{2,1,0:T(4,128)S(1)}, u32[]{:S(2)}, u32[]{:S(2)}) %collective-permute-start.9) | collective-permute-done | bytes 131104 | tf_op jit(solution)/shard_map/ppermute | solution.py:105
  47.4 1.9 %collective-permute-start.13 = (f32[64,4,128]{2,1,0:T(4,128)S(1)}, f32[64,4,128]{2,1,0:T(4,128)S(1)}, u32[]{:S(2)}, u32[]{:S(2)}) collective-permute-start(f32[64,4,128]{2,1,0:T(4,128)S(1)} %collective-permute-done.9), channel_id=1, source_target_pairs={{0,4},{4,8},{8,12},{12,14},{14,10},{10,6},{6,2},{2,0},{1,5},{5,9},... | collective-permute-start | bytes 393224 | tf_op jit(solution)/shard_map/ppermute | solution.py:105
  49.3 1.5 %collective-permute-done.8 = f32[65,4,128]{2,1,0:T(4,128)S(1)} collective-permute-done((f32[65,4,128]{2,1,0:T(4,128)S(1)}, f32[65,4,128]{2,1,0:T(4,128)S(1)}, u32[]{:S(2)}, u32[]{:S(2)}) %collective-permute-start.8) | collective-permute-done | bytes 133152 | tf_op jit(solution)/shard_map/ppermute | solution.py:105
  50.8 1.8 %collective-permute-start.12 = (f32[65,4,128]{2,1,0:T(4,128)S(1)}, f32[65,4,128]{2,1,0:T(4,128)S(1)}, u32[]{:S(2)}, u32[]{:S(2)}) collective-permute-start(f32[65,4,128]{2,1,0:T(4,128)S(1)} %collective-permute-done.8), channel_id=1, source_target_pairs={{0,4},{4,8},{8,12},{12,14},{14,10},{10,6},{6,2},{2,0},{1,5},{5,9},... | collective-permute-start | bytes 399368 | tf_op jit(solution)/shard_map/ppermute | solution.py:105
  52.7 3.1 %collective-permute-done.12 = f32[65,4,128]{2,1,0:T(4,128)S(1)} collective-permute-done((f32[65,4,128]{2,1,0:T(4,128)S(1)}, f32[65,4,128]{2,1,0:T(4,128)S(1)}, u32[]{:S(2)}, u32[]{:S(2)}) %collective-permute-start.12) | collective-permute-done | bytes 133152 | tf_op jit(solution)/shard_map/ppermute | solution.py:105
  56.3 0.9 %copy-done = f32[1032,4,128]{2,1,0:T(4,128)} copy-done((f32[1032,4,128]{2,1,0:T(4,128)}, f32[1032,4,128]{2,1,0:T(4,128)S(1)}, u32[]{:S(2)}) %copy-start) | copy-done | bytes 2113560
  57.2 3.1 %gather_fusion.1 = f32[512,4,128]{2,1,0:T(4,128)S(1)} fusion(f32[1032,4,128]{2,1,0:T(4,128)} %copy-done, s32[1024]{0:T(1024)S(1)} %pad_clamp_fusion), kind=kCustom, calls=%fused_computation.1 | custom fusion | bytes 2099200 | tf_op jit(solution)/shard_map/jit(_take)/gather | solution.py:83
  60.3 1.8 %broadcast_select_fusion = f32[512,4,128]{2,1,0:T(4,128)S(1)} fusion(f32[512,4,128]{2,1,0:T(4,128)S(1)} %gather_fusion.1, pred[512]{0:T(512)(128)(4,1)S(1)} %broadcast_compare_fusion), kind=kLoop, calls=%fused_computation.9 | loop fusion | flops 262144 | bytes 2097664 | tf_op jit(solution)/shard_map/jit(_where)/select_n | solution.py:85
  62.1 3.1 %gather_fusion = f32[512,4,128]{2,1,0:T(4,128)S(1)} fusion(f32[1032,4,128]{2,1,0:T(4,128)} %copy-done, s32[1024]{0:T(1024)S(1)} %pad_clamp_fusion.1), kind=kCustom, calls=%fused_computation | custom fusion | bytes 2099200 | tf_op jit(solution)/shard_map/jit(_take)/gather | solution.py:84
  65.2 1.8 %broadcast_select_fusion.1 = f32[512,4,128]{2,1,0:T(4,128)S(1)} fusion(f32[512,4,128]{2,1,0:T(4,128)S(1)} %gather_fusion, pred[512]{0:T(512)(128)(4,1)S(1)} %get-tuple-element.13), kind=kLoop, calls=%fused_computation.10 | loop fusion | flops 262144 | bytes 2097664 | tf_op jit(solution)/shard_map/jit(_where)/select_n | solution.py:86
  67.0 0.8 %negate_exponential_fusion = (f32[512,1,128]{2,1,0:T(1,128)S(1)}, f32[512,1,128]{2,1,0:T(1,128)S(1)}) fusion(f32[512,4,128]{2,1,0:T(4,128)S(1)} %broadcast_select_fusion.1, f32[512,1,128]{2,1,0:T(1,128)S(1)} %bitcast.26, f32[512,4,128]{2,1,0:T(4,128)S(1)} %broadcast_select_fusion), kind=kLoop, calls=%fused_computation.14 | loop fusion | flops 262144 | bytes 1310720 | tf_op jit(solution)/shard_map/exp | solution.py:88
  67.9 0.4 fusion
  68.6 1.9 %collective-permute-done.14 = f32[256,4,128]{2,1,0:T(4,128)S(1)} collective-permute-done((f32[256,4,128]{2,1,0:T(4,128)S(1)}, f32[256,4,128]{2,1,0:T(4,128)S(1)}, u32[]{:S(2)}, u32[]{:S(2)}) %collective-permute-start.14) | collective-permute-done | bytes 524320 | tf_op jit(solution)/shard_map/ppermute | solution.py:147
  70.5 1.6 %fusion.2 = f32[256,4,128]{2,1,0:T(4,128)} fusion(f32[256,4,128]{2,1,0:T(4,128)S(1)} %collective-permute-done.14, f32[512,3,128]{2,1,0:T(4,128)S(1)} %fusion, f32[512,1,128]{2,1,0:T(1,128)S(1)} %get-tuple-element.18, pred[256]{0:T(512)(128)(4,1)S(1)} %get-tuple-element.11), kind=kLoop, calls=%fused_computation.7 | loop fusion | flops 262144 | bytes 2097408 | tf_op jit(solution)/shard_map/jit(_where)/select_n | solution.py:149
  (49 shorter events, 1.5 us)
Async XLA Ops:
  16.0 21.3 %collective-permute-start = (f32[65,4,128]{2,1,0:T(4,128)S(1)}, f32[65,4,128]{2,1,0:T(4,128)S(1)}, u32[]{:S(2)}, u32[]{:S(2)}) collective-permute-start(f32[65,4,128]{2,1,0:T(4,128)S(1)} %pad_maximum_fusion.1), channel_id=1, source_target_pairs={{0,4},{4,8},{8,12},{12,14},{14,10},{10,6},{6,2},{2,0},{1,5},{5,9},... | collective-permute-start | bytes 399368 | tf_op jit(solution)/shard_map/ppermute | solution.py:105
  19.1 20.3 %collective-permute-start.2 = (f32[65,4,128]{2,1,0:T(4,128)S(1)}, f32[65,4,128]{2,1,0:T(4,128)S(1)}, u32[]{:S(2)}, u32[]{:S(2)}) collective-permute-start(f32[65,4,128]{2,1,0:T(4,128)S(1)} %pad_maximum_fusion.1), channel_id=1, source_target_pairs={{4,0},{8,4},{12,8},{14,12},{10,14},{6,10},{2,6},{0,2},{5,1},{9,5},... | collective-permute-start | bytes 399368 | tf_op jit(solution)/shard_map/ppermute | solution.py:108
  30.1 5.2 %collective-permute-start.1 = (f32[64,4,128]{2,1,0:T(4,128)}, f32[64,4,128]{2,1,0:T(4,128)S(1)}, u32[]{:S(2)}, u32[]{:S(2)}) collective-permute-start(f32[64,4,128]{2,1,0:T(4,128)} %shard_map.74), channel_id=1, source_target_pairs={{0,4},{4,8},{8,12},{12,14},{14,10},{10,6},{6,2},{2,0},{1,5},{5,9},... | collective-permute-start | bytes 393224 | tf_op jit(solution)/shard_map/ppermute | solution.py:105
  32.2 5.2 %collective-permute-start.3 = (f32[64,4,128]{2,1,0:T(4,128)}, f32[64,4,128]{2,1,0:T(4,128)S(1)}, u32[]{:S(2)}, u32[]{:S(2)}) collective-permute-start(f32[64,4,128]{2,1,0:T(4,128)} %shard_map.74), channel_id=1, source_target_pairs={{4,0},{8,4},{12,8},{14,12},{10,14},{6,10},{2,6},{0,2},{5,1},{9,5},... | collective-permute-start | bytes 393224 | tf_op jit(solution)/shard_map/ppermute | solution.py:108
  35.3 6.2 %collective-permute-start.5 = (f32[64,4,128]{2,1,0:T(4,128)S(1)}, f32[64,4,128]{2,1,0:T(4,128)S(1)}, u32[]{:S(2)}, u32[]{:S(2)}) collective-permute-start(f32[64,4,128]{2,1,0:T(4,128)S(1)} %collective-permute-done.1), channel_id=1, source_target_pairs={{0,4},{4,8},{8,12},{12,14},{14,10},{10,6},{6,2},{2,0},{1,5},{5,9},... | collective-permute-start | bytes 393224 | tf_op jit(solution)/shard_map/ppermute | solution.py:105
  37.3 6.0 %collective-permute-start.7 = (f32[64,4,128]{2,1,0:T(4,128)S(1)}, f32[64,4,128]{2,1,0:T(4,128)S(1)}, u32[]{:S(2)}, u32[]{:S(2)}) collective-permute-start(f32[64,4,128]{2,1,0:T(4,128)S(1)} %collective-permute-done.3), channel_id=1, source_target_pairs={{4,0},{8,4},{12,8},{14,12},{10,14},{6,10},{2,6},{0,2},{5,1},{9,5},... | collective-permute-start | bytes 393224 | tf_op jit(solution)/shard_map/ppermute | solution.py:108
  37.4 7.0 %collective-permute-start.4 = (f32[65,4,128]{2,1,0:T(4,128)S(1)}, f32[65,4,128]{2,1,0:T(4,128)S(1)}, u32[]{:S(2)}, u32[]{:S(2)}) collective-permute-start(f32[65,4,128]{2,1,0:T(4,128)S(1)} %collective-permute-done), channel_id=1, source_target_pairs={{0,4},{4,8},{8,12},{12,14},{14,10},{10,6},{6,2},{2,0},{1,5},{5,9},... | collective-permute-start | bytes 399368 | tf_op jit(solution)/shard_map/ppermute | solution.py:105
  39.4 6.8 %collective-permute-start.6 = (f32[65,4,128]{2,1,0:T(4,128)S(1)}, f32[65,4,128]{2,1,0:T(4,128)S(1)}, u32[]{:S(2)}, u32[]{:S(2)}) collective-permute-start(f32[65,4,128]{2,1,0:T(4,128)S(1)} %collective-permute-done.2), channel_id=1, source_target_pairs={{4,0},{8,4},{12,8},{14,12},{10,14},{6,10},{2,6},{0,2},{5,1},{9,5},... | collective-permute-start | bytes 399368 | tf_op jit(solution)/shard_map/ppermute | solution.py:108
  41.6 5.9 %collective-permute-start.9 = (f32[64,4,128]{2,1,0:T(4,128)S(1)}, f32[64,4,128]{2,1,0:T(4,128)S(1)}, u32[]{:S(2)}, u32[]{:S(2)}) collective-permute-start(f32[64,4,128]{2,1,0:T(4,128)S(1)} %collective-permute-done.5), channel_id=1, source_target_pairs={{0,4},{4,8},{8,12},{12,14},{14,10},{10,6},{6,2},{2,0},{1,5},{5,9},... | collective-permute-start | bytes 393224 | tf_op jit(solution)/shard_map/ppermute | solution.py:105
  43.3 9.3 %collective-permute-start.11 = (f32[64,4,128]{2,1,0:T(4,128)S(1)}, f32[64,4,128]{2,1,0:T(4,128)S(1)}, u32[]{:S(2)}, u32[]{:S(2)}) collective-permute-start(f32[64,4,128]{2,1,0:T(4,128)S(1)} %collective-permute-done.7), channel_id=1, source_target_pairs={{4,0},{8,4},{12,8},{14,12},{10,14},{6,10},{2,6},{0,2},{5,1},{9,5},... | collective-permute-start | bytes 393224 | tf_op jit(solution)/shard_map/ppermute | solution.py:108
  44.4 6.4 %collective-permute-start.8 = (f32[65,4,128]{2,1,0:T(4,128)S(1)}, f32[65,4,128]{2,1,0:T(4,128)S(1)}, u32[]{:S(2)}, u32[]{:S(2)}) collective-permute-start(f32[65,4,128]{2,1,0:T(4,128)S(1)} %collective-permute-done.4), channel_id=1, source_target_pairs={{0,4},{4,8},{8,12},{12,14},{14,10},{10,6},{6,2},{2,0},{1,5},{5,9},... | collective-permute-start | bytes 399368 | tf_op jit(solution)/shard_map/ppermute | solution.py:105
  46.3 6.4 %collective-permute-start.10 = (f32[65,4,128]{2,1,0:T(4,128)S(1)}, f32[65,4,128]{2,1,0:T(4,128)S(1)}, u32[]{:S(2)}, u32[]{:S(2)}) collective-permute-start(f32[65,4,128]{2,1,0:T(4,128)S(1)} %collective-permute-done.6), channel_id=1, source_target_pairs={{4,0},{8,4},{12,8},{14,12},{10,14},{6,10},{2,6},{0,2},{5,1},{9,5},... | collective-permute-start | bytes 399368 | tf_op jit(solution)/shard_map/ppermute | solution.py:108
  47.4 8.4 %collective-permute-start.13 = (f32[64,4,128]{2,1,0:T(4,128)S(1)}, f32[64,4,128]{2,1,0:T(4,128)S(1)}, u32[]{:S(2)}, u32[]{:S(2)}) collective-permute-start(f32[64,4,128]{2,1,0:T(4,128)S(1)} %collective-permute-done.9), channel_id=1, source_target_pairs={{0,4},{4,8},{8,12},{12,14},{14,10},{10,6},{6,2},{2,0},{1,5},{5,9},... | collective-permute-start | bytes 393224 | tf_op jit(solution)/shard_map/ppermute | solution.py:105
  50.8 5.0 %collective-permute-start.12 = (f32[65,4,128]{2,1,0:T(4,128)S(1)}, f32[65,4,128]{2,1,0:T(4,128)S(1)}, u32[]{:S(2)}, u32[]{:S(2)}) collective-permute-start(f32[65,4,128]{2,1,0:T(4,128)S(1)} %collective-permute-done.8), channel_id=1, source_target_pairs={{0,4},{4,8},{8,12},{12,14},{14,10},{10,6},{6,2},{2,0},{1,5},{5,9},... | collective-permute-start | bytes 399368 | tf_op jit(solution)/shard_map/ppermute | solution.py:105
  55.8 1.4 %copy-start = (f32[1032,4,128]{2,1,0:T(4,128)}, f32[1032,4,128]{2,1,0:T(4,128)S(1)}, u32[]{:S(2)}) copy-start(f32[1032,4,128]{2,1,0:T(4,128)S(1)} %constant_dynamic-update-slice_fusion) | copy-start | bytes 6340612
  68.5 2.0 %collective-permute-start.14 = (f32[256,4,128]{2,1,0:T(4,128)S(1)}, f32[256,4,128]{2,1,0:T(4,128)S(1)}, u32[]{:S(2)}, u32[]{:S(2)}) collective-permute-start(f32[256,4,128]{2,1,0:T(4,128)S(1)} %pad_maximum_fusion), channel_id=1, source_target_pairs={{0,1},{1,0},{2,3},{3,2},{4,5},{5,4},{6,7},{7,6},{8,9},{9,8},{10,11... | collective-permute-start | bytes 1572872 | tf_op jit(solution)/shard_map/ppermute | solution.py:147

commit v8 on v6

--- a/solution.py
+++ b/solution.py
@@ -10,7 +10,7 @@
 
 def render_kernel(params_ref, density_ref, out_ref):
     block_rows = out_ref.shape[0]
-    pixels = out_ref.shape[2]
+    pixels = out_ref.shape[1] // 4
     sample_count = density_ref.shape[0] // block_rows
     absorb = params_ref[0]
     slopes = [params_ref[1 + channel] for channel in range(3)]
@@ -35,8 +35,8 @@
     row_ids = pl.program_id(0) * block_rows + lax.broadcasted_iota(jnp.int32, (block_rows, pixels), 0)
     visible = row_ids.astype(jnp.float32) < shown
     for channel in range(3):
-        out_ref[:, channel, :] = jnp.where(visible, carry[2 + channel], 0.0)
-    out_ref[:, 3, :] = jnp.where(visible, carry[1], 0.0)
+        out_ref[:, channel * pixels:(channel + 1) * pixels] = jnp.where(visible, carry[2 + channel], 0.0)
+    out_ref[:, 3 * pixels:] = jnp.where(visible, carry[1], 0.0)
 
 
 def render_layers(density_block, shown_rows, absorb, colour_slope, colour_offset, block_rows=8):
@@ -52,13 +52,15 @@
             pl.BlockSpec(memory_space=pltpu.SMEM),
             pl.BlockSpec((block_rows * sample_count, pixels), lambda i: (i, 0)),
         ],
-        out_specs=pl.BlockSpec((block_rows, 4, pixels), lambda i: (i, 0, 0)),
-        out_shape=jax.ShapeDtypeStruct((brick_rows, 4, pixels), jnp.float32),
+        out_specs=pl.BlockSpec((block_rows, 4 * pixels), lambda i: (i, 0)),
+        out_shape=jax.ShapeDtypeStruct((brick_rows, 4 * pixels), jnp.float32),
     )(params, density_block.reshape(brick_rows * sample_count, pixels))
 
 
 def composite_rows(flat, starts, counts, brick_ids, stride, image_rows):
     slot_count = starts.shape[0]
+    pixels = flat.shape[1] // 4
+    zero_row = flat.shape[0] - 1
     offset = image_rows[:, None] - starts[None, :]
     covered = (offset >= 0) & (offset < counts[None, :])
     depth_ids = brick_ids[None, :]
@@ -66,21 +68,16 @@
     back = jnp.max(jnp.where(covered, depth_ids, -1), axis=1)
     is_back = (depth_ids == back[:, None]) & covered
     is_front = (depth_ids == back[:, None] - 1) & covered
-    back_off = jnp.sum(jnp.where(is_back, offset, 0), axis=1)
-    front_off = jnp.sum(jnp.where(is_front, offset, 0), axis=1)
-    back_slot = jnp.sum(jnp.where(is_back, slot_ids, 0), axis=1)
-    front_slot = jnp.sum(jnp.where(is_front, slot_ids, 0), axis=1)
-    has_front = jnp.any(is_front, axis=1)
-    has_back = back >= 0
-    back_idx = jnp.where(has_back, back_slot * stride + back_off, 0)
-    front_idx = jnp.where(has_front, front_slot * stride + front_off, 0)
+    back_idx = jnp.sum(jnp.where(is_back, slot_ids * stride + offset, 0), axis=1)
+    front_idx = jnp.sum(jnp.where(is_front, slot_ids * stride + offset, 0), axis=1)
+    back_idx = jnp.where(back >= 0, back_idx, zero_row)
+    front_idx = jnp.where(jnp.any(is_front, axis=1), front_idx, zero_row)
     back_rows = jnp.take(flat, back_idx, axis=0, mode="clip")
     front_rows = jnp.take(flat, front_idx, axis=0, mode="clip")
-    back_rows = jnp.where(has_back[:, None, None], back_rows, 0.0)
-    front_rows = jnp.where(has_front[:, None, None], front_rows, 0.0)
-    front_depth = front_rows[:, 3:4, :]
-    colours = front_rows[:, :3, :] + jnp.exp(-front_depth) * back_rows[:, :3, :]
-    opacity = 1.0 - jnp.exp(-(front_depth + back_rows[:, 3:4, :]))
+    front_depth = front_rows[:, 3 * pixels:]
+    through = jnp.exp(-front_depth)
+    colours = front_rows[:, :3 * pixels] + jnp.concatenate([through] * 3, axis=1) * back_rows[:, :3 * pixels]
+    opacity = 1.0 - jnp.exp(-(front_depth + back_rows[:, 3 * pixels:]))
     return jnp.concatenate([colours, opacity], axis=1)
 
 
@@ -101,7 +98,7 @@
         if 2 * step < count:
             behind = lax.ppermute(behind, "depth", backward)
             slots.append(behind)
-    return jnp.concatenate(slots, axis=0)
+    return slots
 
 
 def on_device(density, foot_start, foot_rows, extinction, colour_slope, colour_offset, tile_source):
@@ -115,13 +112,14 @@
     start = foot_start[0, 0]
     shown = foot_rows[0, 0]
     layers = render_layers(density[0, 0], shown, extinction[0], colour_slope, colour_offset)
-    brick_rows, channels, pixels = layers.shape
-    lane = lax.broadcasted_iota(jnp.int32, (1, channels, pixels), 2)
+    brick_rows, width = layers.shape
+    lane = lax.broadcasted_iota(jnp.int32, (1, width), 1)
     meta = jnp.where(lane == 0, start, jnp.where(lane == 1, shown, jnp.where(lane == 2, depth_index, 0)))
     stride = brick_rows + 1
     own = jnp.concatenate([layers, meta.astype(jnp.float32)], axis=0)
-    flat = ring_gather(own, depth_count)
-    meta_rows = flat.reshape(depth_count, stride, channels, pixels)[:, brick_rows, 0, :3]
+    slots = ring_gather(own, depth_count)
+    flat = jnp.concatenate(slots + [jnp.zeros((1, width), jnp.float32)], axis=0)
+    meta_rows = jnp.concatenate([slot[brick_rows:, :3] for slot in slots], axis=0)
     starts = meta_rows[:, 0].astype(jnp.int32)
     counts = meta_rows[:, 1].astype(jnp.int32)
     brick_ids = meta_rows[:, 2].astype(jnp.int32)
@@ -135,7 +133,8 @@
     for_partner = rows[owner_rows:]
     received = lax.ppermute(for_partner, "screen", [(0, 1), (1, 0)])
     in_my_half = (wanted_self // half_rows) == screen_index
-    return jnp.where(in_my_half[:, None, None], mine, received)
+    frame = jnp.where(in_my_half[:, None], mine, received)
+    return frame.reshape(owner_rows, 4, width // 4)
 
 
 def solution(mesh):

time: 70 us -> 72 us (1.029)
  local copies, waits for them, and re-layouts: 7.26 us -> 12.9 us
  other arithmetic: 9.96 us -> 5.99 us
  waiting for transfers between devices: 21.1 us -> 21.9 us
    concatenate x1 -> x2, local copies, waits for them, and re-layouts: 0.04 us -> 5.17 us  [the longest x1 5.14 us: on_device(): flat = jnp.concatenate(slots + [jnp.zeros((1, width), jnp.float32)], axis=0)]
    select_n x6 -> x2, other arithmetic: 5.15 us -> 0.12 us  [the longest x1 0.11 us: on_device(): frame = jnp.where(in_my_half[:, None], mine, received)]
    ppermute x4, waiting for transfers between devices: 17.2 us -> 20 us  [ring_gather(): ahead = lax.ppermute(ahead, 'depth', forward)]
    slice x1 -> x8, local copies, waits for them, and re-layouts: 0.01 us -> 2.04 us  [on_device(): slot[brick_rows:, :3]]
    ppermute x3, waiting for transfers between devices: 2 us -> 0.01 us  [ring_gather(): behind = lax.ppermute(behind, 'depth', backward)]
    gather x1, local copies, waits for them, and re-layouts: 3.1 us -> 1.62 us  [composite_rows(): front_rows = jnp.take(flat, front_idx, axis=0, mode='clip')]
    unnamed x10 -> x0, local copies, waits for them, and re-layouts: 1.27 us -> none
    reshape x0 -> x1, local copies, waits for them, and re-layouts: none -> 0.96 us  [on_device(): return frame.reshape(owner_rows, 4, width // 4)]
  transfers between devices with their start and end apart: 8 -> 8, of which waited for: 7 -> 5; matrix products, arithmetic and copies ran while one was open for 3% -> 4% of each run, Pallas kernels for 0% -> 0%
where the time goes in v8:
time: 72 us; the launch traced here: 71.5 us
  waiting for transfers between devices  21.9 us (30%)
  Pallas kernels  20.1 us (28%)
  local copies, waits for them, and re-layouts  12.9 us (18%)
  starting transfers between devices  8.55 us (12%)
  other arithmetic  5.99 us (8%)
  between operations  2.07 us (3%)
    pallas_call x1, Pallas kernels, render_layers(): pl.pallas_call(render_kernel, grid=(brick_rows // block_rows,), in_specs=...  20.1 us
    ppermute x4, waiting for transfers between devices, ring_gather(): ahead = lax.ppermute(ahead, 'depth', forward)  20 us
    ppermute x4, starting transfers between devices, ring_gather(): ahead = lax.ppermute(ahead, 'depth', forward)  7.7 us
    concatenate x1, local copies, waits for them, and re-layouts, on_device(): flat = jnp.concatenate(slots + [jnp.zeros((1, width), jnp.float32)], axis=0)  5.14 us
    gather x1, local copies, waits for them, and re-layouts, composite_rows(): back_rows = jnp.take(flat, back_idx, axis=0, mode='clip')  2.34 us
    slice x8, local copies, waits for them, and re-layouts, on_device(): slot[brick_rows:, :3]  2.04 us
    ppermute x1, waiting for transfers between devices, on_device(): received = lax.ppermute(for_partner, 'screen', [(0, 1), (1, 0)])  1.9 us
    gather x1, local copies, waits for them, and re-layouts, composite_rows(): front_rows = jnp.take(flat, front_idx, axis=0, mode='clip')  1.62 us
  transfers between devices with their start and end apart: 8, of which 5 were waited for; matrix products, arithmetic and copies ran while one was open for 4% of the time, Pallas kernels for 0%

profile of v8, /device:TPU:0, one launch (start us, length us, event | category | flops | bytes accessed | tf_op | source)
XLA Modules:
  0.0 71.5 jit_solution(13569774855654916460)
XLA Ops:
  1.9 1.3 %pad_maximum_fusion.2.params_ref = f32[8]{0:T(128)} fusion(f32[1]{0:T(128)} %bitcast.1, f32[3]{0:T(128)} %param.12, f32[3]{0:T(128)} %param.11, f32[1]{0:T(128)S(6)} %copy.10), kind=kLoop, calls=%fused_computation.47 | loop fusion | flops 24 | bytes 64 | tf_op jit(solution)/shard_map/concatenate | solution.py:44
  3.2 20.1 %shard_map.73 = f32[128,512]{1,0:T(8,128)} custom-call(f32[8]{0:T(128)} %pad_maximum_fusion.2.params_ref, f32[16384,128]{1,0:T(8,128)} %bitcast.7), custom_call_target="tpu_custom_call" | custom-call | tf_op jit(solution)/shard_map/pallas_call | solution.py:48
  23.3 1.0 %pad_maximum_fusion.1 = f32[129,512]{1,0:T(8,128)S(1)} fusion(f32[1,512]{1,0:T(1,128)S(1)} %fusion.13, f32[128,512]{1,0:T(8,128)} %shard_map.73), kind=kLoop, calls=%fused_computation.9 | loop fusion | flops 66048 | bytes 528384 | tf_op jit(solution)/shard_map/concatenate | solution.py:119
  24.3 3.1 %collective-permute-start = (f32[129,512]{1,0:T(8,128)S(1)}, f32[129,512]{1,0:T(8,128)S(1)}, u32[]{:S(2)}, u32[]{:S(2)}) collective-permute-start(f32[129,512]{1,0:T(8,128)S(1)} %pad_maximum_fusion.1), channel_id=1, source_target_pairs={{0,4},{4,8},{8,12},{12,14},{14,10},{10,6},{6,2},{2,0},{1,5},{5,9},... | collective-permute-start | bytes 792584 | tf_op jit(solution)/shard_map/ppermute | solution.py:96
  27.4 0.0 collective-permute-start.1
  27.4 6.6 %collective-permute-done = f32[129,512]{1,0:T(8,128)S(1)} collective-permute-done((f32[129,512]{1,0:T(8,128)S(1)}, f32[129,512]{1,0:T(8,128)S(1)}, u32[]{:S(2)}, u32[]{:S(2)}) %collective-permute-start) | collective-permute-done | bytes 264224 | tf_op jit(solution)/shard_map/ppermute | solution.py:96
  34.0 1.8 %collective-permute-start.2 = (f32[129,512]{1,0:T(8,128)S(1)}, f32[129,512]{1,0:T(8,128)S(1)}, u32[]{:S(2)}, u32[]{:S(2)}) collective-permute-start(f32[129,512]{1,0:T(8,128)S(1)} %collective-permute-done), channel_id=1, source_target_pairs={{0,4},{4,8},{8,12},{12,14},{14,10},{10,6},{6,2},{2,0},{1,5},{5,9},... | collective-permute-start | bytes 792584 | tf_op jit(solution)/shard_map/ppermute | solution.py:96
  35.8 0.2 collective-permute-start.3
  36.0 5.8 %collective-permute-done.2 = f32[129,512]{1,0:T(8,128)S(1)} collective-permute-done((f32[129,512]{1,0:T(8,128)S(1)}, f32[129,512]{1,0:T(8,128)S(1)}, u32[]{:S(2)}, u32[]{:S(2)}) %collective-permute-start.2) | collective-permute-done | bytes 264224 | tf_op jit(solution)/shard_map/ppermute | solution.py:96
  41.8 1.5 %collective-permute-start.4 = (f32[129,512]{1,0:T(8,128)S(1)}, f32[129,512]{1,0:T(8,128)}, u32[]{:S(2)}, u32[]{:S(2)}) collective-permute-start(f32[129,512]{1,0:T(8,128)S(1)} %collective-permute-done.2), channel_id=1, source_target_pairs={{0,4},{4,8},{8,12},{12,14},{14,10},{10,6},{6,2},{2,0},{1,5},{5,9},... | collective-permute-start | bytes 792584 | tf_op jit(solution)/shard_map/ppermute | solution.py:96
  43.3 0.5 collective-permute-start.5
  43.9 5.0 %collective-permute-done.4 = f32[129,512]{1,0:T(8,128)} collective-permute-done((f32[129,512]{1,0:T(8,128)S(1)}, f32[129,512]{1,0:T(8,128)}, u32[]{:S(2)}, u32[]{:S(2)}) %collective-permute-start.4) | collective-permute-done | bytes 264224 | tf_op jit(solution)/shard_map/ppermute | solution.py:96
  48.9 1.3 %collective-permute-start.6 = (f32[129,512]{1,0:T(8,128)}, f32[129,512]{1,0:T(8,128)}, u32[]{:S(2)}, u32[]{:S(2)}) collective-permute-start(f32[129,512]{1,0:T(8,128)} %collective-permute-done.4), channel_id=1, source_target_pairs={{0,4},{4,8},{8,12},{12,14},{14,10},{10,6},{6,2},{2,0},{1,5},{5,9},... | collective-permute-start | bytes 792584 | tf_op jit(solution)/shard_map/ppermute | solution.py:96
  50.2 0.8 %dynamic_slice.7 = s32[256]{0:T(256)S(1)} dynamic-slice(s32[4096]{0:T(1024)} %param.13, s32[]{:T(128)S(6)} %select_n.104), dynamic_slice_sizes={256} | dynamic-slice | bytes 2052 | tf_op jit(solution)/shard_map/dynamic_slice | solution.py:129
  51.0 0.8 %fusion.14 = (pred[256]{0:T(512)(128)(4,1)S(1)}, s32[256]{0:T(256)S(1)}) fusion(s32[]{:T(128)S(6)} %axis_index.25, s32[4096]{0:T(1024)} %param.13, s32[]{:T(128)S(6)} %select_n.99), kind=kLoop, calls=%fused_computation.46 | loop fusion | flops 4096 | bytes 2312 | tf_op jit(solution)/shard_map/eq | solution.py:135
  51.8 0.7 slice.77
  52.5 0.7 slice.78
  53.1 2.6 %collective-permute-done.6 = f32[129,512]{1,0:T(8,128)} collective-permute-done((f32[129,512]{1,0:T(8,128)}, f32[129,512]{1,0:T(8,128)}, u32[]{:S(2)}, u32[]{:S(2)}) %collective-permute-start.6) | collective-permute-done | bytes 264224 | tf_op jit(solution)/shard_map/ppermute | solution.py:96
  55.7 0.7 slice.79
  56.4 0.2 convert_reduce_fusion.1
  56.6 0.1 select_reduce_fusion
  56.7 0.1 fusion.11
  56.8 0.1 fusion.8
  56.9 5.1 %concatenate.34 = f32[1033,512]{1,0:T(8,128)S(1)} concatenate(f32[128,512]{1,0:T(8,128)} %shard_map.73, f32[1,512]{1,0:T(1,128)S(1)} %fusion.13, f32[129,512]{1,0:T(8,128)S(1)} %collective-permute-done, f32[129,512]{1,0:T(8,128)S(1)} %collective-permute-done.1, f32[129,512]{1,0:T(8,128)S(1)} %collective-permute-done.2, f32[129,512]{1,0:T(8,128)S(1)} %collective-permute-done.3, ...), dimensions={0} | concatenate | bytes 4231168 | tf_op jit(solution)/shard_map/concatenate | solution.py:121
  62.1 1.6 %gather_fusion = f32[512,512]{1,0:T(8,128)S(1)} fusion(f32[1033,512]{1,0:T(8,128)S(1)} %concatenate.34, s32[1024]{0:T(1024)S(1)} %pad_clamp_fusion.1), kind=kCustom, calls=%fused_computation | custom fusion | bytes 2099200 | tf_op jit(solution)/shard_map/jit(_take)/gather | solution.py:76
  63.7 2.3 %gather_fusion.1 = f32[512,512]{1,0:T(8,128)} fusion(f32[1033,512]{1,0:T(8,128)S(1)} %concatenate.34, s32[1024]{0:T(1024)S(1)} %pad_clamp_fusion), kind=kCustom, calls=%fused_computation.1 | custom fusion | bytes 2099200 | tf_op jit(solution)/shard_map/jit(_take)/gather | solution.py:75
  66.1 1.0 %negate_exponential_fusion = (f32[512,128]{1,0:T(8,128)S(1)}, f32[512,128]{1,0:T(8,128)S(1)}) fusion(f32[512,512]{1,0:T(8,128)S(1)} %gather_fusion, f32[512,512]{1,0:T(8,128)} %gather_fusion.1), kind=kLoop, calls=%fused_computation.14 | loop fusion | flops 262144 | bytes 1048576 | tf_op jit(solution)/shard_map/exp | solution.py:78
  67.1 1.3 %fusion = f32[512,384]{1,0:T(8,128)S(1)} fusion(f32[512,512]{1,0:T(8,128)} %gather_fusion.1, f32[512,512]{1,0:T(8,128)S(1)} %gather_fusion, f32[512,128]{1,0:T(8,128)S(1)} %get-tuple-element.12), kind=kLoop, calls=%fused_computation.5 | loop fusion | flops 786432 | bytes 2621440 | tf_op jit(solution)/shard_map/add | solution.py:79
  68.4 0.1 collective-permute-start.7
  68.5 1.9 %collective-permute-done.7 = f32[256,512]{1,0:T(8,128)S(1)} collective-permute-done((f32[256,512]{1,0:T(8,128)S(1)}, f32[256,512]{1,0:T(8,128)S(1)}, u32[]{:S(2)}, u32[]{:S(2)}) %collective-permute-start.7) | collective-permute-done | bytes 524320 | tf_op jit(solution)/shard_map/ppermute | solution.py:134
  70.4 0.1 fusion.2
  70.5 1.0 %reshape.156 = f32[256,4,128]{2,1,0:T(4,128)} reshape(f32[256,512]{1,0:T(8,128)S(1)} %fusion.2) | data formatting | bytes 1048576 | tf_op jit(solution)/shard_map/reshape | solution.py:137
  (18 shorter events, 0.1 us)
Async XLA Ops:
  24.3 9.7 %collective-permute-start = (f32[129,512]{1,0:T(8,128)S(1)}, f32[129,512]{1,0:T(8,128)S(1)}, u32[]{:S(2)}, u32[]{:S(2)}) collective-permute-start(f32[129,512]{1,0:T(8,128)S(1)} %pad_maximum_fusion.1), channel_id=1, source_target_pairs={{0,4},{4,8},{8,12},{12,14},{14,10},{10,6},{6,2},{2,0},{1,5},{5,9},... | collective-permute-start | bytes 792584 | tf_op jit(solution)/shard_map/ppermute | solution.py:96
  27.4 8.4 %collective-permute-start.1 = (f32[129,512]{1,0:T(8,128)S(1)}, f32[129,512]{1,0:T(8,128)S(1)}, u32[]{:S(2)}, u32[]{:S(2)}) collective-permute-start(f32[129,512]{1,0:T(8,128)S(1)} %pad_maximum_fusion.1), channel_id=1, source_target_pairs={{4,0},{8,4},{12,8},{14,12},{10,14},{6,10},{2,6},{0,2},{5,1},{9,5},... | collective-permute-start | bytes 792584 | tf_op jit(solution)/shard_map/ppermute | solution.py:99
  34.0 7.8 %collective-permute-start.2 = (f32[129,512]{1,0:T(8,128)S(1)}, f32[129,512]{1,0:T(8,128)S(1)}, u32[]{:S(2)}, u32[]{:S(2)}) collective-permute-start(f32[129,512]{1,0:T(8,128)S(1)} %collective-permute-done), channel_id=1, source_target_pairs={{0,4},{4,8},{8,12},{12,14},{14,10},{10,6},{6,2},{2,0},{1,5},{5,9},... | collective-permute-start | bytes 792584 | tf_op jit(solution)/shard_map/ppermute | solution.py:96
  35.8 7.5 %collective-permute-start.3 = (f32[129,512]{1,0:T(8,128)S(1)}, f32[129,512]{1,0:T(8,128)S(1)}, u32[]{:S(2)}, u32[]{:S(2)}) collective-permute-start(f32[129,512]{1,0:T(8,128)S(1)} %collective-permute-done.1), channel_id=1, source_target_pairs={{4,0},{8,4},{12,8},{14,12},{10,14},{6,10},{2,6},{0,2},{5,1},{9,5},... | collective-permute-start | bytes 792584 | tf_op jit(solution)/shard_map/ppermute | solution.py:99
  41.8 7.0 %collective-permute-start.4 = (f32[129,512]{1,0:T(8,128)S(1)}, f32[129,512]{1,0:T(8,128)}, u32[]{:S(2)}, u32[]{:S(2)}) collective-permute-start(f32[129,512]{1,0:T(8,128)S(1)} %collective-permute-done.2), channel_id=1, source_target_pairs={{0,4},{4,8},{8,12},{12,14},{14,10},{10,6},{6,2},{2,0},{1,5},{5,9},... | collective-permute-start | bytes 792584 | tf_op jit(solution)/shard_map/ppermute | solution.py:96
  43.3 9.2 %collective-permute-start.5 = (f32[129,512]{1,0:T(8,128)S(1)}, f32[129,512]{1,0:T(8,128)}, u32[]{:S(2)}, u32[]{:S(2)}) collective-permute-start(f32[129,512]{1,0:T(8,128)S(1)} %collective-permute-done.3), channel_id=1, source_target_pairs={{4,0},{8,4},{12,8},{14,12},{10,14},{6,10},{2,6},{0,2},{5,1},{9,5},... | collective-permute-start | bytes 792584 | tf_op jit(solution)/shard_map/ppermute | solution.py:99
  48.9 6.9 %collective-permute-start.6 = (f32[129,512]{1,0:T(8,128)}, f32[129,512]{1,0:T(8,128)}, u32[]{:S(2)}, u32[]{:S(2)}) collective-permute-start(f32[129,512]{1,0:T(8,128)} %collective-permute-done.4), channel_id=1, source_target_pairs={{0,4},{4,8},{8,12},{12,14},{14,10},{10,6},{6,2},{2,0},{1,5},{5,9},... | collective-permute-start | bytes 792584 | tf_op jit(solution)/shard_map/ppermute | solution.py:96
  68.4 2.0 %collective-permute-start.7 = (f32[256,512]{1,0:T(8,128)S(1)}, f32[256,512]{1,0:T(8,128)S(1)}, u32[]{:S(2)}, u32[]{:S(2)}) collective-permute-start(f32[256,512]{1,0:T(8,128)S(1)} %pad_maximum_fusion), channel_id=1, source_target_pairs={{0,1},{1,0},{2,3},{3,2},{4,5},{5,4},{6,7},{7,6},{8,9},{9,8},{10,11... | collective-permute-start | bytes 1572872 | tf_op jit(solution)/shard_map/ppermute | solution.py:134

commit v9 on v8

--- a/solution.py
+++ b/solution.py
@@ -8,14 +8,14 @@
 BLK = 256
 
 
-def render_kernel(params_ref, density_ref, out_ref):
+def render_kernel(absorb_ref, slope_ref, offset_ref, shown_ref, density_ref, out_ref):
     block_rows = out_ref.shape[0]
     pixels = out_ref.shape[1] // 4
     sample_count = density_ref.shape[0] // block_rows
-    absorb = params_ref[0]
-    slopes = [params_ref[1 + channel] for channel in range(3)]
-    offsets = [params_ref[4 + channel] for channel in range(3)]
-    shown = params_ref[7]
+    absorb = absorb_ref[0]
+    slopes = [slope_ref[channel] for channel in range(3)]
+    offsets = [offset_ref[channel] for channel in range(3)]
+    shown = shown_ref[0, 0]
 
     def one_step(step, carry):
         transmit, depth_sum = carry[0], carry[1]
@@ -33,7 +33,7 @@
     carry = (jnp.ones((block_rows, pixels), jnp.float32), zeros, zeros, zeros, zeros)
     carry = lax.fori_loop(0, sample_count, one_step, carry, unroll=8)
     row_ids = pl.program_id(0) * block_rows + lax.broadcasted_iota(jnp.int32, (block_rows, pixels), 0)
-    visible = row_ids.astype(jnp.float32) < shown
+    visible = row_ids < shown
     for channel in range(3):
         out_ref[:, channel * pixels:(channel + 1) * pixels] = jnp.where(visible, carry[2 + channel], 0.0)
     out_ref[:, 3 * pixels:] = jnp.where(visible, carry[1], 0.0)
@@ -41,20 +41,19 @@
 
 def render_layers(density_block, shown_rows, absorb, colour_slope, colour_offset, block_rows=8):
     brick_rows, sample_count, pixels = density_block.shape
-    params = jnp.concatenate([
-        absorb.reshape(1), colour_slope, colour_offset,
-        shown_rows.astype(jnp.float32).reshape(1),
-    ])
     return pl.pallas_call(
         render_kernel,
         grid=(brick_rows // block_rows,),
         in_specs=[
             pl.BlockSpec(memory_space=pltpu.SMEM),
+            pl.BlockSpec(memory_space=pltpu.SMEM),
+            pl.BlockSpec(memory_space=pltpu.SMEM),
+            pl.BlockSpec(memory_space=pltpu.SMEM),
             pl.BlockSpec((block_rows * sample_count, pixels), lambda i: (i, 0)),
         ],
         out_specs=pl.BlockSpec((block_rows, 4 * pixels), lambda i: (i, 0)),
         out_shape=jax.ShapeDtypeStruct((brick_rows, 4 * pixels), jnp.float32),
-    )(params, density_block.reshape(brick_rows * sample_count, pixels))
+    )(absorb, colour_slope, colour_offset, shown_rows, density_block.reshape(brick_rows * sample_count, pixels))
 
 
 def composite_rows(flat, starts, counts, brick_ids, stride, image_rows):
@@ -111,7 +110,7 @@
     owner_rows = image_total // (depth_count * screen_count)
     start = foot_start[0, 0]
     shown = foot_rows[0, 0]
-    layers = render_layers(density[0, 0], shown, extinction[0], colour_slope, colour_offset)
+    layers = render_layers(density[0, 0], foot_rows, extinction, colour_slope, colour_offset)
     brick_rows, width = layers.shape
     lane = lax.broadcasted_iota(jnp.int32, (1, width), 1)
     meta = jnp.where(lane == 0, start, jnp.where(lane == 1, shown, jnp.where(lane == 2, depth_index, 0)))
@@ -119,7 +118,7 @@
     own = jnp.concatenate([layers, meta.astype(jnp.float32)], axis=0)
     slots = ring_gather(own, depth_count)
     flat = jnp.concatenate(slots + [jnp.zeros((1, width), jnp.float32)], axis=0)
-    meta_rows = jnp.concatenate([slot[brick_rows:, :3] for slot in slots], axis=0)
+    meta_rows = flat[:depth_count * stride].reshape(depth_count, stride, width)[:, brick_rows, :3]
     starts = meta_rows[:, 0].astype(jnp.int32)
     counts = meta_rows[:, 1].astype(jnp.int32)
     brick_ids = meta_rows[:, 2].astype(jnp.int32)

time: 72 us -> 78.7 us (1.093)
  local copies, waits for them, and re-layouts: 12.9 us -> 20.6 us
  other arithmetic: 5.99 us -> 4.52 us
    concatenate x1 -> x2, local copies, waits for them, and re-layouts: 5.14 us -> 11.8 us  [on_device(): flat = jnp.concatenate(slots + [jnp.zeros((1, width), jnp.float32)], axis=0)]
    reshape x0 -> x1, local copies, waits for them, and re-layouts: none -> 1.63 us  [on_device(): flat[:depth_count * stride].reshape(depth_count, stride, width)]
    concatenate x1 -> x0, other arithmetic: 1.29 us -> none  [render_layers(): jnp.concatenate([absorb.reshape(1), colour_slope, colour_offset, shown_ro...]
    slice x8 -> x2, local copies, waits for them, and re-layouts: 2.04 us -> 0.84 us  [on_device(): flat[:depth_count * stride].reshape(depth_count, stride, width)]
  transfers between devices with their start and end apart: 8 -> 8, of which waited for: 5 -> 5; matrix products, arithmetic and copies ran while one was open for 4% -> 2% of each run, Pallas kernels for 0% -> 0%
where the time goes in v9:
time: 78.7 us; the launch traced here: 78.1 us
  waiting for transfers between devices  21.9 us (28%)
  local copies, waits for them, and re-layouts  20.6 us (26%)
  Pallas kernels  20 us (25%)
  starting transfers between devices  8.87 us (11%)
  other arithmetic  4.52 us (6%)
  between operations  2.11 us (3%)
    pallas_call x1, Pallas kernels, render_layers(): pl.pallas_call(render_kernel, grid=(brick_rows // block_rows,), in_specs=...  20 us
    ppermute x4, waiting for transfers between devices, ring_gather(): ahead = lax.ppermute(ahead, 'depth', forward)  20 us
    concatenate x2, local copies, waits for them, and re-layouts, on_device(): flat = jnp.concatenate(slots + [jnp.zeros((1, width), jnp.float32)], axis=0)  11.8 us
    ppermute x4, starting transfers between devices, ring_gather(): ahead = lax.ppermute(ahead, 'depth', forward)  8.01 us
    gather x1, local copies, waits for them, and re-layouts, composite_rows(): back_rows = jnp.take(flat, back_idx, axis=0, mode='clip')  2.32 us
    ppermute x1, waiting for transfers between devices, on_device(): received = lax.ppermute(for_partner, 'screen', [(0, 1), (1, 0)])  1.9 us
    reshape x1, local copies, waits for them, and re-layouts, on_device(): flat[:depth_count * stride].reshape(depth_count, stride, width)  1.63 us
    gather x1, local copies, waits for them, and re-layouts, composite_rows(): front_rows = jnp.take(flat, front_idx, axis=0, mode='clip')  1.62 us
  transfers between devices with their start and end apart: 8, of which 5 were waited for; matrix products, arithmetic and copies ran while one was open for 2% of the time, Pallas kernels for 0%

profile of v9, /device:TPU:0, one launch (start us, length us, event | category | flops | bytes accessed | tf_op | source)
XLA Modules:
  0.0 78.1 jit_solution(17363150376175768655)
XLA Ops:
  2.0 20.0 %shard_map.73 = f32[128,512]{1,0:T(8,128)} custom-call(f32[1]{0:T(128)S(6)} %copy.13.absorb_ref, f32[3]{0:T(128)} %slope_ref.1, f32[3]{0:T(128)} %offset_ref.1, s32[1,1]{1,0:T(1,128)} %copy.12.shown_ref, f32[16384,128]{1,0:T(8,128)} %bitcast.12), custom_call_target="tpu_custom_call" | custom-call | tf_op jit(solution)/shard_map/pallas_call | solution.py:44
  22.0 1.0 %pad_maximum_fusion.1 = f32[129,512]{1,0:T(8,128)S(1)} fusion(f32[1,512]{1,0:T(1,128)S(1)} %fusion.13, f32[128,512]{1,0:T(8,128)} %shard_map.73), kind=kLoop, calls=%fused_computation.9 | loop fusion | flops 66048 | bytes 528384 | tf_op jit(solution)/shard_map/concatenate | solution.py:118
  23.0 3.1 %collective-permute-start = (f32[129,512]{1,0:T(8,128)S(1)}, f32[129,512]{1,0:T(8,128)S(1)}, u32[]{:S(2)}, u32[]{:S(2)}) collective-permute-start(f32[129,512]{1,0:T(8,128)S(1)} %pad_maximum_fusion.1), channel_id=1, source_target_pairs={{0,4},{4,8},{8,12},{12,14},{14,10},{10,6},{6,2},{2,0},{1,5},{5,9},... | collective-permute-start | bytes 792584 | tf_op jit(solution)/shard_map/ppermute | solution.py:95
  26.0 0.0 collective-permute-start.1
  26.0 6.6 %collective-permute-done = f32[129,512]{1,0:T(8,128)S(1)} collective-permute-done((f32[129,512]{1,0:T(8,128)S(1)}, f32[129,512]{1,0:T(8,128)S(1)}, u32[]{:S(2)}, u32[]{:S(2)}) %collective-permute-start) | collective-permute-done | bytes 264224 | tf_op jit(solution)/shard_map/ppermute | solution.py:95
  32.6 1.8 %collective-permute-start.2 = (f32[129,512]{1,0:T(8,128)S(1)}, f32[129,512]{1,0:T(8,128)S(1)}, u32[]{:S(2)}, u32[]{:S(2)}) collective-permute-start(f32[129,512]{1,0:T(8,128)S(1)} %collective-permute-done), channel_id=1, source_target_pairs={{0,4},{4,8},{8,12},{12,14},{14,10},{10,6},{6,2},{2,0},{1,5},{5,9},... | collective-permute-start | bytes 792584 | tf_op jit(solution)/shard_map/ppermute | solution.py:95
  34.4 0.2 collective-permute-start.3
  34.7 5.8 %collective-permute-done.2 = f32[129,512]{1,0:T(8,128)S(1)} collective-permute-done((f32[129,512]{1,0:T(8,128)S(1)}, f32[129,512]{1,0:T(8,128)S(1)}, u32[]{:S(2)}, u32[]{:S(2)}) %collective-permute-start.2) | collective-permute-done | bytes 264224 | tf_op jit(solution)/shard_map/ppermute | solution.py:95
  40.5 1.5 %collective-permute-start.4 = (f32[129,512]{1,0:T(8,128)S(1)}, f32[129,512]{1,0:T(8,128)S(1)}, u32[]{:S(2)}, u32[]{:S(2)}) collective-permute-start(f32[129,512]{1,0:T(8,128)S(1)} %collective-permute-done.2), channel_id=1, source_target_pairs={{0,4},{4,8},{8,12},{12,14},{14,10},{10,6},{6,2},{2,0},{1,5},{5,9},... | collective-permute-start | bytes 792584 | tf_op jit(solution)/shard_map/ppermute | solution.py:95
  42.0 0.5 collective-permute-start.5
  42.5 4.9 %collective-permute-done.4 = f32[129,512]{1,0:T(8,128)S(1)} collective-permute-done((f32[129,512]{1,0:T(8,128)S(1)}, f32[129,512]{1,0:T(8,128)S(1)}, u32[]{:S(2)}, u32[]{:S(2)}) %collective-permute-start.4) | collective-permute-done | bytes 264224 | tf_op jit(solution)/shard_map/ppermute | solution.py:95
  47.4 1.7 %collective-permute-start.6 = (f32[129,512]{1,0:T(8,128)S(1)}, f32[129,512]{1,0:T(8,128)}, u32[]{:S(2)}, u32[]{:S(2)}) collective-permute-start(f32[129,512]{1,0:T(8,128)S(1)} %collective-permute-done.4), channel_id=1, source_target_pairs={{0,4},{4,8},{8,12},{12,14},{14,10},{10,6},{6,2},{2,0},{1,5},{5,9},... | collective-permute-start | bytes 792584 | tf_op jit(solution)/shard_map/ppermute | solution.py:95
  49.1 0.8 dynamic_slice.7
  49.8 0.8 fusion.14
  50.6 0.7 copy-done.5
  51.3 2.7 %collective-permute-done.6 = f32[129,512]{1,0:T(8,128)} collective-permute-done((f32[129,512]{1,0:T(8,128)S(1)}, f32[129,512]{1,0:T(8,128)}, u32[]{:S(2)}, u32[]{:S(2)}) %collective-permute-start.6) | collective-permute-done | bytes 264224 | tf_op jit(solution)/shard_map/ppermute | solution.py:95
  54.1 5.2 %concatenate.31 = f32[1032,512]{1,0:T(8,128)S(1)} concatenate(f32[128,512]{1,0:T(8,128)} %shard_map.73, f32[1,512]{1,0:T(1,128)S(1)} %fusion.13, f32[129,512]{1,0:T(8,128)S(1)} %collective-permute-done, f32[129,512]{1,0:T(8,128)S(1)} %collective-permute-done.1, f32[129,512]{1,0:T(8,128)S(1)} %collective-permute-done.2, f32[129,512]{1,0:T(8,128)S(1)} %collective-permute-done.3, ...), dimensions={0} | concatenate | bytes 4227072 | tf_op jit(solution)/shard_map/concatenate | solution.py:120
  59.3 1.6 %reshape.155 = f32[8,129,512]{2,1,0:T(8,128)} reshape(f32[1032,512]{1,0:T(8,128)S(1)} %concatenate.31) | data formatting | bytes 4227072 | tf_op jit(solution)/shard_map/reshape | solution.py:121
  60.9 0.8 slice.46
  61.7 0.1 copy.10
  61.8 0.1 select_reduce_fusion
  61.9 0.1 fusion.11
  62.0 0.1 fusion.8
  62.1 6.6 %concatenate.30 = f32[1033,512]{1,0:T(8,128)S(1)} concatenate(f32[128,512]{1,0:T(8,128)S(1)} %copy-done, f32[1,512]{1,0:T(1,128)S(1)} %fusion.13, f32[129,512]{1,0:T(8,128)S(1)} %collective-permute-done, f32[129,512]{1,0:T(8,128)} %copy-done.1, f32[129,512]{1,0:T(8,128)} %copy-done.2, f32[129,512]{1,0:T(8,128)} %copy-done.3, f32[129,512]{1,0:T(8,128)} %copy-done.4, ...), dimensions={0} | concatenate | bytes 4231168 | tf_op jit(solution)/shard_map/concatenate | solution.py:120
  68.7 1.6 %gather_fusion = f32[512,512]{1,0:T(8,128)S(1)} fusion(f32[1033,512]{1,0:T(8,128)S(1)} %concatenate.30, s32[1024]{0:T(1024)S(1)} %pad_clamp_fusion.1), kind=kCustom, calls=%fused_computation | custom fusion | bytes 2099200 | tf_op jit(solution)/shard_map/jit(_take)/gather | solution.py:75
  70.3 2.3 %gather_fusion.1 = f32[512,512]{1,0:T(8,128)} fusion(f32[1033,512]{1,0:T(8,128)S(1)} %concatenate.30, s32[1024]{0:T(1024)S(1)} %pad_clamp_fusion), kind=kCustom, calls=%fused_computation.1 | custom fusion | bytes 2099200 | tf_op jit(solution)/shard_map/jit(_take)/gather | solution.py:74
  72.7 1.0 %negate_exponential_fusion = (f32[512,128]{1,0:T(8,128)S(1)}, f32[512,128]{1,0:T(8,128)S(1)}) fusion(f32[512,512]{1,0:T(8,128)S(1)} %gather_fusion, f32[512,512]{1,0:T(8,128)} %gather_fusion.1), kind=kLoop, calls=%fused_computation.14 | loop fusion | flops 262144 | bytes 1048576 | tf_op jit(solution)/shard_map/exp | solution.py:77
  73.7 1.3 %fusion = f32[512,384]{1,0:T(8,128)S(1)} fusion(f32[512,512]{1,0:T(8,128)} %gather_fusion.1, f32[512,512]{1,0:T(8,128)S(1)} %gather_fusion, f32[512,128]{1,0:T(8,128)S(1)} %get-tuple-element.9), kind=kLoop, calls=%fused_computation.5 | loop fusion | flops 786432 | bytes 2621440 | tf_op jit(solution)/shard_map/add | solution.py:78
  75.0 0.1 collective-permute-start.7
  75.1 1.9 %collective-permute-done.7 = f32[256,512]{1,0:T(8,128)S(1)} collective-permute-done((f32[256,512]{1,0:T(8,128)S(1)}, f32[256,512]{1,0:T(8,128)S(1)}, u32[]{:S(2)}, u32[]{:S(2)}) %collective-permute-start.7) | collective-permute-done | bytes 524320 | tf_op jit(solution)/shard_map/ppermute | solution.py:133
  77.0 0.1 fusion.2
  77.1 1.0 %reshape.156 = f32[256,4,128]{2,1,0:T(4,128)} reshape(f32[256,512]{1,0:T(8,128)S(1)} %fusion.2) | data formatting | bytes 1048576 | tf_op jit(solution)/shard_map/reshape | solution.py:136
  (24 shorter events, 0.1 us)
Async XLA Ops:
  23.0 9.7 %collective-permute-start = (f32[129,512]{1,0:T(8,128)S(1)}, f32[129,512]{1,0:T(8,128)S(1)}, u32[]{:S(2)}, u32[]{:S(2)}) collective-permute-start(f32[129,512]{1,0:T(8,128)S(1)} %pad_maximum_fusion.1), channel_id=1, source_target_pairs={{0,4},{4,8},{8,12},{12,14},{14,10},{10,6},{6,2},{2,0},{1,5},{5,9},... | collective-permute-start | bytes 792584 | tf_op jit(solution)/shard_map/ppermute | solution.py:95
  26.0 8.4 %collective-permute-start.1 = (f32[129,512]{1,0:T(8,128)S(1)}, f32[129,512]{1,0:T(8,128)S(1)}, u32[]{:S(2)}, u32[]{:S(2)}) collective-permute-start(f32[129,512]{1,0:T(8,128)S(1)} %pad_maximum_fusion.1), channel_id=1, source_target_pairs={{4,0},{8,4},{12,8},{14,12},{10,14},{6,10},{2,6},{0,2},{5,1},{9,5},... | collective-permute-start | bytes 792584 | tf_op jit(solution)/shard_map/ppermute | solution.py:98
  32.6 7.8 %collective-permute-start.2 = (f32[129,512]{1,0:T(8,128)S(1)}, f32[129,512]{1,0:T(8,128)S(1)}, u32[]{:S(2)}, u32[]{:S(2)}) collective-permute-start(f32[129,512]{1,0:T(8,128)S(1)} %collective-permute-done), channel_id=1, source_target_pairs={{0,4},{4,8},{8,12},{12,14},{14,10},{10,6},{6,2},{2,0},{1,5},{5,9},... | collective-permute-start | bytes 792584 | tf_op jit(solution)/shard_map/ppermute | solution.py:95
  34.4 24.8 %copy-start.1 = (f32[129,512]{1,0:T(8,128)}, f32[129,512]{1,0:T(8,128)S(1)}, u32[]{:S(2)}) copy-start(f32[129,512]{1,0:T(8,128)S(1)} %collective-permute-done.1) | copy-start | bytes 792580
  34.4 7.5 %collective-permute-start.3 = (f32[129,512]{1,0:T(8,128)S(1)}, f32[129,512]{1,0:T(8,128)S(1)}, u32[]{:S(2)}, u32[]{:S(2)}) collective-permute-start(f32[129,512]{1,0:T(8,128)S(1)} %collective-permute-done.1), channel_id=1, source_target_pairs={{4,0},{8,4},{12,8},{14,12},{10,14},{6,10},{2,6},{0,2},{5,1},{9,5},... | collective-permute-start | bytes 792584 | tf_op jit(solution)/shard_map/ppermute | solution.py:98
  40.5 18.8 %copy-start.2 = (f32[129,512]{1,0:T(8,128)}, f32[129,512]{1,0:T(8,128)S(1)}, u32[]{:S(2)}) copy-start(f32[129,512]{1,0:T(8,128)S(1)} %collective-permute-done.2) | copy-start | bytes 792580
  40.5 6.9 %collective-permute-start.4 = (f32[129,512]{1,0:T(8,128)S(1)}, f32[129,512]{1,0:T(8,128)S(1)}, u32[]{:S(2)}, u32[]{:S(2)}) collective-permute-start(f32[129,512]{1,0:T(8,128)S(1)} %collective-permute-done.2), channel_id=1, source_target_pairs={{0,4},{4,8},{8,12},{12,14},{14,10},{10,6},{6,2},{2,0},{1,5},{5,9},... | collective-permute-start | bytes 792584 | tf_op jit(solution)/shard_map/ppermute | solution.py:95
  42.0 17.3 %copy-start.3 = (f32[129,512]{1,0:T(8,128)}, f32[129,512]{1,0:T(8,128)S(1)}, u32[]{:S(2)}) copy-start(f32[129,512]{1,0:T(8,128)S(1)} %collective-permute-done.3) | copy-start | bytes 792580
  42.0 8.7 %collective-permute-start.5 = (f32[129,512]{1,0:T(8,128)S(1)}, f32[129,512]{1,0:T(8,128)S(1)}, u32[]{:S(2)}, u32[]{:S(2)}) collective-permute-start(f32[129,512]{1,0:T(8,128)S(1)} %collective-permute-done.3), channel_id=1, source_target_pairs={{4,0},{8,4},{12,8},{14,12},{10,14},{6,10},{2,6},{0,2},{5,1},{9,5},... | collective-permute-start | bytes 792584 | tf_op jit(solution)/shard_map/ppermute | solution.py:98
  47.4 3.2 %copy-start.4 = (f32[129,512]{1,0:T(8,128)}, f32[129,512]{1,0:T(8,128)S(1)}, u32[]{:S(2)}) copy-start(f32[129,512]{1,0:T(8,128)S(1)} %collective-permute-done.4) | copy-start | bytes 792580
  47.4 6.7 %collective-permute-start.6 = (f32[129,512]{1,0:T(8,128)S(1)}, f32[129,512]{1,0:T(8,128)}, u32[]{:S(2)}, u32[]{:S(2)}) collective-permute-start(f32[129,512]{1,0:T(8,128)S(1)} %collective-permute-done.4), channel_id=1, source_target_pairs={{0,4},{4,8},{8,12},{12,14},{14,10},{10,6},{6,2},{2,0},{1,5},{5,9},... | collective-permute-start | bytes 792584 | tf_op jit(solution)/shard_map/ppermute | solution.py:95
  50.6 0.7 copy-start.5
  59.3 2.8 %copy-start = (f32[128,512]{1,0:T(8,128)S(1)}, f32[128,512]{1,0:T(8,128)}, u32[]{:S(2)}) copy-start(f32[128,512]{1,0:T(8,128)} %shard_map.73) | copy-start | bytes 786436
  75.0 2.0 %collective-permute-start.7 = (f32[256,512]{1,0:T(8,128)S(1)}, f32[256,512]{1,0:T(8,128)S(1)}, u32[]{:S(2)}, u32[]{:S(2)}) collective-permute-start(f32[256,512]{1,0:T(8,128)S(1)} %pad_maximum_fusion), channel_id=1, source_target_pairs={{0,1},{1,0},{2,3},{3,2},{4,5},{5,4},{6,7},{7,6},{8,9},{9,8},{10,11... | collective-permute-start | bytes 1572872 | tf_op jit(solution)/shard_map/ppermute | solution.py:133

commit v10 on v6

--- a/solution.py
+++ b/solution.py
@@ -8,14 +8,14 @@
 BLK = 256
 
 
-def render_kernel(params_ref, density_ref, out_ref):
+def render_kernel(absorb_ref, slope_ref, offset_ref, shown_ref, density_ref, out_ref):
     block_rows = out_ref.shape[0]
     pixels = out_ref.shape[2]
     sample_count = density_ref.shape[0] // block_rows
-    absorb = params_ref[0]
-    slopes = [params_ref[1 + channel] for channel in range(3)]
-    offsets = [params_ref[4 + channel] for channel in range(3)]
-    shown = params_ref[7]
+    absorb = absorb_ref[0]
+    slopes = [slope_ref[channel] for channel in range(3)]
+    offsets = [offset_ref[channel] for channel in range(3)]
+    shown = shown_ref[0, 0]
 
     def one_step(step, carry):
         transmit, depth_sum = carry[0], carry[1]
@@ -33,7 +33,7 @@
     carry = (jnp.ones((block_rows, pixels), jnp.float32), zeros, zeros, zeros, zeros)
     carry = lax.fori_loop(0, sample_count, one_step, carry, unroll=8)
     row_ids = pl.program_id(0) * block_rows + lax.broadcasted_iota(jnp.int32, (block_rows, pixels), 0)
-    visible = row_ids.astype(jnp.float32) < shown
+    visible = row_ids < shown
     for channel in range(3):
         out_ref[:, channel, :] = jnp.where(visible, carry[2 + channel], 0.0)
     out_ref[:, 3, :] = jnp.where(visible, carry[1], 0.0)
@@ -41,20 +41,19 @@
 
 def render_layers(density_block, shown_rows, absorb, colour_slope, colour_offset, block_rows=8):
     brick_rows, sample_count, pixels = density_block.shape
-    params = jnp.concatenate([
-        absorb.reshape(1), colour_slope, colour_offset,
-        shown_rows.astype(jnp.float32).reshape(1),
-    ])
     return pl.pallas_call(
         render_kernel,
         grid=(brick_rows // block_rows,),
         in_specs=[
             pl.BlockSpec(memory_space=pltpu.SMEM),
+            pl.BlockSpec(memory_space=pltpu.SMEM),
+            pl.BlockSpec(memory_space=pltpu.SMEM),
+            pl.BlockSpec(memory_space=pltpu.SMEM),
             pl.BlockSpec((block_rows * sample_count, pixels), lambda i: (i, 0)),
         ],
         out_specs=pl.BlockSpec((block_rows, 4, pixels), lambda i: (i, 0, 0)),
         out_shape=jax.ShapeDtypeStruct((brick_rows, 4, pixels), jnp.float32),
-    )(params, density_block.reshape(brick_rows * sample_count, pixels))
+    )(absorb, colour_slope, colour_offset, shown_rows, density_block.reshape(brick_rows * sample_count, pixels))
 
 
 def composite_rows(flat, starts, counts, brick_ids, stride, image_rows):
@@ -72,12 +71,11 @@
     front_slot = jnp.sum(jnp.where(is_front, slot_ids, 0), axis=1)
     has_front = jnp.any(is_front, axis=1)
     has_back = back >= 0
-    back_idx = jnp.where(has_back, back_slot * stride + back_off, 0)
-    front_idx = jnp.where(has_front, front_slot * stride + front_off, 0)
+    zero_row = flat.shape[0] - 1
+    back_idx = jnp.where(has_back, back_slot * stride + back_off, zero_row)
+    front_idx = jnp.where(has_front, front_slot * stride + front_off, zero_row)
     back_rows = jnp.take(flat, back_idx, axis=0, mode="clip")
     front_rows = jnp.take(flat, front_idx, axis=0, mode="clip")
-    back_rows = jnp.where(has_back[:, None, None], back_rows, 0.0)
-    front_rows = jnp.where(has_front[:, None, None], front_rows, 0.0)
     front_depth = front_rows[:, 3:4, :]
     colours = front_rows[:, :3, :] + jnp.exp(-front_depth) * back_rows[:, :3, :]
     opacity = 1.0 - jnp.exp(-(front_depth + back_rows[:, 3:4, :]))
@@ -101,7 +99,7 @@
         if 2 * step < count:
             behind = lax.ppermute(behind, "depth", backward)
             slots.append(behind)
-    return jnp.concatenate(slots, axis=0)
+    return jnp.concatenate(slots + [jnp.zeros((1,) + own.shape[1:], own.dtype)], axis=0)
 
 
 def on_device(density, foot_start, foot_rows, extinction, colour_slope, colour_offset, tile_source):
@@ -114,14 +112,14 @@
     owner_rows = image_total // (depth_count * screen_count)
     start = foot_start[0, 0]
     shown = foot_rows[0, 0]
-    layers = render_layers(density[0, 0], shown, extinction[0], colour_slope, colour_offset)
+    layers = render_layers(density[0, 0], foot_rows, extinction, colour_slope, colour_offset)
     brick_rows, channels, pixels = layers.shape
     lane = lax.broadcasted_iota(jnp.int32, (1, channels, pixels), 2)
     meta = jnp.where(lane == 0, start, jnp.where(lane == 1, shown, jnp.where(lane == 2, depth_index, 0)))
     stride = brick_rows + 1
     own = jnp.concatenate([layers, meta.astype(jnp.float32)], axis=0)
     flat = ring_gather(own, depth_count)
-    meta_rows = flat.reshape(depth_count, stride, channels, pixels)[:, brick_rows, 0, :3]
+    meta_rows = flat[:depth_count * stride].reshape(depth_count, stride, channels, pixels)[:, brick_rows, 0, :3]
     starts = meta_rows[:, 0].astype(jnp.int32)
     counts = meta_rows[:, 1].astype(jnp.int32)
     brick_ids = meta_rows[:, 2].astype(jnp.int32)

time: 70 us -> 67.2 us (0.960)
  local copies, waits for them, and re-layouts: 7.26 us -> 15.2 us
  waiting for transfers between devices: 21.1 us -> 14.8 us
  other arithmetic: 9.96 us -> 5.84 us
    unnamed x10, local copies, waits for them, and re-layouts: 1.27 us -> 7.72 us
    ppermute x4, waiting for transfers between devices: 17.2 us -> 12.3 us  [ring_gather(): ahead = lax.ppermute(ahead, 'depth', forward)]
    select_n x4 -> x2, other arithmetic: 3.52 us -> 0.01 us  [the longest x1 0.01 us: composite_rows(): back_idx = jnp.where(has_back, back_slot * stride + back_off, zero_row)]
    ppermute x3, waiting for transfers between devices: 2 us -> 0.54 us  [ring_gather(): behind = lax.ppermute(behind, 'depth', backward)]
    concatenate x1 -> x0, other arithmetic: 1.25 us -> none  [render_layers(): jnp.concatenate([absorb.reshape(1), colour_slope, colour_offset, shown_ro...]
    slice x1, local copies, waits for them, and re-layouts: 0.01 us -> 0.75 us  [on_device(): flat[:depth_count * stride].reshape(depth_count, stride, channels, pixels)]
    concatenate x1 -> x2, local copies, waits for them, and re-layouts: 0.04 us -> 0.78 us  [ring_gather(): jnp.concatenate(slots + [jnp.zeros((1,) + own.shape[1:], own.dtype)], axi...]
  transfers between devices with their start and end apart: 8 -> 8, of which waited for: 7 -> 7; matrix products, arithmetic and copies ran while one was open for 3% -> 13% of each run, Pallas kernels for 0% -> 0%
where the time goes in v10:
time: 67.2 us; the launch traced here: 66.9 us
  Pallas kernels  20.3 us (30%)
  local copies, waits for them, and re-layouts  15.2 us (23%)
  waiting for transfers between devices  14.8 us (22%)
  starting transfers between devices  8.67 us (13%)
  other arithmetic  5.84 us (9%)
  between operations  2.07 us (3%)
    pallas_call x1, Pallas kernels, render_layers(): pl.pallas_call(render_kernel, grid=(brick_rows // block_rows,), in_specs=...  20.3 us
    ppermute x4, waiting for transfers between devices, ring_gather(): ahead = lax.ppermute(ahead, 'depth', forward)  12.3 us
    ppermute x4, starting transfers between devices, ring_gather(): ahead = lax.ppermute(ahead, 'depth', forward)  7.76 us
    unnamed x10, local copies, waits for them, and re-layouts  7.72 us
    gather x1, local copies, waits for them, and re-layouts, composite_rows(): front_rows = jnp.take(flat, front_idx, axis=0, mode='clip')  3.11 us
    gather x1, local copies, waits for them, and re-layouts, composite_rows(): back_rows = jnp.take(flat, back_idx, axis=0, mode='clip')  2.07 us
    ppermute x1, waiting for transfers between devices, on_device(): received = lax.ppermute(for_partner, 'screen', [(0, 1), (1, 0)])  1.9 us
    select_n x1, other arithmetic, on_device(): return jnp.where(in_my_half[:, None, None], mine, received)  1.62 us
  transfers between devices with their start and end apart: 8, of which 7 were waited for; matrix products, arithmetic and copies ran while one was open for 13% of the time, Pallas kernels for 0%

profile of v10, /device:TPU:0, one launch (start us, length us, event | category | flops | bytes accessed | tf_op | source)
XLA Modules:
  0.0 66.9 jit_solution(13531450629948582039)
XLA Ops:
  2.0 20.3 %shard_map.73 = f32[128,4,128]{2,1,0:T(4,128)} custom-call(f32[1]{0:T(128)S(6)} %copy.32.absorb_ref, f32[3]{0:T(128)} %slope_ref.1, f32[3]{0:T(128)} %offset_ref.1, s32[1,1]{1,0:T(1,128)} %copy.31.shown_ref, f32[16384,128]{1,0:T(8,128)} %bitcast.17), custom_call_target="tpu_custom_call" | custom-call | tf_op jit(solution)/shard_map/pallas_call | solution.py:44
  22.3 1.0 %pad_maximum_fusion.1 = f32[129,4,128]{2,1,0:T(4,128)S(1)} fusion(f32[1,4,128]{2,1,0:T(4,128)S(1)} %select_convert_fusion, f32[128,4,128]{2,1,0:T(4,128)} %shard_map.73), kind=kLoop, calls=%fused_computation.9 | loop fusion | flops 66048 | bytes 528384 | tf_op jit(solution)/shard_map/concatenate | solution.py:120
  23.3 3.1 %collective-permute-start = (f32[129,4,128]{2,1,0:T(4,128)S(1)}, f32[129,4,128]{2,1,0:T(4,128)S(1)}, u32[]{:S(2)}, u32[]{:S(2)}) collective-permute-start(f32[129,4,128]{2,1,0:T(4,128)S(1)} %pad_maximum_fusion.1), channel_id=1, source_target_pairs={{0,4},{4,8},{8,12},{12,14},{14,10},{10,6},{6,2},{2,0},{1,5},{5,9},... | collective-permute-start | bytes 792584 | tf_op jit(solution)/shard_map/ppermute | solution.py:97
  26.4 1.7 %constant_dynamic-update-slice_fusion.18 = (f32[1032,4,128]{2,1,0:T(4,128)}, f32[1033,4,128]{2,1,0:T(4,128)S(1)}) fusion(f32[128,4,128]{2,1,0:T(4,128)} %shard_map.73), kind=kLoop, calls=%fused_computation.32 | loop fusion | bytes 786432
  28.1 4.6 %collective-permute-done = f32[129,4,128]{2,1,0:T(4,128)S(1)} collective-permute-done((f32[129,4,128]{2,1,0:T(4,128)S(1)}, f32[129,4,128]{2,1,0:T(4,128)S(1)}, u32[]{:S(2)}, u32[]{:S(2)}) %collective-permute-start) | collective-permute-done | bytes 264224 | tf_op jit(solution)/shard_map/ppermute | solution.py:97
  32.7 1.8 %collective-permute-start.2 = (f32[129,4,128]{2,1,0:T(4,128)S(1)}, f32[129,4,128]{2,1,0:T(4,128)S(1)}, u32[]{:S(2)}, u32[]{:S(2)}) collective-permute-start(f32[129,4,128]{2,1,0:T(4,128)S(1)} %collective-permute-done), channel_id=1, source_target_pairs={{0,4},{4,8},{8,12},{12,14},{14,10},{10,6},{6,2},{2,0},{1,5},{5,9},... | collective-permute-start | bytes 792584 | tf_op jit(solution)/shard_map/ppermute | solution.py:97
  34.5 0.6 constant_dynamic-update-slice_fusion.17
  35.1 0.8 %dynamic_slice.7 = s32[256]{0:T(256)S(1)} dynamic-slice(s32[4096]{0:T(1024)} %param.13, s32[]{:T(128)S(6)} %select_n.103), dynamic_slice_sizes={256} | dynamic-slice | bytes 2052 | tf_op jit(solution)/shard_map/dynamic_slice | solution.py:129
  35.8 0.8 %fusion.8 = (pred[256]{0:T(512)(128)(4,1)S(1)}, s32[256]{0:T(256)S(1)}) fusion(s32[]{:T(128)S(6)} %axis_index.25, s32[4096]{0:T(1024)} %param.13, s32[]{:T(128)S(6)} %select_n.98), kind=kLoop, calls=%fused_computation.60 | loop fusion | flops 4096 | bytes 2312 | tf_op jit(solution)/shard_map/eq | solution.py:135
  36.6 0.3 collective-permute-start.3
  36.9 3.3 %collective-permute-done.2 = f32[129,4,128]{2,1,0:T(4,128)S(1)} collective-permute-done((f32[129,4,128]{2,1,0:T(4,128)S(1)}, f32[129,4,128]{2,1,0:T(4,128)S(1)}, u32[]{:S(2)}, u32[]{:S(2)}) %collective-permute-start.2) | collective-permute-done | bytes 264224 | tf_op jit(solution)/shard_map/ppermute | solution.py:97
  40.2 1.5 %collective-permute-start.4 = (f32[129,4,128]{2,1,0:T(4,128)S(1)}, f32[129,4,128]{2,1,0:T(4,128)S(1)}, u32[]{:S(2)}, u32[]{:S(2)}) collective-permute-start(f32[129,4,128]{2,1,0:T(4,128)S(1)} %collective-permute-done.2), channel_id=1, source_target_pairs={{0,4},{4,8},{8,12},{12,14},{14,10},{10,6},{6,2},{2,0},{1,5},{5,9},... | collective-permute-start | bytes 792584 | tf_op jit(solution)/shard_map/ppermute | solution.py:97
  41.7 0.8 %constant_dynamic-update-slice_fusion.16 = (f32[1032,4,128]{2,1,0:T(4,128)}, f32[1033,4,128]{2,1,0:T(4,128)S(1)}) fusion(f32[1032,4,128]{2,1,0:T(4,128)} %get-tuple-element.36, f32[129,4,128]{2,1,0:T(4,128)S(1)} %collective-permute-done, f32[1033,4,128]{2,1,0:T(4,128)S(1)} %get-tuple-element.37), kind=kLoop, calls=%fused_computation.30 | loop fusion | bytes 792576
  42.5 0.8 %constant_dynamic-update-slice_fusion.15 = (f32[1032,4,128]{2,1,0:T(4,128)}, f32[1033,4,128]{2,1,0:T(4,128)S(1)}) fusion(f32[1032,4,128]{2,1,0:T(4,128)} %get-tuple-element.29, f32[129,4,128]{2,1,0:T(4,128)S(1)} %collective-permute-done.1, f32[1033,4,128]{2,1,0:T(4,128)S(1)} %get-tuple-element.30), kind=kLoop, calls=%fused_computation.29 | loop fusion | bytes 792576
  43.2 0.3 collective-permute-done.3
  43.6 0.5 collective-permute-start.5
  44.1 0.8 %constant_dynamic-update-slice_fusion.14 = (f32[1032,4,128]{2,1,0:T(4,128)}, f32[1033,4,128]{2,1,0:T(4,128)S(1)}) fusion(f32[1032,4,128]{2,1,0:T(4,128)} %get-tuple-element.27, f32[129,4,128]{2,1,0:T(4,128)S(1)} %collective-permute-done.2, f32[1033,4,128]{2,1,0:T(4,128)S(1)} %get-tuple-element.28), kind=kLoop, calls=%fused_computation.28 | loop fusion | bytes 792576
  44.9 1.9 %collective-permute-done.4 = f32[129,4,128]{2,1,0:T(4,128)S(1)} collective-permute-done((f32[129,4,128]{2,1,0:T(4,128)S(1)}, f32[129,4,128]{2,1,0:T(4,128)S(1)}, u32[]{:S(2)}, u32[]{:S(2)}) %collective-permute-start.4) | collective-permute-done | bytes 264224 | tf_op jit(solution)/shard_map/ppermute | solution.py:97
  46.8 1.4 %collective-permute-start.6 = (f32[129,4,128]{2,1,0:T(4,128)S(1)}, f32[129,4,128]{2,1,0:T(4,128)S(1)}, u32[]{:S(2)}, u32[]{:S(2)}) collective-permute-start(f32[129,4,128]{2,1,0:T(4,128)S(1)} %collective-permute-done.4), channel_id=1, source_target_pairs={{0,4},{4,8},{8,12},{12,14},{14,10},{10,6},{6,2},{2,0},{1,5},{5,9},... | collective-permute-start | bytes 792584 | tf_op jit(solution)/shard_map/ppermute | solution.py:97
  48.2 0.8 %constant_dynamic-update-slice_fusion.13 = (f32[1032,4,128]{2,1,0:T(4,128)}, f32[1033,4,128]{2,1,0:T(4,128)S(1)}) fusion(f32[1032,4,128]{2,1,0:T(4,128)} %get-tuple-element.25, f32[129,4,128]{2,1,0:T(4,128)S(1)} %collective-permute-done.3, f32[1033,4,128]{2,1,0:T(4,128)S(1)} %get-tuple-element.26), kind=kLoop, calls=%fused_computation.27 | loop fusion | bytes 792576
  49.0 0.8 %constant_dynamic-update-slice_fusion.12 = (f32[1032,4,128]{2,1,0:T(4,128)}, f32[1033,4,128]{2,1,0:T(4,128)S(1)}) fusion(f32[1032,4,128]{2,1,0:T(4,128)} %get-tuple-element.23, f32[129,4,128]{2,1,0:T(4,128)S(1)} %collective-permute-done.4, f32[1033,4,128]{2,1,0:T(4,128)S(1)} %get-tuple-element.24), kind=kLoop, calls=%fused_computation.26 | loop fusion | bytes 792576
  50.0 0.8 %constant_dynamic-update-slice_fusion.11 = (f32[1032,4,128]{2,1,0:T(4,128)}, f32[1033,4,128]{2,1,0:T(4,128)S(1)}) fusion(f32[1032,4,128]{2,1,0:T(4,128)} %get-tuple-element.21, f32[129,4,128]{2,1,0:T(4,128)S(1)} %collective-permute-done.5, f32[1033,4,128]{2,1,0:T(4,128)S(1)} %get-tuple-element.22), kind=kLoop, calls=%fused_computation.25 | loop fusion | bytes 792576
  50.7 2.5 %collective-permute-done.6 = f32[129,4,128]{2,1,0:T(4,128)S(1)} collective-permute-done((f32[129,4,128]{2,1,0:T(4,128)S(1)}, f32[129,4,128]{2,1,0:T(4,128)S(1)}, u32[]{:S(2)}, u32[]{:S(2)}) %collective-permute-start.6) | collective-permute-done | bytes 264224 | tf_op jit(solution)/shard_map/ppermute | solution.py:97
  53.2 0.8 %constant_dynamic-update-slice_fusion.10 = (f32[1032,4,128]{2,1,0:T(4,128)}, f32[1033,4,128]{2,1,0:T(4,128)S(1)}) fusion(f32[1032,4,128]{2,1,0:T(4,128)} %get-tuple-element.19, f32[129,4,128]{2,1,0:T(4,128)S(1)} %collective-permute-done.6, f32[1033,4,128]{2,1,0:T(4,128)S(1)} %get-tuple-element.20), kind=kLoop, calls=%fused_computation.24 | loop fusion | bytes 792576 | tf_op jit(solution)/shard_map/concatenate | solution.py:102
  54.0 0.8 %slice.46 = f32[8,1,1,3]{3,2,1,0:T(1,128)S(1)} slice(f32[8,129,4,128]{3,2,1,0:T(4,128)} %bitcast.3), slice={[0:8], [128:129], [0:1], [0:3]} | slice | bytes 192 | tf_op jit(solution)/shard_map/slice | solution.py:122
  55.2 1.3 %copy-done = f32[1033,4,128]{2,1,0:T(4,128)} copy-done((f32[1033,4,128]{2,1,0:T(4,128)}, f32[1033,4,128]{2,1,0:T(4,128)S(1)}, u32[]{:S(2)}) %copy-start) | copy-done | bytes 2115608
  56.5 2.1 %gather_fusion.1 = f32[512,4,128]{2,1,0:T(4,128)S(1)} fusion(f32[1033,4,128]{2,1,0:T(4,128)S(1)} %constant_dynamic-update-slice_fusion, s32[1024]{0:T(1024)S(1)} %pad_clamp_fusion), kind=kCustom, calls=%fused_computation.1 | custom fusion | bytes 2099200 | tf_op jit(solution)/shard_map/jit(_take)/gather | solution.py:77
  58.6 3.1 %gather_fusion = f32[512,4,128]{2,1,0:T(4,128)S(1)} fusion(f32[1033,4,128]{2,1,0:T(4,128)} %copy-done, s32[1024]{0:T(1024)S(1)} %pad_clamp_fusion.1), kind=kCustom, calls=%fused_computation | custom fusion | bytes 2099200 | tf_op jit(solution)/shard_map/jit(_take)/gather | solution.py:78
  61.7 0.9 %negate_exponential_fusion = (f32[512,1,128]{2,1,0:T(1,128)S(1)}, f32[512,1,128]{2,1,0:T(1,128)S(1)}) fusion(f32[512,4,128]{2,1,0:T(4,128)S(1)} %gather_fusion, f32[512,1,128]{2,1,0:T(1,128)S(1)} %bitcast.18, f32[512,4,128]{2,1,0:T(4,128)S(1)} %gather_fusion.1), kind=kLoop, calls=%fused_computation.13 | loop fusion | flops 262144 | bytes 1310720 | tf_op jit(solution)/shard_map/exp | solution.py:80
  62.6 0.4 fusion
  63.3 1.9 %collective-permute-done.7 = f32[256,4,128]{2,1,0:T(4,128)S(1)} collective-permute-done((f32[256,4,128]{2,1,0:T(4,128)S(1)}, f32[256,4,128]{2,1,0:T(4,128)S(1)}, u32[]{:S(2)}, u32[]{:S(2)}) %collective-permute-start.7) | collective-permute-done | bytes 524320 | tf_op jit(solution)/shard_map/ppermute | solution.py:134
  65.2 1.6 %fusion.2 = f32[256,4,128]{2,1,0:T(4,128)} fusion(f32[256,4,128]{2,1,0:T(4,128)S(1)} %collective-permute-done.7, f32[512,3,128]{2,1,0:T(4,128)S(1)} %fusion, f32[512,1,128]{2,1,0:T(1,128)S(1)} %get-tuple-element.16, pred[256]{0:T(512)(128)(4,1)S(1)} %get-tuple-element.11), kind=kLoop, calls=%fused_computation.7 | loop fusion | flops 262144 | bytes 2097408 | tf_op jit(solution)/shard_map/jit(_where)/select_n | solution.py:136
  (22 shorter events, 1.0 us)
Async XLA Ops:
  23.3 9.4 %collective-permute-start = (f32[129,4,128]{2,1,0:T(4,128)S(1)}, f32[129,4,128]{2,1,0:T(4,128)S(1)}, u32[]{:S(2)}, u32[]{:S(2)}) collective-permute-start(f32[129,4,128]{2,1,0:T(4,128)S(1)} %pad_maximum_fusion.1), channel_id=1, source_target_pairs={{0,4},{4,8},{8,12},{12,14},{14,10},{10,6},{6,2},{2,0},{1,5},{5,9},... | collective-permute-start | bytes 792584 | tf_op jit(solution)/shard_map/ppermute | solution.py:97
  26.4 10.2 %collective-permute-start.1 = (f32[129,4,128]{2,1,0:T(4,128)S(1)}, f32[129,4,128]{2,1,0:T(4,128)S(1)}, u32[]{:S(2)}, u32[]{:S(2)}) collective-permute-start(f32[129,4,128]{2,1,0:T(4,128)S(1)} %pad_maximum_fusion.1), channel_id=1, source_target_pairs={{4,0},{8,4},{12,8},{14,12},{10,14},{6,10},{2,6},{0,2},{5,1},{9,5},... | collective-permute-start | bytes 792584 | tf_op jit(solution)/shard_map/ppermute | solution.py:100
  32.7 7.5 %collective-permute-start.2 = (f32[129,4,128]{2,1,0:T(4,128)S(1)}, f32[129,4,128]{2,1,0:T(4,128)S(1)}, u32[]{:S(2)}, u32[]{:S(2)}) collective-permute-start(f32[129,4,128]{2,1,0:T(4,128)S(1)} %collective-permute-done), channel_id=1, source_target_pairs={{0,4},{4,8},{8,12},{12,14},{14,10},{10,6},{6,2},{2,0},{1,5},{5,9},... | collective-permute-start | bytes 792584 | tf_op jit(solution)/shard_map/ppermute | solution.py:97
  36.6 7.0 %collective-permute-start.3 = (f32[129,4,128]{2,1,0:T(4,128)S(1)}, f32[129,4,128]{2,1,0:T(4,128)S(1)}, u32[]{:S(2)}, u32[]{:S(2)}) collective-permute-start(f32[129,4,128]{2,1,0:T(4,128)S(1)} %collective-permute-done.1), channel_id=1, source_target_pairs={{4,0},{8,4},{12,8},{14,12},{10,14},{6,10},{2,6},{0,2},{5,1},{9,5},... | collective-permute-start | bytes 792584 | tf_op jit(solution)/shard_map/ppermute | solution.py:100
  40.2 6.6 %collective-permute-start.4 = (f32[129,4,128]{2,1,0:T(4,128)S(1)}, f32[129,4,128]{2,1,0:T(4,128)S(1)}, u32[]{:S(2)}, u32[]{:S(2)}) collective-permute-start(f32[129,4,128]{2,1,0:T(4,128)S(1)} %collective-permute-done.2), channel_id=1, source_target_pairs={{0,4},{4,8},{8,12},{12,14},{14,10},{10,6},{6,2},{2,0},{1,5},{5,9},... | collective-permute-start | bytes 792584 | tf_op jit(solution)/shard_map/ppermute | solution.py:97
  43.6 6.4 %collective-permute-start.5 = (f32[129,4,128]{2,1,0:T(4,128)S(1)}, f32[129,4,128]{2,1,0:T(4,128)S(1)}, u32[]{:S(2)}, u32[]{:S(2)}) collective-permute-start(f32[129,4,128]{2,1,0:T(4,128)S(1)} %collective-permute-done.3), channel_id=1, source_target_pairs={{4,0},{8,4},{12,8},{14,12},{10,14},{6,10},{2,6},{0,2},{5,1},{9,5},... | collective-permute-start | bytes 792584 | tf_op jit(solution)/shard_map/ppermute | solution.py:100
  46.8 6.4 %collective-permute-start.6 = (f32[129,4,128]{2,1,0:T(4,128)S(1)}, f32[129,4,128]{2,1,0:T(4,128)S(1)}, u32[]{:S(2)}, u32[]{:S(2)}) collective-permute-start(f32[129,4,128]{2,1,0:T(4,128)S(1)} %collective-permute-done.4), channel_id=1, source_target_pairs={{0,4},{4,8},{8,12},{12,14},{14,10},{10,6},{6,2},{2,0},{1,5},{5,9},... | collective-permute-start | bytes 792584 | tf_op jit(solution)/shard_map/ppermute | solution.py:97
  55.2 1.4 %copy-start = (f32[1033,4,128]{2,1,0:T(4,128)}, f32[1033,4,128]{2,1,0:T(4,128)S(1)}, u32[]{:S(2)}) copy-start(f32[1033,4,128]{2,1,0:T(4,128)S(1)} %constant_dynamic-update-slice_fusion) | copy-start | bytes 6346756
  63.3 2.0 %collective-permute-start.7 = (f32[256,4,128]{2,1,0:T(4,128)S(1)}, f32[256,4,128]{2,1,0:T(4,128)S(1)}, u32[]{:S(2)}, u32[]{:S(2)}) collective-permute-start(f32[256,4,128]{2,1,0:T(4,128)S(1)} %pad_maximum_fusion), channel_id=1, source_target_pairs={{0,1},{1,0},{2,3},{3,2},{4,5},{5,4},{6,7},{7,6},{8,9},{9,8},{10,11... | collective-permute-start | bytes 1572872 | tf_op jit(solution)/shard_map/ppermute | solution.py:134

commit v11 on v10

--- a/solution.py
+++ b/solution.py
@@ -20,11 +20,11 @@
     def one_step(step, carry):
         transmit, depth_sum = carry[0], carry[1]
         values = density_ref[pl.ds(step, block_rows, stride=sample_count), :]
-        optical = absorb * jax.nn.softplus(values) / sample_count
+        optical = absorb * jnp.log1p(jnp.exp(values)) / sample_count
         passed = jnp.exp(-optical)
         weight = transmit * (1.0 - passed)
         colours = tuple(
-            carry[2 + channel] + weight * jax.nn.sigmoid(slopes[channel] * values + offsets[channel])
+            carry[2 + channel] + weight * (0.5 * jnp.tanh(0.5 * (slopes[channel] * values + offsets[channel])) + 0.5)
             for channel in range(3)
         )
         return (transmit * passed, depth_sum + optical) + colours
@@ -71,7 +71,7 @@
     front_slot = jnp.sum(jnp.where(is_front, slot_ids, 0), axis=1)
     has_front = jnp.any(is_front, axis=1)
     has_back = back >= 0
-    zero_row = flat.shape[0] - 1
+    zero_row = stride - 1
     back_idx = jnp.where(has_back, back_slot * stride + back_off, zero_row)
     front_idx = jnp.where(has_front, front_slot * stride + front_off, zero_row)
     back_rows = jnp.take(flat, back_idx, axis=0, mode="clip")
@@ -99,7 +99,7 @@
         if 2 * step < count:
             behind = lax.ppermute(behind, "depth", backward)
             slots.append(behind)
-    return jnp.concatenate(slots + [jnp.zeros((1,) + own.shape[1:], own.dtype)], axis=0)
+    return jnp.concatenate(slots, axis=0)
 
 
 def on_device(density, foot_start, foot_rows, extinction, colour_slope, colour_offset, tile_source):
@@ -116,10 +116,10 @@
     brick_rows, channels, pixels = layers.shape
     lane = lax.broadcasted_iota(jnp.int32, (1, channels, pixels), 2)
     meta = jnp.where(lane == 0, start, jnp.where(lane == 1, shown, jnp.where(lane == 2, depth_index, 0)))
-    stride = brick_rows + 1
-    own = jnp.concatenate([layers, meta.astype(jnp.float32)], axis=0)
+    stride = brick_rows + 2
+    own = jnp.concatenate([layers, meta.astype(jnp.float32), jnp.zeros_like(meta, jnp.float32)], axis=0)
     flat = ring_gather(own, depth_count)
-    meta_rows = flat[:depth_count * stride].reshape(depth_count, stride, channels, pixels)[:, brick_rows, 0, :3]
+    meta_rows = flat.reshape(depth_count, stride, channels, pixels)[:, brick_rows, 0, :3]
     starts = meta_rows[:, 0].astype(jnp.int32)
     counts = meta_rows[:, 1].astype(jnp.int32)
     brick_ids = meta_rows[:, 2].astype(jnp.int32)

time: 67.2 us -> 64.7 us (0.963)
  local copies, waits for them, and re-layouts: 15.2 us -> 7.28 us
  waiting for transfers between devices: 14.8 us -> 21.3 us
  Pallas kernels: 20.3 us -> 19.4 us
    unnamed x10 -> x11, local copies, waits for them, and re-layouts: 7.72 us -> 1.27 us
    ppermute x4, waiting for transfers between devices: 12.3 us -> 17.5 us  [ring_gather(): ahead = lax.ppermute(ahead, 'depth', forward)]
    ppermute x3, waiting for transfers between devices: 0.54 us -> 1.91 us  [ring_gather(): behind = lax.ppermute(behind, 'depth', backward)]
    pallas_call x1, Pallas kernels: 20.3 us -> 19.4 us  [render_layers(): pl.pallas_call(render_kernel, grid=(brick_rows // block_rows,), in_specs=...]
    slice x1, local copies, waits for them, and re-layouts: 0.75 us -> 0.01 us  [on_device(): flat.reshape(depth_count, stride, channels, pixels)[:, brick_rows, 0, :3]]
    concatenate x2 -> x1, local copies, waits for them, and re-layouts: 0.78 us -> 0.04 us  [ring_gather(): return jnp.concatenate(slots, axis=0)]
  transfers between devices with their start and end apart: 8 -> 8, of which waited for: 7 -> 7; matrix products, arithmetic and copies ran while one was open for 13% -> 3% of each run, Pallas kernels for 0% -> 0%
where the time goes in v11:
time: 64.7 us; the launch traced here: 64.3 us
  waiting for transfers between devices  21.3 us (33%)
  Pallas kernels  19.4 us (30%)
  starting transfers between devices  8.89 us (14%)
  local copies, waits for them, and re-layouts  7.28 us (11%)
  other arithmetic  5.27 us (8%)
  between operations  2.12 us (3%)
    pallas_call x1, Pallas kernels, render_layers(): pl.pallas_call(render_kernel, grid=(brick_rows // block_rows,), in_specs=...  19.4 us
    ppermute x4, waiting for transfers between devices, ring_gather(): ahead = lax.ppermute(ahead, 'depth', forward)  17.5 us
    ppermute x4, starting transfers between devices, ring_gather(): ahead = lax.ppermute(ahead, 'depth', forward)  8.03 us
    gather x1, local copies, waits for them, and re-layouts, composite_rows(): front_rows = jnp.take(flat, front_idx, axis=0, mode='clip')  3.11 us
    gather x1, local copies, waits for them, and re-layouts, composite_rows(): back_rows = jnp.take(flat, back_idx, axis=0, mode='clip')  2.07 us
    ppermute x3, waiting for transfers between devices, ring_gather(): behind = lax.ppermute(behind, 'depth', backward)  1.91 us
    ppermute x1, waiting for transfers between devices, on_device(): received = lax.ppermute(for_partner, 'screen', [(0, 1), (1, 0)])  1.9 us
    select_n x1, other arithmetic, on_device(): return jnp.where(in_my_half[:, None, None], mine, received)  1.62 us
  transfers between devices with their start and end apart: 8, of which 7 were waited for; matrix products, arithmetic and copies ran while one was open for 3% of the time, Pallas kernels for 0%

profile of v11, /device:TPU:0, one launch (start us, length us, event | category | flops | bytes accessed | tf_op | source)
XLA Modules:
  0.0 64.3 jit_solution(6550174608949404991)
XLA Ops:
  1.3 19.4 %shard_map.73 = f32[128,4,128]{2,1,0:T(4,128)} custom-call(f32[1]{0:T(128)S(6)} %copy.24.absorb_ref, f32[3]{0:T(128)} %slope_ref.1, f32[3]{0:T(128)} %offset_ref.1, s32[1,1]{1,0:T(1,128)} %copy.23.shown_ref, f32[16384,128]{1,0:T(8,128)} %bitcast.15), custom_call_target="tpu_custom_call" | custom-call | tf_op jit(solution)/shard_map/pallas_call | solution.py:44
  20.7 1.0 %constant_dynamic-update-slice_fusion.9 = f32[1040,4,128]{2,1,0:T(4,128)S(1)} fusion(f32[128,4,128]{2,1,0:T(4,128)} %shard_map.73), kind=kLoop, calls=%fused_computation.27 | loop fusion | bytes 524288
  22.3 1.0 %pad_maximum_fusion.1 = f32[130,4,128]{2,1,0:T(4,128)S(1)} fusion(f32[1,4,128]{2,1,0:T(4,128)S(1)} %broadcast_in_dim.69, f32[1,4,128]{2,1,0:T(4,128)S(1)} %get-tuple-element.16, f32[128,4,128]{2,1,0:T(4,128)} %shard_map.73), kind=kLoop, calls=%fused_computation.9 | loop fusion | flops 133120 | bytes 532480 | tf_op jit(solution)/shard_map/concatenate | solution.py:120
  23.3 3.1 %collective-permute-start = (f32[130,4,128]{2,1,0:T(4,128)S(1)}, f32[130,4,128]{2,1,0:T(4,128)S(1)}, u32[]{:S(2)}, u32[]{:S(2)}) collective-permute-start(f32[130,4,128]{2,1,0:T(4,128)S(1)} %pad_maximum_fusion.1), channel_id=1, source_target_pairs={{0,4},{4,8},{8,12},{12,14},{14,10},{10,6},{6,2},{2,0},{1,5},{5,9},... | collective-permute-start | bytes 798728 | tf_op jit(solution)/shard_map/ppermute | solution.py:97
  26.4 0.0 collective-permute-start.1
  26.4 6.3 %collective-permute-done = f32[130,4,128]{2,1,0:T(4,128)S(1)} collective-permute-done((f32[130,4,128]{2,1,0:T(4,128)S(1)}, f32[130,4,128]{2,1,0:T(4,128)S(1)}, u32[]{:S(2)}, u32[]{:S(2)}) %collective-permute-start) | collective-permute-done | bytes 266272 | tf_op jit(solution)/shard_map/ppermute | solution.py:97
  32.8 1.8 %collective-permute-start.2 = (f32[130,4,128]{2,1,0:T(4,128)S(1)}, f32[130,4,128]{2,1,0:T(4,128)S(1)}, u32[]{:S(2)}, u32[]{:S(2)}) collective-permute-start(f32[130,4,128]{2,1,0:T(4,128)S(1)} %collective-permute-done), channel_id=1, source_target_pairs={{0,4},{4,8},{8,12},{12,14},{14,10},{10,6},{6,2},{2,0},{1,5},{5,9},... | collective-permute-start | bytes 798728 | tf_op jit(solution)/shard_map/ppermute | solution.py:97
  34.5 0.8 %fusion.8 = (pred[256]{0:T(512)(128)(4,1)S(1)}, s32[256]{0:T(256)S(1)}) fusion(s32[]{:T(128)S(6)} %axis_index.25, s32[4096]{0:T(1024)} %param.13, s32[]{:T(128)S(6)} %select_n.98), kind=kLoop, calls=%fused_computation.51 | loop fusion | flops 4096 | bytes 2312 | tf_op jit(solution)/shard_map/eq | solution.py:135
  35.3 0.8 %dynamic_slice.7 = s32[256]{0:T(256)S(1)} dynamic-slice(s32[4096]{0:T(1024)} %param.13, s32[]{:T(128)S(6)} %select_n.103), dynamic_slice_sizes={256} | dynamic-slice | bytes 2052 | tf_op jit(solution)/shard_map/dynamic_slice | solution.py:129
  36.1 0.0 collective-permute-done.1
  36.1 0.2 collective-permute-start.3
  36.3 4.0 %collective-permute-done.2 = f32[130,4,128]{2,1,0:T(4,128)S(1)} collective-permute-done((f32[130,4,128]{2,1,0:T(4,128)S(1)}, f32[130,4,128]{2,1,0:T(4,128)S(1)}, u32[]{:S(2)}, u32[]{:S(2)}) %collective-permute-start.2) | collective-permute-done | bytes 266272 | tf_op jit(solution)/shard_map/ppermute | solution.py:97
  40.3 1.5 %collective-permute-start.4 = (f32[130,4,128]{2,1,0:T(4,128)S(1)}, f32[130,4,128]{2,1,0:T(4,128)S(1)}, u32[]{:S(2)}, u32[]{:S(2)}) collective-permute-start(f32[130,4,128]{2,1,0:T(4,128)S(1)} %collective-permute-done.2), channel_id=1, source_target_pairs={{0,4},{4,8},{8,12},{12,14},{14,10},{10,6},{6,2},{2,0},{1,5},{5,9},... | collective-permute-start | bytes 798728 | tf_op jit(solution)/shard_map/ppermute | solution.py:97
  41.9 1.2 %collective-permute-done.3 = f32[130,4,128]{2,1,0:T(4,128)S(1)} collective-permute-done((f32[130,4,128]{2,1,0:T(4,128)S(1)}, f32[130,4,128]{2,1,0:T(4,128)S(1)}, u32[]{:S(2)}, u32[]{:S(2)}) %collective-permute-start.3) | collective-permute-done | bytes 266272 | tf_op jit(solution)/shard_map/ppermute | solution.py:100
  43.1 0.5 collective-permute-start.5
  43.7 3.3 %collective-permute-done.4 = f32[130,4,128]{2,1,0:T(4,128)S(1)} collective-permute-done((f32[130,4,128]{2,1,0:T(4,128)S(1)}, f32[130,4,128]{2,1,0:T(4,128)S(1)}, u32[]{:S(2)}, u32[]{:S(2)}) %collective-permute-start.4) | collective-permute-done | bytes 266272 | tf_op jit(solution)/shard_map/ppermute | solution.py:97
  47.0 1.7 %collective-permute-start.6 = (f32[130,4,128]{2,1,0:T(4,128)S(1)}, f32[130,4,128]{2,1,0:T(4,128)S(1)}, u32[]{:S(2)}, u32[]{:S(2)}) collective-permute-start(f32[130,4,128]{2,1,0:T(4,128)S(1)} %collective-permute-done.4), channel_id=1, source_target_pairs={{0,4},{4,8},{8,12},{12,14},{14,10},{10,6},{6,2},{2,0},{1,5},{5,9},... | collective-permute-start | bytes 798728 | tf_op jit(solution)/shard_map/ppermute | solution.py:97
  48.8 0.7 %collective-permute-done.5 = f32[130,4,128]{2,1,0:T(4,128)S(1)} collective-permute-done((f32[130,4,128]{2,1,0:T(4,128)S(1)}, f32[130,4,128]{2,1,0:T(4,128)S(1)}, u32[]{:S(2)}, u32[]{:S(2)}) %collective-permute-start.5) | collective-permute-done | bytes 266272 | tf_op jit(solution)/shard_map/ppermute | solution.py:100
  49.5 3.9 %collective-permute-done.6 = f32[130,4,128]{2,1,0:T(4,128)S(1)} collective-permute-done((f32[130,4,128]{2,1,0:T(4,128)S(1)}, f32[130,4,128]{2,1,0:T(4,128)S(1)}, u32[]{:S(2)}, u32[]{:S(2)}) %collective-permute-start.6) | collective-permute-done | bytes 266272 | tf_op jit(solution)/shard_map/ppermute | solution.py:97
  53.4 0.0 copy-start
  53.5 0.1 copy.12
  53.6 0.1 select_reduce_fusion.2
  53.7 0.1 fusion.9
  53.8 0.1 select_reduce_fusion.1
  53.9 2.1 %gather_fusion.1 = f32[512,4,128]{2,1,0:T(4,128)S(1)} fusion(f32[1040,4,128]{2,1,0:T(4,128)S(1)} %constant_dynamic-update-slice_fusion, s32[1024]{0:T(1024)S(1)} %pad_clamp_fusion), kind=kCustom, calls=%fused_computation.1 | custom fusion | bytes 2099200 | tf_op jit(solution)/shard_map/jit(_take)/gather | solution.py:77
  56.0 3.1 %gather_fusion = f32[512,4,128]{2,1,0:T(4,128)S(1)} fusion(f32[1040,4,128]{2,1,0:T(4,128)} %copy-done, s32[1024]{0:T(1024)S(1)} %pad_clamp_fusion.1), kind=kCustom, calls=%fused_computation | custom fusion | bytes 2099200 | tf_op jit(solution)/shard_map/jit(_take)/gather | solution.py:78
  59.1 0.9 %negate_exponential_fusion = (f32[512,1,128]{2,1,0:T(1,128)S(1)}, f32[512,1,128]{2,1,0:T(1,128)S(1)}) fusion(f32[512,4,128]{2,1,0:T(4,128)S(1)} %gather_fusion, f32[512,1,128]{2,1,0:T(1,128)S(1)} %bitcast.17, f32[512,4,128]{2,1,0:T(4,128)S(1)} %gather_fusion.1), kind=kLoop, calls=%fused_computation.13 | loop fusion | flops 262144 | bytes 1310720 | tf_op jit(solution)/shard_map/exp | solution.py:80
  60.0 0.4 fusion
  60.4 0.2 pad_maximum_fusion
  60.7 0.1 collective-permute-start.7
  60.7 1.9 %collective-permute-done.7 = f32[256,4,128]{2,1,0:T(4,128)S(1)} collective-permute-done((f32[256,4,128]{2,1,0:T(4,128)S(1)}, f32[256,4,128]{2,1,0:T(4,128)S(1)}, u32[]{:S(2)}, u32[]{:S(2)}) %collective-permute-start.7) | collective-permute-done | bytes 524320 | tf_op jit(solution)/shard_map/ppermute | solution.py:134
  62.6 1.6 %fusion.2 = f32[256,4,128]{2,1,0:T(4,128)} fusion(f32[256,4,128]{2,1,0:T(4,128)S(1)} %collective-permute-done.7, f32[512,3,128]{2,1,0:T(4,128)S(1)} %fusion, f32[512,1,128]{2,1,0:T(1,128)S(1)} %get-tuple-element.18, pred[256]{0:T(512)(128)(4,1)S(1)} %get-tuple-element.11), kind=kLoop, calls=%fused_computation.7 | loop fusion | flops 262144 | bytes 2097408 | tf_op jit(solution)/shard_map/jit(_where)/select_n | solution.py:136
  (22 shorter events, 0.4 us)
Async XLA Ops:
  23.3 9.4 %collective-permute-start = (f32[130,4,128]{2,1,0:T(4,128)S(1)}, f32[130,4,128]{2,1,0:T(4,128)S(1)}, u32[]{:S(2)}, u32[]{:S(2)}) collective-permute-start(f32[130,4,128]{2,1,0:T(4,128)S(1)} %pad_maximum_fusion.1), channel_id=1, source_target_pairs={{0,4},{4,8},{8,12},{12,14},{14,10},{10,6},{6,2},{2,0},{1,5},{5,9},... | collective-permute-start | bytes 798728 | tf_op jit(solution)/shard_map/ppermute | solution.py:97
  26.4 9.7 %collective-permute-start.1 = (f32[130,4,128]{2,1,0:T(4,128)S(1)}, f32[130,4,128]{2,1,0:T(4,128)S(1)}, u32[]{:S(2)}, u32[]{:S(2)}) collective-permute-start(f32[130,4,128]{2,1,0:T(4,128)S(1)} %pad_maximum_fusion.1), channel_id=1, source_target_pairs={{4,0},{8,4},{12,8},{14,12},{10,14},{6,10},{2,6},{0,2},{5,1},{9,5},... | collective-permute-start | bytes 798728 | tf_op jit(solution)/shard_map/ppermute | solution.py:100
  32.8 7.6 %collective-permute-start.2 = (f32[130,4,128]{2,1,0:T(4,128)S(1)}, f32[130,4,128]{2,1,0:T(4,128)S(1)}, u32[]{:S(2)}, u32[]{:S(2)}) collective-permute-start(f32[130,4,128]{2,1,0:T(4,128)S(1)} %collective-permute-done), channel_id=1, source_target_pairs={{0,4},{4,8},{8,12},{12,14},{14,10},{10,6},{6,2},{2,0},{1,5},{5,9},... | collective-permute-start | bytes 798728 | tf_op jit(solution)/shard_map/ppermute | solution.py:97
  36.1 7.0 %collective-permute-start.3 = (f32[130,4,128]{2,1,0:T(4,128)S(1)}, f32[130,4,128]{2,1,0:T(4,128)S(1)}, u32[]{:S(2)}, u32[]{:S(2)}) collective-permute-start(f32[130,4,128]{2,1,0:T(4,128)S(1)} %collective-permute-done.1), channel_id=1, source_target_pairs={{4,0},{8,4},{12,8},{14,12},{10,14},{6,10},{2,6},{0,2},{5,1},{9,5},... | collective-permute-start | bytes 798728 | tf_op jit(solution)/shard_map/ppermute | solution.py:100
  40.3 6.7 %collective-permute-start.4 = (f32[130,4,128]{2,1,0:T(4,128)S(1)}, f32[130,4,128]{2,1,0:T(4,128)S(1)}, u32[]{:S(2)}, u32[]{:S(2)}) collective-permute-start(f32[130,4,128]{2,1,0:T(4,128)S(1)} %collective-permute-done.2), channel_id=1, source_target_pairs={{0,4},{4,8},{8,12},{12,14},{14,10},{10,6},{6,2},{2,0},{1,5},{5,9},... | collective-permute-start | bytes 798728 | tf_op jit(solution)/shard_map/ppermute | solution.py:97
  43.1 6.4 %collective-permute-start.5 = (f32[130,4,128]{2,1,0:T(4,128)S(1)}, f32[130,4,128]{2,1,0:T(4,128)S(1)}, u32[]{:S(2)}, u32[]{:S(2)}) collective-permute-start(f32[130,4,128]{2,1,0:T(4,128)S(1)} %collective-permute-done.3), channel_id=1, source_target_pairs={{4,0},{8,4},{12,8},{14,12},{10,14},{6,10},{2,6},{0,2},{5,1},{9,5},... | collective-permute-start | bytes 798728 | tf_op jit(solution)/shard_map/ppermute | solution.py:100
  47.0 6.4 %collective-permute-start.6 = (f32[130,4,128]{2,1,0:T(4,128)S(1)}, f32[130,4,128]{2,1,0:T(4,128)S(1)}, u32[]{:S(2)}, u32[]{:S(2)}) collective-permute-start(f32[130,4,128]{2,1,0:T(4,128)S(1)} %collective-permute-done.4), channel_id=1, source_target_pairs={{0,4},{4,8},{8,12},{12,14},{14,10},{10,6},{6,2},{2,0},{1,5},{5,9},... | collective-permute-start | bytes 798728 | tf_op jit(solution)/shard_map/ppermute | solution.py:97
  53.4 2.5 %copy-start = (f32[1040,4,128]{2,1,0:T(4,128)}, f32[1040,4,128]{2,1,0:T(4,128)S(1)}, u32[]{:S(2)}) copy-start(f32[1040,4,128]{2,1,0:T(4,128)S(1)} %constant_dynamic-update-slice_fusion) | copy-start | bytes 6389764
  60.7 2.0 %collective-permute-start.7 = (f32[256,4,128]{2,1,0:T(4,128)S(1)}, f32[256,4,128]{2,1,0:T(4,128)S(1)}, u32[]{:S(2)}, u32[]{:S(2)}) collective-permute-start(f32[256,4,128]{2,1,0:T(4,128)S(1)} %pad_maximum_fusion), channel_id=1, source_target_pairs={{0,1},{1,0},{2,3},{3,2},{4,5},{5,4},{6,7},{7,6},{8,9},{9,8},{10,11... | collective-permute-start | bytes 1572872 | tf_op jit(solution)/shard_map/ppermute | solution.py:134

commit v12 on v11

--- a/solution.py
+++ b/solution.py
@@ -12,30 +12,30 @@
     block_rows = out_ref.shape[0]
     pixels = out_ref.shape[2]
     sample_count = density_ref.shape[0] // block_rows
-    absorb = absorb_ref[0]
-    slopes = [slope_ref[channel] for channel in range(3)]
-    offsets = [offset_ref[channel] for channel in range(3)]
+    scale = absorb_ref[0] / sample_count
+    half_slopes = [0.5 * slope_ref[channel] for channel in range(3)]
+    half_offsets = [0.5 * offset_ref[channel] for channel in range(3)]
     shown = shown_ref[0, 0]
 
     def one_step(step, carry):
-        transmit, depth_sum = carry[0], carry[1]
+        half_transmit, depth_sum, weight_sum = carry[0], carry[1], carry[2]
         values = density_ref[pl.ds(step, block_rows, stride=sample_count), :]
-        optical = absorb * jnp.log1p(jnp.exp(values)) / sample_count
+        optical = scale * jnp.log1p(jnp.exp(values))
         passed = jnp.exp(-optical)
-        weight = transmit * (1.0 - passed)
+        half_weight = half_transmit * (1.0 - passed)
         colours = tuple(
-            carry[2 + channel] + weight * (0.5 * jnp.tanh(0.5 * (slopes[channel] * values + offsets[channel])) + 0.5)
+            carry[3 + channel] + half_weight * jnp.tanh(half_slopes[channel] * values + half_offsets[channel])
             for channel in range(3)
         )
-        return (transmit * passed, depth_sum + optical) + colours
+        return (half_transmit * passed, depth_sum + optical, weight_sum + half_weight) + colours
 
     zeros = jnp.zeros((block_rows, pixels), jnp.float32)
-    carry = (jnp.ones((block_rows, pixels), jnp.float32), zeros, zeros, zeros, zeros)
+    carry = (jnp.full((block_rows, pixels), 0.5, jnp.float32), zeros, zeros, zeros, zeros, zeros)
     carry = lax.fori_loop(0, sample_count, one_step, carry, unroll=8)
     row_ids = pl.program_id(0) * block_rows + lax.broadcasted_iota(jnp.int32, (block_rows, pixels), 0)
     visible = row_ids < shown
     for channel in range(3):
-        out_ref[:, channel, :] = jnp.where(visible, carry[2 + channel], 0.0)
+        out_ref[:, channel, :] = jnp.where(visible, carry[2] + carry[3 + channel], 0.0)
     out_ref[:, 3, :] = jnp.where(visible, carry[1], 0.0)
 
 

time: 64.7 us -> 63.8 us (0.986)
  Pallas kernels: 19.4 us -> 18.2 us
    pallas_call x1, Pallas kernels: 19.4 us -> 18.2 us  [render_layers(): pl.pallas_call(render_kernel, grid=(brick_rows // block_rows,), in_specs=...]
where the time goes in v12:
time: 63.8 us; the launch traced here: 63.1 us
  waiting for transfers between devices  21.3 us (33%)
  Pallas kernels  18.2 us (29%)
  starting transfers between devices  8.89 us (14%)
  local copies, waits for them, and re-layouts  7.28 us (11%)
  other arithmetic  5.27 us (8%)
  between operations  2.12 us (3%)
    pallas_call x1, Pallas kernels, render_layers(): pl.pallas_call(render_kernel, grid=(brick_rows // block_rows,), in_specs=...  18.2 us
    ppermute x4, waiting for transfers between devices, ring_gather(): ahead = lax.ppermute(ahead, 'depth', forward)  17.5 us
    ppermute x4, starting transfers between devices, ring_gather(): ahead = lax.ppermute(ahead, 'depth', forward)  8.03 us
    gather x1, local copies, waits for them, and re-layouts, composite_rows(): front_rows = jnp.take(flat, front_idx, axis=0, mode='clip')  3.11 us
    gather x1, local copies, waits for them, and re-layouts, composite_rows(): back_rows = jnp.take(flat, back_idx, axis=0, mode='clip')  2.07 us
    ppermute x3, waiting for transfers between devices, ring_gather(): behind = lax.ppermute(behind, 'depth', backward)  1.91 us
    ppermute x1, waiting for transfers between devices, on_device(): received = lax.ppermute(for_partner, 'screen', [(0, 1), (1, 0)])  1.9 us
    select_n x1, other arithmetic, on_device(): return jnp.where(in_my_half[:, None, None], mine, received)  1.62 us
  transfers between devices with their start and end apart: 8, of which 7 were waited for; matrix products, arithmetic and copies ran while one was open for 3% of the time, Pallas kernels for 0%

profile of v12, /device:TPU:0, one launch (start us, length us, event | category | flops | bytes accessed | tf_op | source)
XLA Modules:
  0.0 63.1 jit_solution(7284183834202887150)
XLA Ops:
  1.3 18.2 %shard_map.73 = f32[128,4,128]{2,1,0:T(4,128)} custom-call(f32[1]{0:T(128)S(6)} %copy.24.absorb_ref, f32[3]{0:T(128)} %slope_ref.1, f32[3]{0:T(128)} %offset_ref.1, s32[1,1]{1,0:T(1,128)} %copy.23.shown_ref, f32[16384,128]{1,0:T(8,128)} %bitcast.15), custom_call_target="tpu_custom_call" | custom-call | tf_op jit(solution)/shard_map/pallas_call | solution.py:44
  19.5 1.0 %constant_dynamic-update-slice_fusion.9 = f32[1040,4,128]{2,1,0:T(4,128)S(1)} fusion(f32[128,4,128]{2,1,0:T(4,128)} %shard_map.73), kind=kLoop, calls=%fused_computation.27 | loop fusion | bytes 524288
  21.2 1.0 %pad_maximum_fusion.1 = f32[130,4,128]{2,1,0:T(4,128)S(1)} fusion(f32[1,4,128]{2,1,0:T(4,128)S(1)} %broadcast_in_dim.69, f32[1,4,128]{2,1,0:T(4,128)S(1)} %get-tuple-element.16, f32[128,4,128]{2,1,0:T(4,128)} %shard_map.73), kind=kLoop, calls=%fused_computation.9 | loop fusion | flops 133120 | bytes 532480 | tf_op jit(solution)/shard_map/concatenate | solution.py:120
  22.2 3.1 %collective-permute-start = (f32[130,4,128]{2,1,0:T(4,128)S(1)}, f32[130,4,128]{2,1,0:T(4,128)S(1)}, u32[]{:S(2)}, u32[]{:S(2)}) collective-permute-start(f32[130,4,128]{2,1,0:T(4,128)S(1)} %pad_maximum_fusion.1), channel_id=1, source_target_pairs={{0,4},{4,8},{8,12},{12,14},{14,10},{10,6},{6,2},{2,0},{1,5},{5,9},... | collective-permute-start | bytes 798728 | tf_op jit(solution)/shard_map/ppermute | solution.py:97
  25.3 0.0 collective-permute-start.1
  25.3 6.3 %collective-permute-done = f32[130,4,128]{2,1,0:T(4,128)S(1)} collective-permute-done((f32[130,4,128]{2,1,0:T(4,128)S(1)}, f32[130,4,128]{2,1,0:T(4,128)S(1)}, u32[]{:S(2)}, u32[]{:S(2)}) %collective-permute-start) | collective-permute-done | bytes 266272 | tf_op jit(solution)/shard_map/ppermute | solution.py:97
  31.6 1.8 %collective-permute-start.2 = (f32[130,4,128]{2,1,0:T(4,128)S(1)}, f32[130,4,128]{2,1,0:T(4,128)S(1)}, u32[]{:S(2)}, u32[]{:S(2)}) collective-permute-start(f32[130,4,128]{2,1,0:T(4,128)S(1)} %collective-permute-done), channel_id=1, source_target_pairs={{0,4},{4,8},{8,12},{12,14},{14,10},{10,6},{6,2},{2,0},{1,5},{5,9},... | collective-permute-start | bytes 798728 | tf_op jit(solution)/shard_map/ppermute | solution.py:97
  33.4 0.8 %fusion.8 = (pred[256]{0:T(512)(128)(4,1)S(1)}, s32[256]{0:T(256)S(1)}) fusion(s32[]{:T(128)S(6)} %axis_index.25, s32[4096]{0:T(1024)} %param.13, s32[]{:T(128)S(6)} %select_n.98), kind=kLoop, calls=%fused_computation.51 | loop fusion | flops 4096 | bytes 2312 | tf_op jit(solution)/shard_map/eq | solution.py:135
  34.2 0.8 %dynamic_slice.7 = s32[256]{0:T(256)S(1)} dynamic-slice(s32[4096]{0:T(1024)} %param.13, s32[]{:T(128)S(6)} %select_n.103), dynamic_slice_sizes={256} | dynamic-slice | bytes 2052 | tf_op jit(solution)/shard_map/dynamic_slice | solution.py:129
  34.9 0.0 collective-permute-done.1
  34.9 0.2 collective-permute-start.3
  35.2 4.0 %collective-permute-done.2 = f32[130,4,128]{2,1,0:T(4,128)S(1)} collective-permute-done((f32[130,4,128]{2,1,0:T(4,128)S(1)}, f32[130,4,128]{2,1,0:T(4,128)S(1)}, u32[]{:S(2)}, u32[]{:S(2)}) %collective-permute-start.2) | collective-permute-done | bytes 266272 | tf_op jit(solution)/shard_map/ppermute | solution.py:97
  39.2 1.5 %collective-permute-start.4 = (f32[130,4,128]{2,1,0:T(4,128)S(1)}, f32[130,4,128]{2,1,0:T(4,128)S(1)}, u32[]{:S(2)}, u32[]{:S(2)}) collective-permute-start(f32[130,4,128]{2,1,0:T(4,128)S(1)} %collective-permute-done.2), channel_id=1, source_target_pairs={{0,4},{4,8},{8,12},{12,14},{14,10},{10,6},{6,2},{2,0},{1,5},{5,9},... | collective-permute-start | bytes 798728 | tf_op jit(solution)/shard_map/ppermute | solution.py:97
  40.7 1.2 %collective-permute-done.3 = f32[130,4,128]{2,1,0:T(4,128)S(1)} collective-permute-done((f32[130,4,128]{2,1,0:T(4,128)S(1)}, f32[130,4,128]{2,1,0:T(4,128)S(1)}, u32[]{:S(2)}, u32[]{:S(2)}) %collective-permute-start.3) | collective-permute-done | bytes 266272 | tf_op jit(solution)/shard_map/ppermute | solution.py:100
  41.9 0.5 collective-permute-start.5
  42.5 3.3 %collective-permute-done.4 = f32[130,4,128]{2,1,0:T(4,128)S(1)} collective-permute-done((f32[130,4,128]{2,1,0:T(4,128)S(1)}, f32[130,4,128]{2,1,0:T(4,128)S(1)}, u32[]{:S(2)}, u32[]{:S(2)}) %collective-permute-start.4) | collective-permute-done | bytes 266272 | tf_op jit(solution)/shard_map/ppermute | solution.py:97
  45.8 1.7 %collective-permute-start.6 = (f32[130,4,128]{2,1,0:T(4,128)S(1)}, f32[130,4,128]{2,1,0:T(4,128)S(1)}, u32[]{:S(2)}, u32[]{:S(2)}) collective-permute-start(f32[130,4,128]{2,1,0:T(4,128)S(1)} %collective-permute-done.4), channel_id=1, source_target_pairs={{0,4},{4,8},{8,12},{12,14},{14,10},{10,6},{6,2},{2,0},{1,5},{5,9},... | collective-permute-start | bytes 798728 | tf_op jit(solution)/shard_map/ppermute | solution.py:97
  47.6 0.7 %collective-permute-done.5 = f32[130,4,128]{2,1,0:T(4,128)S(1)} collective-permute-done((f32[130,4,128]{2,1,0:T(4,128)S(1)}, f32[130,4,128]{2,1,0:T(4,128)S(1)}, u32[]{:S(2)}, u32[]{:S(2)}) %collective-permute-start.5) | collective-permute-done | bytes 266272 | tf_op jit(solution)/shard_map/ppermute | solution.py:100
  48.4 3.9 %collective-permute-done.6 = f32[130,4,128]{2,1,0:T(4,128)S(1)} collective-permute-done((f32[130,4,128]{2,1,0:T(4,128)S(1)}, f32[130,4,128]{2,1,0:T(4,128)S(1)}, u32[]{:S(2)}, u32[]{:S(2)}) %collective-permute-start.6) | collective-permute-done | bytes 266272 | tf_op jit(solution)/shard_map/ppermute | solution.py:97
  52.3 0.0 copy-start
  52.3 0.1 copy.12
  52.4 0.1 select_reduce_fusion.2
  52.5 0.1 fusion.9
  52.6 0.1 select_reduce_fusion.1
  52.7 2.1 %gather_fusion.1 = f32[512,4,128]{2,1,0:T(4,128)S(1)} fusion(f32[1040,4,128]{2,1,0:T(4,128)S(1)} %constant_dynamic-update-slice_fusion, s32[1024]{0:T(1024)S(1)} %pad_clamp_fusion), kind=kCustom, calls=%fused_computation.1 | custom fusion | bytes 2099200 | tf_op jit(solution)/shard_map/jit(_take)/gather | solution.py:77
  54.8 3.1 %gather_fusion = f32[512,4,128]{2,1,0:T(4,128)S(1)} fusion(f32[1040,4,128]{2,1,0:T(4,128)} %copy-done, s32[1024]{0:T(1024)S(1)} %pad_clamp_fusion.1), kind=kCustom, calls=%fused_computation | custom fusion | bytes 2099200 | tf_op jit(solution)/shard_map/jit(_take)/gather | solution.py:78
  58.0 0.9 %negate_exponential_fusion = (f32[512,1,128]{2,1,0:T(1,128)S(1)}, f32[512,1,128]{2,1,0:T(1,128)S(1)}) fusion(f32[512,4,128]{2,1,0:T(4,128)S(1)} %gather_fusion, f32[512,1,128]{2,1,0:T(1,128)S(1)} %bitcast.17, f32[512,4,128]{2,1,0:T(4,128)S(1)} %gather_fusion.1), kind=kLoop, calls=%fused_computation.13 | loop fusion | flops 262144 | bytes 1310720 | tf_op jit(solution)/shard_map/exp | solution.py:80
  58.8 0.4 fusion
  59.3 0.2 pad_maximum_fusion
  59.5 0.1 collective-permute-start.7
  59.6 1.9 %collective-permute-done.7 = f32[256,4,128]{2,1,0:T(4,128)S(1)} collective-permute-done((f32[256,4,128]{2,1,0:T(4,128)S(1)}, f32[256,4,128]{2,1,0:T(4,128)S(1)}, u32[]{:S(2)}, u32[]{:S(2)}) %collective-permute-start.7) | collective-permute-done | bytes 524320 | tf_op jit(solution)/shard_map/ppermute | solution.py:134
  61.5 1.6 %fusion.2 = f32[256,4,128]{2,1,0:T(4,128)} fusion(f32[256,4,128]{2,1,0:T(4,128)S(1)} %collective-permute-done.7, f32[512,3,128]{2,1,0:T(4,128)S(1)} %fusion, f32[512,1,128]{2,1,0:T(1,128)S(1)} %get-tuple-element.18, pred[256]{0:T(512)(128)(4,1)S(1)} %get-tuple-element.11), kind=kLoop, calls=%fused_computation.7 | loop fusion | flops 262144 | bytes 2097408 | tf_op jit(solution)/shard_map/jit(_where)/select_n | solution.py:136
  (22 shorter events, 0.4 us)
Async XLA Ops:
  22.2 9.4 %collective-permute-start = (f32[130,4,128]{2,1,0:T(4,128)S(1)}, f32[130,4,128]{2,1,0:T(4,128)S(1)}, u32[]{:S(2)}, u32[]{:S(2)}) collective-permute-start(f32[130,4,128]{2,1,0:T(4,128)S(1)} %pad_maximum_fusion.1), channel_id=1, source_target_pairs={{0,4},{4,8},{8,12},{12,14},{14,10},{10,6},{6,2},{2,0},{1,5},{5,9},... | collective-permute-start | bytes 798728 | tf_op jit(solution)/shard_map/ppermute | solution.py:97
  25.3 9.7 %collective-permute-start.1 = (f32[130,4,128]{2,1,0:T(4,128)S(1)}, f32[130,4,128]{2,1,0:T(4,128)S(1)}, u32[]{:S(2)}, u32[]{:S(2)}) collective-permute-start(f32[130,4,128]{2,1,0:T(4,128)S(1)} %pad_maximum_fusion.1), channel_id=1, source_target_pairs={{4,0},{8,4},{12,8},{14,12},{10,14},{6,10},{2,6},{0,2},{5,1},{9,5},... | collective-permute-start | bytes 798728 | tf_op jit(solution)/shard_map/ppermute | solution.py:100
  31.6 7.6 %collective-permute-start.2 = (f32[130,4,128]{2,1,0:T(4,128)S(1)}, f32[130,4,128]{2,1,0:T(4,128)S(1)}, u32[]{:S(2)}, u32[]{:S(2)}) collective-permute-start(f32[130,4,128]{2,1,0:T(4,128)S(1)} %collective-permute-done), channel_id=1, source_target_pairs={{0,4},{4,8},{8,12},{12,14},{14,10},{10,6},{6,2},{2,0},{1,5},{5,9},... | collective-permute-start | bytes 798728 | tf_op jit(solution)/shard_map/ppermute | solution.py:97
  34.9 7.0 %collective-permute-start.3 = (f32[130,4,128]{2,1,0:T(4,128)S(1)}, f32[130,4,128]{2,1,0:T(4,128)S(1)}, u32[]{:S(2)}, u32[]{:S(2)}) collective-permute-start(f32[130,4,128]{2,1,0:T(4,128)S(1)} %collective-permute-done.1), channel_id=1, source_target_pairs={{4,0},{8,4},{12,8},{14,12},{10,14},{6,10},{2,6},{0,2},{5,1},{9,5},... | collective-permute-start | bytes 798728 | tf_op jit(solution)/shard_map/ppermute | solution.py:100
  39.2 6.7 %collective-permute-start.4 = (f32[130,4,128]{2,1,0:T(4,128)S(1)}, f32[130,4,128]{2,1,0:T(4,128)S(1)}, u32[]{:S(2)}, u32[]{:S(2)}) collective-permute-start(f32[130,4,128]{2,1,0:T(4,128)S(1)} %collective-permute-done.2), channel_id=1, source_target_pairs={{0,4},{4,8},{8,12},{12,14},{14,10},{10,6},{6,2},{2,0},{1,5},{5,9},... | collective-permute-start | bytes 798728 | tf_op jit(solution)/shard_map/ppermute | solution.py:97
  41.9 6.4 %collective-permute-start.5 = (f32[130,4,128]{2,1,0:T(4,128)S(1)}, f32[130,4,128]{2,1,0:T(4,128)S(1)}, u32[]{:S(2)}, u32[]{:S(2)}) collective-permute-start(f32[130,4,128]{2,1,0:T(4,128)S(1)} %collective-permute-done.3), channel_id=1, source_target_pairs={{4,0},{8,4},{12,8},{14,12},{10,14},{6,10},{2,6},{0,2},{5,1},{9,5},... | collective-permute-start | bytes 798728 | tf_op jit(solution)/shard_map/ppermute | solution.py:100
  45.8 6.4 %collective-permute-start.6 = (f32[130,4,128]{2,1,0:T(4,128)S(1)}, f32[130,4,128]{2,1,0:T(4,128)S(1)}, u32[]{:S(2)}, u32[]{:S(2)}) collective-permute-start(f32[130,4,128]{2,1,0:T(4,128)S(1)} %collective-permute-done.4), channel_id=1, source_target_pairs={{0,4},{4,8},{8,12},{12,14},{14,10},{10,6},{6,2},{2,0},{1,5},{5,9},... | collective-permute-start | bytes 798728 | tf_op jit(solution)/shard_map/ppermute | solution.py:97
  52.3 2.5 %copy-start = (f32[1040,4,128]{2,1,0:T(4,128)}, f32[1040,4,128]{2,1,0:T(4,128)S(1)}, u32[]{:S(2)}) copy-start(f32[1040,4,128]{2,1,0:T(4,128)S(1)} %constant_dynamic-update-slice_fusion) | copy-start | bytes 6389764
  59.5 2.0 %collective-permute-start.7 = (f32[256,4,128]{2,1,0:T(4,128)S(1)}, f32[256,4,128]{2,1,0:T(4,128)S(1)}, u32[]{:S(2)}, u32[]{:S(2)}) collective-permute-start(f32[256,4,128]{2,1,0:T(4,128)S(1)} %pad_maximum_fusion), channel_id=1, source_target_pairs={{0,1},{1,0},{2,3},{3,2},{4,5},{5,4},{6,7},{7,6},{8,9},{9,8},{10,11... | collective-permute-start | bytes 1572872 | tf_op jit(solution)/shard_map/ppermute | solution.py:134

commit v13 on v12

--- a/solution.py
+++ b/solution.py
@@ -31,7 +31,7 @@
 
     zeros = jnp.zeros((block_rows, pixels), jnp.float32)
     carry = (jnp.full((block_rows, pixels), 0.5, jnp.float32), zeros, zeros, zeros, zeros, zeros)
-    carry = lax.fori_loop(0, sample_count, one_step, carry, unroll=8)
+    carry = lax.fori_loop(0, sample_count, one_step, carry, unroll=16)
     row_ids = pl.program_id(0) * block_rows + lax.broadcasted_iota(jnp.int32, (block_rows, pixels), 0)
     visible = row_ids < shown
     for channel in range(3):
@@ -39,7 +39,7 @@
     out_ref[:, 3, :] = jnp.where(visible, carry[1], 0.0)
 
 
-def render_layers(density_block, shown_rows, absorb, colour_slope, colour_offset, block_rows=8):
+def render_layers(density_block, shown_rows, absorb, colour_slope, colour_offset, block_rows=16):
     brick_rows, sample_count, pixels = density_block.shape
     return pl.pallas_call(
         render_kernel,

time: 63.8 us -> 59.6 us (0.934)
  Pallas kernels: 18.2 us -> 14.4 us
    pallas_call x1, Pallas kernels: 18.2 us -> 14.4 us  [render_layers(): pl.pallas_call(render_kernel, grid=(brick_rows // block_rows,), in_specs=...]
where the time goes in v13:
time: 59.6 us; the launch traced here: 59.3 us
  waiting for transfers between devices  21.3 us (36%)
  Pallas kernels  14.4 us (24%)
  starting transfers between devices  8.89 us (15%)
  local copies, waits for them, and re-layouts  7.28 us (12%)
  other arithmetic  5.27 us (9%)
  between operations  2.12 us (4%)
    ppermute x4, waiting for transfers between devices, ring_gather(): ahead = lax.ppermute(ahead, 'depth', forward)  17.5 us
    pallas_call x1, Pallas kernels, render_layers(): pl.pallas_call(render_kernel, grid=(brick_rows // block_rows,), in_specs=...  14.4 us
    ppermute x4, starting transfers between devices, ring_gather(): ahead = lax.ppermute(ahead, 'depth', forward)  8.03 us
    gather x1, local copies, waits for them, and re-layouts, composite_rows(): front_rows = jnp.take(flat, front_idx, axis=0, mode='clip')  3.11 us
    gather x1, local copies, waits for them, and re-layouts, composite_rows(): back_rows = jnp.take(flat, back_idx, axis=0, mode='clip')  2.07 us
    ppermute x3, waiting for transfers between devices, ring_gather(): behind = lax.ppermute(behind, 'depth', backward)  1.91 us
    ppermute x1, waiting for transfers between devices, on_device(): received = lax.ppermute(for_partner, 'screen', [(0, 1), (1, 0)])  1.9 us
    select_n x1, other arithmetic, on_device(): return jnp.where(in_my_half[:, None, None], mine, received)  1.62 us
  transfers between devices with their start and end apart: 8, of which 7 were waited for; matrix products, arithmetic and copies ran while one was open for 3% of the time, Pallas kernels for 0%

profile of v13, /device:TPU:0, one launch (start us, length us, event | category | flops | bytes accessed | tf_op | source)
XLA Modules:
  0.0 59.3 jit_solution(11738089492665335691)
XLA Ops:
  1.3 14.4 %shard_map.73 = f32[128,4,128]{2,1,0:T(4,128)} custom-call(f32[1]{0:T(128)S(6)} %copy.24.absorb_ref, f32[3]{0:T(128)} %slope_ref.1, f32[3]{0:T(128)} %offset_ref.1, s32[1,1]{1,0:T(1,128)} %copy.23.shown_ref, f32[16384,128]{1,0:T(8,128)} %bitcast.15), custom_call_target="tpu_custom_call" | custom-call | tf_op jit(solution)/shard_map/pallas_call | solution.py:44
  15.7 1.0 %constant_dynamic-update-slice_fusion.9 = f32[1040,4,128]{2,1,0:T(4,128)S(1)} fusion(f32[128,4,128]{2,1,0:T(4,128)} %shard_map.73), kind=kLoop, calls=%fused_computation.27 | loop fusion | bytes 524288
  17.3 1.0 %pad_maximum_fusion.1 = f32[130,4,128]{2,1,0:T(4,128)S(1)} fusion(f32[1,4,128]{2,1,0:T(4,128)S(1)} %broadcast_in_dim.69, f32[1,4,128]{2,1,0:T(4,128)S(1)} %get-tuple-element.16, f32[128,4,128]{2,1,0:T(4,128)} %shard_map.73), kind=kLoop, calls=%fused_computation.9 | loop fusion | flops 133120 | bytes 532480 | tf_op jit(solution)/shard_map/concatenate | solution.py:120
  18.3 3.1 %collective-permute-start = (f32[130,4,128]{2,1,0:T(4,128)S(1)}, f32[130,4,128]{2,1,0:T(4,128)S(1)}, u32[]{:S(2)}, u32[]{:S(2)}) collective-permute-start(f32[130,4,128]{2,1,0:T(4,128)S(1)} %pad_maximum_fusion.1), channel_id=1, source_target_pairs={{0,4},{4,8},{8,12},{12,14},{14,10},{10,6},{6,2},{2,0},{1,5},{5,9},... | collective-permute-start | bytes 798728 | tf_op jit(solution)/shard_map/ppermute | solution.py:97
  21.4 0.0 collective-permute-start.1
  21.4 6.3 %collective-permute-done = f32[130,4,128]{2,1,0:T(4,128)S(1)} collective-permute-done((f32[130,4,128]{2,1,0:T(4,128)S(1)}, f32[130,4,128]{2,1,0:T(4,128)S(1)}, u32[]{:S(2)}, u32[]{:S(2)}) %collective-permute-start) | collective-permute-done | bytes 266272 | tf_op jit(solution)/shard_map/ppermute | solution.py:97
  27.8 1.8 %collective-permute-start.2 = (f32[130,4,128]{2,1,0:T(4,128)S(1)}, f32[130,4,128]{2,1,0:T(4,128)S(1)}, u32[]{:S(2)}, u32[]{:S(2)}) collective-permute-start(f32[130,4,128]{2,1,0:T(4,128)S(1)} %collective-permute-done), channel_id=1, source_target_pairs={{0,4},{4,8},{8,12},{12,14},{14,10},{10,6},{6,2},{2,0},{1,5},{5,9},... | collective-permute-start | bytes 798728 | tf_op jit(solution)/shard_map/ppermute | solution.py:97
  29.6 0.8 %fusion.8 = (pred[256]{0:T(512)(128)(4,1)S(1)}, s32[256]{0:T(256)S(1)}) fusion(s32[]{:T(128)S(6)} %axis_index.25, s32[4096]{0:T(1024)} %param.13, s32[]{:T(128)S(6)} %select_n.98), kind=kLoop, calls=%fused_computation.51 | loop fusion | flops 4096 | bytes 2312 | tf_op jit(solution)/shard_map/eq | solution.py:135
  30.3 0.8 %dynamic_slice.7 = s32[256]{0:T(256)S(1)} dynamic-slice(s32[4096]{0:T(1024)} %param.13, s32[]{:T(128)S(6)} %select_n.103), dynamic_slice_sizes={256} | dynamic-slice | bytes 2052 | tf_op jit(solution)/shard_map/dynamic_slice | solution.py:129
  31.1 0.0 collective-permute-done.1
  31.1 0.2 collective-permute-start.3
  31.3 4.0 %collective-permute-done.2 = f32[130,4,128]{2,1,0:T(4,128)S(1)} collective-permute-done((f32[130,4,128]{2,1,0:T(4,128)S(1)}, f32[130,4,128]{2,1,0:T(4,128)S(1)}, u32[]{:S(2)}, u32[]{:S(2)}) %collective-permute-start.2) | collective-permute-done | bytes 266272 | tf_op jit(solution)/shard_map/ppermute | solution.py:97
  35.3 1.5 %collective-permute-start.4 = (f32[130,4,128]{2,1,0:T(4,128)S(1)}, f32[130,4,128]{2,1,0:T(4,128)S(1)}, u32[]{:S(2)}, u32[]{:S(2)}) collective-permute-start(f32[130,4,128]{2,1,0:T(4,128)S(1)} %collective-permute-done.2), channel_id=1, source_target_pairs={{0,4},{4,8},{8,12},{12,14},{14,10},{10,6},{6,2},{2,0},{1,5},{5,9},... | collective-permute-start | bytes 798728 | tf_op jit(solution)/shard_map/ppermute | solution.py:97
  36.9 1.2 %collective-permute-done.3 = f32[130,4,128]{2,1,0:T(4,128)S(1)} collective-permute-done((f32[130,4,128]{2,1,0:T(4,128)S(1)}, f32[130,4,128]{2,1,0:T(4,128)S(1)}, u32[]{:S(2)}, u32[]{:S(2)}) %collective-permute-start.3) | collective-permute-done | bytes 266272 | tf_op jit(solution)/shard_map/ppermute | solution.py:100
  38.1 0.5 collective-permute-start.5
  38.7 3.3 %collective-permute-done.4 = f32[130,4,128]{2,1,0:T(4,128)S(1)} collective-permute-done((f32[130,4,128]{2,1,0:T(4,128)S(1)}, f32[130,4,128]{2,1,0:T(4,128)S(1)}, u32[]{:S(2)}, u32[]{:S(2)}) %collective-permute-start.4) | collective-permute-done | bytes 266272 | tf_op jit(solution)/shard_map/ppermute | solution.py:97
  42.0 1.7 %collective-permute-start.6 = (f32[130,4,128]{2,1,0:T(4,128)S(1)}, f32[130,4,128]{2,1,0:T(4,128)S(1)}, u32[]{:S(2)}, u32[]{:S(2)}) collective-permute-start(f32[130,4,128]{2,1,0:T(4,128)S(1)} %collective-permute-done.4), channel_id=1, source_target_pairs={{0,4},{4,8},{8,12},{12,14},{14,10},{10,6},{6,2},{2,0},{1,5},{5,9},... | collective-permute-start | bytes 798728 | tf_op jit(solution)/shard_map/ppermute | solution.py:97
  43.8 0.7 %collective-permute-done.5 = f32[130,4,128]{2,1,0:T(4,128)S(1)} collective-permute-done((f32[130,4,128]{2,1,0:T(4,128)S(1)}, f32[130,4,128]{2,1,0:T(4,128)S(1)}, u32[]{:S(2)}, u32[]{:S(2)}) %collective-permute-start.5) | collective-permute-done | bytes 266272 | tf_op jit(solution)/shard_map/ppermute | solution.py:100
  44.5 3.9 %collective-permute-done.6 = f32[130,4,128]{2,1,0:T(4,128)S(1)} collective-permute-done((f32[130,4,128]{2,1,0:T(4,128)S(1)}, f32[130,4,128]{2,1,0:T(4,128)S(1)}, u32[]{:S(2)}, u32[]{:S(2)}) %collective-permute-start.6) | collective-permute-done | bytes 266272 | tf_op jit(solution)/shard_map/ppermute | solution.py:97
  48.5 0.0 copy-start
  48.5 0.1 copy.12
  48.6 0.1 select_reduce_fusion.2
  48.7 0.1 fusion.9
  48.8 0.1 select_reduce_fusion.1
  48.9 2.1 %gather_fusion.1 = f32[512,4,128]{2,1,0:T(4,128)S(1)} fusion(f32[1040,4,128]{2,1,0:T(4,128)S(1)} %constant_dynamic-update-slice_fusion, s32[1024]{0:T(1024)S(1)} %pad_clamp_fusion), kind=kCustom, calls=%fused_computation.1 | custom fusion | bytes 2099200 | tf_op jit(solution)/shard_map/jit(_take)/gather | solution.py:77
  51.0 3.1 %gather_fusion = f32[512,4,128]{2,1,0:T(4,128)S(1)} fusion(f32[1040,4,128]{2,1,0:T(4,128)} %copy-done, s32[1024]{0:T(1024)S(1)} %pad_clamp_fusion.1), kind=kCustom, calls=%fused_computation | custom fusion | bytes 2099200 | tf_op jit(solution)/shard_map/jit(_take)/gather | solution.py:78
  54.1 0.9 %negate_exponential_fusion = (f32[512,1,128]{2,1,0:T(1,128)S(1)}, f32[512,1,128]{2,1,0:T(1,128)S(1)}) fusion(f32[512,4,128]{2,1,0:T(4,128)S(1)} %gather_fusion, f32[512,1,128]{2,1,0:T(1,128)S(1)} %bitcast.17, f32[512,4,128]{2,1,0:T(4,128)S(1)} %gather_fusion.1), kind=kLoop, calls=%fused_computation.13 | loop fusion | flops 262144 | bytes 1310720 | tf_op jit(solution)/shard_map/exp | solution.py:80
  55.0 0.4 fusion
  55.4 0.2 pad_maximum_fusion
  55.7 0.1 collective-permute-start.7
  55.7 1.9 %collective-permute-done.7 = f32[256,4,128]{2,1,0:T(4,128)S(1)} collective-permute-done((f32[256,4,128]{2,1,0:T(4,128)S(1)}, f32[256,4,128]{2,1,0:T(4,128)S(1)}, u32[]{:S(2)}, u32[]{:S(2)}) %collective-permute-start.7) | collective-permute-done | bytes 524320 | tf_op jit(solution)/shard_map/ppermute | solution.py:134
  57.6 1.6 %fusion.2 = f32[256,4,128]{2,1,0:T(4,128)} fusion(f32[256,4,128]{2,1,0:T(4,128)S(1)} %collective-permute-done.7, f32[512,3,128]{2,1,0:T(4,128)S(1)} %fusion, f32[512,1,128]{2,1,0:T(1,128)S(1)} %get-tuple-element.18, pred[256]{0:T(512)(128)(4,1)S(1)} %get-tuple-element.11), kind=kLoop, calls=%fused_computation.7 | loop fusion | flops 262144 | bytes 2097408 | tf_op jit(solution)/shard_map/jit(_where)/select_n | solution.py:136
  (22 shorter events, 0.4 us)
Async XLA Ops:
  18.3 9.4 %collective-permute-start = (f32[130,4,128]{2,1,0:T(4,128)S(1)}, f32[130,4,128]{2,1,0:T(4,128)S(1)}, u32[]{:S(2)}, u32[]{:S(2)}) collective-permute-start(f32[130,4,128]{2,1,0:T(4,128)S(1)} %pad_maximum_fusion.1), channel_id=1, source_target_pairs={{0,4},{4,8},{8,12},{12,14},{14,10},{10,6},{6,2},{2,0},{1,5},{5,9},... | collective-permute-start | bytes 798728 | tf_op jit(solution)/shard_map/ppermute | solution.py:97
  21.4 9.7 %collective-permute-start.1 = (f32[130,4,128]{2,1,0:T(4,128)S(1)}, f32[130,4,128]{2,1,0:T(4,128)S(1)}, u32[]{:S(2)}, u32[]{:S(2)}) collective-permute-start(f32[130,4,128]{2,1,0:T(4,128)S(1)} %pad_maximum_fusion.1), channel_id=1, source_target_pairs={{4,0},{8,4},{12,8},{14,12},{10,14},{6,10},{2,6},{0,2},{5,1},{9,5},... | collective-permute-start | bytes 798728 | tf_op jit(solution)/shard_map/ppermute | solution.py:100
  27.8 7.6 %collective-permute-start.2 = (f32[130,4,128]{2,1,0:T(4,128)S(1)}, f32[130,4,128]{2,1,0:T(4,128)S(1)}, u32[]{:S(2)}, u32[]{:S(2)}) collective-permute-start(f32[130,4,128]{2,1,0:T(4,128)S(1)} %collective-permute-done), channel_id=1, source_target_pairs={{0,4},{4,8},{8,12},{12,14},{14,10},{10,6},{6,2},{2,0},{1,5},{5,9},... | collective-permute-start | bytes 798728 | tf_op jit(solution)/shard_map/ppermute | solution.py:97
  31.1 7.0 %collective-permute-start.3 = (f32[130,4,128]{2,1,0:T(4,128)S(1)}, f32[130,4,128]{2,1,0:T(4,128)S(1)}, u32[]{:S(2)}, u32[]{:S(2)}) collective-permute-start(f32[130,4,128]{2,1,0:T(4,128)S(1)} %collective-permute-done.1), channel_id=1, source_target_pairs={{4,0},{8,4},{12,8},{14,12},{10,14},{6,10},{2,6},{0,2},{5,1},{9,5},... | collective-permute-start | bytes 798728 | tf_op jit(solution)/shard_map/ppermute | solution.py:100
  35.3 6.7 %collective-permute-start.4 = (f32[130,4,128]{2,1,0:T(4,128)S(1)}, f32[130,4,128]{2,1,0:T(4,128)S(1)}, u32[]{:S(2)}, u32[]{:S(2)}) collective-permute-start(f32[130,4,128]{2,1,0:T(4,128)S(1)} %collective-permute-done.2), channel_id=1, source_target_pairs={{0,4},{4,8},{8,12},{12,14},{14,10},{10,6},{6,2},{2,0},{1,5},{5,9},... | collective-permute-start | bytes 798728 | tf_op jit(solution)/shard_map/ppermute | solution.py:97
  38.1 6.4 %collective-permute-start.5 = (f32[130,4,128]{2,1,0:T(4,128)S(1)}, f32[130,4,128]{2,1,0:T(4,128)S(1)}, u32[]{:S(2)}, u32[]{:S(2)}) collective-permute-start(f32[130,4,128]{2,1,0:T(4,128)S(1)} %collective-permute-done.3), channel_id=1, source_target_pairs={{4,0},{8,4},{12,8},{14,12},{10,14},{6,10},{2,6},{0,2},{5,1},{9,5},... | collective-permute-start | bytes 798728 | tf_op jit(solution)/shard_map/ppermute | solution.py:100
  42.0 6.4 %collective-permute-start.6 = (f32[130,4,128]{2,1,0:T(4,128)S(1)}, f32[130,4,128]{2,1,0:T(4,128)S(1)}, u32[]{:S(2)}, u32[]{:S(2)}) collective-permute-start(f32[130,4,128]{2,1,0:T(4,128)S(1)} %collective-permute-done.4), channel_id=1, source_target_pairs={{0,4},{4,8},{8,12},{12,14},{14,10},{10,6},{6,2},{2,0},{1,5},{5,9},... | collective-permute-start | bytes 798728 | tf_op jit(solution)/shard_map/ppermute | solution.py:97
  48.5 2.5 %copy-start = (f32[1040,4,128]{2,1,0:T(4,128)}, f32[1040,4,128]{2,1,0:T(4,128)S(1)}, u32[]{:S(2)}) copy-start(f32[1040,4,128]{2,1,0:T(4,128)S(1)} %constant_dynamic-update-slice_fusion) | copy-start | bytes 6389764
  55.7 2.0 %collective-permute-start.7 = (f32[256,4,128]{2,1,0:T(4,128)S(1)}, f32[256,4,128]{2,1,0:T(4,128)S(1)}, u32[]{:S(2)}, u32[]{:S(2)}) collective-permute-start(f32[256,4,128]{2,1,0:T(4,128)S(1)} %pad_maximum_fusion), channel_id=1, source_target_pairs={{0,1},{1,0},{2,3},{3,2},{4,5},{5,4},{6,7},{7,6},{8,9},{9,8},{10,11... | collective-permute-start | bytes 1572872 | tf_op jit(solution)/shard_map/ppermute | solution.py:134

commit v14 on v13

--- a/solution.py
+++ b/solution.py
@@ -74,12 +74,33 @@
     zero_row = stride - 1
     back_idx = jnp.where(has_back, back_slot * stride + back_off, zero_row)
     front_idx = jnp.where(has_front, front_slot * stride + front_off, zero_row)
-    back_rows = jnp.take(flat, back_idx, axis=0, mode="clip")
-    front_rows = jnp.take(flat, front_idx, axis=0, mode="clip")
-    front_depth = front_rows[:, 3:4, :]
-    colours = front_rows[:, :3, :] + jnp.exp(-front_depth) * back_rows[:, :3, :]
-    opacity = 1.0 - jnp.exp(-(front_depth + back_rows[:, 3:4, :]))
-    return jnp.concatenate([colours, opacity], axis=1)
+    return back_idx, front_idx
+
+
+def blend_kernel(back_idx_ref, front_idx_ref, flat_ref, out_ref):
+    def one_row(row, carry):
+        back = flat_ref[back_idx_ref[row]]
+        front = flat_ref[front_idx_ref[row]]
+        front_depth = front[3:4, :]
+        out_ref[row, 0:3, :] = front[0:3, :] + jnp.exp(-front_depth) * back[0:3, :]
+        out_ref[row, 3:4, :] = 1.0 - jnp.exp(-(front_depth + back[3:4, :]))
+        return carry
+
+    lax.fori_loop(0, out_ref.shape[0], one_row, 0, unroll=8)
+
+
+def blend_rows(flat, back_idx, front_idx):
+    rows = back_idx.shape[0]
+    return pl.pallas_call(
+        blend_kernel,
+        grid_spec=pltpu.PrefetchScalarGridSpec(
+            num_scalar_prefetch=2,
+            grid=(1,),
+            in_specs=[pl.BlockSpec(flat.shape, lambda i, *_: (0, 0, 0))],
+            out_specs=pl.BlockSpec((rows,) + flat.shape[1:], lambda i, *_: (0, 0, 0)),
+        ),
+        out_shape=jax.ShapeDtypeStruct((rows,) + flat.shape[1:], flat.dtype),
+    )(back_idx, front_idx, flat)
 
 
 def ring_order(count):
@@ -127,10 +148,10 @@
     partner_owner = depth_index * screen_count + (1 - screen_index)
     wanted_self = lax.dynamic_slice_in_dim(tile_source, self_owner * owner_rows, owner_rows)
     wanted_partner = lax.dynamic_slice_in_dim(tile_source, partner_owner * owner_rows, owner_rows)
-    wanted = jnp.concatenate([wanted_self, wanted_partner])
-    rows = composite_rows(flat, starts, counts, brick_ids, stride, wanted % half_rows)
-    mine = rows[:owner_rows]
-    for_partner = rows[owner_rows:]
+    wanted = jnp.concatenate([wanted_partner, wanted_self])
+    back_idx, front_idx = composite_rows(flat, starts, counts, brick_ids, stride, wanted % half_rows)
+    for_partner = blend_rows(flat, back_idx[:owner_rows], front_idx[:owner_rows])
+    mine = blend_rows(flat, back_idx[owner_rows:], front_idx[owner_rows:])
     received = lax.ppermute(for_partner, "screen", [(0, 1), (1, 0)])
     in_my_half = (wanted_self // half_rows) == screen_index
     return jnp.where(in_my_half[:, None, None], mine, received)

time: 59.6 us -> 61.2 us (1.027)
  Pallas kernels: 14.4 us -> 22.6 us
  local copies, waits for them, and re-layouts: 7.28 us -> 3.55 us
  waiting for transfers between devices: 21.3 us -> 19.5 us
  other arithmetic: 5.27 us -> 4.29 us
    pallas_call x0 -> x2, Pallas kernels: none -> 8.22 us  [blend_rows(): pl.pallas_call(blend_kernel, grid_spec=pltpu.PrefetchScalarGridSpec(num_s...]
    gather x2 -> x0, local copies, waits for them, and re-layouts: 5.18 us -> none  [the longest x1 3.11 us: composite_rows(): front_rows = jnp.take(flat, front_idx, axis=0, mode='clip')]
    ppermute x1, waiting for transfers between devices: 1.9 us -> 0.01 us  [on_device(): received = lax.ppermute(for_partner, 'screen', [(0, 1), (1, 0)])]
    slice x0 -> x2, local copies, waits for them, and re-layouts: none -> 1.47 us  [the longest x1 0.88 us: on_device(): front_idx[:owner_rows]]
    exp x1 -> x0, other arithmetic: 0.85 us -> none  [composite_rows(): colours = front_rows[:, :3, :] + jnp.exp(-front_depth) * back_rows[:, :3, :]]
  transfers between devices with their start and end apart: 8 -> 8, of which waited for: 7 -> 6; matrix products, arithmetic and copies ran while one was open for 3% -> 3% of each run, Pallas kernels for 0% -> 7%
where the time goes in v14:
time: 61.2 us; the launch traced here: 60.7 us
  Pallas kernels  22.6 us (37%)
  waiting for transfers between devices  19.5 us (32%)
  starting transfers between devices  8.82 us (14%)
  other arithmetic  4.29 us (7%)
  local copies, waits for them, and re-layouts  3.55 us (6%)
  between operations  2.05 us (3%)
    ppermute x4, waiting for transfers between devices, ring_gather(): ahead = lax.ppermute(ahead, 'depth', forward)  17.5 us
    pallas_call x1, Pallas kernels, render_layers(): pl.pallas_call(render_kernel, grid=(brick_rows // block_rows,), in_specs=...  14.4 us
    pallas_call x2, Pallas kernels, blend_rows(): pl.pallas_call(blend_kernel, grid_spec=pltpu.PrefetchScalarGridSpec(num_s...  8.22 us
    ppermute x4, starting transfers between devices, ring_gather(): ahead = lax.ppermute(ahead, 'depth', forward)  8.03 us
    select_n x1, other arithmetic, on_device(): return jnp.where(in_my_half[:, None, None], mine, received)  2.17 us
    ppermute x3, waiting for transfers between devices, ring_gather(): behind = lax.ppermute(behind, 'depth', backward)  1.91 us
    unnamed x11, local copies, waits for them, and re-layouts  1.27 us
  transfers between devices with their start and end apart: 8, of which 6 were waited for; matrix products, arithmetic and copies ran while one was open for 3% of the time, Pallas kernels for 7%

profile of v14, /device:TPU:0, one launch (start us, length us, event | category | flops | bytes accessed | tf_op | source)
XLA Modules:
  0.0 60.7 jit_solution(18078421186206785491)
XLA Ops:
  1.3 14.4 %shard_map.73 = f32[128,4,128]{2,1,0:T(4,128)} custom-call(f32[1]{0:T(128)S(6)} %copy.22.absorb_ref, f32[3]{0:T(128)} %slope_ref.1, f32[3]{0:T(128)} %offset_ref.1, s32[1,1]{1,0:T(1,128)} %copy.21.shown_ref, f32[16384,128]{1,0:T(8,128)} %bitcast.14), custom_call_target="tpu_custom_call" | custom-call | tf_op jit(solution)/shard_map/pallas_call | solution.py:44
  15.7 1.0 %constant_dynamic-update-slice_fusion.9 = f32[1040,4,128]{2,1,0:T(4,128)S(1)} fusion(f32[128,4,128]{2,1,0:T(4,128)} %shard_map.73), kind=kLoop, calls=%fused_computation.15 | loop fusion | bytes 524288
  17.3 1.0 %pad_maximum_fusion = f32[130,4,128]{2,1,0:T(4,128)S(1)} fusion(f32[1,4,128]{2,1,0:T(4,128)S(1)} %broadcast_in_dim.68, f32[1,4,128]{2,1,0:T(4,128)S(1)} %get-tuple-element.16, f32[128,4,128]{2,1,0:T(4,128)} %shard_map.73), kind=kLoop, calls=%fused_computation | loop fusion | flops 133120 | bytes 532480 | tf_op jit(solution)/shard_map/concatenate | solution.py:141
  18.3 3.1 %collective-permute-start = (f32[130,4,128]{2,1,0:T(4,128)S(1)}, f32[130,4,128]{2,1,0:T(4,128)S(1)}, u32[]{:S(2)}, u32[]{:S(2)}) collective-permute-start(f32[130,4,128]{2,1,0:T(4,128)S(1)} %pad_maximum_fusion), channel_id=1, source_target_pairs={{0,4},{4,8},{8,12},{12,14},{14,10},{10,6},{6,2},{2,0},{1,5},{5,9},... | collective-permute-start | bytes 798728 | tf_op jit(solution)/shard_map/ppermute | solution.py:118
  21.4 0.0 collective-permute-start.1
  21.4 6.3 %collective-permute-done = f32[130,4,128]{2,1,0:T(4,128)S(1)} collective-permute-done((f32[130,4,128]{2,1,0:T(4,128)S(1)}, f32[130,4,128]{2,1,0:T(4,128)S(1)}, u32[]{:S(2)}, u32[]{:S(2)}) %collective-permute-start) | collective-permute-done | bytes 266272 | tf_op jit(solution)/shard_map/ppermute | solution.py:118
  27.8 1.8 %collective-permute-start.2 = (f32[130,4,128]{2,1,0:T(4,128)S(1)}, f32[130,4,128]{2,1,0:T(4,128)S(1)}, u32[]{:S(2)}, u32[]{:S(2)}) collective-permute-start(f32[130,4,128]{2,1,0:T(4,128)S(1)} %collective-permute-done), channel_id=1, source_target_pairs={{0,4},{4,8},{8,12},{12,14},{14,10},{10,6},{6,2},{2,0},{1,5},{5,9},... | collective-permute-start | bytes 798728 | tf_op jit(solution)/shard_map/ppermute | solution.py:118
  29.6 0.8 %fusion.4 = (pred[256]{0:T(512)(128)(4,1)S(1)}, s32[256]{0:T(256)S(1)}) fusion(s32[]{:T(128)S(6)} %axis_index.25, s32[4096]{0:T(1024)} %param.13, s32[]{:T(128)S(6)} %select_n.78), kind=kLoop, calls=%fused_computation.37 | loop fusion | flops 4096 | bytes 2312 | tf_op jit(solution)/shard_map/eq | solution.py:156
  30.3 0.8 %dynamic_slice.7 = s32[256]{0:T(256)S(1)} dynamic-slice(s32[4096]{0:T(1024)} %param.13, s32[]{:T(128)S(6)} %select_n.80), dynamic_slice_sizes={256} | dynamic-slice | bytes 2052 | tf_op jit(solution)/shard_map/dynamic_slice | solution.py:150
  31.1 0.0 collective-permute-done.1
  31.1 0.2 collective-permute-start.3
  31.3 4.0 %collective-permute-done.2 = f32[130,4,128]{2,1,0:T(4,128)S(1)} collective-permute-done((f32[130,4,128]{2,1,0:T(4,128)S(1)}, f32[130,4,128]{2,1,0:T(4,128)S(1)}, u32[]{:S(2)}, u32[]{:S(2)}) %collective-permute-start.2) | collective-permute-done | bytes 266272 | tf_op jit(solution)/shard_map/ppermute | solution.py:118
  35.3 1.5 %collective-permute-start.4 = (f32[130,4,128]{2,1,0:T(4,128)S(1)}, f32[130,4,128]{2,1,0:T(4,128)S(1)}, u32[]{:S(2)}, u32[]{:S(2)}) collective-permute-start(f32[130,4,128]{2,1,0:T(4,128)S(1)} %collective-permute-done.2), channel_id=1, source_target_pairs={{0,4},{4,8},{8,12},{12,14},{14,10},{10,6},{6,2},{2,0},{1,5},{5,9},... | collective-permute-start | bytes 798728 | tf_op jit(solution)/shard_map/ppermute | solution.py:118
  36.9 1.2 %collective-permute-done.3 = f32[130,4,128]{2,1,0:T(4,128)S(1)} collective-permute-done((f32[130,4,128]{2,1,0:T(4,128)S(1)}, f32[130,4,128]{2,1,0:T(4,128)S(1)}, u32[]{:S(2)}, u32[]{:S(2)}) %collective-permute-start.3) | collective-permute-done | bytes 266272 | tf_op jit(solution)/shard_map/ppermute | solution.py:121
  38.1 0.5 collective-permute-start.5
  38.7 3.3 %collective-permute-done.4 = f32[130,4,128]{2,1,0:T(4,128)S(1)} collective-permute-done((f32[130,4,128]{2,1,0:T(4,128)S(1)}, f32[130,4,128]{2,1,0:T(4,128)S(1)}, u32[]{:S(2)}, u32[]{:S(2)}) %collective-permute-start.4) | collective-permute-done | bytes 266272 | tf_op jit(solution)/shard_map/ppermute | solution.py:118
  42.0 1.7 %collective-permute-start.6 = (f32[130,4,128]{2,1,0:T(4,128)S(1)}, f32[130,4,128]{2,1,0:T(4,128)S(1)}, u32[]{:S(2)}, u32[]{:S(2)}) collective-permute-start(f32[130,4,128]{2,1,0:T(4,128)S(1)} %collective-permute-done.4), channel_id=1, source_target_pairs={{0,4},{4,8},{8,12},{12,14},{14,10},{10,6},{6,2},{2,0},{1,5},{5,9},... | collective-permute-start | bytes 798728 | tf_op jit(solution)/shard_map/ppermute | solution.py:118
  43.8 0.7 %collective-permute-done.5 = f32[130,4,128]{2,1,0:T(4,128)S(1)} collective-permute-done((f32[130,4,128]{2,1,0:T(4,128)S(1)}, f32[130,4,128]{2,1,0:T(4,128)S(1)}, u32[]{:S(2)}, u32[]{:S(2)}) %collective-permute-start.5) | collective-permute-done | bytes 266272 | tf_op jit(solution)/shard_map/ppermute | solution.py:121
  44.5 3.9 %collective-permute-done.6 = f32[130,4,128]{2,1,0:T(4,128)S(1)} collective-permute-done((f32[130,4,128]{2,1,0:T(4,128)S(1)}, f32[130,4,128]{2,1,0:T(4,128)S(1)}, u32[]{:S(2)}, u32[]{:S(2)}) %collective-permute-start.6) | collective-permute-done | bytes 266272 | tf_op jit(solution)/shard_map/ppermute | solution.py:118
  48.5 0.0 copy-start
  48.5 0.1 copy.10
  48.6 0.1 select_reduce_fusion.2
  48.7 0.1 fusion.5
  48.8 0.1 select_reduce_fusion
  48.9 0.9 %fusion.6 = (s32[256]{0:T(256)}, s32[256]{0:T(256)}) fusion(s32[512]{0:T(512)S(1)} %add_select_fusion.1), kind=kLoop, calls=%fused_computation.44 | loop fusion | bytes 4096 | tf_op jit(solution)/shard_map/slice | solution.py:153
  49.7 0.6 fusion.7
  50.3 0.0 copy-done
  50.3 4.1 %shard_map.75 = f32[256,4,128]{2,1,0:T(4,128)} custom-call(s32[256]{0:T(256)} %get-tuple-element.19.back_idx_ref, s32[256]{0:T(256)} %get-tuple-element.17.front_idx_ref, f32[1040,4,128]{2,1,0:T(4,128)} %copy-done), custom_call_target="tpu_custom_call" | custom-call | tf_op jit(solution)/shard_map/pallas_call | solution.py:94
  54.5 0.0 collective-permute-start.7
  54.5 4.1 %shard_map.74 = f32[256,4,128]{2,1,0:T(4,128)} custom-call(s32[256]{0:T(256)} %get-tuple-element.20.back_idx_ref, s32[256]{0:T(256)} %get-tuple-element.18.front_idx_ref, f32[1040,4,128]{2,1,0:T(4,128)} %copy-done), custom_call_target="tpu_custom_call" | custom-call | tf_op jit(solution)/shard_map/pallas_call | solution.py:94
  58.6 0.0 collective-permute-done.7
  58.6 2.2 %broadcast_select_fusion = f32[256,4,128]{2,1,0:T(4,128)} fusion(f32[256,4,128]{2,1,0:T(4,128)} %shard_map.74, f32[256,4,128]{2,1,0:T(4,128)S(1)} %collective-permute-done.7, pred[256]{0:T(512)(128)(4,1)S(1)} %get-tuple-element.11), kind=kLoop, calls=%fused_computation.1 | loop fusion | flops 131072 | bytes 1573120 | tf_op jit(solution)/shard_map/jit(_where)/select_n | solution.py:157
  (18 shorter events, 0.3 us)
Async XLA Ops:
  18.3 9.4 %collective-permute-start = (f32[130,4,128]{2,1,0:T(4,128)S(1)}, f32[130,4,128]{2,1,0:T(4,128)S(1)}, u32[]{:S(2)}, u32[]{:S(2)}) collective-permute-start(f32[130,4,128]{2,1,0:T(4,128)S(1)} %pad_maximum_fusion), channel_id=1, source_target_pairs={{0,4},{4,8},{8,12},{12,14},{14,10},{10,6},{6,2},{2,0},{1,5},{5,9},... | collective-permute-start | bytes 798728 | tf_op jit(solution)/shard_map/ppermute | solution.py:118
  21.4 9.7 %collective-permute-start.1 = (f32[130,4,128]{2,1,0:T(4,128)S(1)}, f32[130,4,128]{2,1,0:T(4,128)S(1)}, u32[]{:S(2)}, u32[]{:S(2)}) collective-permute-start(f32[130,4,128]{2,1,0:T(4,128)S(1)} %pad_maximum_fusion), channel_id=1, source_target_pairs={{4,0},{8,4},{12,8},{14,12},{10,14},{6,10},{2,6},{0,2},{5,1},{9,5},... | collective-permute-start | bytes 798728 | tf_op jit(solution)/shard_map/ppermute | solution.py:121
  27.8 7.6 %collective-permute-start.2 = (f32[130,4,128]{2,1,0:T(4,128)S(1)}, f32[130,4,128]{2,1,0:T(4,128)S(1)}, u32[]{:S(2)}, u32[]{:S(2)}) collective-permute-start(f32[130,4,128]{2,1,0:T(4,128)S(1)} %collective-permute-done), channel_id=1, source_target_pairs={{0,4},{4,8},{8,12},{12,14},{14,10},{10,6},{6,2},{2,0},{1,5},{5,9},... | collective-permute-start | bytes 798728 | tf_op jit(solution)/shard_map/ppermute | solution.py:118
  31.1 7.0 %collective-permute-start.3 = (f32[130,4,128]{2,1,0:T(4,128)S(1)}, f32[130,4,128]{2,1,0:T(4,128)S(1)}, u32[]{:S(2)}, u32[]{:S(2)}) collective-permute-start(f32[130,4,128]{2,1,0:T(4,128)S(1)} %collective-permute-done.1), channel_id=1, source_target_pairs={{4,0},{8,4},{12,8},{14,12},{10,14},{6,10},{2,6},{0,2},{5,1},{9,5},... | collective-permute-start | bytes 798728 | tf_op jit(solution)/shard_map/ppermute | solution.py:121
  35.3 6.7 %collective-permute-start.4 = (f32[130,4,128]{2,1,0:T(4,128)S(1)}, f32[130,4,128]{2,1,0:T(4,128)S(1)}, u32[]{:S(2)}, u32[]{:S(2)}) collective-permute-start(f32[130,4,128]{2,1,0:T(4,128)S(1)} %collective-permute-done.2), channel_id=1, source_target_pairs={{0,4},{4,8},{8,12},{12,14},{14,10},{10,6},{6,2},{2,0},{1,5},{5,9},... | collective-permute-start | bytes 798728 | tf_op jit(solution)/shard_map/ppermute | solution.py:118
  38.1 6.4 %collective-permute-start.5 = (f32[130,4,128]{2,1,0:T(4,128)S(1)}, f32[130,4,128]{2,1,0:T(4,128)S(1)}, u32[]{:S(2)}, u32[]{:S(2)}) collective-permute-start(f32[130,4,128]{2,1,0:T(4,128)S(1)} %collective-permute-done.3), channel_id=1, source_target_pairs={{4,0},{8,4},{12,8},{14,12},{10,14},{6,10},{2,6},{0,2},{5,1},{9,5},... | collective-permute-start | bytes 798728 | tf_op jit(solution)/shard_map/ppermute | solution.py:121
  42.0 6.4 %collective-permute-start.6 = (f32[130,4,128]{2,1,0:T(4,128)S(1)}, f32[130,4,128]{2,1,0:T(4,128)S(1)}, u32[]{:S(2)}, u32[]{:S(2)}) collective-permute-start(f32[130,4,128]{2,1,0:T(4,128)S(1)} %collective-permute-done.4), channel_id=1, source_target_pairs={{0,4},{4,8},{8,12},{12,14},{14,10},{10,6},{6,2},{2,0},{1,5},{5,9},... | collective-permute-start | bytes 798728 | tf_op jit(solution)/shard_map/ppermute | solution.py:118
  48.5 1.9 %copy-start = (f32[1040,4,128]{2,1,0:T(4,128)}, f32[1040,4,128]{2,1,0:T(4,128)S(1)}, u32[]{:S(2)}) copy-start(f32[1040,4,128]{2,1,0:T(4,128)S(1)} %constant_dynamic-update-slice_fusion.flat_ref) | copy-start | bytes 6389764
  54.5 4.1 %collective-permute-start.7 = (f32[256,4,128]{2,1,0:T(4,128)}, f32[256,4,128]{2,1,0:T(4,128)S(1)}, u32[]{:S(2)}, u32[]{:S(2)}) collective-permute-start(f32[256,4,128]{2,1,0:T(4,128)} %shard_map.75), channel_id=1, source_target_pairs={{0,1},{1,0},{2,3},{3,2},{4,5},{5,4},{6,7},{7,6},{8,9},{9,8},{10,11... | collective-permute-start | bytes 1572872 | tf_op jit(solution)/shard_map/ppermute | solution.py:155

commit v15 on v13

--- a/solution.py
+++ b/solution.py
@@ -127,11 +127,9 @@
     partner_owner = depth_index * screen_count + (1 - screen_index)
     wanted_self = lax.dynamic_slice_in_dim(tile_source, self_owner * owner_rows, owner_rows)
     wanted_partner = lax.dynamic_slice_in_dim(tile_source, partner_owner * owner_rows, owner_rows)
-    wanted = jnp.concatenate([wanted_self, wanted_partner])
-    rows = composite_rows(flat, starts, counts, brick_ids, stride, wanted % half_rows)
-    mine = rows[:owner_rows]
-    for_partner = rows[owner_rows:]
+    for_partner = composite_rows(flat, starts, counts, brick_ids, stride, wanted_partner % half_rows)
     received = lax.ppermute(for_partner, "screen", [(0, 1), (1, 0)])
+    mine = composite_rows(flat, starts, counts, brick_ids, stride, wanted_self % half_rows)
     in_my_half = (wanted_self // half_rows) == screen_index
     return jnp.where(in_my_half[:, None, None], mine, received)
 

time: 59.6 us -> 61.1 us (1.025)
  local copies, waits for them, and re-layouts: 7.28 us -> 8.54 us
  other arithmetic: 5.27 us -> 6.1 us
  waiting for transfers between devices: 21.3 us -> 20.6 us
    gather x1 -> x2, local copies, waits for them, and re-layouts: 2.07 us -> 3.61 us  [composite_rows(): back_rows = jnp.take(flat, back_idx, axis=0, mode='clip')]
    ppermute x3, waiting for transfers between devices: 1.91 us -> 0.65 us  [ring_gather(): behind = lax.ppermute(behind, 'depth', backward)]
    ppermute x4, waiting for transfers between devices: 17.5 us -> 18.7 us  [ring_gather(): ahead = lax.ppermute(ahead, 'depth', forward)]
    select_n x1, other arithmetic: 0.01 us -> 0.84 us  [on_device(): wanted_partner % half_rows]
    dynamic_slice x1 -> x0, local copies, waits for them, and re-layouts: 0.76 us -> none  [on_device(): lax.dynamic_slice_in_dim(tile_source, partner_owner * owner_rows, owner_r...]
    ppermute x1, waiting for transfers between devices: 1.9 us -> 1.27 us  [on_device(): received = lax.ppermute(for_partner, 'screen', [(0, 1), (1, 0)])]
    gather x1 -> x2, local copies, waits for them, and re-layouts: 3.11 us -> 3.61 us  [composite_rows(): front_rows = jnp.take(flat, front_idx, axis=0, mode='clip')]
  transfers between devices with their start and end apart: 8 -> 8, of which waited for: 7 -> 7; matrix products, arithmetic and copies ran while one was open for 3% -> 4% of each run, Pallas kernels for 0% -> 0%
where the time goes in v15:
time: 61.1 us; the launch traced here: 60.7 us
  waiting for transfers between devices  20.6 us (34%)
  Pallas kernels  14.4 us (24%)
  starting transfers between devices  8.94 us (15%)
  local copies, waits for them, and re-layouts  8.54 us (14%)
  other arithmetic  6.1 us (10%)
  between operations  2.18 us (4%)
    ppermute x4, waiting for transfers between devices, ring_gather(): ahead = lax.ppermute(ahead, 'depth', forward)  18.7 us
    pallas_call x1, Pallas kernels, render_layers(): pl.pallas_call(render_kernel, grid=(brick_rows // block_rows,), in_specs=...  14.4 us
    ppermute x4, starting transfers between devices, ring_gather(): ahead = lax.ppermute(ahead, 'depth', forward)  8.03 us
    gather x2, local copies, waits for them, and re-layouts, composite_rows(): front_rows = jnp.take(flat, front_idx, axis=0, mode='clip')  3.61 us
    gather x2, local copies, waits for them, and re-layouts, composite_rows(): back_rows = jnp.take(flat, back_idx, axis=0, mode='clip')  3.61 us
    select_n x1, other arithmetic, on_device(): return jnp.where(in_my_half[:, None, None], mine, received)  1.62 us
    ppermute x1, waiting for transfers between devices, on_device(): received = lax.ppermute(for_partner, 'screen', [(0, 1), (1, 0)])  1.27 us
    unnamed x11, local copies, waits for them, and re-layouts  1.27 us
  transfers between devices with their start and end apart: 8, of which 7 were waited for; matrix products, arithmetic and copies ran while one was open for 4% of the time, Pallas kernels for 0%

profile of v15, /device:TPU:0, one launch (start us, length us, event | category | flops | bytes accessed | tf_op | source)
XLA Modules:
  0.0 60.7 jit_solution(12593893961959159324)
XLA Ops:
  1.3 14.4 %shard_map.73 = f32[128,4,128]{2,1,0:T(4,128)} custom-call(f32[1]{0:T(128)S(6)} %copy.25.absorb_ref, f32[3]{0:T(128)} %slope_ref.1, f32[3]{0:T(128)} %offset_ref.1, s32[1,1]{1,0:T(1,128)} %copy.24.shown_ref, f32[16384,128]{1,0:T(8,128)} %bitcast.16), custom_call_target="tpu_custom_call" | custom-call | tf_op jit(solution)/shard_map/pallas_call | solution.py:44
  15.7 1.0 %constant_dynamic-update-slice_fusion.9 = f32[1040,4,128]{2,1,0:T(4,128)S(1)} fusion(f32[128,4,128]{2,1,0:T(4,128)} %shard_map.73), kind=kLoop, calls=%fused_computation.28 | loop fusion | bytes 524288
  17.3 1.0 %pad_maximum_fusion.1 = f32[130,4,128]{2,1,0:T(4,128)S(1)} fusion(f32[1,4,128]{2,1,0:T(4,128)S(1)} %broadcast_in_dim.98, f32[1,4,128]{2,1,0:T(4,128)S(1)} %get-tuple-element.23, f32[128,4,128]{2,1,0:T(4,128)} %shard_map.73), kind=kLoop, calls=%fused_computation.10 | loop fusion | flops 133120 | bytes 532480 | tf_op jit(solution)/shard_map/concatenate | solution.py:120
  18.3 3.1 %collective-permute-start = (f32[130,4,128]{2,1,0:T(4,128)S(1)}, f32[130,4,128]{2,1,0:T(4,128)S(1)}, u32[]{:S(2)}, u32[]{:S(2)}) collective-permute-start(f32[130,4,128]{2,1,0:T(4,128)S(1)} %pad_maximum_fusion.1), channel_id=1, source_target_pairs={{0,4},{4,8},{8,12},{12,14},{14,10},{10,6},{6,2},{2,0},{1,5},{5,9},... | collective-permute-start | bytes 798728 | tf_op jit(solution)/shard_map/ppermute | solution.py:97
  21.4 6.3 %collective-permute-done = f32[130,4,128]{2,1,0:T(4,128)S(1)} collective-permute-done((f32[130,4,128]{2,1,0:T(4,128)S(1)}, f32[130,4,128]{2,1,0:T(4,128)S(1)}, u32[]{:S(2)}, u32[]{:S(2)}) %collective-permute-start) | collective-permute-done | bytes 266272 | tf_op jit(solution)/shard_map/ppermute | solution.py:97
  27.8 1.8 %collective-permute-start.2 = (f32[130,4,128]{2,1,0:T(4,128)S(1)}, f32[130,4,128]{2,1,0:T(4,128)S(1)}, u32[]{:S(2)}, u32[]{:S(2)}) collective-permute-start(f32[130,4,128]{2,1,0:T(4,128)S(1)} %collective-permute-done), channel_id=1, source_target_pairs={{0,4},{4,8},{8,12},{12,14},{14,10},{10,6},{6,2},{2,0},{1,5},{5,9},... | collective-permute-start | bytes 798728 | tf_op jit(solution)/shard_map/ppermute | solution.py:97
  29.6 0.8 %and_select_fusion = (s32[256]{0:T(256)S(1)}, s32[256]{0:T(256)S(1)}) fusion(s32[4096]{0:T(1024)} %param.13, s32[]{:T(128)S(6)} %select_n.154, s32[]{:T(128)S(6)} %select_n.139), kind=kLoop, calls=%fused_computation.61 | loop fusion | flops 5632 | bytes 4104 | tf_op jit(solution)/shard_map/jit(remainder)/select_n | solution.py:130
  30.4 0.3 collective-permute-start.3
  30.7 0.8 %fusion.11 = pred[256]{0:T(512)(128)(4,1)S(1)} fusion(s32[]{:T(128)S(6)} %axis_index.25, s32[4096]{0:T(1024)} %param.13, s32[]{:T(128)S(6)} %select_n.139), kind=kLoop, calls=%fused_computation.72 | loop fusion | flops 4096 | bytes 1288 | tf_op jit(solution)/shard_map/eq | solution.py:133
  31.5 3.9 %collective-permute-done.2 = f32[130,4,128]{2,1,0:T(4,128)S(1)} collective-permute-done((f32[130,4,128]{2,1,0:T(4,128)S(1)}, f32[130,4,128]{2,1,0:T(4,128)S(1)}, u32[]{:S(2)}, u32[]{:S(2)}) %collective-permute-start.2) | collective-permute-done | bytes 266272 | tf_op jit(solution)/shard_map/ppermute | solution.py:97
  35.3 1.5 %collective-permute-start.4 = (f32[130,4,128]{2,1,0:T(4,128)S(1)}, f32[130,4,128]{2,1,0:T(4,128)S(1)}, u32[]{:S(2)}, u32[]{:S(2)}) collective-permute-start(f32[130,4,128]{2,1,0:T(4,128)S(1)} %collective-permute-done.2), channel_id=1, source_target_pairs={{0,4},{4,8},{8,12},{12,14},{14,10},{10,6},{6,2},{2,0},{1,5},{5,9},... | collective-permute-start | bytes 798728 | tf_op jit(solution)/shard_map/ppermute | solution.py:97
  36.9 0.5 collective-permute-done.3
  37.4 0.5 collective-permute-start.5
  38.0 4.0 %collective-permute-done.4 = f32[130,4,128]{2,1,0:T(4,128)S(1)} collective-permute-done((f32[130,4,128]{2,1,0:T(4,128)S(1)}, f32[130,4,128]{2,1,0:T(4,128)S(1)}, u32[]{:S(2)}, u32[]{:S(2)}) %collective-permute-start.4) | collective-permute-done | bytes 266272 | tf_op jit(solution)/shard_map/ppermute | solution.py:97
  42.0 1.7 %collective-permute-start.6 = (f32[130,4,128]{2,1,0:T(4,128)S(1)}, f32[130,4,128]{2,1,0:T(4,128)S(1)}, u32[]{:S(2)}, u32[]{:S(2)}) collective-permute-start(f32[130,4,128]{2,1,0:T(4,128)S(1)} %collective-permute-done.4), channel_id=1, source_target_pairs={{0,4},{4,8},{8,12},{12,14},{14,10},{10,6},{6,2},{2,0},{1,5},{5,9},... | collective-permute-start | bytes 798728 | tf_op jit(solution)/shard_map/ppermute | solution.py:97
  43.8 0.1 collective-permute-done.5
  43.9 4.5 %collective-permute-done.6 = f32[130,4,128]{2,1,0:T(4,128)S(1)} collective-permute-done((f32[130,4,128]{2,1,0:T(4,128)S(1)}, f32[130,4,128]{2,1,0:T(4,128)S(1)}, u32[]{:S(2)}, u32[]{:S(2)}) %collective-permute-start.6) | collective-permute-done | bytes 266272 | tf_op jit(solution)/shard_map/ppermute | solution.py:97
  48.5 0.1 copy.13
  48.6 0.1 select_reduce_fusion.5
  48.7 0.1 fusion.12
  48.8 0.1 select_reduce_fusion.4
  48.9 1.0 %gather_fusion.1 = f32[256,4,128]{2,1,0:T(4,128)S(1)} fusion(f32[1040,4,128]{2,1,0:T(4,128)S(1)} %constant_dynamic-update-slice_fusion, s32[1024]{0:T(1024)S(1)} %pad_clamp_fusion.2), kind=kCustom, calls=%fused_computation.1 | custom fusion | bytes 1049600 | tf_op jit(solution)/shard_map/jit(_take)/gather | solution.py:77
  49.9 1.0 %gather_fusion = f32[256,4,128]{2,1,0:T(4,128)S(1)} fusion(f32[1040,4,128]{2,1,0:T(4,128)S(1)} %constant_dynamic-update-slice_fusion, s32[1024]{0:T(1024)S(1)} %pad_clamp_fusion.3), kind=kCustom, calls=%fused_computation | custom fusion | bytes 1049600 | tf_op jit(solution)/shard_map/jit(_take)/gather | solution.py:78
  51.0 2.6 %gather_fusion.3 = f32[256,4,128]{2,1,0:T(4,128)S(1)} fusion(f32[1040,4,128]{2,1,0:T(4,128)} %copy-done, s32[1024]{0:T(1024)S(1)} %pad_clamp_fusion), kind=kCustom, calls=%fused_computation.3 | custom fusion | bytes 1049600 | tf_op jit(solution)/shard_map/jit(_take)/gather | solution.py:77
  53.6 2.6 %gather_fusion.2 = f32[256,4,128]{2,1,0:T(4,128)S(1)} fusion(f32[1040,4,128]{2,1,0:T(4,128)} %copy-done, s32[1024]{0:T(1024)S(1)} %pad_clamp_fusion.1), kind=kCustom, calls=%fused_computation.2 | custom fusion | bytes 1049600 | tf_op jit(solution)/shard_map/jit(_take)/gather | solution.py:78
  56.3 0.4 negate_exponential_fusion
  56.7 0.2 fusion
  56.9 0.2 pad_maximum_fusion
  57.2 0.4 negate_exponential_fusion.1
  57.6 0.2 fusion.1
  57.8 1.3 %collective-permute-done.7 = f32[256,4,128]{2,1,0:T(4,128)S(1)} collective-permute-done((f32[256,4,128]{2,1,0:T(4,128)S(1)}, f32[256,4,128]{2,1,0:T(4,128)S(1)}, u32[]{:S(2)}, u32[]{:S(2)}) %collective-permute-start.7) | collective-permute-done | bytes 524320 | tf_op jit(solution)/shard_map/ppermute | solution.py:131
  59.1 1.6 %maximum_select_fusion = f32[256,4,128]{2,1,0:T(4,128)} fusion(f32[256,4,128]{2,1,0:T(4,128)S(1)} %collective-permute-done.7, f32[256,1,128]{2,1,0:T(1,128)S(1)} %get-tuple-element.25, f32[256,3,128]{2,1,0:T(4,128)S(1)} %fusion.1, pred[256]{0:T(512)(128)(4,1)S(1)} %fusion.11), kind=kLoop, calls=%fused_computation.8 | loop fusion | flops 262144 | bytes 1573120 | tf_op jit(solution)/shard_map/jit(_where)/select_n | solution.py:134
  (31 shorter events, 0.5 us)
Async XLA Ops:
  18.3 9.4 %collective-permute-start = (f32[130,4,128]{2,1,0:T(4,128)S(1)}, f32[130,4,128]{2,1,0:T(4,128)S(1)}, u32[]{:S(2)}, u32[]{:S(2)}) collective-permute-start(f32[130,4,128]{2,1,0:T(4,128)S(1)} %pad_maximum_fusion.1), channel_id=1, source_target_pairs={{0,4},{4,8},{8,12},{12,14},{14,10},{10,6},{6,2},{2,0},{1,5},{5,9},... | collective-permute-start | bytes 798728 | tf_op jit(solution)/shard_map/ppermute | solution.py:97
  21.4 9.0 %collective-permute-start.1 = (f32[130,4,128]{2,1,0:T(4,128)S(1)}, f32[130,4,128]{2,1,0:T(4,128)S(1)}, u32[]{:S(2)}, u32[]{:S(2)}) collective-permute-start(f32[130,4,128]{2,1,0:T(4,128)S(1)} %pad_maximum_fusion.1), channel_id=1, source_target_pairs={{4,0},{8,4},{12,8},{14,12},{10,14},{6,10},{2,6},{0,2},{5,1},{9,5},... | collective-permute-start | bytes 798728 | tf_op jit(solution)/shard_map/ppermute | solution.py:100
  27.8 7.6 %collective-permute-start.2 = (f32[130,4,128]{2,1,0:T(4,128)S(1)}, f32[130,4,128]{2,1,0:T(4,128)S(1)}, u32[]{:S(2)}, u32[]{:S(2)}) collective-permute-start(f32[130,4,128]{2,1,0:T(4,128)S(1)} %collective-permute-done), channel_id=1, source_target_pairs={{0,4},{4,8},{8,12},{12,14},{14,10},{10,6},{6,2},{2,0},{1,5},{5,9},... | collective-permute-start | bytes 798728 | tf_op jit(solution)/shard_map/ppermute | solution.py:97
  30.4 7.0 %collective-permute-start.3 = (f32[130,4,128]{2,1,0:T(4,128)S(1)}, f32[130,4,128]{2,1,0:T(4,128)S(1)}, u32[]{:S(2)}, u32[]{:S(2)}) collective-permute-start(f32[130,4,128]{2,1,0:T(4,128)S(1)} %collective-permute-done.1), channel_id=1, source_target_pairs={{4,0},{8,4},{12,8},{14,12},{10,14},{6,10},{2,6},{0,2},{5,1},{9,5},... | collective-permute-start | bytes 798728 | tf_op jit(solution)/shard_map/ppermute | solution.py:100
  35.3 6.7 %collective-permute-start.4 = (f32[130,4,128]{2,1,0:T(4,128)S(1)}, f32[130,4,128]{2,1,0:T(4,128)S(1)}, u32[]{:S(2)}, u32[]{:S(2)}) collective-permute-start(f32[130,4,128]{2,1,0:T(4,128)S(1)} %collective-permute-done.2), channel_id=1, source_target_pairs={{0,4},{4,8},{8,12},{12,14},{14,10},{10,6},{6,2},{2,0},{1,5},{5,9},... | collective-permute-start | bytes 798728 | tf_op jit(solution)/shard_map/ppermute | solution.py:97
  37.4 6.4 %collective-permute-start.5 = (f32[130,4,128]{2,1,0:T(4,128)S(1)}, f32[130,4,128]{2,1,0:T(4,128)S(1)}, u32[]{:S(2)}, u32[]{:S(2)}) collective-permute-start(f32[130,4,128]{2,1,0:T(4,128)S(1)} %collective-permute-done.3), channel_id=1, source_target_pairs={{4,0},{8,4},{12,8},{14,12},{10,14},{6,10},{2,6},{0,2},{5,1},{9,5},... | collective-permute-start | bytes 798728 | tf_op jit(solution)/shard_map/ppermute | solution.py:100
  42.0 6.4 %collective-permute-start.6 = (f32[130,4,128]{2,1,0:T(4,128)S(1)}, f32[130,4,128]{2,1,0:T(4,128)S(1)}, u32[]{:S(2)}, u32[]{:S(2)}) collective-permute-start(f32[130,4,128]{2,1,0:T(4,128)S(1)} %collective-permute-done.4), channel_id=1, source_target_pairs={{0,4},{4,8},{8,12},{12,14},{14,10},{10,6},{6,2},{2,0},{1,5},{5,9},... | collective-permute-start | bytes 798728 | tf_op jit(solution)/shard_map/ppermute | solution.py:97
  48.5 2.5 %copy-start = (f32[1040,4,128]{2,1,0:T(4,128)}, f32[1040,4,128]{2,1,0:T(4,128)S(1)}, u32[]{:S(2)}) copy-start(f32[1040,4,128]{2,1,0:T(4,128)S(1)} %constant_dynamic-update-slice_fusion) | copy-start | bytes 6389764
  57.1 2.0 %collective-permute-start.7 = (f32[256,4,128]{2,1,0:T(4,128)S(1)}, f32[256,4,128]{2,1,0:T(4,128)S(1)}, u32[]{:S(2)}, u32[]{:S(2)}) collective-permute-start(f32[256,4,128]{2,1,0:T(4,128)S(1)} %pad_maximum_fusion), channel_id=1, source_target_pairs={{0,1},{1,0},{2,3},{3,2},{4,5},{5,4},{6,7},{7,6},{8,9},{9,8},{10,11... | collective-permute-start | bytes 1572872 | tf_op jit(solution)/shard_map/ppermute | solution.py:131

commit v16 on v13

--- a/solution.py
+++ b/solution.py
@@ -93,12 +93,16 @@
     slots = [own]
     ahead = own
     behind = own
-    for step in range(1, count // 2 + 1):
+    for step in range(1, (count + 1) // 2):
         ahead = lax.ppermute(ahead, "depth", forward)
-        slots.append(ahead)
-        if 2 * step < count:
-            behind = lax.ppermute(behind, "depth", backward)
-            slots.append(behind)
+        behind = lax.ppermute(behind, "depth", backward)
+        slots += [ahead, behind]
+    if count % 2 == 0 and count > 1:
+        middle = own.shape[0] // 2
+        slots.append(jnp.concatenate([
+            lax.ppermute(ahead[:middle], "depth", forward),
+            lax.ppermute(behind[middle:], "depth", backward),
+        ], axis=0))
     return jnp.concatenate(slots, axis=0)
 
 

time: 59.6 us -> 59.9 us (level)
    ppermute x0 -> x2, waiting for transfers between devices: none -> 4.47 us  [the longest x1 2.81 us: ring_gather(): lax.ppermute(ahead[:middle], 'depth', forward)]
    ppermute x4 -> x3, waiting for transfers between devices: 17.5 us -> 14.8 us  [ring_gather(): ahead = lax.ppermute(ahead, 'depth', forward)]
    ppermute x0 -> x2, starting transfers between devices: none -> 2.13 us  [the longest x1 1.67 us: ring_gather(): lax.ppermute(ahead[:middle], 'depth', forward)]
    ppermute x3, waiting for transfers between devices: 1.91 us -> 0.01 us  [ring_gather(): behind = lax.ppermute(behind, 'depth', backward)]
    ppermute x4 -> x3, starting transfers between devices: 8.03 us -> 6.35 us  [ring_gather(): ahead = lax.ppermute(ahead, 'depth', forward)]
    unnamed x11 -> x12, local copies, waits for them, and re-layouts: 1.27 us -> 1.29 us
  transfers between devices with their start and end apart: 8 -> 9, of which waited for: 7 -> 6; matrix products, arithmetic and copies ran while one was open for 3% -> 3% of each run, Pallas kernels for 0% -> 0%
where the time goes in v16:
time: 59.9 us; the launch traced here: 59.6 us
  waiting for transfers between devices  21.2 us (35%)
  Pallas kernels  14.4 us (24%)
  starting transfers between devices  9.34 us (16%)
  local copies, waits for them, and re-layouts  7.3 us (12%)
  other arithmetic  5.27 us (9%)
  between operations  2.14 us (4%)
    ppermute x3, waiting for transfers between devices, ring_gather(): ahead = lax.ppermute(ahead, 'depth', forward)  14.8 us
    pallas_call x1, Pallas kernels, render_layers(): pl.pallas_call(render_kernel, grid=(brick_rows // block_rows,), in_specs=...  14.4 us
    ppermute x3, starting transfers between devices, ring_gather(): ahead = lax.ppermute(ahead, 'depth', forward)  6.35 us
    gather x1, local copies, waits for them, and re-layouts, composite_rows(): front_rows = jnp.take(flat, front_idx, axis=0, mode='clip')  3.11 us
    ppermute x1, waiting for transfers between devices, ring_gather(): lax.ppermute(ahead[:middle], 'depth', forward)  2.81 us
    gather x1, local copies, waits for them, and re-layouts, composite_rows(): back_rows = jnp.take(flat, back_idx, axis=0, mode='clip')  2.07 us
    ppermute x1, waiting for transfers between devices, on_device(): received = lax.ppermute(for_partner, 'screen', [(0, 1), (1, 0)])  1.9 us
    ppermute x1, starting transfers between devices, ring_gather(): lax.ppermute(ahead[:middle], 'depth', forward)  1.67 us
  transfers between devices with their start and end apart: 9, of which 6 were waited for; matrix products, arithmetic and copies ran while one was open for 3% of the time, Pallas kernels for 0%

profile of v16, /device:TPU:0, one launch (start us, length us, event | category | flops | bytes accessed | tf_op | source)
XLA Modules:
  0.0 59.6 jit_solution(5176534943509561431)
XLA Ops:
  1.3 14.4 %shard_map.73 = f32[128,4,128]{2,1,0:T(4,128)} custom-call(f32[1]{0:T(128)S(6)} %copy.25.absorb_ref, f32[3]{0:T(128)} %slope_ref.1, f32[3]{0:T(128)} %offset_ref.1, s32[1,1]{1,0:T(1,128)} %copy.24.shown_ref, f32[16384,128]{1,0:T(8,128)} %bitcast.15), custom_call_target="tpu_custom_call" | custom-call | tf_op jit(solution)/shard_map/pallas_call | solution.py:44
  15.7 1.0 %constant_dynamic-update-slice_fusion.10 = f32[1040,4,128]{2,1,0:T(4,128)S(1)} fusion(f32[128,4,128]{2,1,0:T(4,128)} %shard_map.73), kind=kLoop, calls=%fused_computation.28 | loop fusion | bytes 524288
  17.3 1.0 %pad_maximum_fusion.1 = f32[130,4,128]{2,1,0:T(4,128)S(1)} fusion(f32[1,4,128]{2,1,0:T(4,128)S(1)} %broadcast_in_dim.69, f32[1,4,128]{2,1,0:T(4,128)S(1)} %get-tuple-element.16, f32[128,4,128]{2,1,0:T(4,128)} %shard_map.73), kind=kLoop, calls=%fused_computation.9 | loop fusion | flops 133120 | bytes 532480 | tf_op jit(solution)/shard_map/concatenate | solution.py:124
  18.3 3.1 %collective-permute-start = (f32[130,4,128]{2,1,0:T(4,128)S(1)}, f32[130,4,128]{2,1,0:T(4,128)S(1)}, u32[]{:S(2)}, u32[]{:S(2)}) collective-permute-start(f32[130,4,128]{2,1,0:T(4,128)S(1)} %pad_maximum_fusion.1), channel_id=1, source_target_pairs={{0,4},{4,8},{8,12},{12,14},{14,10},{10,6},{6,2},{2,0},{1,5},{5,9},... | collective-permute-start | bytes 798728 | tf_op jit(solution)/shard_map/ppermute | solution.py:97
  21.4 0.0 collective-permute-start.1
  21.4 6.3 %collective-permute-done = f32[130,4,128]{2,1,0:T(4,128)S(1)} collective-permute-done((f32[130,4,128]{2,1,0:T(4,128)S(1)}, f32[130,4,128]{2,1,0:T(4,128)S(1)}, u32[]{:S(2)}, u32[]{:S(2)}) %collective-permute-start) | collective-permute-done | bytes 266272 | tf_op jit(solution)/shard_map/ppermute | solution.py:97
  27.8 1.8 %collective-permute-start.2 = (f32[130,4,128]{2,1,0:T(4,128)S(1)}, f32[130,4,128]{2,1,0:T(4,128)S(1)}, u32[]{:S(2)}, u32[]{:S(2)}) collective-permute-start(f32[130,4,128]{2,1,0:T(4,128)S(1)} %collective-permute-done), channel_id=1, source_target_pairs={{0,4},{4,8},{8,12},{12,14},{14,10},{10,6},{6,2},{2,0},{1,5},{5,9},... | collective-permute-start | bytes 798728 | tf_op jit(solution)/shard_map/ppermute | solution.py:97
  29.6 0.0 collective-permute-done.1
  29.6 0.2 collective-permute-start.3
  29.8 0.8 %fusion.8 = (pred[256]{0:T(512)(128)(4,1)S(1)}, s32[256]{0:T(256)S(1)}) fusion(s32[]{:T(128)S(6)} %axis_index.25, s32[4096]{0:T(1024)} %param.13, s32[]{:T(128)S(6)} %select_n.98), kind=kLoop, calls=%fused_computation.52 | loop fusion | flops 4096 | bytes 2312 | tf_op jit(solution)/shard_map/eq | solution.py:139
  30.6 0.8 %dynamic_slice.7 = s32[256]{0:T(256)S(1)} dynamic-slice(s32[4096]{0:T(1024)} %param.13, s32[]{:T(128)S(6)} %select_n.103), dynamic_slice_sizes={256} | dynamic-slice | bytes 2052 | tf_op jit(solution)/shard_map/dynamic_slice | solution.py:133
  31.4 4.0 %collective-permute-done.2 = f32[130,4,128]{2,1,0:T(4,128)S(1)} collective-permute-done((f32[130,4,128]{2,1,0:T(4,128)S(1)}, f32[130,4,128]{2,1,0:T(4,128)S(1)}, u32[]{:S(2)}, u32[]{:S(2)}) %collective-permute-start.2) | collective-permute-done | bytes 266272 | tf_op jit(solution)/shard_map/ppermute | solution.py:97
  35.3 1.5 %collective-permute-start.4 = (f32[130,4,128]{2,1,0:T(4,128)S(1)}, f32[130,4,128]{2,1,0:T(4,128)S(1)}, u32[]{:S(2)}, u32[]{:S(2)}) collective-permute-start(f32[130,4,128]{2,1,0:T(4,128)S(1)} %collective-permute-done.2), channel_id=1, source_target_pairs={{0,4},{4,8},{8,12},{12,14},{14,10},{10,6},{6,2},{2,0},{1,5},{5,9},... | collective-permute-start | bytes 798728 | tf_op jit(solution)/shard_map/ppermute | solution.py:97
  36.8 0.0 collective-permute-done.3
  36.8 0.5 collective-permute-start.5
  37.5 4.5 %collective-permute-done.4 = f32[130,4,128]{2,1,0:T(4,128)S(1)} collective-permute-done((f32[130,4,128]{2,1,0:T(4,128)S(1)}, f32[130,4,128]{2,1,0:T(4,128)S(1)}, u32[]{:S(2)}, u32[]{:S(2)}) %collective-permute-start.4) | collective-permute-done | bytes 266272 | tf_op jit(solution)/shard_map/ppermute | solution.py:97
  42.0 1.7 %collective-permute-start.6 = (f32[65,4,128]{2,1,0:T(4,128)S(1)}, f32[65,4,128]{2,1,0:T(4,128)S(1)}, u32[]{:S(2)}, u32[]{:S(2)}) collective-permute-start(f32[65,4,128]{2,1,0:T(4,128)S(1)} %slice.52), channel_id=1, source_target_pairs={{0,4},{4,8},{8,12},{12,14},{14,10},{10,6},{6,2},{2,0},{1,5},{5,9},... | collective-permute-start | bytes 399368 | tf_op jit(solution)/shard_map/ppermute | solution.py:103
  43.7 0.5 collective-permute-start.7
  44.2 2.8 %collective-permute-done.6 = f32[65,4,128]{2,1,0:T(4,128)S(1)} collective-permute-done((f32[65,4,128]{2,1,0:T(4,128)S(1)}, f32[65,4,128]{2,1,0:T(4,128)S(1)}, u32[]{:S(2)}, u32[]{:S(2)}) %collective-permute-start.6) | collective-permute-done | bytes 133152 | tf_op jit(solution)/shard_map/ppermute | solution.py:103
  47.1 1.7 %collective-permute-done.7 = f32[65,4,128]{2,1,0:T(4,128)S(1)} collective-permute-done((f32[65,4,128]{2,1,0:T(4,128)S(1)}, f32[65,4,128]{2,1,0:T(4,128)S(1)}, u32[]{:S(2)}, u32[]{:S(2)}) %collective-permute-start.7) | collective-permute-done | bytes 133152 | tf_op jit(solution)/shard_map/ppermute | solution.py:104
  48.8 0.1 copy.12
  48.9 0.1 select_reduce_fusion.2
  49.0 0.1 fusion.9
  49.1 0.1 select_reduce_fusion.1
  49.2 2.1 %gather_fusion.1 = f32[512,4,128]{2,1,0:T(4,128)S(1)} fusion(f32[1040,4,128]{2,1,0:T(4,128)S(1)} %constant_dynamic-update-slice_fusion, s32[1024]{0:T(1024)S(1)} %pad_clamp_fusion), kind=kCustom, calls=%fused_computation.1 | custom fusion | bytes 2099200 | tf_op jit(solution)/shard_map/jit(_take)/gather | solution.py:77
  51.3 3.1 %gather_fusion = f32[512,4,128]{2,1,0:T(4,128)S(1)} fusion(f32[1040,4,128]{2,1,0:T(4,128)} %copy-done, s32[1024]{0:T(1024)S(1)} %pad_clamp_fusion.1), kind=kCustom, calls=%fused_computation | custom fusion | bytes 2099200 | tf_op jit(solution)/shard_map/jit(_take)/gather | solution.py:78
  54.4 0.9 %negate_exponential_fusion = (f32[512,1,128]{2,1,0:T(1,128)S(1)}, f32[512,1,128]{2,1,0:T(1,128)S(1)}) fusion(f32[512,4,128]{2,1,0:T(4,128)S(1)} %gather_fusion, f32[512,1,128]{2,1,0:T(1,128)S(1)} %bitcast.17, f32[512,4,128]{2,1,0:T(4,128)S(1)} %gather_fusion.1), kind=kLoop, calls=%fused_computation.13 | loop fusion | flops 262144 | bytes 1310720 | tf_op jit(solution)/shard_map/exp | solution.py:80
  55.3 0.4 fusion
  55.7 0.2 pad_maximum_fusion
  56.0 0.1 collective-permute-start.8
  56.0 1.9 %collective-permute-done.8 = f32[256,4,128]{2,1,0:T(4,128)S(1)} collective-permute-done((f32[256,4,128]{2,1,0:T(4,128)S(1)}, f32[256,4,128]{2,1,0:T(4,128)S(1)}, u32[]{:S(2)}, u32[]{:S(2)}) %collective-permute-start.8) | collective-permute-done | bytes 524320 | tf_op jit(solution)/shard_map/ppermute | solution.py:138
  57.9 1.6 %fusion.2 = f32[256,4,128]{2,1,0:T(4,128)} fusion(f32[256,4,128]{2,1,0:T(4,128)S(1)} %collective-permute-done.8, f32[512,3,128]{2,1,0:T(4,128)S(1)} %fusion, f32[512,1,128]{2,1,0:T(1,128)S(1)} %get-tuple-element.18, pred[256]{0:T(512)(128)(4,1)S(1)} %get-tuple-element.11), kind=kLoop, calls=%fused_computation.7 | loop fusion | flops 262144 | bytes 2097408 | tf_op jit(solution)/shard_map/jit(_where)/select_n | solution.py:140
  (27 shorter events, 0.4 us)
Async XLA Ops:
  18.3 9.4 %collective-permute-start = (f32[130,4,128]{2,1,0:T(4,128)S(1)}, f32[130,4,128]{2,1,0:T(4,128)S(1)}, u32[]{:S(2)}, u32[]{:S(2)}) collective-permute-start(f32[130,4,128]{2,1,0:T(4,128)S(1)} %pad_maximum_fusion.1), channel_id=1, source_target_pairs={{0,4},{4,8},{8,12},{12,14},{14,10},{10,6},{6,2},{2,0},{1,5},{5,9},... | collective-permute-start | bytes 798728 | tf_op jit(solution)/shard_map/ppermute | solution.py:97
  21.4 8.1 %collective-permute-start.1 = (f32[130,4,128]{2,1,0:T(4,128)S(1)}, f32[130,4,128]{2,1,0:T(4,128)S(1)}, u32[]{:S(2)}, u32[]{:S(2)}) collective-permute-start(f32[130,4,128]{2,1,0:T(4,128)S(1)} %pad_maximum_fusion.1), channel_id=1, source_target_pairs={{4,0},{8,4},{12,8},{14,12},{10,14},{6,10},{2,6},{0,2},{5,1},{9,5},... | collective-permute-start | bytes 798728 | tf_op jit(solution)/shard_map/ppermute | solution.py:98
  27.8 7.6 %collective-permute-start.2 = (f32[130,4,128]{2,1,0:T(4,128)S(1)}, f32[130,4,128]{2,1,0:T(4,128)S(1)}, u32[]{:S(2)}, u32[]{:S(2)}) collective-permute-start(f32[130,4,128]{2,1,0:T(4,128)S(1)} %collective-permute-done), channel_id=1, source_target_pairs={{0,4},{4,8},{8,12},{12,14},{14,10},{10,6},{6,2},{2,0},{1,5},{5,9},... | collective-permute-start | bytes 798728 | tf_op jit(solution)/shard_map/ppermute | solution.py:97
  29.6 7.3 %collective-permute-start.3 = (f32[130,4,128]{2,1,0:T(4,128)S(1)}, f32[130,4,128]{2,1,0:T(4,128)S(1)}, u32[]{:S(2)}, u32[]{:S(2)}) collective-permute-start(f32[130,4,128]{2,1,0:T(4,128)S(1)} %collective-permute-done.1), channel_id=1, source_target_pairs={{4,0},{8,4},{12,8},{14,12},{10,14},{6,10},{2,6},{0,2},{5,1},{9,5},... | collective-permute-start | bytes 798728 | tf_op jit(solution)/shard_map/ppermute | solution.py:98
  35.3 6.7 %collective-permute-start.4 = (f32[130,4,128]{2,1,0:T(4,128)S(1)}, f32[130,4,128]{2,1,0:T(4,128)S(1)}, u32[]{:S(2)}, u32[]{:S(2)}) collective-permute-start(f32[130,4,128]{2,1,0:T(4,128)S(1)} %collective-permute-done.2), channel_id=1, source_target_pairs={{0,4},{4,8},{8,12},{12,14},{14,10},{10,6},{6,2},{2,0},{1,5},{5,9},... | collective-permute-start | bytes 798728 | tf_op jit(solution)/shard_map/ppermute | solution.py:97
  36.8 6.9 %collective-permute-start.5 = (f32[130,4,128]{2,1,0:T(4,128)S(1)}, f32[130,4,128]{2,1,0:T(4,128)S(1)}, u32[]{:S(2)}, u32[]{:S(2)}) collective-permute-start(f32[130,4,128]{2,1,0:T(4,128)S(1)} %collective-permute-done.3), channel_id=1, source_target_pairs={{4,0},{8,4},{12,8},{14,12},{10,14},{6,10},{2,6},{0,2},{5,1},{9,5},... | collective-permute-start | bytes 798728 | tf_op jit(solution)/shard_map/ppermute | solution.py:98
  42.0 5.0 %collective-permute-start.6 = (f32[65,4,128]{2,1,0:T(4,128)S(1)}, f32[65,4,128]{2,1,0:T(4,128)S(1)}, u32[]{:S(2)}, u32[]{:S(2)}) collective-permute-start(f32[65,4,128]{2,1,0:T(4,128)S(1)} %slice.52), channel_id=1, source_target_pairs={{0,4},{4,8},{8,12},{12,14},{14,10},{10,6},{6,2},{2,0},{1,5},{5,9},... | collective-permute-start | bytes 399368 | tf_op jit(solution)/shard_map/ppermute | solution.py:103
  43.7 5.0 %collective-permute-start.7 = (f32[65,4,128]{2,1,0:T(4,128)S(1)}, f32[65,4,128]{2,1,0:T(4,128)S(1)}, u32[]{:S(2)}, u32[]{:S(2)}) collective-permute-start(f32[65,4,128]{2,1,0:T(4,128)S(1)} %slice.53), channel_id=1, source_target_pairs={{4,0},{8,4},{12,8},{14,12},{10,14},{6,10},{2,6},{0,2},{5,1},{9,5},... | collective-permute-start | bytes 399368 | tf_op jit(solution)/shard_map/ppermute | solution.py:104
  48.8 2.5 %copy-start = (f32[1040,4,128]{2,1,0:T(4,128)}, f32[1040,4,128]{2,1,0:T(4,128)S(1)}, u32[]{:S(2)}) copy-start(f32[1040,4,128]{2,1,0:T(4,128)S(1)} %constant_dynamic-update-slice_fusion) | copy-start | bytes 6389764
  56.0 2.0 %collective-permute-start.8 = (f32[256,4,128]{2,1,0:T(4,128)S(1)}, f32[256,4,128]{2,1,0:T(4,128)S(1)}, u32[]{:S(2)}, u32[]{:S(2)}) collective-permute-start(f32[256,4,128]{2,1,0:T(4,128)S(1)} %pad_maximum_fusion), channel_id=1, source_target_pairs={{0,1},{1,0},{2,3},{3,2},{4,5},{5,4},{6,7},{7,6},{8,9},{9,8},{10,11... | collective-permute-start | bytes 1572872 | tf_op jit(solution)/shard_map/ppermute | solution.py:138

commit v17 on v13

--- a/solution.py
+++ b/solution.py
@@ -1,3 +1,5 @@
+import functools
+
 import jax
 import jax.numpy as jnp
 from jax import lax
@@ -8,7 +10,7 @@
 BLK = 256
 
 
-def render_kernel(absorb_ref, slope_ref, offset_ref, shown_ref, density_ref, out_ref):
+def render_kernel(first_block, absorb_ref, slope_ref, offset_ref, shown_ref, density_ref, out_ref):
     block_rows = out_ref.shape[0]
     pixels = out_ref.shape[2]
     sample_count = density_ref.shape[0] // block_rows
@@ -32,31 +34,33 @@
     zeros = jnp.zeros((block_rows, pixels), jnp.float32)
     carry = (jnp.full((block_rows, pixels), 0.5, jnp.float32), zeros, zeros, zeros, zeros, zeros)
     carry = lax.fori_loop(0, sample_count, one_step, carry, unroll=16)
-    row_ids = pl.program_id(0) * block_rows + lax.broadcasted_iota(jnp.int32, (block_rows, pixels), 0)
+    row_ids = (pl.program_id(0) + first_block) * block_rows + lax.broadcasted_iota(jnp.int32, (block_rows, pixels), 0)
     visible = row_ids < shown
     for channel in range(3):
         out_ref[:, channel, :] = jnp.where(visible, carry[2] + carry[3 + channel], 0.0)
     out_ref[:, 3, :] = jnp.where(visible, carry[1], 0.0)
 
 
-def render_layers(density_block, shown_rows, absorb, colour_slope, colour_offset, block_rows=16):
+def render_layers(density_block, shown_rows, absorb, colour_slope, colour_offset, first_row, row_count,
+                  block_rows=16):
     brick_rows, sample_count, pixels = density_block.shape
+    first_block = first_row // block_rows
     return pl.pallas_call(
-        render_kernel,
-        grid=(brick_rows // block_rows,),
+        functools.partial(render_kernel, first_block),
+        grid=(row_count // block_rows,),
         in_specs=[
             pl.BlockSpec(memory_space=pltpu.SMEM),
             pl.BlockSpec(memory_space=pltpu.SMEM),
             pl.BlockSpec(memory_space=pltpu.SMEM),
             pl.BlockSpec(memory_space=pltpu.SMEM),
-            pl.BlockSpec((block_rows * sample_count, pixels), lambda i: (i, 0)),
+            pl.BlockSpec((block_rows * sample_count, pixels), lambda i: (i + first_block, 0)),
         ],
         out_specs=pl.BlockSpec((block_rows, 4, pixels), lambda i: (i, 0, 0)),
-        out_shape=jax.ShapeDtypeStruct((brick_rows, 4, pixels), jnp.float32),
+        out_shape=jax.ShapeDtypeStruct((row_count, 4, pixels), jnp.float32),
     )(absorb, colour_slope, colour_offset, shown_rows, density_block.reshape(brick_rows * sample_count, pixels))
 
 
-def composite_rows(flat, starts, counts, brick_ids, stride, image_rows):
+def composite_rows(flat, starts, counts, brick_ids, stride, split, image_rows):
     slot_count = starts.shape[0]
     offset = image_rows[:, None] - starts[None, :]
     covered = (offset >= 0) & (offset < counts[None, :])
@@ -71,7 +75,9 @@
     front_slot = jnp.sum(jnp.where(is_front, slot_ids, 0), axis=1)
     has_front = jnp.any(is_front, axis=1)
     has_back = back >= 0
-    zero_row = stride - 1
+    zero_row = split + 1
+    back_off = back_off + 2 * (back_off >= split).astype(jnp.int32)
+    front_off = front_off + 2 * (front_off >= split).astype(jnp.int32)
     back_idx = jnp.where(has_back, back_slot * stride + back_off, zero_row)
     front_idx = jnp.where(has_front, front_slot * stride + front_off, zero_row)
     back_rows = jnp.take(flat, back_idx, axis=0, mode="clip")
@@ -99,7 +105,7 @@
         if 2 * step < count:
             behind = lax.ppermute(behind, "depth", backward)
             slots.append(behind)
-    return jnp.concatenate(slots, axis=0)
+    return slots
 
 
 def on_device(density, foot_start, foot_rows, extinction, colour_slope, colour_offset, tile_source):
@@ -112,14 +118,20 @@
     owner_rows = image_total // (depth_count * screen_count)
     start = foot_start[0, 0]
     shown = foot_rows[0, 0]
-    layers = render_layers(density[0, 0], foot_rows, extinction, colour_slope, colour_offset)
-    brick_rows, channels, pixels = layers.shape
+    brick_rows, pixels = density.shape[2], density.shape[4]
+    channels = 4
+    split = brick_rows // 2
     lane = lax.broadcasted_iota(jnp.int32, (1, channels, pixels), 2)
     meta = jnp.where(lane == 0, start, jnp.where(lane == 1, shown, jnp.where(lane == 2, depth_index, 0)))
     stride = brick_rows + 2
-    own = jnp.concatenate([layers, meta.astype(jnp.float32), jnp.zeros_like(meta, jnp.float32)], axis=0)
-    flat = ring_gather(own, depth_count)
-    meta_rows = flat.reshape(depth_count, stride, channels, pixels)[:, brick_rows, 0, :3]
+    front_half = render_layers(density[0, 0], foot_rows, extinction, colour_slope, colour_offset, 0, split)
+    front_own = jnp.concatenate([front_half, meta.astype(jnp.float32), jnp.zeros_like(meta, jnp.float32)], axis=0)
+    front_slots = ring_gather(front_own, depth_count)
+    back_half = render_layers(density[0, 0], foot_rows, extinction, colour_slope, colour_offset, split,
+                              brick_rows - split)
+    back_slots = ring_gather(back_half, depth_count)
+    flat = jnp.concatenate([part for pair in zip(front_slots, back_slots) for part in pair], axis=0)
+    meta_rows = flat.reshape(depth_count, stride, channels, pixels)[:, split, 0, :3]
     starts = meta_rows[:, 0].astype(jnp.int32)
     counts = meta_rows[:, 1].astype(jnp.int32)
     brick_ids = meta_rows[:, 2].astype(jnp.int32)
@@ -128,7 +140,7 @@
     wanted_self = lax.dynamic_slice_in_dim(tile_source, self_owner * owner_rows, owner_rows)
     wanted_partner = lax.dynamic_slice_in_dim(tile_source, partner_owner * owner_rows, owner_rows)
     wanted = jnp.concatenate([wanted_self, wanted_partner])
-    rows = composite_rows(flat, starts, counts, brick_ids, stride, wanted % half_rows)
+    rows = composite_rows(flat, starts, counts, brick_ids, stride, split, wanted % half_rows)
     mine = rows[:owner_rows]
     for_partner = rows[owner_rows:]
     received = lax.ppermute(for_partner, "screen", [(0, 1), (1, 0)])

time: 59.6 us -> 60.1 us (level)
  waiting for transfers between devices: 21.3 us -> 11 us
  starting transfers between devices: 8.89 us -> 17 us
  Pallas kernels: 14.4 us -> 16.2 us
  local copies, waits for them, and re-layouts: 7.28 us -> 8.17 us
    ppermute x4 -> x8, waiting for transfers between devices: 17.5 us -> 9.06 us  [ring_gather(): ahead = lax.ppermute(ahead, 'depth', forward)]
    ppermute x4 -> x8, starting transfers between devices: 8.03 us -> 16.3 us  [ring_gather(): ahead = lax.ppermute(ahead, 'depth', forward)]
    ppermute x3 -> x6, waiting for transfers between devices: 1.91 us -> 0.02 us  [ring_gather(): behind = lax.ppermute(behind, 'depth', backward)]
    pallas_call x1 -> x2, Pallas kernels: 14.4 us -> 16.2 us  [render_layers(): pl.pallas_call(functools.partial(render_kernel, first_block), grid=(row_c...]
    unnamed x11 -> x19, local copies, waits for them, and re-layouts: 1.27 us -> 2.18 us
  transfers between devices with their start and end apart: 8 -> 15, of which waited for: 7 -> 7; matrix products, arithmetic and copies ran while one was open for 3% -> 5% of each run, Pallas kernels for 0% -> 14%
where the time goes in v17:
time: 60.1 us; the launch traced here: 59.8 us
  starting transfers between devices  17 us (28%)
  Pallas kernels  16.2 us (27%)
  waiting for transfers between devices  11 us (18%)
  local copies, waits for them, and re-layouts  8.17 us (14%)
  other arithmetic  5.21 us (9%)
  between operations  2.24 us (4%)
    ppermute x8, starting transfers between devices, ring_gather(): ahead = lax.ppermute(ahead, 'depth', forward)  16.3 us
    pallas_call x2, Pallas kernels, render_layers(): pl.pallas_call(functools.partial(render_kernel, first_block), grid=(row_c...  16.2 us
    ppermute x8, waiting for transfers between devices, ring_gather(): ahead = lax.ppermute(ahead, 'depth', forward)  9.06 us
    gather x1, local copies, waits for them, and re-layouts, composite_rows(): front_rows = jnp.take(flat, front_idx, axis=0, mode='clip')  3.11 us
    unnamed x19, local copies, waits for them, and re-layouts  2.18 us
    gather x1, local copies, waits for them, and re-layouts, composite_rows(): back_rows = jnp.take(flat, back_idx, axis=0, mode='clip')  2.07 us
    ppermute x1, waiting for transfers between devices, on_device(): received = lax.ppermute(for_partner, 'screen', [(0, 1), (1, 0)])  1.9 us
    select_n x1, other arithmetic, on_device(): return jnp.where(in_my_half[:, None, None], mine, received)  1.62 us
  transfers between devices with their start and end apart: 15, of which 7 were waited for; matrix products, arithmetic and copies ran while one was open for 5% of the time, Pallas kernels for 14%

profile of v17, /device:TPU:0, one launch (start us, length us, event | category | flops | bytes accessed | tf_op | source)
XLA Modules:
  0.0 59.8 jit_solution(16670793059953518011)
XLA Ops:
  1.3 8.1 %shard_map.73 = f32[64,4,128]{2,1,0:T(4,128)} custom-call(f32[1]{0:T(128)S(6)} %copy.33.absorb_ref, f32[3]{0:T(128)} %slope_ref.3, f32[3]{0:T(128)} %offset_ref.3, s32[1,1]{1,0:T(1,128)} %copy.32.shown_ref, f32[16384,128]{1,0:T(8,128)} %bitcast.21), custom_call_target="tpu_custom_call" | custom-call | tf_op jit(solution)/shard_map/pallas_call | solution.py:48
  9.4 0.9 %constant_dynamic-update-slice_fusion.17 = f32[1040,4,128]{2,1,0:T(4,128)S(1)} fusion(f32[64,4,128]{2,1,0:T(4,128)} %shard_map.73), kind=kLoop, calls=%fused_computation.35 | loop fusion | bytes 262144
  11.0 0.9 %pad_maximum_fusion.1 = f32[66,4,128]{2,1,0:T(4,128)S(1)} fusion(f32[1,4,128]{2,1,0:T(4,128)S(1)} %broadcast_in_dim.69, f32[1,4,128]{2,1,0:T(4,128)S(1)} %get-tuple-element.16, f32[64,4,128]{2,1,0:T(4,128)} %shard_map.73), kind=kLoop, calls=%fused_computation.13 | loop fusion | flops 67584 | bytes 270336 | tf_op jit(solution)/shard_map/concatenate | solution.py:128
  12.0 3.1 %collective-permute-start = (f32[66,4,128]{2,1,0:T(4,128)S(1)}, f32[66,4,128]{2,1,0:T(4,128)S(1)}, u32[]{:S(2)}, u32[]{:S(2)}) collective-permute-start(f32[66,4,128]{2,1,0:T(4,128)S(1)} %pad_maximum_fusion.1), channel_id=1, source_target_pairs={{0,4},{4,8},{8,12},{12,14},{14,10},{10,6},{6,2},{2,0},{1,5},{5,9},... | collective-permute-start | bytes 405512 | tf_op jit(solution)/shard_map/ppermute | solution.py:103
  15.0 8.1 %shard_map.74 = f32[64,4,128]{2,1,0:T(4,128)} custom-call(f32[1]{0:T(128)S(6)} %copy.33.absorb_ref, f32[3]{0:T(128)} %slope_ref.3, f32[3]{0:T(128)} %offset_ref.3, s32[1,1]{1,0:T(1,128)} %copy.32.shown_ref, f32[16384,128]{1,0:T(8,128)} %bitcast.22), custom_call_target="tpu_custom_call" | custom-call | tf_op jit(solution)/shard_map/pallas_call | solution.py:48
  23.1 2.0 %collective-permute-start.1 = (f32[64,4,128]{2,1,0:T(4,128)}, f32[64,4,128]{2,1,0:T(4,128)S(1)}, u32[]{:S(2)}, u32[]{:S(2)}) collective-permute-start(f32[64,4,128]{2,1,0:T(4,128)} %shard_map.74), channel_id=1, source_target_pairs={{0,4},{4,8},{8,12},{12,14},{14,10},{10,6},{6,2},{2,0},{1,5},{5,9},... | collective-permute-start | bytes 393224 | tf_op jit(solution)/shard_map/ppermute | solution.py:103
  25.2 0.8 %fusion.12 = (pred[256]{0:T(512)(128)(4,1)S(1)}, s32[256]{0:T(256)S(1)}) fusion(s32[]{:T(128)S(6)} %axis_index.25, s32[4096]{0:T(1024)} %param.13, s32[]{:T(128)S(6)} %select_n.92), kind=kLoop, calls=%fused_computation.68 | loop fusion | flops 4096 | bytes 2312 | tf_op jit(solution)/shard_map/eq | solution.py:147
  25.9 0.8 %dynamic_slice.7 = s32[256]{0:T(256)S(1)} dynamic-slice(s32[4096]{0:T(1024)} %param.13, s32[]{:T(128)S(6)} %select_n.97), dynamic_slice_sizes={256} | dynamic-slice | bytes 2052 | tf_op jit(solution)/shard_map/dynamic_slice | solution.py:141
  26.7 0.9 %constant_dynamic-update-slice_fusion.14 = f32[1040,4,128]{2,1,0:T(4,128)S(1)} fusion(f32[1040,4,128]{2,1,0:T(4,128)S(1)} %constant_dynamic-update-slice_fusion.15, f32[64,4,128]{2,1,0:T(4,128)} %shard_map.74), kind=kLoop, calls=%fused_computation.32 | loop fusion | bytes 262144
  27.6 0.7 %collective-permute-done.1 = f32[64,4,128]{2,1,0:T(4,128)S(1)} collective-permute-done((f32[64,4,128]{2,1,0:T(4,128)}, f32[64,4,128]{2,1,0:T(4,128)S(1)}, u32[]{:S(2)}, u32[]{:S(2)}) %collective-permute-start.1) | collective-permute-done | bytes 131104 | tf_op jit(solution)/shard_map/ppermute | solution.py:103
  28.3 2.0 %collective-permute-start.5 = (f32[64,4,128]{2,1,0:T(4,128)S(1)}, f32[64,4,128]{2,1,0:T(4,128)S(1)}, u32[]{:S(2)}, u32[]{:S(2)}) collective-permute-start(f32[64,4,128]{2,1,0:T(4,128)S(1)} %collective-permute-done.1), channel_id=1, source_target_pairs={{0,4},{4,8},{8,12},{12,14},{14,10},{10,6},{6,2},{2,0},{1,5},{5,9},... | collective-permute-start | bytes 393224 | tf_op jit(solution)/shard_map/ppermute | solution.py:103
  30.4 2.0 %collective-permute-start.4 = (f32[66,4,128]{2,1,0:T(4,128)S(1)}, f32[66,4,128]{2,1,0:T(4,128)S(1)}, u32[]{:S(2)}, u32[]{:S(2)}) collective-permute-start(f32[66,4,128]{2,1,0:T(4,128)S(1)} %collective-permute-done), channel_id=1, source_target_pairs={{0,4},{4,8},{8,12},{12,14},{14,10},{10,6},{6,2},{2,0},{1,5},{5,9},... | collective-permute-start | bytes 405512 | tf_op jit(solution)/shard_map/ppermute | solution.py:103
  32.4 0.1 collective-permute-start.6
  32.6 2.0 %collective-permute-done.5 = f32[64,4,128]{2,1,0:T(4,128)S(1)} collective-permute-done((f32[64,4,128]{2,1,0:T(4,128)S(1)}, f32[64,4,128]{2,1,0:T(4,128)S(1)}, u32[]{:S(2)}, u32[]{:S(2)}) %collective-permute-start.5) | collective-permute-done | bytes 131104 | tf_op jit(solution)/shard_map/ppermute | solution.py:103
  34.6 1.8 %collective-permute-start.9 = (f32[64,4,128]{2,1,0:T(4,128)S(1)}, f32[64,4,128]{2,1,0:T(4,128)S(1)}, u32[]{:S(2)}, u32[]{:S(2)}) collective-permute-start(f32[64,4,128]{2,1,0:T(4,128)S(1)} %collective-permute-done.5), channel_id=1, source_target_pairs={{0,4},{4,8},{8,12},{12,14},{14,10},{10,6},{6,2},{2,0},{1,5},{5,9},... | collective-permute-start | bytes 393224 | tf_op jit(solution)/shard_map/ppermute | solution.py:103
  36.4 0.2 collective-permute-start.11
  36.6 0.9 %collective-permute-done.4 = f32[66,4,128]{2,1,0:T(4,128)S(1)} collective-permute-done((f32[66,4,128]{2,1,0:T(4,128)S(1)}, f32[66,4,128]{2,1,0:T(4,128)S(1)}, u32[]{:S(2)}, u32[]{:S(2)}) %collective-permute-start.4) | collective-permute-done | bytes 135200 | tf_op jit(solution)/shard_map/ppermute | solution.py:103
  37.5 1.8 %collective-permute-start.8 = (f32[66,4,128]{2,1,0:T(4,128)S(1)}, f32[66,4,128]{2,1,0:T(4,128)S(1)}, u32[]{:S(2)}, u32[]{:S(2)}) collective-permute-start(f32[66,4,128]{2,1,0:T(4,128)S(1)} %collective-permute-done.4), channel_id=1, source_target_pairs={{0,4},{4,8},{8,12},{12,14},{14,10},{10,6},{6,2},{2,0},{1,5},{5,9},... | collective-permute-start | bytes 405512 | tf_op jit(solution)/shard_map/ppermute | solution.py:103
  39.3 0.3 collective-permute-start.10
  39.7 0.9 %collective-permute-done.9 = f32[64,4,128]{2,1,0:T(4,128)S(1)} collective-permute-done((f32[64,4,128]{2,1,0:T(4,128)S(1)}, f32[64,4,128]{2,1,0:T(4,128)S(1)}, u32[]{:S(2)}, u32[]{:S(2)}) %collective-permute-start.9) | collective-permute-done | bytes 131104 | tf_op jit(solution)/shard_map/ppermute | solution.py:103
  40.6 1.8 %collective-permute-start.13 = (f32[64,4,128]{2,1,0:T(4,128)S(1)}, f32[64,4,128]{2,1,0:T(4,128)S(1)}, u32[]{:S(2)}, u32[]{:S(2)}) collective-permute-start(f32[64,4,128]{2,1,0:T(4,128)S(1)} %collective-permute-done.9), channel_id=1, source_target_pairs={{0,4},{4,8},{8,12},{12,14},{14,10},{10,6},{6,2},{2,0},{1,5},{5,9},... | collective-permute-start | bytes 393224 | tf_op jit(solution)/shard_map/ppermute | solution.py:103
  42.4 1.5 %collective-permute-done.8 = f32[66,4,128]{2,1,0:T(4,128)S(1)} collective-permute-done((f32[66,4,128]{2,1,0:T(4,128)S(1)}, f32[66,4,128]{2,1,0:T(4,128)S(1)}, u32[]{:S(2)}, u32[]{:S(2)}) %collective-permute-start.8) | collective-permute-done | bytes 135200 | tf_op jit(solution)/shard_map/ppermute | solution.py:103
  43.9 1.8 %collective-permute-start.12 = (f32[66,4,128]{2,1,0:T(4,128)S(1)}, f32[66,4,128]{2,1,0:T(4,128)S(1)}, u32[]{:S(2)}, u32[]{:S(2)}) collective-permute-start(f32[66,4,128]{2,1,0:T(4,128)S(1)} %collective-permute-done.8), channel_id=1, source_target_pairs={{0,4},{4,8},{8,12},{12,14},{14,10},{10,6},{6,2},{2,0},{1,5},{5,9},... | collective-permute-start | bytes 405512 | tf_op jit(solution)/shard_map/ppermute | solution.py:103
  45.8 3.1 %collective-permute-done.12 = f32[66,4,128]{2,1,0:T(4,128)S(1)} collective-permute-done((f32[66,4,128]{2,1,0:T(4,128)S(1)}, f32[66,4,128]{2,1,0:T(4,128)S(1)}, u32[]{:S(2)}, u32[]{:S(2)}) %collective-permute-start.12) | collective-permute-done | bytes 135200 | tf_op jit(solution)/shard_map/ppermute | solution.py:103
  49.3 0.1 fusion.4
  49.4 2.1 %gather_fusion.1 = f32[512,4,128]{2,1,0:T(4,128)S(1)} fusion(f32[1040,4,128]{2,1,0:T(4,128)S(1)} %constant_dynamic-update-slice_fusion, s32[1024]{0:T(1024)S(1)} %pad_clamp_fusion), kind=kCustom, calls=%fused_computation.1 | custom fusion | bytes 2099200 | tf_op jit(solution)/shard_map/jit(_take)/gather | solution.py:83
  51.5 3.1 %gather_fusion = f32[512,4,128]{2,1,0:T(4,128)S(1)} fusion(f32[1040,4,128]{2,1,0:T(4,128)} %copy-done, s32[1024]{0:T(1024)S(1)} %pad_clamp_fusion.1), kind=kCustom, calls=%fused_computation | custom fusion | bytes 2099200 | tf_op jit(solution)/shard_map/jit(_take)/gather | solution.py:84
  54.7 0.9 %negate_exponential_fusion = (f32[512,1,128]{2,1,0:T(1,128)S(1)}, f32[512,1,128]{2,1,0:T(1,128)S(1)}) fusion(f32[512,4,128]{2,1,0:T(4,128)S(1)} %gather_fusion, f32[512,1,128]{2,1,0:T(1,128)S(1)} %bitcast.24, f32[512,4,128]{2,1,0:T(4,128)S(1)} %gather_fusion.1), kind=kLoop, calls=%fused_computation.12 | loop fusion | flops 262144 | bytes 1310720 | tf_op jit(solution)/shard_map/exp | solution.py:86
  55.5 0.4 fusion
  56.0 0.2 pad_maximum_fusion
  56.3 1.9 %collective-permute-done.14 = f32[256,4,128]{2,1,0:T(4,128)S(1)} collective-permute-done((f32[256,4,128]{2,1,0:T(4,128)S(1)}, f32[256,4,128]{2,1,0:T(4,128)S(1)}, u32[]{:S(2)}, u32[]{:S(2)}) %collective-permute-start.14) | collective-permute-done | bytes 524320 | tf_op jit(solution)/shard_map/ppermute | solution.py:146
  58.2 1.6 %fusion.2 = f32[256,4,128]{2,1,0:T(4,128)} fusion(f32[256,4,128]{2,1,0:T(4,128)S(1)} %collective-permute-done.14, f32[512,3,128]{2,1,0:T(4,128)S(1)} %fusion, f32[512,1,128]{2,1,0:T(1,128)S(1)} %get-tuple-element.18, pred[256]{0:T(512)(128)(4,1)S(1)} %get-tuple-element.11), kind=kLoop, calls=%fused_computation.7 | loop fusion | flops 262144 | bytes 2097408 | tf_op jit(solution)/shard_map/jit(_where)/select_n | solution.py:148
  (48 shorter events, 0.8 us)
Async XLA Ops:
  12.0 18.4 %collective-permute-start = (f32[66,4,128]{2,1,0:T(4,128)S(1)}, f32[66,4,128]{2,1,0:T(4,128)S(1)}, u32[]{:S(2)}, u32[]{:S(2)}) collective-permute-start(f32[66,4,128]{2,1,0:T(4,128)S(1)} %pad_maximum_fusion.1), channel_id=1, source_target_pairs={{0,4},{4,8},{8,12},{12,14},{14,10},{10,6},{6,2},{2,0},{1,5},{5,9},... | collective-permute-start | bytes 405512 | tf_op jit(solution)/shard_map/ppermute | solution.py:103
  15.0 17.4 %collective-permute-start.2 = (f32[66,4,128]{2,1,0:T(4,128)S(1)}, f32[66,4,128]{2,1,0:T(4,128)S(1)}, u32[]{:S(2)}, u32[]{:S(2)}) collective-permute-start(f32[66,4,128]{2,1,0:T(4,128)S(1)} %pad_maximum_fusion.1), channel_id=1, source_target_pairs={{4,0},{8,4},{12,8},{14,12},{10,14},{6,10},{2,6},{0,2},{5,1},{9,5},... | collective-permute-start | bytes 405512 | tf_op jit(solution)/shard_map/ppermute | solution.py:106
  23.1 5.2 %collective-permute-start.1 = (f32[64,4,128]{2,1,0:T(4,128)}, f32[64,4,128]{2,1,0:T(4,128)S(1)}, u32[]{:S(2)}, u32[]{:S(2)}) collective-permute-start(f32[64,4,128]{2,1,0:T(4,128)} %shard_map.74), channel_id=1, source_target_pairs={{0,4},{4,8},{8,12},{12,14},{14,10},{10,6},{6,2},{2,0},{1,5},{5,9},... | collective-permute-start | bytes 393224 | tf_op jit(solution)/shard_map/ppermute | solution.py:103
  25.2 5.2 %collective-permute-start.3 = (f32[64,4,128]{2,1,0:T(4,128)}, f32[64,4,128]{2,1,0:T(4,128)S(1)}, u32[]{:S(2)}, u32[]{:S(2)}) collective-permute-start(f32[64,4,128]{2,1,0:T(4,128)} %shard_map.74), channel_id=1, source_target_pairs={{4,0},{8,4},{12,8},{14,12},{10,14},{6,10},{2,6},{0,2},{5,1},{9,5},... | collective-permute-start | bytes 393224 | tf_op jit(solution)/shard_map/ppermute | solution.py:106
  28.3 6.3 %collective-permute-start.5 = (f32[64,4,128]{2,1,0:T(4,128)S(1)}, f32[64,4,128]{2,1,0:T(4,128)S(1)}, u32[]{:S(2)}, u32[]{:S(2)}) collective-permute-start(f32[64,4,128]{2,1,0:T(4,128)S(1)} %collective-permute-done.1), channel_id=1, source_target_pairs={{0,4},{4,8},{8,12},{12,14},{14,10},{10,6},{6,2},{2,0},{1,5},{5,9},... | collective-permute-start | bytes 393224 | tf_op jit(solution)/shard_map/ppermute | solution.py:103
  30.3 6.1 %collective-permute-start.7 = (f32[64,4,128]{2,1,0:T(4,128)S(1)}, f32[64,4,128]{2,1,0:T(4,128)S(1)}, u32[]{:S(2)}, u32[]{:S(2)}) collective-permute-start(f32[64,4,128]{2,1,0:T(4,128)S(1)} %collective-permute-done.3), channel_id=1, source_target_pairs={{4,0},{8,4},{12,8},{14,12},{10,14},{6,10},{2,6},{0,2},{5,1},{9,5},... | collective-permute-start | bytes 393224 | tf_op jit(solution)/shard_map/ppermute | solution.py:106
  30.4 7.1 %collective-permute-start.4 = (f32[66,4,128]{2,1,0:T(4,128)S(1)}, f32[66,4,128]{2,1,0:T(4,128)S(1)}, u32[]{:S(2)}, u32[]{:S(2)}) collective-permute-start(f32[66,4,128]{2,1,0:T(4,128)S(1)} %collective-permute-done), channel_id=1, source_target_pairs={{0,4},{4,8},{8,12},{12,14},{14,10},{10,6},{6,2},{2,0},{1,5},{5,9},... | collective-permute-start | bytes 405512 | tf_op jit(solution)/shard_map/ppermute | solution.py:103
  32.4 6.9 %collective-permute-start.6 = (f32[66,4,128]{2,1,0:T(4,128)S(1)}, f32[66,4,128]{2,1,0:T(4,128)S(1)}, u32[]{:S(2)}, u32[]{:S(2)}) collective-permute-start(f32[66,4,128]{2,1,0:T(4,128)S(1)} %collective-permute-done.2), channel_id=1, source_target_pairs={{4,0},{8,4},{12,8},{14,12},{10,14},{6,10},{2,6},{0,2},{5,1},{9,5},... | collective-permute-start | bytes 405512 | tf_op jit(solution)/shard_map/ppermute | solution.py:106
  34.6 6.0 %collective-permute-start.9 = (f32[64,4,128]{2,1,0:T(4,128)S(1)}, f32[64,4,128]{2,1,0:T(4,128)S(1)}, u32[]{:S(2)}, u32[]{:S(2)}) collective-permute-start(f32[64,4,128]{2,1,0:T(4,128)S(1)} %collective-permute-done.5), channel_id=1, source_target_pairs={{0,4},{4,8},{8,12},{12,14},{14,10},{10,6},{6,2},{2,0},{1,5},{5,9},... | collective-permute-start | bytes 393224 | tf_op jit(solution)/shard_map/ppermute | solution.py:103
  36.4 9.4 %collective-permute-start.11 = (f32[64,4,128]{2,1,0:T(4,128)S(1)}, f32[64,4,128]{2,1,0:T(4,128)S(1)}, u32[]{:S(2)}, u32[]{:S(2)}) collective-permute-start(f32[64,4,128]{2,1,0:T(4,128)S(1)} %collective-permute-done.7), channel_id=1, source_target_pairs={{4,0},{8,4},{12,8},{14,12},{10,14},{6,10},{2,6},{0,2},{5,1},{9,5},... | collective-permute-start | bytes 393224 | tf_op jit(solution)/shard_map/ppermute | solution.py:106
  37.5 6.4 %collective-permute-start.8 = (f32[66,4,128]{2,1,0:T(4,128)S(1)}, f32[66,4,128]{2,1,0:T(4,128)S(1)}, u32[]{:S(2)}, u32[]{:S(2)}) collective-permute-start(f32[66,4,128]{2,1,0:T(4,128)S(1)} %collective-permute-done.4), channel_id=1, source_target_pairs={{0,4},{4,8},{8,12},{12,14},{14,10},{10,6},{6,2},{2,0},{1,5},{5,9},... | collective-permute-start | bytes 405512 | tf_op jit(solution)/shard_map/ppermute | solution.py:103
  39.3 6.4 %collective-permute-start.10 = (f32[66,4,128]{2,1,0:T(4,128)S(1)}, f32[66,4,128]{2,1,0:T(4,128)S(1)}, u32[]{:S(2)}, u32[]{:S(2)}) collective-permute-start(f32[66,4,128]{2,1,0:T(4,128)S(1)} %collective-permute-done.6), channel_id=1, source_target_pairs={{4,0},{8,4},{12,8},{14,12},{10,14},{6,10},{2,6},{0,2},{5,1},{9,5},... | collective-permute-start | bytes 405512 | tf_op jit(solution)/shard_map/ppermute | solution.py:106
  40.6 8.4 %collective-permute-start.13 = (f32[64,4,128]{2,1,0:T(4,128)S(1)}, f32[64,4,128]{2,1,0:T(4,128)S(1)}, u32[]{:S(2)}, u32[]{:S(2)}) collective-permute-start(f32[64,4,128]{2,1,0:T(4,128)S(1)} %collective-permute-done.9), channel_id=1, source_target_pairs={{0,4},{4,8},{8,12},{12,14},{14,10},{10,6},{6,2},{2,0},{1,5},{5,9},... | collective-permute-start | bytes 393224 | tf_op jit(solution)/shard_map/ppermute | solution.py:103
  43.9 5.0 %collective-permute-start.12 = (f32[66,4,128]{2,1,0:T(4,128)S(1)}, f32[66,4,128]{2,1,0:T(4,128)S(1)}, u32[]{:S(2)}, u32[]{:S(2)}) collective-permute-start(f32[66,4,128]{2,1,0:T(4,128)S(1)} %collective-permute-done.8), channel_id=1, source_target_pairs={{0,4},{4,8},{8,12},{12,14},{14,10},{10,6},{6,2},{2,0},{1,5},{5,9},... | collective-permute-start | bytes 405512 | tf_op jit(solution)/shard_map/ppermute | solution.py:103
  49.0 2.6 %copy-start = (f32[1040,4,128]{2,1,0:T(4,128)}, f32[1040,4,128]{2,1,0:T(4,128)S(1)}, u32[]{:S(2)}) copy-start(f32[1040,4,128]{2,1,0:T(4,128)S(1)} %constant_dynamic-update-slice_fusion) | copy-start | bytes 6389764
  56.2 2.0 %collective-permute-start.14 = (f32[256,4,128]{2,1,0:T(4,128)S(1)}, f32[256,4,128]{2,1,0:T(4,128)S(1)}, u32[]{:S(2)}, u32[]{:S(2)}) collective-permute-start(f32[256,4,128]{2,1,0:T(4,128)S(1)} %pad_maximum_fusion), channel_id=1, source_target_pairs={{0,1},{1,0},{2,3},{3,2},{4,5},{5,4},{6,7},{7,6},{8,9},{9,8},{10,11... | collective-permute-start | bytes 1572872 | tf_op jit(solution)/shard_map/ppermute | solution.py:146

commit v18 on v13

--- a/solution.py
+++ b/solution.py
@@ -74,8 +74,8 @@
     zero_row = stride - 1
     back_idx = jnp.where(has_back, back_slot * stride + back_off, zero_row)
     front_idx = jnp.where(has_front, front_slot * stride + front_off, zero_row)
-    back_rows = jnp.take(flat, back_idx, axis=0, mode="clip")
-    front_rows = jnp.take(flat, front_idx, axis=0, mode="clip")
+    back_rows = flat.at[back_idx].get(mode="promise_in_bounds")
+    front_rows = flat.at[front_idx].get(mode="promise_in_bounds")
     front_depth = front_rows[:, 3:4, :]
     colours = front_rows[:, :3, :] + jnp.exp(-front_depth) * back_rows[:, :3, :]
     opacity = 1.0 - jnp.exp(-(front_depth + back_rows[:, 3:4, :]))

time: 59.6 us -> 59.6 us (level)
  no operation moved by 1% of the time
where the time goes in v18:
time: 59.6 us; the launch traced here: 59.3 us
  waiting for transfers between devices  21.3 us (36%)
  Pallas kernels  14.4 us (24%)
  starting transfers between devices  8.89 us (15%)
  local copies, waits for them, and re-layouts  7.28 us (12%)
  other arithmetic  5.28 us (9%)
  between operations  2.13 us (4%)
    ppermute x4, waiting for transfers between devices, ring_gather(): ahead = lax.ppermute(ahead, 'depth', forward)  17.5 us
    pallas_call x1, Pallas kernels, render_layers(): pl.pallas_call(render_kernel, grid=(brick_rows // block_rows,), in_specs=...  14.4 us
    ppermute x4, starting transfers between devices, ring_gather(): ahead = lax.ppermute(ahead, 'depth', forward)  8.03 us
    gather x1, local copies, waits for them, and re-layouts, composite_rows(): front_rows = flat.at[front_idx].get(mode='promise_in_bounds')  3.11 us
    gather x1, local copies, waits for them, and re-layouts, composite_rows(): back_rows = flat.at[back_idx].get(mode='promise_in_bounds')  2.07 us
    ppermute x3, waiting for transfers between devices, ring_gather(): behind = lax.ppermute(behind, 'depth', backward)  1.91 us
    ppermute x1, waiting for transfers between devices, on_device(): received = lax.ppermute(for_partner, 'screen', [(0, 1), (1, 0)])  1.9 us
    select_n x1, other arithmetic, on_device(): return jnp.where(in_my_half[:, None, None], mine, received)  1.62 us
  transfers between devices with their start and end apart: 8, of which 7 were waited for; matrix products, arithmetic and copies ran while one was open for 3% of the time, Pallas kernels for 0%

profile of v18, /device:TPU:0, one launch (start us, length us, event | category | flops | bytes accessed | tf_op | source)
XLA Modules:
  0.0 59.3 jit_solution(16457670511456973749)
XLA Ops:
  1.3 14.4 %shard_map.73 = f32[128,4,128]{2,1,0:T(4,128)} custom-call(f32[1]{0:T(128)S(6)} %copy.25.absorb_ref, f32[3]{0:T(128)} %slope_ref.1, f32[3]{0:T(128)} %offset_ref.1, s32[1,1]{1,0:T(1,128)} %copy.24.shown_ref, f32[16384,128]{1,0:T(8,128)} %bitcast.19), custom_call_target="tpu_custom_call" | custom-call | tf_op jit(solution)/shard_map/pallas_call | solution.py:44
  15.7 1.0 %constant_dynamic-update-slice_fusion.9 = f32[1040,4,128]{2,1,0:T(4,128)S(1)} fusion(f32[128,4,128]{2,1,0:T(4,128)} %shard_map.73), kind=kLoop, calls=%fused_computation.27 | loop fusion | bytes 524288
  17.3 1.0 %pad_maximum_fusion.1 = f32[130,4,128]{2,1,0:T(4,128)S(1)} fusion(f32[1,4,128]{2,1,0:T(4,128)S(1)} %broadcast_in_dim.68, f32[1,4,128]{2,1,0:T(4,128)S(1)} %get-tuple-element.16, f32[128,4,128]{2,1,0:T(4,128)} %shard_map.73), kind=kLoop, calls=%fused_computation.9 | loop fusion | flops 133120 | bytes 532480 | tf_op jit(solution)/shard_map/concatenate | solution.py:120
  18.3 3.1 %collective-permute-start = (f32[130,4,128]{2,1,0:T(4,128)S(1)}, f32[130,4,128]{2,1,0:T(4,128)S(1)}, u32[]{:S(2)}, u32[]{:S(2)}) collective-permute-start(f32[130,4,128]{2,1,0:T(4,128)S(1)} %pad_maximum_fusion.1), channel_id=1, source_target_pairs={{0,4},{4,8},{8,12},{12,14},{14,10},{10,6},{6,2},{2,0},{1,5},{5,9},... | collective-permute-start | bytes 798728 | tf_op jit(solution)/shard_map/ppermute | solution.py:97
  21.4 0.0 collective-permute-start.1
  21.4 6.3 %collective-permute-done = f32[130,4,128]{2,1,0:T(4,128)S(1)} collective-permute-done((f32[130,4,128]{2,1,0:T(4,128)S(1)}, f32[130,4,128]{2,1,0:T(4,128)S(1)}, u32[]{:S(2)}, u32[]{:S(2)}) %collective-permute-start) | collective-permute-done | bytes 266272 | tf_op jit(solution)/shard_map/ppermute | solution.py:97
  27.8 1.8 %collective-permute-start.2 = (f32[130,4,128]{2,1,0:T(4,128)S(1)}, f32[130,4,128]{2,1,0:T(4,128)S(1)}, u32[]{:S(2)}, u32[]{:S(2)}) collective-permute-start(f32[130,4,128]{2,1,0:T(4,128)S(1)} %collective-permute-done), channel_id=1, source_target_pairs={{0,4},{4,8},{8,12},{12,14},{14,10},{10,6},{6,2},{2,0},{1,5},{5,9},... | collective-permute-start | bytes 798728 | tf_op jit(solution)/shard_map/ppermute | solution.py:97
  29.6 0.8 %fusion.8 = (pred[256]{0:T(512)(128)(4,1)S(1)}, s32[256]{0:T(256)S(1)}) fusion(s32[]{:T(128)S(6)} %axis_index.25, s32[4096]{0:T(1024)} %param.13, s32[]{:T(128)S(6)} %select_n.118), kind=kLoop, calls=%fused_computation.53 | loop fusion | flops 4096 | bytes 2312 | tf_op jit(solution)/shard_map/eq | solution.py:135
  30.3 0.8 %dynamic_slice.7 = s32[256]{0:T(256)S(1)} dynamic-slice(s32[4096]{0:T(1024)} %param.13, s32[]{:T(128)S(6)} %select_n.123), dynamic_slice_sizes={256} | dynamic-slice | bytes 2052 | tf_op jit(solution)/shard_map/dynamic_slice | solution.py:129
  31.1 0.0 collective-permute-done.1
  31.1 0.2 collective-permute-start.3
  31.3 4.0 %collective-permute-done.2 = f32[130,4,128]{2,1,0:T(4,128)S(1)} collective-permute-done((f32[130,4,128]{2,1,0:T(4,128)S(1)}, f32[130,4,128]{2,1,0:T(4,128)S(1)}, u32[]{:S(2)}, u32[]{:S(2)}) %collective-permute-start.2) | collective-permute-done | bytes 266272 | tf_op jit(solution)/shard_map/ppermute | solution.py:97
  35.3 1.5 %collective-permute-start.4 = (f32[130,4,128]{2,1,0:T(4,128)S(1)}, f32[130,4,128]{2,1,0:T(4,128)S(1)}, u32[]{:S(2)}, u32[]{:S(2)}) collective-permute-start(f32[130,4,128]{2,1,0:T(4,128)S(1)} %collective-permute-done.2), channel_id=1, source_target_pairs={{0,4},{4,8},{8,12},{12,14},{14,10},{10,6},{6,2},{2,0},{1,5},{5,9},... | collective-permute-start | bytes 798728 | tf_op jit(solution)/shard_map/ppermute | solution.py:97
  36.9 1.2 %collective-permute-done.3 = f32[130,4,128]{2,1,0:T(4,128)S(1)} collective-permute-done((f32[130,4,128]{2,1,0:T(4,128)S(1)}, f32[130,4,128]{2,1,0:T(4,128)S(1)}, u32[]{:S(2)}, u32[]{:S(2)}) %collective-permute-start.3) | collective-permute-done | bytes 266272 | tf_op jit(solution)/shard_map/ppermute | solution.py:100
  38.1 0.5 collective-permute-start.5
  38.7 3.3 %collective-permute-done.4 = f32[130,4,128]{2,1,0:T(4,128)S(1)} collective-permute-done((f32[130,4,128]{2,1,0:T(4,128)S(1)}, f32[130,4,128]{2,1,0:T(4,128)S(1)}, u32[]{:S(2)}, u32[]{:S(2)}) %collective-permute-start.4) | collective-permute-done | bytes 266272 | tf_op jit(solution)/shard_map/ppermute | solution.py:97
  42.0 1.7 %collective-permute-start.6 = (f32[130,4,128]{2,1,0:T(4,128)S(1)}, f32[130,4,128]{2,1,0:T(4,128)S(1)}, u32[]{:S(2)}, u32[]{:S(2)}) collective-permute-start(f32[130,4,128]{2,1,0:T(4,128)S(1)} %collective-permute-done.4), channel_id=1, source_target_pairs={{0,4},{4,8},{8,12},{12,14},{14,10},{10,6},{6,2},{2,0},{1,5},{5,9},... | collective-permute-start | bytes 798728 | tf_op jit(solution)/shard_map/ppermute | solution.py:97
  43.8 0.7 %collective-permute-done.5 = f32[130,4,128]{2,1,0:T(4,128)S(1)} collective-permute-done((f32[130,4,128]{2,1,0:T(4,128)S(1)}, f32[130,4,128]{2,1,0:T(4,128)S(1)}, u32[]{:S(2)}, u32[]{:S(2)}) %collective-permute-start.5) | collective-permute-done | bytes 266272 | tf_op jit(solution)/shard_map/ppermute | solution.py:100
  44.5 3.9 %collective-permute-done.6 = f32[130,4,128]{2,1,0:T(4,128)S(1)} collective-permute-done((f32[130,4,128]{2,1,0:T(4,128)S(1)}, f32[130,4,128]{2,1,0:T(4,128)S(1)}, u32[]{:S(2)}, u32[]{:S(2)}) %collective-permute-start.6) | collective-permute-done | bytes 266272 | tf_op jit(solution)/shard_map/ppermute | solution.py:97
  48.5 0.1 copy.13
  48.6 0.1 select_reduce_fusion.2
  48.7 0.1 fusion.9
  48.8 0.1 select_reduce_fusion.1
  48.9 2.1 %gather_fusion.1 = f32[512,4,128]{2,1,0:T(4,128)S(1)} fusion(f32[1040,4,128]{2,1,0:T(4,128)S(1)} %constant_dynamic-update-slice_fusion, s32[1024]{0:T(1024)S(1)} %pad_clamp_fusion), kind=kCustom, calls=%fused_computation.1 | custom fusion | bytes 2099200 | tf_op jit(solution)/shard_map/gather | solution.py:77
  51.0 0.0 copy-done
  51.0 3.1 %gather_fusion = f32[512,4,128]{2,1,0:T(4,128)S(1)} fusion(f32[1040,4,128]{2,1,0:T(4,128)} %copy-done, s32[1024]{0:T(1024)S(1)} %pad_clamp_fusion.1), kind=kCustom, calls=%fused_computation | custom fusion | bytes 2099200 | tf_op jit(solution)/shard_map/gather | solution.py:78
  54.2 0.9 %negate_exponential_fusion = (f32[512,1,128]{2,1,0:T(1,128)S(1)}, f32[512,1,128]{2,1,0:T(1,128)S(1)}) fusion(f32[512,4,128]{2,1,0:T(4,128)S(1)} %gather_fusion, f32[512,1,128]{2,1,0:T(1,128)S(1)} %bitcast.21, f32[512,4,128]{2,1,0:T(4,128)S(1)} %gather_fusion.1), kind=kLoop, calls=%fused_computation.13 | loop fusion | flops 262144 | bytes 1310720 | tf_op jit(solution)/shard_map/exp | solution.py:80
  55.0 0.4 fusion
  55.4 0.2 pad_maximum_fusion
  55.7 0.1 collective-permute-start.7
  55.8 1.9 %collective-permute-done.7 = f32[256,4,128]{2,1,0:T(4,128)S(1)} collective-permute-done((f32[256,4,128]{2,1,0:T(4,128)S(1)}, f32[256,4,128]{2,1,0:T(4,128)S(1)}, u32[]{:S(2)}, u32[]{:S(2)}) %collective-permute-start.7) | collective-permute-done | bytes 524320 | tf_op jit(solution)/shard_map/ppermute | solution.py:134
  57.7 1.6 %fusion.2 = f32[256,4,128]{2,1,0:T(4,128)} fusion(f32[256,4,128]{2,1,0:T(4,128)S(1)} %collective-permute-done.7, f32[512,3,128]{2,1,0:T(4,128)S(1)} %fusion, f32[512,1,128]{2,1,0:T(1,128)S(1)} %get-tuple-element.18, pred[256]{0:T(512)(128)(4,1)S(1)} %get-tuple-element.11), kind=kLoop, calls=%fused_computation.7 | loop fusion | flops 262144 | bytes 2097408 | tf_op jit(solution)/shard_map/jit(_where)/select_n | solution.py:136
  (24 shorter events, 0.4 us)
Async XLA Ops:
  18.3 9.4 %collective-permute-start = (f32[130,4,128]{2,1,0:T(4,128)S(1)}, f32[130,4,128]{2,1,0:T(4,128)S(1)}, u32[]{:S(2)}, u32[]{:S(2)}) collective-permute-start(f32[130,4,128]{2,1,0:T(4,128)S(1)} %pad_maximum_fusion.1), channel_id=1, source_target_pairs={{0,4},{4,8},{8,12},{12,14},{14,10},{10,6},{6,2},{2,0},{1,5},{5,9},... | collective-permute-start | bytes 798728 | tf_op jit(solution)/shard_map/ppermute | solution.py:97
  21.4 9.7 %collective-permute-start.1 = (f32[130,4,128]{2,1,0:T(4,128)S(1)}, f32[130,4,128]{2,1,0:T(4,128)S(1)}, u32[]{:S(2)}, u32[]{:S(2)}) collective-permute-start(f32[130,4,128]{2,1,0:T(4,128)S(1)} %pad_maximum_fusion.1), channel_id=1, source_target_pairs={{4,0},{8,4},{12,8},{14,12},{10,14},{6,10},{2,6},{0,2},{5,1},{9,5},... | collective-permute-start | bytes 798728 | tf_op jit(solution)/shard_map/ppermute | solution.py:100
  27.8 7.6 %collective-permute-start.2 = (f32[130,4,128]{2,1,0:T(4,128)S(1)}, f32[130,4,128]{2,1,0:T(4,128)S(1)}, u32[]{:S(2)}, u32[]{:S(2)}) collective-permute-start(f32[130,4,128]{2,1,0:T(4,128)S(1)} %collective-permute-done), channel_id=1, source_target_pairs={{0,4},{4,8},{8,12},{12,14},{14,10},{10,6},{6,2},{2,0},{1,5},{5,9},... | collective-permute-start | bytes 798728 | tf_op jit(solution)/shard_map/ppermute | solution.py:97
  31.1 7.0 %collective-permute-start.3 = (f32[130,4,128]{2,1,0:T(4,128)S(1)}, f32[130,4,128]{2,1,0:T(4,128)S(1)}, u32[]{:S(2)}, u32[]{:S(2)}) collective-permute-start(f32[130,4,128]{2,1,0:T(4,128)S(1)} %collective-permute-done.1), channel_id=1, source_target_pairs={{4,0},{8,4},{12,8},{14,12},{10,14},{6,10},{2,6},{0,2},{5,1},{9,5},... | collective-permute-start | bytes 798728 | tf_op jit(solution)/shard_map/ppermute | solution.py:100
  35.3 6.7 %collective-permute-start.4 = (f32[130,4,128]{2,1,0:T(4,128)S(1)}, f32[130,4,128]{2,1,0:T(4,128)S(1)}, u32[]{:S(2)}, u32[]{:S(2)}) collective-permute-start(f32[130,4,128]{2,1,0:T(4,128)S(1)} %collective-permute-done.2), channel_id=1, source_target_pairs={{0,4},{4,8},{8,12},{12,14},{14,10},{10,6},{6,2},{2,0},{1,5},{5,9},... | collective-permute-start | bytes 798728 | tf_op jit(solution)/shard_map/ppermute | solution.py:97
  38.1 6.4 %collective-permute-start.5 = (f32[130,4,128]{2,1,0:T(4,128)S(1)}, f32[130,4,128]{2,1,0:T(4,128)S(1)}, u32[]{:S(2)}, u32[]{:S(2)}) collective-permute-start(f32[130,4,128]{2,1,0:T(4,128)S(1)} %collective-permute-done.3), channel_id=1, source_target_pairs={{4,0},{8,4},{12,8},{14,12},{10,14},{6,10},{2,6},{0,2},{5,1},{9,5},... | collective-permute-start | bytes 798728 | tf_op jit(solution)/shard_map/ppermute | solution.py:100
  42.0 6.4 %collective-permute-start.6 = (f32[130,4,128]{2,1,0:T(4,128)S(1)}, f32[130,4,128]{2,1,0:T(4,128)S(1)}, u32[]{:S(2)}, u32[]{:S(2)}) collective-permute-start(f32[130,4,128]{2,1,0:T(4,128)S(1)} %collective-permute-done.4), channel_id=1, source_target_pairs={{0,4},{4,8},{8,12},{12,14},{14,10},{10,6},{6,2},{2,0},{1,5},{5,9},... | collective-permute-start | bytes 798728 | tf_op jit(solution)/shard_map/ppermute | solution.py:97
  48.5 2.5 %copy-start = (f32[1040,4,128]{2,1,0:T(4,128)}, f32[1040,4,128]{2,1,0:T(4,128)S(1)}, u32[]{:S(2)}) copy-start(f32[1040,4,128]{2,1,0:T(4,128)S(1)} %constant_dynamic-update-slice_fusion) | copy-start | bytes 6389764
  55.7 2.0 %collective-permute-start.7 = (f32[256,4,128]{2,1,0:T(4,128)S(1)}, f32[256,4,128]{2,1,0:T(4,128)S(1)}, u32[]{:S(2)}, u32[]{:S(2)}) collective-permute-start(f32[256,4,128]{2,1,0:T(4,128)S(1)} %pad_maximum_fusion), channel_id=1, source_target_pairs={{0,1},{1,0},{2,3},{3,2},{4,5},{5,4},{6,7},{7,6},{8,9},{9,8},{10,11... | collective-permute-start | bytes 1572872 | tf_op jit(solution)/shard_map/ppermute | solution.py:134

commit v19 on v13

--- a/solution.py
+++ b/solution.py
@@ -8,7 +8,8 @@
 BLK = 256
 
 
-def render_kernel(absorb_ref, slope_ref, offset_ref, shown_ref, density_ref, out_ref):
+def render_kernel(absorb_ref, slope_ref, offset_ref, shown_ref, density_ref, slot_ref, out_ref):
+    del slot_ref
     block_rows = out_ref.shape[0]
     pixels = out_ref.shape[2]
     sample_count = density_ref.shape[0] // block_rows
@@ -39,7 +40,7 @@
     out_ref[:, 3, :] = jnp.where(visible, carry[1], 0.0)
 
 
-def render_layers(density_block, shown_rows, absorb, colour_slope, colour_offset, block_rows=16):
+def render_layers(density_block, shown_rows, absorb, colour_slope, colour_offset, slot, block_rows=16):
     brick_rows, sample_count, pixels = density_block.shape
     return pl.pallas_call(
         render_kernel,
@@ -50,10 +51,13 @@
             pl.BlockSpec(memory_space=pltpu.SMEM),
             pl.BlockSpec(memory_space=pltpu.SMEM),
             pl.BlockSpec((block_rows * sample_count, pixels), lambda i: (i, 0)),
+            pl.BlockSpec(memory_space=pl.ANY),
         ],
         out_specs=pl.BlockSpec((block_rows, 4, pixels), lambda i: (i, 0, 0)),
-        out_shape=jax.ShapeDtypeStruct((brick_rows, 4, pixels), jnp.float32),
-    )(absorb, colour_slope, colour_offset, shown_rows, density_block.reshape(brick_rows * sample_count, pixels))
+        out_shape=jax.ShapeDtypeStruct(slot.shape, jnp.float32),
+        input_output_aliases={5: 0},
+    )(absorb, colour_slope, colour_offset, shown_rows, density_block.reshape(brick_rows * sample_count, pixels),
+      slot)
 
 
 def composite_rows(flat, starts, counts, brick_ids, stride, image_rows):
@@ -112,12 +116,14 @@
     owner_rows = image_total // (depth_count * screen_count)
     start = foot_start[0, 0]
     shown = foot_rows[0, 0]
-    layers = render_layers(density[0, 0], foot_rows, extinction, colour_slope, colour_offset)
-    brick_rows, channels, pixels = layers.shape
+    brick_rows, pixels = density.shape[2], density.shape[4]
+    channels = 4
     lane = lax.broadcasted_iota(jnp.int32, (1, channels, pixels), 2)
     meta = jnp.where(lane == 0, start, jnp.where(lane == 1, shown, jnp.where(lane == 2, depth_index, 0)))
     stride = brick_rows + 2
-    own = jnp.concatenate([layers, meta.astype(jnp.float32), jnp.zeros_like(meta, jnp.float32)], axis=0)
+    slot = jnp.concatenate([jnp.zeros((brick_rows, channels, pixels), jnp.float32), meta.astype(jnp.float32),
+                            jnp.zeros((1, channels, pixels), jnp.float32)], axis=0)
+    own = render_layers(density[0, 0], foot_rows, extinction, colour_slope, colour_offset, slot)
     flat = ring_gather(own, depth_count)
     meta_rows = flat.reshape(depth_count, stride, channels, pixels)[:, brick_rows, 0, :3]
     starts = meta_rows[:, 0].astype(jnp.int32)

time: 59.6 us -> 58.8 us (0.987)
    ppermute x4, waiting for transfers between devices: 17.5 us -> 14.7 us  [ring_gather(): ahead = lax.ppermute(ahead, 'depth', forward)]
    ppermute x3, waiting for transfers between devices: 1.91 us -> 4.26 us  [ring_gather(): behind = lax.ppermute(behind, 'depth', backward)]
    unnamed x11 -> x10, local copies, waits for them, and re-layouts: 1.27 us -> 1.27 us
  transfers between devices with their start and end apart: 8 -> 8, of which waited for: 7 -> 7; matrix products, arithmetic and copies ran while one was open for 3% -> 5% of each run, Pallas kernels for 0% -> 0%
where the time goes in v19:
time: 58.8 us; the launch traced here: 58.5 us
  waiting for transfers between devices  20.8 us (35%)
  Pallas kernels  14.4 us (24%)
  starting transfers between devices  8.59 us (15%)
  local copies, waits for them, and re-layouts  7.35 us (12%)
  other arithmetic  5.23 us (9%)
  between operations  2.14 us (4%)
    ppermute x4, waiting for transfers between devices, ring_gather(): ahead = lax.ppermute(ahead, 'depth', forward)  14.7 us
    pallas_call x1, Pallas kernels, render_layers(): pl.pallas_call(render_kernel, grid=(brick_rows // block_rows,), in_specs=...  14.4 us
    ppermute x4, starting transfers between devices, ring_gather(): ahead = lax.ppermute(ahead, 'depth', forward)  7.69 us
    ppermute x3, waiting for transfers between devices, ring_gather(): behind = lax.ppermute(behind, 'depth', backward)  4.26 us
    gather x1, local copies, waits for them, and re-layouts, composite_rows(): front_rows = jnp.take(flat, front_idx, axis=0, mode='clip')  3.11 us
    gather x1, local copies, waits for them, and re-layouts, composite_rows(): back_rows = jnp.take(flat, back_idx, axis=0, mode='clip')  2.07 us
    ppermute x1, waiting for transfers between devices, on_device(): received = lax.ppermute(for_partner, 'screen', [(0, 1), (1, 0)])  1.9 us
    select_n x1, other arithmetic, on_device(): return jnp.where(in_my_half[:, None, None], mine, received)  1.62 us
  transfers between devices with their start and end apart: 8, of which 7 were waited for; matrix products, arithmetic and copies ran while one was open for 5% of the time, Pallas kernels for 0%

profile of v19, /device:TPU:0, one launch (start us, length us, event | category | flops | bytes accessed | tf_op | source)
XLA Modules:
  0.0 58.5 jit_solution(13961314371214428225)
XLA Ops:
  1.3 0.1 pad.6.clone
  2.1 1.0 %maximum_maximum_fusion.slot_ref = f32[130,4,128]{2,1,0:T(4,128)} fusion(f32[1,4,128]{2,1,0:T(4,128)S(1)} %select_convert_fusion, f32[130]{0:T(256)S(1)} %pad.6.clone, f32[130]{0:T(256)S(1)} %pad.4.clone), kind=kLoop, calls=%fused_computation.9 | loop fusion | flops 133120 | bytes 269328 | tf_op jit(solution)/shard_map/concatenate | solution.py:124
  3.1 14.4 %shard_map.73 = f32[130,4,128]{2,1,0:T(4,128)} custom-call(f32[1]{0:T(128)S(6)} %copy.24.absorb_ref, f32[3]{0:T(128)} %slope_ref.1, f32[3]{0:T(128)} %offset_ref.1, s32[1,1]{1,0:T(1,128)} %copy.23.shown_ref, f32[16384,128]{1,0:T(8,128)} %bitcast.16, f32[130,4,128]{2,1,0:T(4,128)} %maximum_maximum_fusion.slot_ref), custom_call_target="tpu_custom_call", output_to_operand_aliasing={{}: (5, {})} | custom-call | tf_op jit(solution)/shard_map/pallas_call | solution.py:45
  17.5 3.0 %collective-permute-start = (f32[130,4,128]{2,1,0:T(4,128)}, f32[130,4,128]{2,1,0:T(4,128)S(1)}, u32[]{:S(2)}, u32[]{:S(2)}) collective-permute-start(f32[130,4,128]{2,1,0:T(4,128)} %shard_map.73), channel_id=1, source_target_pairs={{0,4},{4,8},{8,12},{12,14},{14,10},{10,6},{6,2},{2,0},{1,5},{5,9},... | collective-permute-start | bytes 798728 | tf_op jit(solution)/shard_map/ppermute | solution.py:101
  20.5 0.0 collective-permute-start.1
  20.5 6.5 %collective-permute-done = f32[130,4,128]{2,1,0:T(4,128)S(1)} collective-permute-done((f32[130,4,128]{2,1,0:T(4,128)}, f32[130,4,128]{2,1,0:T(4,128)S(1)}, u32[]{:S(2)}, u32[]{:S(2)}) %collective-permute-start) | collective-permute-done | bytes 266272 | tf_op jit(solution)/shard_map/ppermute | solution.py:101
  27.1 1.8 %collective-permute-start.2 = (f32[130,4,128]{2,1,0:T(4,128)S(1)}, f32[130,4,128]{2,1,0:T(4,128)S(1)}, u32[]{:S(2)}, u32[]{:S(2)}) collective-permute-start(f32[130,4,128]{2,1,0:T(4,128)S(1)} %collective-permute-done), channel_id=1, source_target_pairs={{0,4},{4,8},{8,12},{12,14},{14,10},{10,6},{6,2},{2,0},{1,5},{5,9},... | collective-permute-start | bytes 798728 | tf_op jit(solution)/shard_map/ppermute | solution.py:101
  28.9 0.8 %fusion.8 = (pred[256]{0:T(512)(128)(4,1)S(1)}, s32[256]{0:T(256)S(1)}) fusion(s32[]{:T(128)S(6)} %axis_index.25, s32[4096]{0:T(1024)} %param.13, s32[]{:T(128)S(6)} %select_n.98), kind=kLoop, calls=%fused_computation.49 | loop fusion | flops 4096 | bytes 2312 | tf_op jit(solution)/shard_map/eq | solution.py:141
  29.6 0.8 %dynamic_slice.7 = s32[256]{0:T(256)S(1)} dynamic-slice(s32[4096]{0:T(1024)} %param.13, s32[]{:T(128)S(6)} %select_n.103), dynamic_slice_sizes={256} | dynamic-slice | bytes 2052 | tf_op jit(solution)/shard_map/dynamic_slice | solution.py:135
  30.4 1.0 %constant_dynamic-update-slice_fusion.7 = f32[1040,4,128]{2,1,0:T(4,128)S(1)} fusion(f32[130,4,128]{2,1,0:T(4,128)} %shard_map.73), kind=kLoop, calls=%fused_computation.27 | loop fusion | bytes 532480
  31.4 0.0 collective-permute-done.1
  31.4 0.3 collective-permute-start.3
  31.7 3.0 %collective-permute-done.2 = f32[130,4,128]{2,1,0:T(4,128)S(1)} collective-permute-done((f32[130,4,128]{2,1,0:T(4,128)S(1)}, f32[130,4,128]{2,1,0:T(4,128)S(1)}, u32[]{:S(2)}, u32[]{:S(2)}) %collective-permute-start.2) | collective-permute-done | bytes 266272 | tf_op jit(solution)/shard_map/ppermute | solution.py:101
  34.6 1.5 %collective-permute-start.4 = (f32[130,4,128]{2,1,0:T(4,128)S(1)}, f32[130,4,128]{2,1,0:T(4,128)S(1)}, u32[]{:S(2)}, u32[]{:S(2)}) collective-permute-start(f32[130,4,128]{2,1,0:T(4,128)S(1)} %collective-permute-done.2), channel_id=1, source_target_pairs={{0,4},{4,8},{8,12},{12,14},{14,10},{10,6},{6,2},{2,0},{1,5},{5,9},... | collective-permute-start | bytes 798728 | tf_op jit(solution)/shard_map/ppermute | solution.py:101
  36.2 2.2 %collective-permute-done.3 = f32[130,4,128]{2,1,0:T(4,128)S(1)} collective-permute-done((f32[130,4,128]{2,1,0:T(4,128)S(1)}, f32[130,4,128]{2,1,0:T(4,128)S(1)}, u32[]{:S(2)}, u32[]{:S(2)}) %collective-permute-start.3) | collective-permute-done | bytes 266272 | tf_op jit(solution)/shard_map/ppermute | solution.py:104
  38.4 0.5 collective-permute-start.5
  39.0 2.3 %collective-permute-done.4 = f32[130,4,128]{2,1,0:T(4,128)S(1)} collective-permute-done((f32[130,4,128]{2,1,0:T(4,128)S(1)}, f32[130,4,128]{2,1,0:T(4,128)S(1)}, u32[]{:S(2)}, u32[]{:S(2)}) %collective-permute-start.4) | collective-permute-done | bytes 266272 | tf_op jit(solution)/shard_map/ppermute | solution.py:101
  41.3 1.4 %collective-permute-start.6 = (f32[130,4,128]{2,1,0:T(4,128)S(1)}, f32[130,4,128]{2,1,0:T(4,128)S(1)}, u32[]{:S(2)}, u32[]{:S(2)}) collective-permute-start(f32[130,4,128]{2,1,0:T(4,128)S(1)} %collective-permute-done.4), channel_id=1, source_target_pairs={{0,4},{4,8},{8,12},{12,14},{14,10},{10,6},{6,2},{2,0},{1,5},{5,9},... | collective-permute-start | bytes 798728 | tf_op jit(solution)/shard_map/ppermute | solution.py:101
  42.8 2.1 %collective-permute-done.5 = f32[130,4,128]{2,1,0:T(4,128)S(1)} collective-permute-done((f32[130,4,128]{2,1,0:T(4,128)S(1)}, f32[130,4,128]{2,1,0:T(4,128)S(1)}, u32[]{:S(2)}, u32[]{:S(2)}) %collective-permute-start.5) | collective-permute-done | bytes 266272 | tf_op jit(solution)/shard_map/ppermute | solution.py:104
  44.9 2.9 %collective-permute-done.6 = f32[130,4,128]{2,1,0:T(4,128)S(1)} collective-permute-done((f32[130,4,128]{2,1,0:T(4,128)S(1)}, f32[130,4,128]{2,1,0:T(4,128)S(1)}, u32[]{:S(2)}, u32[]{:S(2)}) %collective-permute-start.6) | collective-permute-done | bytes 266272 | tf_op jit(solution)/shard_map/ppermute | solution.py:101
  47.8 0.1 copy.13
  47.9 0.1 select_reduce_fusion.2
  48.0 0.1 fusion.9
  48.1 0.1 select_reduce_fusion.1
  48.2 2.1 %gather_fusion.1 = f32[512,4,128]{2,1,0:T(4,128)S(1)} fusion(f32[1040,4,128]{2,1,0:T(4,128)S(1)} %constant_dynamic-update-slice_fusion, s32[1024]{0:T(1024)S(1)} %pad_clamp_fusion), kind=kCustom, calls=%fused_computation.1 | custom fusion | bytes 2099200 | tf_op jit(solution)/shard_map/jit(_take)/gather | solution.py:81
  50.3 3.1 %gather_fusion = f32[512,4,128]{2,1,0:T(4,128)S(1)} fusion(f32[1040,4,128]{2,1,0:T(4,128)} %copy-done, s32[1024]{0:T(1024)S(1)} %pad_clamp_fusion.1), kind=kCustom, calls=%fused_computation | custom fusion | bytes 2099200 | tf_op jit(solution)/shard_map/jit(_take)/gather | solution.py:82
  53.4 0.8 %negate_exponential_fusion = (f32[512,1,128]{2,1,0:T(1,128)S(1)}, f32[512,1,128]{2,1,0:T(1,128)S(1)}) fusion(f32[512,4,128]{2,1,0:T(4,128)S(1)} %gather_fusion, f32[512,1,128]{2,1,0:T(1,128)S(1)} %bitcast.18, f32[512,4,128]{2,1,0:T(4,128)S(1)} %gather_fusion.1), kind=kLoop, calls=%fused_computation.13 | loop fusion | flops 262144 | bytes 1310720 | tf_op jit(solution)/shard_map/exp | solution.py:84
  54.3 0.4 fusion
  54.7 0.2 pad_maximum_fusion
  54.9 0.1 collective-permute-start.7
  55.0 1.9 %collective-permute-done.7 = f32[256,4,128]{2,1,0:T(4,128)S(1)} collective-permute-done((f32[256,4,128]{2,1,0:T(4,128)S(1)}, f32[256,4,128]{2,1,0:T(4,128)S(1)}, u32[]{:S(2)}, u32[]{:S(2)}) %collective-permute-start.7) | collective-permute-done | bytes 524320 | tf_op jit(solution)/shard_map/ppermute | solution.py:140
  56.9 1.6 %fusion.2 = f32[256,4,128]{2,1,0:T(4,128)} fusion(f32[256,4,128]{2,1,0:T(4,128)S(1)} %collective-permute-done.7, f32[512,3,128]{2,1,0:T(4,128)S(1)} %fusion, f32[512,1,128]{2,1,0:T(1,128)S(1)} %get-tuple-element.16, pred[256]{0:T(512)(128)(4,1)S(1)} %get-tuple-element.11), kind=kLoop, calls=%fused_computation.7 | loop fusion | flops 262144 | bytes 2097408 | tf_op jit(solution)/shard_map/jit(_where)/select_n | solution.py:142
  (23 shorter events, 0.4 us)
Async XLA Ops:
  17.5 9.6 %collective-permute-start = (f32[130,4,128]{2,1,0:T(4,128)}, f32[130,4,128]{2,1,0:T(4,128)S(1)}, u32[]{:S(2)}, u32[]{:S(2)}) collective-permute-start(f32[130,4,128]{2,1,0:T(4,128)} %shard_map.73), channel_id=1, source_target_pairs={{0,4},{4,8},{8,12},{12,14},{14,10},{10,6},{6,2},{2,0},{1,5},{5,9},... | collective-permute-start | bytes 798728 | tf_op jit(solution)/shard_map/ppermute | solution.py:101
  20.5 10.8 %collective-permute-start.1 = (f32[130,4,128]{2,1,0:T(4,128)}, f32[130,4,128]{2,1,0:T(4,128)S(1)}, u32[]{:S(2)}, u32[]{:S(2)}) collective-permute-start(f32[130,4,128]{2,1,0:T(4,128)} %shard_map.73), channel_id=1, source_target_pairs={{4,0},{8,4},{12,8},{14,12},{10,14},{6,10},{2,6},{0,2},{5,1},{9,5},... | collective-permute-start | bytes 798728 | tf_op jit(solution)/shard_map/ppermute | solution.py:104
  27.1 7.6 %collective-permute-start.2 = (f32[130,4,128]{2,1,0:T(4,128)S(1)}, f32[130,4,128]{2,1,0:T(4,128)S(1)}, u32[]{:S(2)}, u32[]{:S(2)}) collective-permute-start(f32[130,4,128]{2,1,0:T(4,128)S(1)} %collective-permute-done), channel_id=1, source_target_pairs={{0,4},{4,8},{8,12},{12,14},{14,10},{10,6},{6,2},{2,0},{1,5},{5,9},... | collective-permute-start | bytes 798728 | tf_op jit(solution)/shard_map/ppermute | solution.py:101
  31.4 7.0 %collective-permute-start.3 = (f32[130,4,128]{2,1,0:T(4,128)S(1)}, f32[130,4,128]{2,1,0:T(4,128)S(1)}, u32[]{:S(2)}, u32[]{:S(2)}) collective-permute-start(f32[130,4,128]{2,1,0:T(4,128)S(1)} %collective-permute-done.1), channel_id=1, source_target_pairs={{4,0},{8,4},{12,8},{14,12},{10,14},{6,10},{2,6},{0,2},{5,1},{9,5},... | collective-permute-start | bytes 798728 | tf_op jit(solution)/shard_map/ppermute | solution.py:104
  34.6 6.7 %collective-permute-start.4 = (f32[130,4,128]{2,1,0:T(4,128)S(1)}, f32[130,4,128]{2,1,0:T(4,128)S(1)}, u32[]{:S(2)}, u32[]{:S(2)}) collective-permute-start(f32[130,4,128]{2,1,0:T(4,128)S(1)} %collective-permute-done.2), channel_id=1, source_target_pairs={{0,4},{4,8},{8,12},{12,14},{14,10},{10,6},{6,2},{2,0},{1,5},{5,9},... | collective-permute-start | bytes 798728 | tf_op jit(solution)/shard_map/ppermute | solution.py:101
  38.4 6.4 %collective-permute-start.5 = (f32[130,4,128]{2,1,0:T(4,128)S(1)}, f32[130,4,128]{2,1,0:T(4,128)S(1)}, u32[]{:S(2)}, u32[]{:S(2)}) collective-permute-start(f32[130,4,128]{2,1,0:T(4,128)S(1)} %collective-permute-done.3), channel_id=1, source_target_pairs={{4,0},{8,4},{12,8},{14,12},{10,14},{6,10},{2,6},{0,2},{5,1},{9,5},... | collective-permute-start | bytes 798728 | tf_op jit(solution)/shard_map/ppermute | solution.py:104
  41.3 6.4 %collective-permute-start.6 = (f32[130,4,128]{2,1,0:T(4,128)S(1)}, f32[130,4,128]{2,1,0:T(4,128)S(1)}, u32[]{:S(2)}, u32[]{:S(2)}) collective-permute-start(f32[130,4,128]{2,1,0:T(4,128)S(1)} %collective-permute-done.4), channel_id=1, source_target_pairs={{0,4},{4,8},{8,12},{12,14},{14,10},{10,6},{6,2},{2,0},{1,5},{5,9},... | collective-permute-start | bytes 798728 | tf_op jit(solution)/shard_map/ppermute | solution.py:101
  47.8 2.5 %copy-start = (f32[1040,4,128]{2,1,0:T(4,128)}, f32[1040,4,128]{2,1,0:T(4,128)S(1)}, u32[]{:S(2)}) copy-start(f32[1040,4,128]{2,1,0:T(4,128)S(1)} %constant_dynamic-update-slice_fusion) | copy-start | bytes 6389764
  54.9 2.0 %collective-permute-start.7 = (f32[256,4,128]{2,1,0:T(4,128)S(1)}, f32[256,4,128]{2,1,0:T(4,128)S(1)}, u32[]{:S(2)}, u32[]{:S(2)}) collective-permute-start(f32[256,4,128]{2,1,0:T(4,128)S(1)} %pad_maximum_fusion), channel_id=1, source_target_pairs={{0,1},{1,0},{2,3},{3,2},{4,5},{5,4},{6,7},{7,6},{8,9},{9,8},{10,11... | collective-permute-start | bytes 1572872 | tf_op jit(solution)/shard_map/ppermute | solution.py:140

commit v20 on v19

--- a/solution.py
+++ b/solution.py
@@ -32,7 +32,7 @@
 
     zeros = jnp.zeros((block_rows, pixels), jnp.float32)
     carry = (jnp.full((block_rows, pixels), 0.5, jnp.float32), zeros, zeros, zeros, zeros, zeros)
-    carry = lax.fori_loop(0, sample_count, one_step, carry, unroll=16)
+    carry = lax.fori_loop(0, sample_count, one_step, carry, unroll=32)
     row_ids = pl.program_id(0) * block_rows + lax.broadcasted_iota(jnp.int32, (block_rows, pixels), 0)
     visible = row_ids < shown
     for channel in range(3):

time: 58.8 us -> 58.4 us (level)
  no operation moved by 1% of the time
where the time goes in v20:
time: 58.4 us; the launch traced here: 58.2 us
  waiting for transfers between devices  20.8 us (36%)
  Pallas kernels  14 us (24%)
  starting transfers between devices  8.59 us (15%)
  local copies, waits for them, and re-layouts  7.35 us (13%)
  other arithmetic  5.23 us (9%)
  between operations  2.14 us (4%)
    ppermute x4, waiting for transfers between devices, ring_gather(): ahead = lax.ppermute(ahead, 'depth', forward)  14.7 us
    pallas_call x1, Pallas kernels, render_layers(): pl.pallas_call(render_kernel, grid=(brick_rows // block_rows,), in_specs=...  14 us
    ppermute x4, starting transfers between devices, ring_gather(): ahead = lax.ppermute(ahead, 'depth', forward)  7.69 us
    ppermute x3, waiting for transfers between devices, ring_gather(): behind = lax.ppermute(behind, 'depth', backward)  4.26 us
    gather x1, local copies, waits for them, and re-layouts, composite_rows(): front_rows = jnp.take(flat, front_idx, axis=0, mode='clip')  3.11 us
    gather x1, local copies, waits for them, and re-layouts, composite_rows(): back_rows = jnp.take(flat, back_idx, axis=0, mode='clip')  2.07 us
    ppermute x1, waiting for transfers between devices, on_device(): received = lax.ppermute(for_partner, 'screen', [(0, 1), (1, 0)])  1.9 us
    select_n x1, other arithmetic, on_device(): return jnp.where(in_my_half[:, None, None], mine, received)  1.62 us
  transfers between devices with their start and end apart: 8, of which 7 were waited for; matrix products, arithmetic and copies ran while one was open for 5% of the time, Pallas kernels for 0%

profile of v20, /device:TPU:0, one launch (start us, length us, event | category | flops | bytes accessed | tf_op | source)
XLA Modules:
  0.0 58.2 jit_solution(3883471769769744280)
XLA Ops:
  1.3 0.1 pad.6.clone
  2.1 1.0 %maximum_maximum_fusion.slot_ref = f32[130,4,128]{2,1,0:T(4,128)} fusion(f32[1,4,128]{2,1,0:T(4,128)S(1)} %select_convert_fusion, f32[130]{0:T(256)S(1)} %pad.6.clone, f32[130]{0:T(256)S(1)} %pad.4.clone), kind=kLoop, calls=%fused_computation.9 | loop fusion | flops 133120 | bytes 269328 | tf_op jit(solution)/shard_map/concatenate | solution.py:124
  3.1 14.0 %shard_map.73 = f32[130,4,128]{2,1,0:T(4,128)} custom-call(f32[1]{0:T(128)S(6)} %copy.24.absorb_ref, f32[3]{0:T(128)} %slope_ref.1, f32[3]{0:T(128)} %offset_ref.1, s32[1,1]{1,0:T(1,128)} %copy.23.shown_ref, f32[16384,128]{1,0:T(8,128)} %bitcast.16, f32[130,4,128]{2,1,0:T(4,128)} %maximum_maximum_fusion.slot_ref), custom_call_target="tpu_custom_call", output_to_operand_aliasing={{}: (5, {})} | custom-call | tf_op jit(solution)/shard_map/pallas_call | solution.py:45
  17.1 3.0 %collective-permute-start = (f32[130,4,128]{2,1,0:T(4,128)}, f32[130,4,128]{2,1,0:T(4,128)S(1)}, u32[]{:S(2)}, u32[]{:S(2)}) collective-permute-start(f32[130,4,128]{2,1,0:T(4,128)} %shard_map.73), channel_id=1, source_target_pairs={{0,4},{4,8},{8,12},{12,14},{14,10},{10,6},{6,2},{2,0},{1,5},{5,9},... | collective-permute-start | bytes 798728 | tf_op jit(solution)/shard_map/ppermute | solution.py:101
  20.2 0.0 collective-permute-start.1
  20.2 6.5 %collective-permute-done = f32[130,4,128]{2,1,0:T(4,128)S(1)} collective-permute-done((f32[130,4,128]{2,1,0:T(4,128)}, f32[130,4,128]{2,1,0:T(4,128)S(1)}, u32[]{:S(2)}, u32[]{:S(2)}) %collective-permute-start) | collective-permute-done | bytes 266272 | tf_op jit(solution)/shard_map/ppermute | solution.py:101
  26.7 1.8 %collective-permute-start.2 = (f32[130,4,128]{2,1,0:T(4,128)S(1)}, f32[130,4,128]{2,1,0:T(4,128)S(1)}, u32[]{:S(2)}, u32[]{:S(2)}) collective-permute-start(f32[130,4,128]{2,1,0:T(4,128)S(1)} %collective-permute-done), channel_id=1, source_target_pairs={{0,4},{4,8},{8,12},{12,14},{14,10},{10,6},{6,2},{2,0},{1,5},{5,9},... | collective-permute-start | bytes 798728 | tf_op jit(solution)/shard_map/ppermute | solution.py:101
  28.5 0.8 %fusion.8 = (pred[256]{0:T(512)(128)(4,1)S(1)}, s32[256]{0:T(256)S(1)}) fusion(s32[]{:T(128)S(6)} %axis_index.25, s32[4096]{0:T(1024)} %param.13, s32[]{:T(128)S(6)} %select_n.98), kind=kLoop, calls=%fused_computation.49 | loop fusion | flops 4096 | bytes 2312 | tf_op jit(solution)/shard_map/eq | solution.py:141
  29.3 0.8 %dynamic_slice.7 = s32[256]{0:T(256)S(1)} dynamic-slice(s32[4096]{0:T(1024)} %param.13, s32[]{:T(128)S(6)} %select_n.103), dynamic_slice_sizes={256} | dynamic-slice | bytes 2052 | tf_op jit(solution)/shard_map/dynamic_slice | solution.py:135
  30.0 1.0 %constant_dynamic-update-slice_fusion.7 = f32[1040,4,128]{2,1,0:T(4,128)S(1)} fusion(f32[130,4,128]{2,1,0:T(4,128)} %shard_map.73), kind=kLoop, calls=%fused_computation.27 | loop fusion | bytes 532480
  31.0 0.0 collective-permute-done.1
  31.0 0.3 collective-permute-start.3
  31.3 3.0 %collective-permute-done.2 = f32[130,4,128]{2,1,0:T(4,128)S(1)} collective-permute-done((f32[130,4,128]{2,1,0:T(4,128)S(1)}, f32[130,4,128]{2,1,0:T(4,128)S(1)}, u32[]{:S(2)}, u32[]{:S(2)}) %collective-permute-start.2) | collective-permute-done | bytes 266272 | tf_op jit(solution)/shard_map/ppermute | solution.py:101
  34.3 1.5 %collective-permute-start.4 = (f32[130,4,128]{2,1,0:T(4,128)S(1)}, f32[130,4,128]{2,1,0:T(4,128)S(1)}, u32[]{:S(2)}, u32[]{:S(2)}) collective-permute-start(f32[130,4,128]{2,1,0:T(4,128)S(1)} %collective-permute-done.2), channel_id=1, source_target_pairs={{0,4},{4,8},{8,12},{12,14},{14,10},{10,6},{6,2},{2,0},{1,5},{5,9},... | collective-permute-start | bytes 798728 | tf_op jit(solution)/shard_map/ppermute | solution.py:101
  35.9 2.2 %collective-permute-done.3 = f32[130,4,128]{2,1,0:T(4,128)S(1)} collective-permute-done((f32[130,4,128]{2,1,0:T(4,128)S(1)}, f32[130,4,128]{2,1,0:T(4,128)S(1)}, u32[]{:S(2)}, u32[]{:S(2)}) %collective-permute-start.3) | collective-permute-done | bytes 266272 | tf_op jit(solution)/shard_map/ppermute | solution.py:104
  38.1 0.5 collective-permute-start.5
  38.6 2.3 %collective-permute-done.4 = f32[130,4,128]{2,1,0:T(4,128)S(1)} collective-permute-done((f32[130,4,128]{2,1,0:T(4,128)S(1)}, f32[130,4,128]{2,1,0:T(4,128)S(1)}, u32[]{:S(2)}, u32[]{:S(2)}) %collective-permute-start.4) | collective-permute-done | bytes 266272 | tf_op jit(solution)/shard_map/ppermute | solution.py:101
  40.9 1.4 %collective-permute-start.6 = (f32[130,4,128]{2,1,0:T(4,128)S(1)}, f32[130,4,128]{2,1,0:T(4,128)S(1)}, u32[]{:S(2)}, u32[]{:S(2)}) collective-permute-start(f32[130,4,128]{2,1,0:T(4,128)S(1)} %collective-permute-done.4), channel_id=1, source_target_pairs={{0,4},{4,8},{8,12},{12,14},{14,10},{10,6},{6,2},{2,0},{1,5},{5,9},... | collective-permute-start | bytes 798728 | tf_op jit(solution)/shard_map/ppermute | solution.py:101
  42.4 2.1 %collective-permute-done.5 = f32[130,4,128]{2,1,0:T(4,128)S(1)} collective-permute-done((f32[130,4,128]{2,1,0:T(4,128)S(1)}, f32[130,4,128]{2,1,0:T(4,128)S(1)}, u32[]{:S(2)}, u32[]{:S(2)}) %collective-permute-start.5) | collective-permute-done | bytes 266272 | tf_op jit(solution)/shard_map/ppermute | solution.py:104
  44.5 2.9 %collective-permute-done.6 = f32[130,4,128]{2,1,0:T(4,128)S(1)} collective-permute-done((f32[130,4,128]{2,1,0:T(4,128)S(1)}, f32[130,4,128]{2,1,0:T(4,128)S(1)}, u32[]{:S(2)}, u32[]{:S(2)}) %collective-permute-start.6) | collective-permute-done | bytes 266272 | tf_op jit(solution)/shard_map/ppermute | solution.py:101
  47.4 0.1 copy.13
  47.5 0.1 select_reduce_fusion.2
  47.6 0.1 fusion.9
  47.7 0.1 select_reduce_fusion.1
  47.8 2.1 %gather_fusion.1 = f32[512,4,128]{2,1,0:T(4,128)S(1)} fusion(f32[1040,4,128]{2,1,0:T(4,128)S(1)} %constant_dynamic-update-slice_fusion, s32[1024]{0:T(1024)S(1)} %pad_clamp_fusion), kind=kCustom, calls=%fused_computation.1 | custom fusion | bytes 2099200 | tf_op jit(solution)/shard_map/jit(_take)/gather | solution.py:81
  49.9 3.1 %gather_fusion = f32[512,4,128]{2,1,0:T(4,128)S(1)} fusion(f32[1040,4,128]{2,1,0:T(4,128)} %copy-done, s32[1024]{0:T(1024)S(1)} %pad_clamp_fusion.1), kind=kCustom, calls=%fused_computation | custom fusion | bytes 2099200 | tf_op jit(solution)/shard_map/jit(_take)/gather | solution.py:82
  53.1 0.8 %negate_exponential_fusion = (f32[512,1,128]{2,1,0:T(1,128)S(1)}, f32[512,1,128]{2,1,0:T(1,128)S(1)}) fusion(f32[512,4,128]{2,1,0:T(4,128)S(1)} %gather_fusion, f32[512,1,128]{2,1,0:T(1,128)S(1)} %bitcast.18, f32[512,4,128]{2,1,0:T(4,128)S(1)} %gather_fusion.1), kind=kLoop, calls=%fused_computation.13 | loop fusion | flops 262144 | bytes 1310720 | tf_op jit(solution)/shard_map/exp | solution.py:84
  53.9 0.4 fusion
  54.3 0.2 pad_maximum_fusion
  54.6 0.1 collective-permute-start.7
  54.6 1.9 %collective-permute-done.7 = f32[256,4,128]{2,1,0:T(4,128)S(1)} collective-permute-done((f32[256,4,128]{2,1,0:T(4,128)S(1)}, f32[256,4,128]{2,1,0:T(4,128)S(1)}, u32[]{:S(2)}, u32[]{:S(2)}) %collective-permute-start.7) | collective-permute-done | bytes 524320 | tf_op jit(solution)/shard_map/ppermute | solution.py:140
  56.5 1.6 %fusion.2 = f32[256,4,128]{2,1,0:T(4,128)} fusion(f32[256,4,128]{2,1,0:T(4,128)S(1)} %collective-permute-done.7, f32[512,3,128]{2,1,0:T(4,128)S(1)} %fusion, f32[512,1,128]{2,1,0:T(1,128)S(1)} %get-tuple-element.16, pred[256]{0:T(512)(128)(4,1)S(1)} %get-tuple-element.11), kind=kLoop, calls=%fused_computation.7 | loop fusion | flops 262144 | bytes 2097408 | tf_op jit(solution)/shard_map/jit(_where)/select_n | solution.py:142
  (23 shorter events, 0.4 us)
Async XLA Ops:
  17.1 9.6 %collective-permute-start = (f32[130,4,128]{2,1,0:T(4,128)}, f32[130,4,128]{2,1,0:T(4,128)S(1)}, u32[]{:S(2)}, u32[]{:S(2)}) collective-permute-start(f32[130,4,128]{2,1,0:T(4,128)} %shard_map.73), channel_id=1, source_target_pairs={{0,4},{4,8},{8,12},{12,14},{14,10},{10,6},{6,2},{2,0},{1,5},{5,9},... | collective-permute-start | bytes 798728 | tf_op jit(solution)/shard_map/ppermute | solution.py:101
  20.2 10.8 %collective-permute-start.1 = (f32[130,4,128]{2,1,0:T(4,128)}, f32[130,4,128]{2,1,0:T(4,128)S(1)}, u32[]{:S(2)}, u32[]{:S(2)}) collective-permute-start(f32[130,4,128]{2,1,0:T(4,128)} %shard_map.73), channel_id=1, source_target_pairs={{4,0},{8,4},{12,8},{14,12},{10,14},{6,10},{2,6},{0,2},{5,1},{9,5},... | collective-permute-start | bytes 798728 | tf_op jit(solution)/shard_map/ppermute | solution.py:104
  26.7 7.6 %collective-permute-start.2 = (f32[130,4,128]{2,1,0:T(4,128)S(1)}, f32[130,4,128]{2,1,0:T(4,128)S(1)}, u32[]{:S(2)}, u32[]{:S(2)}) collective-permute-start(f32[130,4,128]{2,1,0:T(4,128)S(1)} %collective-permute-done), channel_id=1, source_target_pairs={{0,4},{4,8},{8,12},{12,14},{14,10},{10,6},{6,2},{2,0},{1,5},{5,9},... | collective-permute-start | bytes 798728 | tf_op jit(solution)/shard_map/ppermute | solution.py:101
  31.0 7.0 %collective-permute-start.3 = (f32[130,4,128]{2,1,0:T(4,128)S(1)}, f32[130,4,128]{2,1,0:T(4,128)S(1)}, u32[]{:S(2)}, u32[]{:S(2)}) collective-permute-start(f32[130,4,128]{2,1,0:T(4,128)S(1)} %collective-permute-done.1), channel_id=1, source_target_pairs={{4,0},{8,4},{12,8},{14,12},{10,14},{6,10},{2,6},{0,2},{5,1},{9,5},... | collective-permute-start | bytes 798728 | tf_op jit(solution)/shard_map/ppermute | solution.py:104
  34.3 6.7 %collective-permute-start.4 = (f32[130,4,128]{2,1,0:T(4,128)S(1)}, f32[130,4,128]{2,1,0:T(4,128)S(1)}, u32[]{:S(2)}, u32[]{:S(2)}) collective-permute-start(f32[130,4,128]{2,1,0:T(4,128)S(1)} %collective-permute-done.2), channel_id=1, source_target_pairs={{0,4},{4,8},{8,12},{12,14},{14,10},{10,6},{6,2},{2,0},{1,5},{5,9},... | collective-permute-start | bytes 798728 | tf_op jit(solution)/shard_map/ppermute | solution.py:101
  38.1 6.4 %collective-permute-start.5 = (f32[130,4,128]{2,1,0:T(4,128)S(1)}, f32[130,4,128]{2,1,0:T(4,128)S(1)}, u32[]{:S(2)}, u32[]{:S(2)}) collective-permute-start(f32[130,4,128]{2,1,0:T(4,128)S(1)} %collective-permute-done.3), channel_id=1, source_target_pairs={{4,0},{8,4},{12,8},{14,12},{10,14},{6,10},{2,6},{0,2},{5,1},{9,5},... | collective-permute-start | bytes 798728 | tf_op jit(solution)/shard_map/ppermute | solution.py:104
  40.9 6.4 %collective-permute-start.6 = (f32[130,4,128]{2,1,0:T(4,128)S(1)}, f32[130,4,128]{2,1,0:T(4,128)S(1)}, u32[]{:S(2)}, u32[]{:S(2)}) collective-permute-start(f32[130,4,128]{2,1,0:T(4,128)S(1)} %collective-permute-done.4), channel_id=1, source_target_pairs={{0,4},{4,8},{8,12},{12,14},{14,10},{10,6},{6,2},{2,0},{1,5},{5,9},... | collective-permute-start | bytes 798728 | tf_op jit(solution)/shard_map/ppermute | solution.py:101
  47.4 2.5 %copy-start = (f32[1040,4,128]{2,1,0:T(4,128)}, f32[1040,4,128]{2,1,0:T(4,128)S(1)}, u32[]{:S(2)}) copy-start(f32[1040,4,128]{2,1,0:T(4,128)S(1)} %constant_dynamic-update-slice_fusion) | copy-start | bytes 6389764
  54.6 2.0 %collective-permute-start.7 = (f32[256,4,128]{2,1,0:T(4,128)S(1)}, f32[256,4,128]{2,1,0:T(4,128)S(1)}, u32[]{:S(2)}, u32[]{:S(2)}) collective-permute-start(f32[256,4,128]{2,1,0:T(4,128)S(1)} %pad_maximum_fusion), channel_id=1, source_target_pairs={{0,1},{1,0},{2,3},{3,2},{4,5},{5,4},{6,7},{7,6},{8,9},{9,8},{10,11... | collective-permute-start | bytes 1572872 | tf_op jit(solution)/shard_map/ppermute | solution.py:140

commit v21 on v20

--- a/solution.py
+++ b/solution.py
@@ -118,11 +118,10 @@
     shown = foot_rows[0, 0]
     brick_rows, pixels = density.shape[2], density.shape[4]
     channels = 4
-    lane = lax.broadcasted_iota(jnp.int32, (1, channels, pixels), 2)
-    meta = jnp.where(lane == 0, start, jnp.where(lane == 1, shown, jnp.where(lane == 2, depth_index, 0)))
     stride = brick_rows + 2
-    slot = jnp.concatenate([jnp.zeros((brick_rows, channels, pixels), jnp.float32), meta.astype(jnp.float32),
-                            jnp.zeros((1, channels, pixels), jnp.float32)], axis=0)
+    meta = jnp.stack([start, shown, depth_index.astype(start.dtype)]).astype(jnp.float32)
+    slot = lax.dynamic_update_slice(jnp.zeros((stride, channels, pixels), jnp.float32),
+                                    meta.reshape(1, 1, 3), (brick_rows, 0, 0))
     own = render_layers(density[0, 0], foot_rows, extinction, colour_slope, colour_offset, slot)
     flat = ring_gather(own, depth_count)
     meta_rows = flat.reshape(depth_count, stride, channels, pixels)[:, brick_rows, 0, :3]

time: 58.4 us -> 58.1 us (level)
  other arithmetic: 5.23 us -> 4.24 us
  local copies, waits for them, and re-layouts: 7.35 us -> 8.02 us
    concatenate x1 -> x0, other arithmetic: 1.05 us -> none  [on_device(): jnp.concatenate([jnp.zeros((brick_rows, channels, pixels), jnp.float32),...]
    dynamic_update_slice x0 -> x1, local copies, waits for them, and re-layouts: none -> 0.74 us  [on_device(): lax.dynamic_update_slice(jnp.zeros((stride, channels, pixels), jnp.float3...]
where the time goes in v21:
time: 58.1 us; the launch traced here: 57.8 us
  waiting for transfers between devices  20.8 us (36%)
  Pallas kernels  14 us (24%)
  starting transfers between devices  8.59 us (15%)
  local copies, waits for them, and re-layouts  8.02 us (14%)
  other arithmetic  4.24 us (7%)
  between operations  2.1 us (4%)
    ppermute x4, waiting for transfers between devices, ring_gather(): ahead = lax.ppermute(ahead, 'depth', forward)  14.7 us
    pallas_call x1, Pallas kernels, render_layers(): pl.pallas_call(render_kernel, grid=(brick_rows // block_rows,), in_specs=...  14 us
    ppermute x4, starting transfers between devices, ring_gather(): ahead = lax.ppermute(ahead, 'depth', forward)  7.69 us
    ppermute x3, waiting for transfers between devices, ring_gather(): behind = lax.ppermute(behind, 'depth', backward)  4.26 us
    gather x1, local copies, waits for them, and re-layouts, composite_rows(): front_rows = jnp.take(flat, front_idx, axis=0, mode='clip')  3.11 us
    gather x1, local copies, waits for them, and re-layouts, composite_rows(): back_rows = jnp.take(flat, back_idx, axis=0, mode='clip')  2.07 us
    ppermute x1, waiting for transfers between devices, on_device(): received = lax.ppermute(for_partner, 'screen', [(0, 1), (1, 0)])  1.9 us
    select_n x1, other arithmetic, on_device(): return jnp.where(in_my_half[:, None, None], mine, received)  1.63 us
  transfers between devices with their start and end apart: 8, of which 7 were waited for; matrix products, arithmetic and copies ran while one was open for 5% of the time, Pallas kernels for 0%

profile of v21, /device:TPU:0, one launch (start us, length us, event | category | flops | bytes accessed | tf_op | source)
XLA Modules:
  0.0 57.8 jit_solution(16887836979486440113)
XLA Ops:
  1.9 0.1 add_convert_fusion
  2.0 0.7 %dynamic_update_slice.3.slot_ref = f32[130,4,128]{2,1,0:T(4,128)} pad(f32[1,1,3]{2,1,0:T(1,128)S(1)} %add_convert_fusion, f32[]{:T(128)} %constant.55.clone.1), padding=128_1x0_3x0_125 | pad | bytes 266256 | tf_op jit(solution)/shard_map/dynamic_update_slice | solution.py:123
  2.8 14.0 %shard_map.73 = f32[130,4,128]{2,1,0:T(4,128)} custom-call(f32[1]{0:T(128)S(6)} %copy.24.absorb_ref, f32[3]{0:T(128)} %slope_ref.1, f32[3]{0:T(128)} %offset_ref.1, s32[1,1]{1,0:T(1,128)} %copy.23.shown_ref, f32[16384,128]{1,0:T(8,128)} %bitcast.16, f32[130,4,128]{2,1,0:T(4,128)} %dynamic_update_slice.3.slot_ref), custom_call_target="tpu_custom_call", output_to_operand_aliasing={{}: (5, {})} | custom-call | tf_op jit(solution)/shard_map/pallas_call | solution.py:45
  16.8 3.0 %collective-permute-start = (f32[130,4,128]{2,1,0:T(4,128)}, f32[130,4,128]{2,1,0:T(4,128)S(1)}, u32[]{:S(2)}, u32[]{:S(2)}) collective-permute-start(f32[130,4,128]{2,1,0:T(4,128)} %shard_map.73), channel_id=1, source_target_pairs={{0,4},{4,8},{8,12},{12,14},{14,10},{10,6},{6,2},{2,0},{1,5},{5,9},... | collective-permute-start | bytes 798728 | tf_op jit(solution)/shard_map/ppermute | solution.py:101
  19.8 0.0 collective-permute-start.1
  19.8 6.5 %collective-permute-done = f32[130,4,128]{2,1,0:T(4,128)S(1)} collective-permute-done((f32[130,4,128]{2,1,0:T(4,128)}, f32[130,4,128]{2,1,0:T(4,128)S(1)}, u32[]{:S(2)}, u32[]{:S(2)}) %collective-permute-start) | collective-permute-done | bytes 266272 | tf_op jit(solution)/shard_map/ppermute | solution.py:101
  26.3 1.8 %collective-permute-start.2 = (f32[130,4,128]{2,1,0:T(4,128)S(1)}, f32[130,4,128]{2,1,0:T(4,128)S(1)}, u32[]{:S(2)}, u32[]{:S(2)}) collective-permute-start(f32[130,4,128]{2,1,0:T(4,128)S(1)} %collective-permute-done), channel_id=1, source_target_pairs={{0,4},{4,8},{8,12},{12,14},{14,10},{10,6},{6,2},{2,0},{1,5},{5,9},... | collective-permute-start | bytes 798728 | tf_op jit(solution)/shard_map/ppermute | solution.py:101
  28.1 0.8 %fusion.8 = (pred[256]{0:T(512)(128)(4,1)S(1)}, s32[256]{0:T(256)S(1)}) fusion(s32[]{:T(128)S(6)} %axis_index.25, s32[4096]{0:T(1024)} %param.13, s32[]{:T(128)S(6)} %select_n.70), kind=kLoop, calls=%fused_computation.46 | loop fusion | flops 4096 | bytes 2312 | tf_op jit(solution)/shard_map/eq | solution.py:140
  28.9 0.8 %dynamic_slice.7 = s32[256]{0:T(256)S(1)} dynamic-slice(s32[4096]{0:T(1024)} %param.13, s32[]{:T(128)S(6)} %select_n.72), dynamic_slice_sizes={256} | dynamic-slice | bytes 2052 | tf_op jit(solution)/shard_map/dynamic_slice | solution.py:134
  29.7 1.0 %constant_dynamic-update-slice_fusion.7 = f32[1040,4,128]{2,1,0:T(4,128)S(1)} fusion(f32[130,4,128]{2,1,0:T(4,128)} %shard_map.73), kind=kLoop, calls=%fused_computation.26 | loop fusion | bytes 532480
  30.6 0.0 collective-permute-done.1
  30.7 0.3 collective-permute-start.3
  31.0 3.0 %collective-permute-done.2 = f32[130,4,128]{2,1,0:T(4,128)S(1)} collective-permute-done((f32[130,4,128]{2,1,0:T(4,128)S(1)}, f32[130,4,128]{2,1,0:T(4,128)S(1)}, u32[]{:S(2)}, u32[]{:S(2)}) %collective-permute-start.2) | collective-permute-done | bytes 266272 | tf_op jit(solution)/shard_map/ppermute | solution.py:101
  33.9 1.5 %collective-permute-start.4 = (f32[130,4,128]{2,1,0:T(4,128)S(1)}, f32[130,4,128]{2,1,0:T(4,128)S(1)}, u32[]{:S(2)}, u32[]{:S(2)}) collective-permute-start(f32[130,4,128]{2,1,0:T(4,128)S(1)} %collective-permute-done.2), channel_id=1, source_target_pairs={{0,4},{4,8},{8,12},{12,14},{14,10},{10,6},{6,2},{2,0},{1,5},{5,9},... | collective-permute-start | bytes 798728 | tf_op jit(solution)/shard_map/ppermute | solution.py:101
  35.5 2.2 %collective-permute-done.3 = f32[130,4,128]{2,1,0:T(4,128)S(1)} collective-permute-done((f32[130,4,128]{2,1,0:T(4,128)S(1)}, f32[130,4,128]{2,1,0:T(4,128)S(1)}, u32[]{:S(2)}, u32[]{:S(2)}) %collective-permute-start.3) | collective-permute-done | bytes 266272 | tf_op jit(solution)/shard_map/ppermute | solution.py:104
  37.7 0.5 collective-permute-start.5
  38.3 2.3 %collective-permute-done.4 = f32[130,4,128]{2,1,0:T(4,128)S(1)} collective-permute-done((f32[130,4,128]{2,1,0:T(4,128)S(1)}, f32[130,4,128]{2,1,0:T(4,128)S(1)}, u32[]{:S(2)}, u32[]{:S(2)}) %collective-permute-start.4) | collective-permute-done | bytes 266272 | tf_op jit(solution)/shard_map/ppermute | solution.py:101
  40.6 1.4 %collective-permute-start.6 = (f32[130,4,128]{2,1,0:T(4,128)S(1)}, f32[130,4,128]{2,1,0:T(4,128)S(1)}, u32[]{:S(2)}, u32[]{:S(2)}) collective-permute-start(f32[130,4,128]{2,1,0:T(4,128)S(1)} %collective-permute-done.4), channel_id=1, source_target_pairs={{0,4},{4,8},{8,12},{12,14},{14,10},{10,6},{6,2},{2,0},{1,5},{5,9},... | collective-permute-start | bytes 798728 | tf_op jit(solution)/shard_map/ppermute | solution.py:101
  42.1 2.1 %collective-permute-done.5 = f32[130,4,128]{2,1,0:T(4,128)S(1)} collective-permute-done((f32[130,4,128]{2,1,0:T(4,128)S(1)}, f32[130,4,128]{2,1,0:T(4,128)S(1)}, u32[]{:S(2)}, u32[]{:S(2)}) %collective-permute-start.5) | collective-permute-done | bytes 266272 | tf_op jit(solution)/shard_map/ppermute | solution.py:104
  44.1 2.9 %collective-permute-done.6 = f32[130,4,128]{2,1,0:T(4,128)S(1)} collective-permute-done((f32[130,4,128]{2,1,0:T(4,128)S(1)}, f32[130,4,128]{2,1,0:T(4,128)S(1)}, u32[]{:S(2)}, u32[]{:S(2)}) %collective-permute-start.6) | collective-permute-done | bytes 266272 | tf_op jit(solution)/shard_map/ppermute | solution.py:101
  47.1 0.1 copy.13
  47.2 0.1 select_reduce_fusion.2
  47.3 0.1 fusion.9
  47.3 0.1 select_reduce_fusion.1
  47.5 2.1 %gather_fusion.1 = f32[512,4,128]{2,1,0:T(4,128)S(1)} fusion(f32[1040,4,128]{2,1,0:T(4,128)S(1)} %constant_dynamic-update-slice_fusion, s32[1024]{0:T(1024)S(1)} %pad_clamp_fusion), kind=kCustom, calls=%fused_computation.1 | custom fusion | bytes 2099200 | tf_op jit(solution)/shard_map/jit(_take)/gather | solution.py:81
  49.6 3.1 %gather_fusion = f32[512,4,128]{2,1,0:T(4,128)S(1)} fusion(f32[1040,4,128]{2,1,0:T(4,128)} %copy-done, s32[1024]{0:T(1024)S(1)} %pad_clamp_fusion.1), kind=kCustom, calls=%fused_computation | custom fusion | bytes 2099200 | tf_op jit(solution)/shard_map/jit(_take)/gather | solution.py:82
  52.7 0.8 %negate_exponential_fusion = (f32[512,1,128]{2,1,0:T(1,128)S(1)}, f32[512,1,128]{2,1,0:T(1,128)S(1)}) fusion(f32[512,4,128]{2,1,0:T(4,128)S(1)} %gather_fusion, f32[512,1,128]{2,1,0:T(1,128)S(1)} %bitcast.18, f32[512,4,128]{2,1,0:T(4,128)S(1)} %gather_fusion.1), kind=kLoop, calls=%fused_computation.12 | loop fusion | flops 262144 | bytes 1310720 | tf_op jit(solution)/shard_map/exp | solution.py:84
  53.6 0.4 fusion
  53.9 0.2 pad_maximum_fusion
  54.2 0.1 collective-permute-start.7
  54.3 1.9 %collective-permute-done.7 = f32[256,4,128]{2,1,0:T(4,128)S(1)} collective-permute-done((f32[256,4,128]{2,1,0:T(4,128)S(1)}, f32[256,4,128]{2,1,0:T(4,128)S(1)}, u32[]{:S(2)}, u32[]{:S(2)}) %collective-permute-start.7) | collective-permute-done | bytes 524320 | tf_op jit(solution)/shard_map/ppermute | solution.py:139
  56.2 1.6 %fusion.2 = f32[256,4,128]{2,1,0:T(4,128)} fusion(f32[256,4,128]{2,1,0:T(4,128)S(1)} %collective-permute-done.7, f32[512,3,128]{2,1,0:T(4,128)S(1)} %fusion, f32[512,1,128]{2,1,0:T(1,128)S(1)} %get-tuple-element.16, pred[256]{0:T(512)(128)(4,1)S(1)} %get-tuple-element.11), kind=kLoop, calls=%fused_computation.7 | loop fusion | flops 262144 | bytes 2097408 | tf_op jit(solution)/shard_map/jit(_where)/select_n | solution.py:141
  (17 shorter events, 0.3 us)
Async XLA Ops:
  16.8 9.6 %collective-permute-start = (f32[130,4,128]{2,1,0:T(4,128)}, f32[130,4,128]{2,1,0:T(4,128)S(1)}, u32[]{:S(2)}, u32[]{:S(2)}) collective-permute-start(f32[130,4,128]{2,1,0:T(4,128)} %shard_map.73), channel_id=1, source_target_pairs={{0,4},{4,8},{8,12},{12,14},{14,10},{10,6},{6,2},{2,0},{1,5},{5,9},... | collective-permute-start | bytes 798728 | tf_op jit(solution)/shard_map/ppermute | solution.py:101
  19.8 10.8 %collective-permute-start.1 = (f32[130,4,128]{2,1,0:T(4,128)}, f32[130,4,128]{2,1,0:T(4,128)S(1)}, u32[]{:S(2)}, u32[]{:S(2)}) collective-permute-start(f32[130,4,128]{2,1,0:T(4,128)} %shard_map.73), channel_id=1, source_target_pairs={{4,0},{8,4},{12,8},{14,12},{10,14},{6,10},{2,6},{0,2},{5,1},{9,5},... | collective-permute-start | bytes 798728 | tf_op jit(solution)/shard_map/ppermute | solution.py:104
  26.3 7.6 %collective-permute-start.2 = (f32[130,4,128]{2,1,0:T(4,128)S(1)}, f32[130,4,128]{2,1,0:T(4,128)S(1)}, u32[]{:S(2)}, u32[]{:S(2)}) collective-permute-start(f32[130,4,128]{2,1,0:T(4,128)S(1)} %collective-permute-done), channel_id=1, source_target_pairs={{0,4},{4,8},{8,12},{12,14},{14,10},{10,6},{6,2},{2,0},{1,5},{5,9},... | collective-permute-start | bytes 798728 | tf_op jit(solution)/shard_map/ppermute | solution.py:101
  30.7 7.0 %collective-permute-start.3 = (f32[130,4,128]{2,1,0:T(4,128)S(1)}, f32[130,4,128]{2,1,0:T(4,128)S(1)}, u32[]{:S(2)}, u32[]{:S(2)}) collective-permute-start(f32[130,4,128]{2,1,0:T(4,128)S(1)} %collective-permute-done.1), channel_id=1, source_target_pairs={{4,0},{8,4},{12,8},{14,12},{10,14},{6,10},{2,6},{0,2},{5,1},{9,5},... | collective-permute-start | bytes 798728 | tf_op jit(solution)/shard_map/ppermute | solution.py:104
  33.9 6.7 %collective-permute-start.4 = (f32[130,4,128]{2,1,0:T(4,128)S(1)}, f32[130,4,128]{2,1,0:T(4,128)S(1)}, u32[]{:S(2)}, u32[]{:S(2)}) collective-permute-start(f32[130,4,128]{2,1,0:T(4,128)S(1)} %collective-permute-done.2), channel_id=1, source_target_pairs={{0,4},{4,8},{8,12},{12,14},{14,10},{10,6},{6,2},{2,0},{1,5},{5,9},... | collective-permute-start | bytes 798728 | tf_op jit(solution)/shard_map/ppermute | solution.py:101
  37.7 6.4 %collective-permute-start.5 = (f32[130,4,128]{2,1,0:T(4,128)S(1)}, f32[130,4,128]{2,1,0:T(4,128)S(1)}, u32[]{:S(2)}, u32[]{:S(2)}) collective-permute-start(f32[130,4,128]{2,1,0:T(4,128)S(1)} %collective-permute-done.3), channel_id=1, source_target_pairs={{4,0},{8,4},{12,8},{14,12},{10,14},{6,10},{2,6},{0,2},{5,1},{9,5},... | collective-permute-start | bytes 798728 | tf_op jit(solution)/shard_map/ppermute | solution.py:104
  40.6 6.4 %collective-permute-start.6 = (f32[130,4,128]{2,1,0:T(4,128)S(1)}, f32[130,4,128]{2,1,0:T(4,128)S(1)}, u32[]{:S(2)}, u32[]{:S(2)}) collective-permute-start(f32[130,4,128]{2,1,0:T(4,128)S(1)} %collective-permute-done.4), channel_id=1, source_target_pairs={{0,4},{4,8},{8,12},{12,14},{14,10},{10,6},{6,2},{2,0},{1,5},{5,9},... | collective-permute-start | bytes 798728 | tf_op jit(solution)/shard_map/ppermute | solution.py:101
  47.0 2.5 %copy-start = (f32[1040,4,128]{2,1,0:T(4,128)}, f32[1040,4,128]{2,1,0:T(4,128)S(1)}, u32[]{:S(2)}) copy-start(f32[1040,4,128]{2,1,0:T(4,128)S(1)} %constant_dynamic-update-slice_fusion) | copy-start | bytes 6389764
  54.2 2.0 %collective-permute-start.7 = (f32[256,4,128]{2,1,0:T(4,128)S(1)}, f32[256,4,128]{2,1,0:T(4,128)S(1)}, u32[]{:S(2)}, u32[]{:S(2)}) collective-permute-start(f32[256,4,128]{2,1,0:T(4,128)S(1)} %pad_maximum_fusion), channel_id=1, source_target_pairs={{0,1},{1,0},{2,3},{3,2},{4,5},{5,4},{6,7},{7,6},{8,9},{9,8},{10,11... | collective-permute-start | bytes 1572872 | tf_op jit(solution)/shard_map/ppermute | solution.py:139

commit v22 on v21

--- a/solution.py
+++ b/solution.py
@@ -78,8 +78,8 @@
     zero_row = stride - 1
     back_idx = jnp.where(has_back, back_slot * stride + back_off, zero_row)
     front_idx = jnp.where(has_front, front_slot * stride + front_off, zero_row)
-    back_rows = jnp.take(flat, back_idx, axis=0, mode="clip")
-    front_rows = jnp.take(flat, front_idx, axis=0, mode="clip")
+    picked = jnp.take(flat, jnp.concatenate([back_idx, front_idx]), axis=0, mode="clip")
+    back_rows, front_rows = picked[:back_idx.shape[0]], picked[back_idx.shape[0]:]
     front_depth = front_rows[:, 3:4, :]
     colours = front_rows[:, :3, :] + jnp.exp(-front_depth) * back_rows[:, :3, :]
     opacity = 1.0 - jnp.exp(-(front_depth + back_rows[:, 3:4, :]))

time: 58.1 us -> 59.3 us (1.021)
  local copies, waits for them, and re-layouts: 8.02 us -> 9.31 us
    unnamed x10, local copies, waits for them, and re-layouts: 1.27 us -> 2.61 us
    gather x2 -> x1, local copies, waits for them, and re-layouts: 5.18 us -> 5.14 us  [composite_rows(): jnp.take(flat, jnp.concatenate([back_idx, front_idx]), axis=0, mode='clip')]
where the time goes in v22:
time: 59.3 us; the launch traced here: 59 us
  waiting for transfers between devices  20.8 us (35%)
  Pallas kernels  14 us (24%)
  local copies, waits for them, and re-layouts  9.31 us (16%)
  starting transfers between devices  8.59 us (14%)
  other arithmetic  4.24 us (7%)
  between operations  2.06 us (3%)
    ppermute x4, waiting for transfers between devices, ring_gather(): ahead = lax.ppermute(ahead, 'depth', forward)  14.7 us
    pallas_call x1, Pallas kernels, render_layers(): pl.pallas_call(render_kernel, grid=(brick_rows // block_rows,), in_specs=...  14 us
    ppermute x4, starting transfers between devices, ring_gather(): ahead = lax.ppermute(ahead, 'depth', forward)  7.69 us
    gather x1, local copies, waits for them, and re-layouts, composite_rows(): jnp.take(flat, jnp.concatenate([back_idx, front_idx]), axis=0, mode='clip')  5.14 us
    ppermute x3, waiting for transfers between devices, ring_gather(): behind = lax.ppermute(behind, 'depth', backward)  4.26 us
    unnamed x10, local copies, waits for them, and re-layouts  2.61 us
    ppermute x1, waiting for transfers between devices, on_device(): received = lax.ppermute(for_partner, 'screen', [(0, 1), (1, 0)])  1.9 us
    select_n x1, other arithmetic, on_device(): return jnp.where(in_my_half[:, None, None], mine, received)  1.62 us
  transfers between devices with their start and end apart: 8, of which 7 were waited for; matrix products, arithmetic and copies ran while one was open for 5% of the time, Pallas kernels for 0%

profile of v22, /device:TPU:0, one launch (start us, length us, event | category | flops | bytes accessed | tf_op | source)
XLA Modules:
  0.0 59.0 jit_solution(7023341717959979357)
XLA Ops:
  1.9 0.1 add_convert_fusion
  2.0 0.7 %dynamic_update_slice.3.slot_ref = f32[130,4,128]{2,1,0:T(4,128)} pad(f32[1,1,3]{2,1,0:T(1,128)S(1)} %add_convert_fusion, f32[]{:T(128)} %constant.55.clone.1), padding=128_1x0_3x0_125 | pad | bytes 266256 | tf_op jit(solution)/shard_map/dynamic_update_slice | solution.py:123
  2.8 14.0 %shard_map.73 = f32[130,4,128]{2,1,0:T(4,128)} custom-call(f32[1]{0:T(128)S(6)} %copy.24.absorb_ref, f32[3]{0:T(128)} %slope_ref.1, f32[3]{0:T(128)} %offset_ref.1, s32[1,1]{1,0:T(1,128)} %copy.23.shown_ref, f32[16384,128]{1,0:T(8,128)} %bitcast.16, f32[130,4,128]{2,1,0:T(4,128)} %dynamic_update_slice.3.slot_ref), custom_call_target="tpu_custom_call", output_to_operand_aliasing={{}: (5, {})} | custom-call | tf_op jit(solution)/shard_map/pallas_call | solution.py:45
  16.8 3.0 %collective-permute-start = (f32[130,4,128]{2,1,0:T(4,128)}, f32[130,4,128]{2,1,0:T(4,128)S(1)}, u32[]{:S(2)}, u32[]{:S(2)}) collective-permute-start(f32[130,4,128]{2,1,0:T(4,128)} %shard_map.73), channel_id=1, source_target_pairs={{0,4},{4,8},{8,12},{12,14},{14,10},{10,6},{6,2},{2,0},{1,5},{5,9},... | collective-permute-start | bytes 798728 | tf_op jit(solution)/shard_map/ppermute | solution.py:101
  19.8 0.0 collective-permute-start.1
  19.8 6.5 %collective-permute-done = f32[130,4,128]{2,1,0:T(4,128)S(1)} collective-permute-done((f32[130,4,128]{2,1,0:T(4,128)}, f32[130,4,128]{2,1,0:T(4,128)S(1)}, u32[]{:S(2)}, u32[]{:S(2)}) %collective-permute-start) | collective-permute-done | bytes 266272 | tf_op jit(solution)/shard_map/ppermute | solution.py:101
  26.3 1.8 %collective-permute-start.2 = (f32[130,4,128]{2,1,0:T(4,128)S(1)}, f32[130,4,128]{2,1,0:T(4,128)S(1)}, u32[]{:S(2)}, u32[]{:S(2)}) collective-permute-start(f32[130,4,128]{2,1,0:T(4,128)S(1)} %collective-permute-done), channel_id=1, source_target_pairs={{0,4},{4,8},{8,12},{12,14},{14,10},{10,6},{6,2},{2,0},{1,5},{5,9},... | collective-permute-start | bytes 798728 | tf_op jit(solution)/shard_map/ppermute | solution.py:101
  28.1 0.8 %fusion.8 = (pred[256]{0:T(512)(128)(4,1)S(1)}, s32[256]{0:T(256)S(1)}) fusion(s32[]{:T(128)S(6)} %axis_index.25, s32[4096]{0:T(1024)} %param.13, s32[]{:T(128)S(6)} %select_n.50), kind=kLoop, calls=%fused_computation.44 | loop fusion | flops 4096 | bytes 2312 | tf_op jit(solution)/shard_map/eq | solution.py:140
  28.9 0.8 %dynamic_slice.7 = s32[256]{0:T(256)S(1)} dynamic-slice(s32[4096]{0:T(1024)} %param.13, s32[]{:T(128)S(6)} %select_n.52), dynamic_slice_sizes={256} | dynamic-slice | bytes 2052 | tf_op jit(solution)/shard_map/dynamic_slice | solution.py:134
  29.7 1.0 %constant_dynamic-update-slice_fusion.7 = f32[1040,4,128]{2,1,0:T(4,128)S(1)} fusion(f32[130,4,128]{2,1,0:T(4,128)} %shard_map.73), kind=kLoop, calls=%fused_computation.25 | loop fusion | bytes 532480
  30.6 0.0 collective-permute-done.1
  30.7 0.3 collective-permute-start.3
  31.0 3.0 %collective-permute-done.2 = f32[130,4,128]{2,1,0:T(4,128)S(1)} collective-permute-done((f32[130,4,128]{2,1,0:T(4,128)S(1)}, f32[130,4,128]{2,1,0:T(4,128)S(1)}, u32[]{:S(2)}, u32[]{:S(2)}) %collective-permute-start.2) | collective-permute-done | bytes 266272 | tf_op jit(solution)/shard_map/ppermute | solution.py:101
  33.9 1.5 %collective-permute-start.4 = (f32[130,4,128]{2,1,0:T(4,128)S(1)}, f32[130,4,128]{2,1,0:T(4,128)S(1)}, u32[]{:S(2)}, u32[]{:S(2)}) collective-permute-start(f32[130,4,128]{2,1,0:T(4,128)S(1)} %collective-permute-done.2), channel_id=1, source_target_pairs={{0,4},{4,8},{8,12},{12,14},{14,10},{10,6},{6,2},{2,0},{1,5},{5,9},... | collective-permute-start | bytes 798728 | tf_op jit(solution)/shard_map/ppermute | solution.py:101
  35.5 2.2 %collective-permute-done.3 = f32[130,4,128]{2,1,0:T(4,128)S(1)} collective-permute-done((f32[130,4,128]{2,1,0:T(4,128)S(1)}, f32[130,4,128]{2,1,0:T(4,128)S(1)}, u32[]{:S(2)}, u32[]{:S(2)}) %collective-permute-start.3) | collective-permute-done | bytes 266272 | tf_op jit(solution)/shard_map/ppermute | solution.py:104
  37.7 0.5 collective-permute-start.5
  38.3 2.3 %collective-permute-done.4 = f32[130,4,128]{2,1,0:T(4,128)S(1)} collective-permute-done((f32[130,4,128]{2,1,0:T(4,128)S(1)}, f32[130,4,128]{2,1,0:T(4,128)S(1)}, u32[]{:S(2)}, u32[]{:S(2)}) %collective-permute-start.4) | collective-permute-done | bytes 266272 | tf_op jit(solution)/shard_map/ppermute | solution.py:101
  40.6 1.4 %collective-permute-start.6 = (f32[130,4,128]{2,1,0:T(4,128)S(1)}, f32[130,4,128]{2,1,0:T(4,128)S(1)}, u32[]{:S(2)}, u32[]{:S(2)}) collective-permute-start(f32[130,4,128]{2,1,0:T(4,128)S(1)} %collective-permute-done.4), channel_id=1, source_target_pairs={{0,4},{4,8},{8,12},{12,14},{14,10},{10,6},{6,2},{2,0},{1,5},{5,9},... | collective-permute-start | bytes 798728 | tf_op jit(solution)/shard_map/ppermute | solution.py:101
  42.1 2.1 %collective-permute-done.5 = f32[130,4,128]{2,1,0:T(4,128)S(1)} collective-permute-done((f32[130,4,128]{2,1,0:T(4,128)S(1)}, f32[130,4,128]{2,1,0:T(4,128)S(1)}, u32[]{:S(2)}, u32[]{:S(2)}) %collective-permute-start.5) | collective-permute-done | bytes 266272 | tf_op jit(solution)/shard_map/ppermute | solution.py:104
  44.1 2.9 %collective-permute-done.6 = f32[130,4,128]{2,1,0:T(4,128)S(1)} collective-permute-done((f32[130,4,128]{2,1,0:T(4,128)S(1)}, f32[130,4,128]{2,1,0:T(4,128)S(1)}, u32[]{:S(2)}, u32[]{:S(2)}) %collective-permute-start.6) | collective-permute-done | bytes 266272 | tf_op jit(solution)/shard_map/ppermute | solution.py:101
  47.0 0.0 copy-start
  47.1 1.3 %copy-done = f32[1040,4,128]{2,1,0:T(4,128)} copy-done((f32[1040,4,128]{2,1,0:T(4,128)}, f32[1040,4,128]{2,1,0:T(4,128)S(1)}, u32[]{:S(2)}) %copy-start) | copy-done | bytes 2129944
  48.4 0.1 copy.13
  48.5 0.1 select_reduce_fusion.2
  48.6 0.1 select_reduce_fusion
  48.8 5.1 %gather_fusion = f32[1024,4,128]{2,1,0:T(4,128)S(1)} fusion(f32[1040,4,128]{2,1,0:T(4,128)} %copy-done, s32[1024]{0:T(1024)S(1)} %add_clamp_fusion), kind=kCustom, calls=%fused_computation | custom fusion | bytes 4198400 | tf_op jit(solution)/shard_map/jit(_take)/gather | solution.py:81
  53.9 0.8 %negate_exponential_fusion = (f32[512,1,128]{2,1,0:T(1,128)S(1)}, f32[512,1,128]{2,1,0:T(1,128)S(1)}) fusion(f32[1024,4,128]{2,1,0:T(4,128)S(1)} %gather_fusion, f32[512,1,128]{2,1,0:T(1,128)S(1)} %bitcast.18), kind=kLoop, calls=%fused_computation.11 | loop fusion | flops 262144 | bytes 1310720 | tf_op jit(solution)/shard_map/exp | solution.py:84
  54.8 0.4 fusion
  55.2 0.2 pad_maximum_fusion
  55.4 0.1 collective-permute-start.7
  55.5 1.9 %collective-permute-done.7 = f32[256,4,128]{2,1,0:T(4,128)S(1)} collective-permute-done((f32[256,4,128]{2,1,0:T(4,128)S(1)}, f32[256,4,128]{2,1,0:T(4,128)S(1)}, u32[]{:S(2)}, u32[]{:S(2)}) %collective-permute-start.7) | collective-permute-done | bytes 524320 | tf_op jit(solution)/shard_map/ppermute | solution.py:139
  57.4 1.6 %fusion.2 = f32[256,4,128]{2,1,0:T(4,128)} fusion(f32[256,4,128]{2,1,0:T(4,128)S(1)} %collective-permute-done.7, f32[512,3,128]{2,1,0:T(4,128)S(1)} %fusion, f32[512,1,128]{2,1,0:T(1,128)S(1)} %get-tuple-element.15, pred[256]{0:T(512)(128)(4,1)S(1)} %get-tuple-element.11), kind=kLoop, calls=%fused_computation.6 | loop fusion | flops 262144 | bytes 2097408 | tf_op jit(solution)/shard_map/jit(_where)/select_n | solution.py:141
  (15 shorter events, 0.3 us)
Async XLA Ops:
  16.8 9.6 %collective-permute-start = (f32[130,4,128]{2,1,0:T(4,128)}, f32[130,4,128]{2,1,0:T(4,128)S(1)}, u32[]{:S(2)}, u32[]{:S(2)}) collective-permute-start(f32[130,4,128]{2,1,0:T(4,128)} %shard_map.73), channel_id=1, source_target_pairs={{0,4},{4,8},{8,12},{12,14},{14,10},{10,6},{6,2},{2,0},{1,5},{5,9},... | collective-permute-start | bytes 798728 | tf_op jit(solution)/shard_map/ppermute | solution.py:101
  19.8 10.8 %collective-permute-start.1 = (f32[130,4,128]{2,1,0:T(4,128)}, f32[130,4,128]{2,1,0:T(4,128)S(1)}, u32[]{:S(2)}, u32[]{:S(2)}) collective-permute-start(f32[130,4,128]{2,1,0:T(4,128)} %shard_map.73), channel_id=1, source_target_pairs={{4,0},{8,4},{12,8},{14,12},{10,14},{6,10},{2,6},{0,2},{5,1},{9,5},... | collective-permute-start | bytes 798728 | tf_op jit(solution)/shard_map/ppermute | solution.py:104
  26.3 7.6 %collective-permute-start.2 = (f32[130,4,128]{2,1,0:T(4,128)S(1)}, f32[130,4,128]{2,1,0:T(4,128)S(1)}, u32[]{:S(2)}, u32[]{:S(2)}) collective-permute-start(f32[130,4,128]{2,1,0:T(4,128)S(1)} %collective-permute-done), channel_id=1, source_target_pairs={{0,4},{4,8},{8,12},{12,14},{14,10},{10,6},{6,2},{2,0},{1,5},{5,9},... | collective-permute-start | bytes 798728 | tf_op jit(solution)/shard_map/ppermute | solution.py:101
  30.7 7.0 %collective-permute-start.3 = (f32[130,4,128]{2,1,0:T(4,128)S(1)}, f32[130,4,128]{2,1,0:T(4,128)S(1)}, u32[]{:S(2)}, u32[]{:S(2)}) collective-permute-start(f32[130,4,128]{2,1,0:T(4,128)S(1)} %collective-permute-done.1), channel_id=1, source_target_pairs={{4,0},{8,4},{12,8},{14,12},{10,14},{6,10},{2,6},{0,2},{5,1},{9,5},... | collective-permute-start | bytes 798728 | tf_op jit(solution)/shard_map/ppermute | solution.py:104
  33.9 6.7 %collective-permute-start.4 = (f32[130,4,128]{2,1,0:T(4,128)S(1)}, f32[130,4,128]{2,1,0:T(4,128)S(1)}, u32[]{:S(2)}, u32[]{:S(2)}) collective-permute-start(f32[130,4,128]{2,1,0:T(4,128)S(1)} %collective-permute-done.2), channel_id=1, source_target_pairs={{0,4},{4,8},{8,12},{12,14},{14,10},{10,6},{6,2},{2,0},{1,5},{5,9},... | collective-permute-start | bytes 798728 | tf_op jit(solution)/shard_map/ppermute | solution.py:101
  37.7 6.4 %collective-permute-start.5 = (f32[130,4,128]{2,1,0:T(4,128)S(1)}, f32[130,4,128]{2,1,0:T(4,128)S(1)}, u32[]{:S(2)}, u32[]{:S(2)}) collective-permute-start(f32[130,4,128]{2,1,0:T(4,128)S(1)} %collective-permute-done.3), channel_id=1, source_target_pairs={{4,0},{8,4},{12,8},{14,12},{10,14},{6,10},{2,6},{0,2},{5,1},{9,5},... | collective-permute-start | bytes 798728 | tf_op jit(solution)/shard_map/ppermute | solution.py:104
  40.6 6.4 %collective-permute-start.6 = (f32[130,4,128]{2,1,0:T(4,128)S(1)}, f32[130,4,128]{2,1,0:T(4,128)S(1)}, u32[]{:S(2)}, u32[]{:S(2)}) collective-permute-start(f32[130,4,128]{2,1,0:T(4,128)S(1)} %collective-permute-done.4), channel_id=1, source_target_pairs={{0,4},{4,8},{8,12},{12,14},{14,10},{10,6},{6,2},{2,0},{1,5},{5,9},... | collective-permute-start | bytes 798728 | tf_op jit(solution)/shard_map/ppermute | solution.py:101
  47.0 1.4 %copy-start = (f32[1040,4,128]{2,1,0:T(4,128)}, f32[1040,4,128]{2,1,0:T(4,128)S(1)}, u32[]{:S(2)}) copy-start(f32[1040,4,128]{2,1,0:T(4,128)S(1)} %constant_dynamic-update-slice_fusion) | copy-start | bytes 6389764
  55.4 2.0 %collective-permute-start.7 = (f32[256,4,128]{2,1,0:T(4,128)S(1)}, f32[256,4,128]{2,1,0:T(4,128)S(1)}, u32[]{:S(2)}, u32[]{:S(2)}) collective-permute-start(f32[256,4,128]{2,1,0:T(4,128)S(1)} %pad_maximum_fusion), channel_id=1, source_target_pairs={{0,1},{1,0},{2,3},{3,2},{4,5},{5,4},{6,7},{7,6},{8,9},{9,8},{10,11... | collective-permute-start | bytes 1572872 | tf_op jit(solution)/shard_map/ppermute | solution.py:139

commit v23 on v21

--- a/solution.py
+++ b/solution.py
@@ -132,11 +132,10 @@
     partner_owner = depth_index * screen_count + (1 - screen_index)
     wanted_self = lax.dynamic_slice_in_dim(tile_source, self_owner * owner_rows, owner_rows)
     wanted_partner = lax.dynamic_slice_in_dim(tile_source, partner_owner * owner_rows, owner_rows)
-    wanted = jnp.concatenate([wanted_self, wanted_partner])
-    rows = composite_rows(flat, starts, counts, brick_ids, stride, wanted % half_rows)
-    mine = rows[:owner_rows]
-    for_partner = rows[owner_rows:]
+    for_partner = composite_rows(flat, starts, counts, brick_ids, stride, wanted_partner % half_rows)
     received = lax.ppermute(for_partner, "screen", [(0, 1), (1, 0)])
+    flat, for_partner = lax.optimization_barrier((flat, for_partner))
+    mine = composite_rows(flat, starts, counts, brick_ids, stride, wanted_self % half_rows)
     in_my_half = (wanted_self // half_rows) == screen_index
     return jnp.where(in_my_half[:, None, None], mine, received)
 

time: 58.1 us -> 56.8 us (0.978)
  other arithmetic: 4.24 us -> 6.89 us
  waiting for transfers between devices: 20.8 us -> 18.6 us
  local copies, waits for them, and re-layouts: 8.02 us -> 6.04 us
    ppermute x1, waiting for transfers between devices: 1.9 us -> 0.01 us  [on_device(): received = lax.ppermute(for_partner, 'screen', [(0, 1), (1, 0)])]
    ppermute x3, waiting for transfers between devices: 4.26 us -> 2.59 us  [ring_gather(): behind = lax.ppermute(behind, 'depth', backward)]
    ppermute x4, waiting for transfers between devices: 14.7 us -> 16 us  [ring_gather(): ahead = lax.ppermute(ahead, 'depth', forward)]
    gather x1 -> x2, local copies, waits for them, and re-layouts: 3.11 us -> 1.99 us  [composite_rows(): front_rows = jnp.take(flat, front_idx, axis=0, mode='clip')]
    select_n x1, other arithmetic: 1.63 us -> 2.58 us  [on_device(): return jnp.where(in_my_half[:, None, None], mine, received)]
    select_n x1 -> x2, other arithmetic: 0.01 us -> 0.85 us  [the longest x1 0.84 us: on_device(): wanted_partner % half_rows]
    concatenate x1, other arithmetic: 0.24 us -> 1.03 us  [composite_rows(): return jnp.concatenate([colours, opacity], axis=1)]
    dynamic_slice x1 -> x0, local copies, waits for them, and re-layouts: 0.76 us -> none  [on_device(): lax.dynamic_slice_in_dim(tile_source, partner_owner * owner_rows, owner_r...]
  transfers between devices with their start and end apart: 8 -> 8, of which waited for: 7 -> 6; matrix products, arithmetic and copies ran while one was open for 5% -> 10% of each run, Pallas kernels for 0% -> 0%
where the time goes in v23:
time: 56.8 us; the launch traced here: 56.4 us
  waiting for transfers between devices  18.6 us (33%)
  Pallas kernels  14 us (25%)
  starting transfers between devices  8.82 us (16%)
  other arithmetic  6.89 us (12%)
  local copies, waits for them, and re-layouts  6.04 us (11%)
  between operations  2.11 us (4%)
    ppermute x4, waiting for transfers between devices, ring_gather(): ahead = lax.ppermute(ahead, 'depth', forward)  16 us
    pallas_call x1, Pallas kernels, render_layers(): pl.pallas_call(render_kernel, grid=(brick_rows // block_rows,), in_specs=...  14 us
    ppermute x4, starting transfers between devices, ring_gather(): ahead = lax.ppermute(ahead, 'depth', forward)  7.99 us
    ppermute x3, waiting for transfers between devices, ring_gather(): behind = lax.ppermute(behind, 'depth', backward)  2.59 us
    select_n x1, other arithmetic, on_device(): return jnp.where(in_my_half[:, None, None], mine, received)  2.58 us
    gather x2, local copies, waits for them, and re-layouts, composite_rows(): front_rows = jnp.take(flat, front_idx, axis=0, mode='clip')  1.99 us
    gather x2, local copies, waits for them, and re-layouts, composite_rows(): back_rows = jnp.take(flat, back_idx, axis=0, mode='clip')  1.99 us
    unnamed x8, local copies, waits for them, and re-layouts  1.27 us
  transfers between devices with their start and end apart: 8, of which 6 were waited for; matrix products, arithmetic and copies ran while one was open for 10% of the time, Pallas kernels for 0%

profile of v23, /device:TPU:0, one launch (start us, length us, event | category | flops | bytes accessed | tf_op | source)
XLA Modules:
  0.0 56.4 jit_solution(845079402831672405)
XLA Ops:
  1.9 0.1 add_convert_fusion
  2.0 0.7 %dynamic_update_slice.3.slot_ref = f32[130,4,128]{2,1,0:T(4,128)} pad(f32[1,1,3]{2,1,0:T(1,128)S(1)} %add_convert_fusion, f32[]{:T(128)} %constant.61.clone.1), padding=128_1x0_3x0_125 | pad | bytes 266256 | tf_op jit(solution)/shard_map/dynamic_update_slice | solution.py:123
  2.8 14.0 %shard_map.73 = f32[130,4,128]{2,1,0:T(4,128)} custom-call(f32[1]{0:T(128)S(6)} %copy.25.absorb_ref, f32[3]{0:T(128)} %slope_ref.1, f32[3]{0:T(128)} %offset_ref.1, s32[1,1]{1,0:T(1,128)} %copy.24.shown_ref, f32[16384,128]{1,0:T(8,128)} %bitcast.17, f32[130,4,128]{2,1,0:T(4,128)} %dynamic_update_slice.3.slot_ref), custom_call_target="tpu_custom_call", output_to_operand_aliasing={{}: (5, {})} | custom-call | tf_op jit(solution)/shard_map/pallas_call | solution.py:45
  16.8 3.0 %collective-permute-start = (f32[130,4,128]{2,1,0:T(4,128)}, f32[130,4,128]{2,1,0:T(4,128)S(1)}, u32[]{:S(2)}, u32[]{:S(2)}) collective-permute-start(f32[130,4,128]{2,1,0:T(4,128)} %shard_map.73), channel_id=1, source_target_pairs={{0,4},{4,8},{8,12},{12,14},{14,10},{10,6},{6,2},{2,0},{1,5},{5,9},... | collective-permute-start | bytes 798728 | tf_op jit(solution)/shard_map/ppermute | solution.py:101
  19.8 6.5 %collective-permute-done = f32[130,4,128]{2,1,0:T(4,128)S(1)} collective-permute-done((f32[130,4,128]{2,1,0:T(4,128)}, f32[130,4,128]{2,1,0:T(4,128)S(1)}, u32[]{:S(2)}, u32[]{:S(2)}) %collective-permute-start) | collective-permute-done | bytes 266272 | tf_op jit(solution)/shard_map/ppermute | solution.py:101
  26.3 1.8 %collective-permute-start.2 = (f32[130,4,128]{2,1,0:T(4,128)S(1)}, f32[130,4,128]{2,1,0:T(4,128)S(1)}, u32[]{:S(2)}, u32[]{:S(2)}) collective-permute-start(f32[130,4,128]{2,1,0:T(4,128)S(1)} %collective-permute-done), channel_id=1, source_target_pairs={{0,4},{4,8},{8,12},{12,14},{14,10},{10,6},{6,2},{2,0},{1,5},{5,9},... | collective-permute-start | bytes 798728 | tf_op jit(solution)/shard_map/ppermute | solution.py:101
  28.1 0.8 %and_select_fusion.1 = (s32[256]{0:T(256)S(1)}, s32[256]{0:T(256)S(1)}) fusion(s32[4096]{0:T(1024)} %param.13, s32[]{:T(128)S(6)} %select_n.113, s32[]{:T(128)S(6)} %select_n.111), kind=kLoop, calls=%fused_computation.59 | loop fusion | flops 5632 | bytes 4104 | tf_op jit(solution)/shard_map/jit(remainder)/select_n | solution.py:135
  29.0 1.0 %constant_dynamic-update-slice_fusion.7 = f32[1040,4,128]{2,1,0:T(4,128)S(1)} fusion(f32[130,4,128]{2,1,0:T(4,128)} %shard_map.73), kind=kLoop, calls=%fused_computation.33 | loop fusion | bytes 532480
  30.0 0.3 collective-permute-start.3
  30.3 0.8 %fusion.11 = pred[256]{0:T(512)(128)(4,1)S(1)} fusion(s32[]{:T(128)S(6)} %axis_index.25, s32[4096]{0:T(1024)} %param.13, s32[]{:T(128)S(6)} %select_n.111), kind=kLoop, calls=%fused_computation.67 | loop fusion | flops 4096 | bytes 1288 | tf_op jit(solution)/shard_map/eq | solution.py:139
  31.0 2.9 %collective-permute-done.2 = f32[130,4,128]{2,1,0:T(4,128)S(1)} collective-permute-done((f32[130,4,128]{2,1,0:T(4,128)S(1)}, f32[130,4,128]{2,1,0:T(4,128)S(1)}, u32[]{:S(2)}, u32[]{:S(2)}) %collective-permute-start.2) | collective-permute-done | bytes 266272 | tf_op jit(solution)/shard_map/ppermute | solution.py:101
  33.9 1.5 %collective-permute-start.4 = (f32[130,4,128]{2,1,0:T(4,128)S(1)}, f32[130,4,128]{2,1,0:T(4,128)S(1)}, u32[]{:S(2)}, u32[]{:S(2)}) collective-permute-start(f32[130,4,128]{2,1,0:T(4,128)S(1)} %collective-permute-done.2), channel_id=1, source_target_pairs={{0,4},{4,8},{8,12},{12,14},{14,10},{10,6},{6,2},{2,0},{1,5},{5,9},... | collective-permute-start | bytes 798728 | tf_op jit(solution)/shard_map/ppermute | solution.py:101
  35.5 1.5 %collective-permute-done.3 = f32[130,4,128]{2,1,0:T(4,128)S(1)} collective-permute-done((f32[130,4,128]{2,1,0:T(4,128)S(1)}, f32[130,4,128]{2,1,0:T(4,128)S(1)}, u32[]{:S(2)}, u32[]{:S(2)}) %collective-permute-start.3) | collective-permute-done | bytes 266272 | tf_op jit(solution)/shard_map/ppermute | solution.py:104
  37.0 0.5 collective-permute-start.5
  37.6 3.0 %collective-permute-done.4 = f32[130,4,128]{2,1,0:T(4,128)S(1)} collective-permute-done((f32[130,4,128]{2,1,0:T(4,128)S(1)}, f32[130,4,128]{2,1,0:T(4,128)S(1)}, u32[]{:S(2)}, u32[]{:S(2)}) %collective-permute-start.4) | collective-permute-done | bytes 266272 | tf_op jit(solution)/shard_map/ppermute | solution.py:101
  40.6 1.7 %collective-permute-start.6 = (f32[130,4,128]{2,1,0:T(4,128)S(1)}, f32[130,4,128]{2,1,0:T(4,128)S(1)}, u32[]{:S(2)}, u32[]{:S(2)}) collective-permute-start(f32[130,4,128]{2,1,0:T(4,128)S(1)} %collective-permute-done.4), channel_id=1, source_target_pairs={{0,4},{4,8},{8,12},{12,14},{14,10},{10,6},{6,2},{2,0},{1,5},{5,9},... | collective-permute-start | bytes 798728 | tf_op jit(solution)/shard_map/ppermute | solution.py:101
  42.4 1.1 %collective-permute-done.5 = f32[130,4,128]{2,1,0:T(4,128)S(1)} collective-permute-done((f32[130,4,128]{2,1,0:T(4,128)S(1)}, f32[130,4,128]{2,1,0:T(4,128)S(1)}, u32[]{:S(2)}, u32[]{:S(2)}) %collective-permute-start.5) | collective-permute-done | bytes 266272 | tf_op jit(solution)/shard_map/ppermute | solution.py:104
  43.5 3.5 %collective-permute-done.6 = f32[130,4,128]{2,1,0:T(4,128)S(1)} collective-permute-done((f32[130,4,128]{2,1,0:T(4,128)S(1)}, f32[130,4,128]{2,1,0:T(4,128)S(1)}, u32[]{:S(2)}, u32[]{:S(2)}) %collective-permute-start.6) | collective-permute-done | bytes 266272 | tf_op jit(solution)/shard_map/ppermute | solution.py:101
  47.1 0.1 copy.14
  47.1 0.1 select_reduce_fusion.2
  47.2 0.1 fusion.12
  47.3 0.1 select_reduce_fusion.1
  47.5 1.0 %gather_fusion.1 = f32[256,4,128]{2,1,0:T(4,128)S(1)} fusion(f32[1040,4,128]{2,1,0:T(4,128)S(1)} %constant_dynamic-update-slice_fusion, s32[1024]{0:T(1024)S(1)} %pad_clamp_fusion.2), kind=kCustom, calls=%fused_computation.1 | custom fusion | bytes 1049600 | tf_op jit(solution)/shard_map/jit(_take)/gather | solution.py:81
  48.5 1.0 %gather_fusion = f32[256,4,128]{2,1,0:T(4,128)S(1)} fusion(f32[1040,4,128]{2,1,0:T(4,128)S(1)} %constant_dynamic-update-slice_fusion, s32[1024]{0:T(1024)S(1)} %pad_clamp_fusion.3), kind=kCustom, calls=%fused_computation | custom fusion | bytes 1049600 | tf_op jit(solution)/shard_map/jit(_take)/gather | solution.py:82
  49.5 0.4 negate_exponential_fusion.1
  50.0 0.2 fusion.1
  50.2 1.0 %pad_maximum_fusion = f32[256,4,128]{2,1,0:T(4,128)} fusion(f32[256,1,128]{2,1,0:T(1,128)S(1)} %get-tuple-element.27, f32[256,3,128]{2,1,0:T(4,128)S(1)} %fusion.1), kind=kLoop, calls=%fused_computation.8 | loop fusion | flops 131072 | bytes 1048576 | tf_op jit(solution)/shard_map/concatenate | solution.py:86
  51.2 1.0 %gather_fusion.3 = f32[256,4,128]{2,1,0:T(4,128)S(1)} fusion(f32[1040,4,128]{2,1,0:T(4,128)S(1)} %constant_dynamic-update-slice_fusion, s32[1024]{0:T(1024)S(1)} %pad_clamp_fusion), kind=kCustom, calls=%fused_computation.3 | custom fusion | bytes 1049600 | tf_op jit(solution)/shard_map/jit(_take)/gather | solution.py:81
  52.2 1.0 %gather_fusion.2 = f32[256,4,128]{2,1,0:T(4,128)S(1)} fusion(f32[1040,4,128]{2,1,0:T(4,128)S(1)} %constant_dynamic-update-slice_fusion, s32[1024]{0:T(1024)S(1)} %pad_clamp_fusion.1), kind=kCustom, calls=%fused_computation.2 | custom fusion | bytes 1049600 | tf_op jit(solution)/shard_map/jit(_take)/gather | solution.py:82
  53.2 0.4 negate_exponential_fusion
  53.7 0.2 fusion
  53.9 2.6 %maximum_select_fusion = f32[256,4,128]{2,1,0:T(4,128)} fusion(f32[256,4,128]{2,1,0:T(4,128)} %collective-permute-done.7, f32[256,1,128]{2,1,0:T(1,128)S(1)} %get-tuple-element.25, f32[256,3,128]{2,1,0:T(4,128)S(1)} %fusion, pred[256]{0:T(512)(128)(4,1)S(1)} %fusion.11), kind=kLoop, calls=%fused_computation.9 | loop fusion | flops 262144 | bytes 1573120 | tf_op jit(solution)/shard_map/jit(_where)/select_n | solution.py:140
  (23 shorter events, 0.4 us)
Async XLA Ops:
  16.8 9.6 %collective-permute-start = (f32[130,4,128]{2,1,0:T(4,128)}, f32[130,4,128]{2,1,0:T(4,128)S(1)}, u32[]{:S(2)}, u32[]{:S(2)}) collective-permute-start(f32[130,4,128]{2,1,0:T(4,128)} %shard_map.73), channel_id=1, source_target_pairs={{0,4},{4,8},{8,12},{12,14},{14,10},{10,6},{6,2},{2,0},{1,5},{5,9},... | collective-permute-start | bytes 798728 | tf_op jit(solution)/shard_map/ppermute | solution.py:101
  19.8 10.2 %collective-permute-start.1 = (f32[130,4,128]{2,1,0:T(4,128)}, f32[130,4,128]{2,1,0:T(4,128)S(1)}, u32[]{:S(2)}, u32[]{:S(2)}) collective-permute-start(f32[130,4,128]{2,1,0:T(4,128)} %shard_map.73), channel_id=1, source_target_pairs={{4,0},{8,4},{12,8},{14,12},{10,14},{6,10},{2,6},{0,2},{5,1},{9,5},... | collective-permute-start | bytes 798728 | tf_op jit(solution)/shard_map/ppermute | solution.py:104
  26.3 7.6 %collective-permute-start.2 = (f32[130,4,128]{2,1,0:T(4,128)S(1)}, f32[130,4,128]{2,1,0:T(4,128)S(1)}, u32[]{:S(2)}, u32[]{:S(2)}) collective-permute-start(f32[130,4,128]{2,1,0:T(4,128)S(1)} %collective-permute-done), channel_id=1, source_target_pairs={{0,4},{4,8},{8,12},{12,14},{14,10},{10,6},{6,2},{2,0},{1,5},{5,9},... | collective-permute-start | bytes 798728 | tf_op jit(solution)/shard_map/ppermute | solution.py:101
  30.0 7.0 %collective-permute-start.3 = (f32[130,4,128]{2,1,0:T(4,128)S(1)}, f32[130,4,128]{2,1,0:T(4,128)S(1)}, u32[]{:S(2)}, u32[]{:S(2)}) collective-permute-start(f32[130,4,128]{2,1,0:T(4,128)S(1)} %collective-permute-done.1), channel_id=1, source_target_pairs={{4,0},{8,4},{12,8},{14,12},{10,14},{6,10},{2,6},{0,2},{5,1},{9,5},... | collective-permute-start | bytes 798728 | tf_op jit(solution)/shard_map/ppermute | solution.py:104
  33.9 6.7 %collective-permute-start.4 = (f32[130,4,128]{2,1,0:T(4,128)S(1)}, f32[130,4,128]{2,1,0:T(4,128)S(1)}, u32[]{:S(2)}, u32[]{:S(2)}) collective-permute-start(f32[130,4,128]{2,1,0:T(4,128)S(1)} %collective-permute-done.2), channel_id=1, source_target_pairs={{0,4},{4,8},{8,12},{12,14},{14,10},{10,6},{6,2},{2,0},{1,5},{5,9},... | collective-permute-start | bytes 798728 | tf_op jit(solution)/shard_map/ppermute | solution.py:101
  37.0 6.4 %collective-permute-start.5 = (f32[130,4,128]{2,1,0:T(4,128)S(1)}, f32[130,4,128]{2,1,0:T(4,128)S(1)}, u32[]{:S(2)}, u32[]{:S(2)}) collective-permute-start(f32[130,4,128]{2,1,0:T(4,128)S(1)} %collective-permute-done.3), channel_id=1, source_target_pairs={{4,0},{8,4},{12,8},{14,12},{10,14},{6,10},{2,6},{0,2},{5,1},{9,5},... | collective-permute-start | bytes 798728 | tf_op jit(solution)/shard_map/ppermute | solution.py:104
  40.6 6.4 %collective-permute-start.6 = (f32[130,4,128]{2,1,0:T(4,128)S(1)}, f32[130,4,128]{2,1,0:T(4,128)S(1)}, u32[]{:S(2)}, u32[]{:S(2)}) collective-permute-start(f32[130,4,128]{2,1,0:T(4,128)S(1)} %collective-permute-done.4), channel_id=1, source_target_pairs={{0,4},{4,8},{8,12},{12,14},{14,10},{10,6},{6,2},{2,0},{1,5},{5,9},... | collective-permute-start | bytes 798728 | tf_op jit(solution)/shard_map/ppermute | solution.py:101
  51.2 2.6 %collective-permute-start.7 = (f32[256,4,128]{2,1,0:T(4,128)}, f32[256,4,128]{2,1,0:T(4,128)}, u32[]{:S(2)}, u32[]{:S(2)}) collective-permute-start(f32[256,4,128]{2,1,0:T(4,128)} %pad_maximum_fusion), channel_id=1, source_target_pairs={{0,1},{1,0},{2,3},{3,2},{4,5},{5,4},{6,7},{7,6},{8,9},{9,8},{10,11... | collective-permute-start | bytes 1572872 | tf_op jit(solution)/shard_map/ppermute | solution.py:136

commit v24 on v23

--- a/solution.py
+++ b/solution.py
@@ -32,7 +32,7 @@
 
     zeros = jnp.zeros((block_rows, pixels), jnp.float32)
     carry = (jnp.full((block_rows, pixels), 0.5, jnp.float32), zeros, zeros, zeros, zeros, zeros)
-    carry = lax.fori_loop(0, sample_count, one_step, carry, unroll=32)
+    carry = lax.fori_loop(0, sample_count, one_step, carry, unroll=64)
     row_ids = pl.program_id(0) * block_rows + lax.broadcasted_iota(jnp.int32, (block_rows, pixels), 0)
     visible = row_ids < shown
     for channel in range(3):

time: 56.8 us -> 56.6 us (level)
  no operation moved by 1% of the time
where the time goes in v24:
time: 56.6 us; the launch traced here: 56.3 us
  waiting for transfers between devices  18.6 us (33%)
  Pallas kernels  13.8 us (24%)
  starting transfers between devices  8.82 us (16%)
  other arithmetic  6.89 us (12%)
  local copies, waits for them, and re-layouts  6.04 us (11%)
  between operations  2.11 us (4%)
    ppermute x4, waiting for transfers between devices, ring_gather(): ahead = lax.ppermute(ahead, 'depth', forward)  16 us
    pallas_call x1, Pallas kernels, render_layers(): pl.pallas_call(render_kernel, grid=(brick_rows // block_rows,), in_specs=...  13.8 us
    ppermute x4, starting transfers between devices, ring_gather(): ahead = lax.ppermute(ahead, 'depth', forward)  7.99 us
    ppermute x3, waiting for transfers between devices, ring_gather(): behind = lax.ppermute(behind, 'depth', backward)  2.59 us
    select_n x1, other arithmetic, on_device(): return jnp.where(in_my_half[:, None, None], mine, received)  2.58 us
    gather x2, local copies, waits for them, and re-layouts, composite_rows(): front_rows = jnp.take(flat, front_idx, axis=0, mode='clip')  1.99 us
    gather x2, local copies, waits for them, and re-layouts, composite_rows(): back_rows = jnp.take(flat, back_idx, axis=0, mode='clip')  1.99 us
    unnamed x8, local copies, waits for them, and re-layouts  1.27 us
  transfers between devices with their start and end apart: 8, of which 6 were waited for; matrix products, arithmetic and copies ran while one was open for 10% of the time, Pallas kernels for 0%

profile of v24, /device:TPU:0, one launch (start us, length us, event | category | flops | bytes accessed | tf_op | source)
XLA Modules:
  0.0 56.3 jit_solution(16213150701411106606)
XLA Ops:
  1.9 0.1 add_convert_fusion
  2.0 0.7 %dynamic_update_slice.3.slot_ref = f32[130,4,128]{2,1,0:T(4,128)} pad(f32[1,1,3]{2,1,0:T(1,128)S(1)} %add_convert_fusion, f32[]{:T(128)} %constant.61.clone.1), padding=128_1x0_3x0_125 | pad | bytes 266256 | tf_op jit(solution)/shard_map/dynamic_update_slice | solution.py:123
  2.8 13.8 %shard_map.73 = f32[130,4,128]{2,1,0:T(4,128)} custom-call(f32[1]{0:T(128)S(6)} %copy.25.absorb_ref, f32[3]{0:T(128)} %slope_ref.1, f32[3]{0:T(128)} %offset_ref.1, s32[1,1]{1,0:T(1,128)} %copy.24.shown_ref, f32[16384,128]{1,0:T(8,128)} %bitcast.17, f32[130,4,128]{2,1,0:T(4,128)} %dynamic_update_slice.3.slot_ref), custom_call_target="tpu_custom_call", output_to_operand_aliasing={{}: (5, {})} | custom-call | tf_op jit(solution)/shard_map/pallas_call | solution.py:45
  16.6 3.0 %collective-permute-start = (f32[130,4,128]{2,1,0:T(4,128)}, f32[130,4,128]{2,1,0:T(4,128)S(1)}, u32[]{:S(2)}, u32[]{:S(2)}) collective-permute-start(f32[130,4,128]{2,1,0:T(4,128)} %shard_map.73), channel_id=1, source_target_pairs={{0,4},{4,8},{8,12},{12,14},{14,10},{10,6},{6,2},{2,0},{1,5},{5,9},... | collective-permute-start | bytes 798728 | tf_op jit(solution)/shard_map/ppermute | solution.py:101
  19.6 6.5 %collective-permute-done = f32[130,4,128]{2,1,0:T(4,128)S(1)} collective-permute-done((f32[130,4,128]{2,1,0:T(4,128)}, f32[130,4,128]{2,1,0:T(4,128)S(1)}, u32[]{:S(2)}, u32[]{:S(2)}) %collective-permute-start) | collective-permute-done | bytes 266272 | tf_op jit(solution)/shard_map/ppermute | solution.py:101
  26.2 1.8 %collective-permute-start.2 = (f32[130,4,128]{2,1,0:T(4,128)S(1)}, f32[130,4,128]{2,1,0:T(4,128)S(1)}, u32[]{:S(2)}, u32[]{:S(2)}) collective-permute-start(f32[130,4,128]{2,1,0:T(4,128)S(1)} %collective-permute-done), channel_id=1, source_target_pairs={{0,4},{4,8},{8,12},{12,14},{14,10},{10,6},{6,2},{2,0},{1,5},{5,9},... | collective-permute-start | bytes 798728 | tf_op jit(solution)/shard_map/ppermute | solution.py:101
  28.0 0.8 %and_select_fusion.1 = (s32[256]{0:T(256)S(1)}, s32[256]{0:T(256)S(1)}) fusion(s32[4096]{0:T(1024)} %param.13, s32[]{:T(128)S(6)} %select_n.113, s32[]{:T(128)S(6)} %select_n.111), kind=kLoop, calls=%fused_computation.59 | loop fusion | flops 5632 | bytes 4104 | tf_op jit(solution)/shard_map/jit(remainder)/select_n | solution.py:135
  28.8 1.0 %constant_dynamic-update-slice_fusion.7 = f32[1040,4,128]{2,1,0:T(4,128)S(1)} fusion(f32[130,4,128]{2,1,0:T(4,128)} %shard_map.73), kind=kLoop, calls=%fused_computation.33 | loop fusion | bytes 532480
  29.8 0.3 collective-permute-start.3
  30.1 0.8 %fusion.11 = pred[256]{0:T(512)(128)(4,1)S(1)} fusion(s32[]{:T(128)S(6)} %axis_index.25, s32[4096]{0:T(1024)} %param.13, s32[]{:T(128)S(6)} %select_n.111), kind=kLoop, calls=%fused_computation.67 | loop fusion | flops 4096 | bytes 1288 | tf_op jit(solution)/shard_map/eq | solution.py:139
  30.8 2.9 %collective-permute-done.2 = f32[130,4,128]{2,1,0:T(4,128)S(1)} collective-permute-done((f32[130,4,128]{2,1,0:T(4,128)S(1)}, f32[130,4,128]{2,1,0:T(4,128)S(1)}, u32[]{:S(2)}, u32[]{:S(2)}) %collective-permute-start.2) | collective-permute-done | bytes 266272 | tf_op jit(solution)/shard_map/ppermute | solution.py:101
  33.8 1.5 %collective-permute-start.4 = (f32[130,4,128]{2,1,0:T(4,128)S(1)}, f32[130,4,128]{2,1,0:T(4,128)S(1)}, u32[]{:S(2)}, u32[]{:S(2)}) collective-permute-start(f32[130,4,128]{2,1,0:T(4,128)S(1)} %collective-permute-done.2), channel_id=1, source_target_pairs={{0,4},{4,8},{8,12},{12,14},{14,10},{10,6},{6,2},{2,0},{1,5},{5,9},... | collective-permute-start | bytes 798728 | tf_op jit(solution)/shard_map/ppermute | solution.py:101
  35.3 1.5 %collective-permute-done.3 = f32[130,4,128]{2,1,0:T(4,128)S(1)} collective-permute-done((f32[130,4,128]{2,1,0:T(4,128)S(1)}, f32[130,4,128]{2,1,0:T(4,128)S(1)}, u32[]{:S(2)}, u32[]{:S(2)}) %collective-permute-start.3) | collective-permute-done | bytes 266272 | tf_op jit(solution)/shard_map/ppermute | solution.py:104
  36.8 0.5 collective-permute-start.5
  37.4 3.0 %collective-permute-done.4 = f32[130,4,128]{2,1,0:T(4,128)S(1)} collective-permute-done((f32[130,4,128]{2,1,0:T(4,128)S(1)}, f32[130,4,128]{2,1,0:T(4,128)S(1)}, u32[]{:S(2)}, u32[]{:S(2)}) %collective-permute-start.4) | collective-permute-done | bytes 266272 | tf_op jit(solution)/shard_map/ppermute | solution.py:101
  40.4 1.7 %collective-permute-start.6 = (f32[130,4,128]{2,1,0:T(4,128)S(1)}, f32[130,4,128]{2,1,0:T(4,128)S(1)}, u32[]{:S(2)}, u32[]{:S(2)}) collective-permute-start(f32[130,4,128]{2,1,0:T(4,128)S(1)} %collective-permute-done.4), channel_id=1, source_target_pairs={{0,4},{4,8},{8,12},{12,14},{14,10},{10,6},{6,2},{2,0},{1,5},{5,9},... | collective-permute-start | bytes 798728 | tf_op jit(solution)/shard_map/ppermute | solution.py:101
  42.2 1.1 %collective-permute-done.5 = f32[130,4,128]{2,1,0:T(4,128)S(1)} collective-permute-done((f32[130,4,128]{2,1,0:T(4,128)S(1)}, f32[130,4,128]{2,1,0:T(4,128)S(1)}, u32[]{:S(2)}, u32[]{:S(2)}) %collective-permute-start.5) | collective-permute-done | bytes 266272 | tf_op jit(solution)/shard_map/ppermute | solution.py:104
  43.3 3.5 %collective-permute-done.6 = f32[130,4,128]{2,1,0:T(4,128)S(1)} collective-permute-done((f32[130,4,128]{2,1,0:T(4,128)S(1)}, f32[130,4,128]{2,1,0:T(4,128)S(1)}, u32[]{:S(2)}, u32[]{:S(2)}) %collective-permute-start.6) | collective-permute-done | bytes 266272 | tf_op jit(solution)/shard_map/ppermute | solution.py:101
  46.9 0.1 copy.14
  47.0 0.1 select_reduce_fusion.2
  47.1 0.1 fusion.12
  47.2 0.1 select_reduce_fusion.1
  47.3 1.0 %gather_fusion.1 = f32[256,4,128]{2,1,0:T(4,128)S(1)} fusion(f32[1040,4,128]{2,1,0:T(4,128)S(1)} %constant_dynamic-update-slice_fusion, s32[1024]{0:T(1024)S(1)} %pad_clamp_fusion.2), kind=kCustom, calls=%fused_computation.1 | custom fusion | bytes 1049600 | tf_op jit(solution)/shard_map/jit(_take)/gather | solution.py:81
  48.3 1.0 %gather_fusion = f32[256,4,128]{2,1,0:T(4,128)S(1)} fusion(f32[1040,4,128]{2,1,0:T(4,128)S(1)} %constant_dynamic-update-slice_fusion, s32[1024]{0:T(1024)S(1)} %pad_clamp_fusion.3), kind=kCustom, calls=%fused_computation | custom fusion | bytes 1049600 | tf_op jit(solution)/shard_map/jit(_take)/gather | solution.py:82
  49.4 0.4 negate_exponential_fusion.1
  49.8 0.2 fusion.1
  50.0 1.0 %pad_maximum_fusion = f32[256,4,128]{2,1,0:T(4,128)} fusion(f32[256,1,128]{2,1,0:T(1,128)S(1)} %get-tuple-element.27, f32[256,3,128]{2,1,0:T(4,128)S(1)} %fusion.1), kind=kLoop, calls=%fused_computation.8 | loop fusion | flops 131072 | bytes 1048576 | tf_op jit(solution)/shard_map/concatenate | solution.py:86
  51.0 1.0 %gather_fusion.3 = f32[256,4,128]{2,1,0:T(4,128)S(1)} fusion(f32[1040,4,128]{2,1,0:T(4,128)S(1)} %constant_dynamic-update-slice_fusion, s32[1024]{0:T(1024)S(1)} %pad_clamp_fusion), kind=kCustom, calls=%fused_computation.3 | custom fusion | bytes 1049600 | tf_op jit(solution)/shard_map/jit(_take)/gather | solution.py:81
  52.0 1.0 %gather_fusion.2 = f32[256,4,128]{2,1,0:T(4,128)S(1)} fusion(f32[1040,4,128]{2,1,0:T(4,128)S(1)} %constant_dynamic-update-slice_fusion, s32[1024]{0:T(1024)S(1)} %pad_clamp_fusion.1), kind=kCustom, calls=%fused_computation.2 | custom fusion | bytes 1049600 | tf_op jit(solution)/shard_map/jit(_take)/gather | solution.py:82
  53.0 0.4 negate_exponential_fusion
  53.5 0.2 fusion
  53.7 2.6 %maximum_select_fusion = f32[256,4,128]{2,1,0:T(4,128)} fusion(f32[256,4,128]{2,1,0:T(4,128)} %collective-permute-done.7, f32[256,1,128]{2,1,0:T(1,128)S(1)} %get-tuple-element.25, f32[256,3,128]{2,1,0:T(4,128)S(1)} %fusion, pred[256]{0:T(512)(128)(4,1)S(1)} %fusion.11), kind=kLoop, calls=%fused_computation.9 | loop fusion | flops 262144 | bytes 1573120 | tf_op jit(solution)/shard_map/jit(_where)/select_n | solution.py:140
  (23 shorter events, 0.4 us)
Async XLA Ops:
  16.6 9.6 %collective-permute-start = (f32[130,4,128]{2,1,0:T(4,128)}, f32[130,4,128]{2,1,0:T(4,128)S(1)}, u32[]{:S(2)}, u32[]{:S(2)}) collective-permute-start(f32[130,4,128]{2,1,0:T(4,128)} %shard_map.73), channel_id=1, source_target_pairs={{0,4},{4,8},{8,12},{12,14},{14,10},{10,6},{6,2},{2,0},{1,5},{5,9},... | collective-permute-start | bytes 798728 | tf_op jit(solution)/shard_map/ppermute | solution.py:101
  19.6 10.2 %collective-permute-start.1 = (f32[130,4,128]{2,1,0:T(4,128)}, f32[130,4,128]{2,1,0:T(4,128)S(1)}, u32[]{:S(2)}, u32[]{:S(2)}) collective-permute-start(f32[130,4,128]{2,1,0:T(4,128)} %shard_map.73), channel_id=1, source_target_pairs={{4,0},{8,4},{12,8},{14,12},{10,14},{6,10},{2,6},{0,2},{5,1},{9,5},... | collective-permute-start | bytes 798728 | tf_op jit(solution)/shard_map/ppermute | solution.py:104
  26.2 7.6 %collective-permute-start.2 = (f32[130,4,128]{2,1,0:T(4,128)S(1)}, f32[130,4,128]{2,1,0:T(4,128)S(1)}, u32[]{:S(2)}, u32[]{:S(2)}) collective-permute-start(f32[130,4,128]{2,1,0:T(4,128)S(1)} %collective-permute-done), channel_id=1, source_target_pairs={{0,4},{4,8},{8,12},{12,14},{14,10},{10,6},{6,2},{2,0},{1,5},{5,9},... | collective-permute-start | bytes 798728 | tf_op jit(solution)/shard_map/ppermute | solution.py:101
  29.8 7.0 %collective-permute-start.3 = (f32[130,4,128]{2,1,0:T(4,128)S(1)}, f32[130,4,128]{2,1,0:T(4,128)S(1)}, u32[]{:S(2)}, u32[]{:S(2)}) collective-permute-start(f32[130,4,128]{2,1,0:T(4,128)S(1)} %collective-permute-done.1), channel_id=1, source_target_pairs={{4,0},{8,4},{12,8},{14,12},{10,14},{6,10},{2,6},{0,2},{5,1},{9,5},... | collective-permute-start | bytes 798728 | tf_op jit(solution)/shard_map/ppermute | solution.py:104
  33.8 6.7 %collective-permute-start.4 = (f32[130,4,128]{2,1,0:T(4,128)S(1)}, f32[130,4,128]{2,1,0:T(4,128)S(1)}, u32[]{:S(2)}, u32[]{:S(2)}) collective-permute-start(f32[130,4,128]{2,1,0:T(4,128)S(1)} %collective-permute-done.2), channel_id=1, source_target_pairs={{0,4},{4,8},{8,12},{12,14},{14,10},{10,6},{6,2},{2,0},{1,5},{5,9},... | collective-permute-start | bytes 798728 | tf_op jit(solution)/shard_map/ppermute | solution.py:101
  36.8 6.4 %collective-permute-start.5 = (f32[130,4,128]{2,1,0:T(4,128)S(1)}, f32[130,4,128]{2,1,0:T(4,128)S(1)}, u32[]{:S(2)}, u32[]{:S(2)}) collective-permute-start(f32[130,4,128]{2,1,0:T(4,128)S(1)} %collective-permute-done.3), channel_id=1, source_target_pairs={{4,0},{8,4},{12,8},{14,12},{10,14},{6,10},{2,6},{0,2},{5,1},{9,5},... | collective-permute-start | bytes 798728 | tf_op jit(solution)/shard_map/ppermute | solution.py:104
  40.4 6.4 %collective-permute-start.6 = (f32[130,4,128]{2,1,0:T(4,128)S(1)}, f32[130,4,128]{2,1,0:T(4,128)S(1)}, u32[]{:S(2)}, u32[]{:S(2)}) collective-permute-start(f32[130,4,128]{2,1,0:T(4,128)S(1)} %collective-permute-done.4), channel_id=1, source_target_pairs={{0,4},{4,8},{8,12},{12,14},{14,10},{10,6},{6,2},{2,0},{1,5},{5,9},... | collective-permute-start | bytes 798728 | tf_op jit(solution)/shard_map/ppermute | solution.py:101
  51.0 2.6 %collective-permute-start.7 = (f32[256,4,128]{2,1,0:T(4,128)}, f32[256,4,128]{2,1,0:T(4,128)}, u32[]{:S(2)}, u32[]{:S(2)}) collective-permute-start(f32[256,4,128]{2,1,0:T(4,128)} %pad_maximum_fusion), channel_id=1, source_target_pairs={{0,1},{1,0},{2,3},{3,2},{4,5},{5,4},{6,7},{7,6},{8,9},{9,8},{10,11... | collective-permute-start | bytes 1572872 | tf_op jit(solution)/shard_map/ppermute | solution.py:136

commit v25 on v24

--- a/solution.py
+++ b/solution.py
@@ -81,9 +81,10 @@
     back_rows = jnp.take(flat, back_idx, axis=0, mode="clip")
     front_rows = jnp.take(flat, front_idx, axis=0, mode="clip")
     front_depth = front_rows[:, 3:4, :]
-    colours = front_rows[:, :3, :] + jnp.exp(-front_depth) * back_rows[:, :3, :]
+    is_colour = lax.broadcasted_iota(jnp.int32, front_rows.shape, 1) < 3
+    colours = front_rows + jnp.exp(-front_depth) * back_rows
     opacity = 1.0 - jnp.exp(-(front_depth + back_rows[:, 3:4, :]))
-    return jnp.concatenate([colours, opacity], axis=1)
+    return jnp.where(is_colour, colours, opacity)
 
 
 def ring_order(count):

time: 56.6 us -> 56.9 us (level)
  waiting for transfers between devices: 18.6 us -> 19.3 us
    select_n x1 -> x2, other arithmetic: 0.84 us -> 1.91 us  [the longest x1 1.07 us: composite_rows(): return jnp.where(is_colour, colours, opacity)]
    concatenate x1 -> x0, other arithmetic: 1.03 us -> none  [composite_rows(): return jnp.concatenate([colours, opacity], axis=1)]
    ppermute x4, waiting for transfers between devices: 16 us -> 16.7 us  [ring_gather(): ahead = lax.ppermute(ahead, 'depth', forward)]
  transfers between devices with their start and end apart: 8 -> 8, of which waited for: 6 -> 6; matrix products, arithmetic and copies ran while one was open for 10% -> 9% of each run, Pallas kernels for 0% -> 0%
where the time goes in v25:
time: 56.9 us; the launch traced here: 56.6 us
  waiting for transfers between devices  19.3 us (34%)
  Pallas kernels  13.8 us (24%)
  starting transfers between devices  8.82 us (16%)
  other arithmetic  6.47 us (11%)
  local copies, waits for them, and re-layouts  6.03 us (11%)
  between operations  2.09 us (4%)
    ppermute x4, waiting for transfers between devices, ring_gather(): ahead = lax.ppermute(ahead, 'depth', forward)  16.7 us
    pallas_call x1, Pallas kernels, render_layers(): pl.pallas_call(render_kernel, grid=(brick_rows // block_rows,), in_specs=...  13.8 us
    ppermute x4, starting transfers between devices, ring_gather(): ahead = lax.ppermute(ahead, 'depth', forward)  7.99 us
    select_n x1, other arithmetic, on_device(): return jnp.where(in_my_half[:, None, None], mine, received)  2.61 us
    ppermute x3, waiting for transfers between devices, ring_gather(): behind = lax.ppermute(behind, 'depth', backward)  2.59 us
    gather x2, local copies, waits for them, and re-layouts, composite_rows(): back_rows = jnp.take(flat, back_idx, axis=0, mode='clip')  1.99 us
    gather x2, local copies, waits for them, and re-layouts, composite_rows(): front_rows = jnp.take(flat, front_idx, axis=0, mode='clip')  1.99 us
    unnamed x8, local copies, waits for them, and re-layouts  1.27 us
  transfers between devices with their start and end apart: 8, of which 6 were waited for; matrix products, arithmetic and copies ran while one was open for 9% of the time, Pallas kernels for 0%

profile of v25, /device:TPU:0, one launch (start us, length us, event | category | flops | bytes accessed | tf_op | source)
XLA Modules:
  0.0 56.6 jit_solution(17206827007326127307)
XLA Ops:
  1.9 0.1 add_convert_fusion
  2.0 0.7 %dynamic_update_slice.3.slot_ref = f32[130,4,128]{2,1,0:T(4,128)} pad(f32[1,1,3]{2,1,0:T(1,128)S(1)} %add_convert_fusion, f32[]{:T(128)} %constant.63.clone.1), padding=128_1x0_3x0_125 | pad | bytes 266256 | tf_op jit(solution)/shard_map/dynamic_update_slice | solution.py:124
  2.8 13.8 %shard_map.73 = f32[130,4,128]{2,1,0:T(4,128)} custom-call(f32[1]{0:T(128)S(6)} %copy.22.absorb_ref, f32[3]{0:T(128)} %slope_ref.1, f32[3]{0:T(128)} %offset_ref.1, s32[1,1]{1,0:T(1,128)} %copy.21.shown_ref, f32[16384,128]{1,0:T(8,128)} %bitcast.18, f32[130,4,128]{2,1,0:T(4,128)} %dynamic_update_slice.3.slot_ref), custom_call_target="tpu_custom_call", output_to_operand_aliasing={{}: (5, {})} | custom-call | tf_op jit(solution)/shard_map/pallas_call | solution.py:45
  16.6 3.0 %collective-permute-start = (f32[130,4,128]{2,1,0:T(4,128)}, f32[130,4,128]{2,1,0:T(4,128)S(1)}, u32[]{:S(2)}, u32[]{:S(2)}) collective-permute-start(f32[130,4,128]{2,1,0:T(4,128)} %shard_map.73), channel_id=1, source_target_pairs={{0,4},{4,8},{8,12},{12,14},{14,10},{10,6},{6,2},{2,0},{1,5},{5,9},... | collective-permute-start | bytes 798728 | tf_op jit(solution)/shard_map/ppermute | solution.py:102
  19.6 0.0 collective-permute-start.1
  19.6 6.5 %collective-permute-done = f32[130,4,128]{2,1,0:T(4,128)S(1)} collective-permute-done((f32[130,4,128]{2,1,0:T(4,128)}, f32[130,4,128]{2,1,0:T(4,128)S(1)}, u32[]{:S(2)}, u32[]{:S(2)}) %collective-permute-start) | collective-permute-done | bytes 266272 | tf_op jit(solution)/shard_map/ppermute | solution.py:102
  26.2 1.8 %collective-permute-start.2 = (f32[130,4,128]{2,1,0:T(4,128)S(1)}, f32[130,4,128]{2,1,0:T(4,128)S(1)}, u32[]{:S(2)}, u32[]{:S(2)}) collective-permute-start(f32[130,4,128]{2,1,0:T(4,128)S(1)} %collective-permute-done), channel_id=1, source_target_pairs={{0,4},{4,8},{8,12},{12,14},{14,10},{10,6},{6,2},{2,0},{1,5},{5,9},... | collective-permute-start | bytes 798728 | tf_op jit(solution)/shard_map/ppermute | solution.py:102
  28.0 0.8 %and_select_fusion = (s32[256]{0:T(256)S(1)}, s32[256]{0:T(256)S(1)}) fusion(s32[4096]{0:T(1024)} %param.13, s32[]{:T(128)S(6)} %select_n.118, s32[]{:T(128)S(6)} %select_n.120), kind=kLoop, calls=%fused_computation.53 | loop fusion | flops 5632 | bytes 4104 | tf_op jit(solution)/shard_map/jit(remainder)/select_n | solution.py:139
  28.8 1.0 %constant_dynamic-update-slice_fusion.7 = f32[1040,4,128]{2,1,0:T(4,128)S(1)} fusion(f32[130,4,128]{2,1,0:T(4,128)} %shard_map.73), kind=kLoop, calls=%fused_computation.29 | loop fusion | bytes 532480
  29.8 0.0 collective-permute-done.1
  29.8 0.3 collective-permute-start.3
  30.1 3.7 %collective-permute-done.2 = f32[130,4,128]{2,1,0:T(4,128)S(1)} collective-permute-done((f32[130,4,128]{2,1,0:T(4,128)S(1)}, f32[130,4,128]{2,1,0:T(4,128)S(1)}, u32[]{:S(2)}, u32[]{:S(2)}) %collective-permute-start.2) | collective-permute-done | bytes 266272 | tf_op jit(solution)/shard_map/ppermute | solution.py:102
  33.8 1.5 %collective-permute-start.4 = (f32[130,4,128]{2,1,0:T(4,128)S(1)}, f32[130,4,128]{2,1,0:T(4,128)S(1)}, u32[]{:S(2)}, u32[]{:S(2)}) collective-permute-start(f32[130,4,128]{2,1,0:T(4,128)S(1)} %collective-permute-done.2), channel_id=1, source_target_pairs={{0,4},{4,8},{8,12},{12,14},{14,10},{10,6},{6,2},{2,0},{1,5},{5,9},... | collective-permute-start | bytes 798728 | tf_op jit(solution)/shard_map/ppermute | solution.py:102
  35.3 1.5 %collective-permute-done.3 = f32[130,4,128]{2,1,0:T(4,128)S(1)} collective-permute-done((f32[130,4,128]{2,1,0:T(4,128)S(1)}, f32[130,4,128]{2,1,0:T(4,128)S(1)}, u32[]{:S(2)}, u32[]{:S(2)}) %collective-permute-start.3) | collective-permute-done | bytes 266272 | tf_op jit(solution)/shard_map/ppermute | solution.py:105
  36.8 0.5 collective-permute-start.5
  37.4 3.0 %collective-permute-done.4 = f32[130,4,128]{2,1,0:T(4,128)S(1)} collective-permute-done((f32[130,4,128]{2,1,0:T(4,128)S(1)}, f32[130,4,128]{2,1,0:T(4,128)S(1)}, u32[]{:S(2)}, u32[]{:S(2)}) %collective-permute-start.4) | collective-permute-done | bytes 266272 | tf_op jit(solution)/shard_map/ppermute | solution.py:102
  40.4 1.7 %collective-permute-start.6 = (f32[130,4,128]{2,1,0:T(4,128)S(1)}, f32[130,4,128]{2,1,0:T(4,128)S(1)}, u32[]{:S(2)}, u32[]{:S(2)}) collective-permute-start(f32[130,4,128]{2,1,0:T(4,128)S(1)} %collective-permute-done.4), channel_id=1, source_target_pairs={{0,4},{4,8},{8,12},{12,14},{14,10},{10,6},{6,2},{2,0},{1,5},{5,9},... | collective-permute-start | bytes 798728 | tf_op jit(solution)/shard_map/ppermute | solution.py:102
  42.2 1.1 %collective-permute-done.5 = f32[130,4,128]{2,1,0:T(4,128)S(1)} collective-permute-done((f32[130,4,128]{2,1,0:T(4,128)S(1)}, f32[130,4,128]{2,1,0:T(4,128)S(1)}, u32[]{:S(2)}, u32[]{:S(2)}) %collective-permute-start.5) | collective-permute-done | bytes 266272 | tf_op jit(solution)/shard_map/ppermute | solution.py:105
  43.3 3.5 %collective-permute-done.6 = f32[130,4,128]{2,1,0:T(4,128)S(1)} collective-permute-done((f32[130,4,128]{2,1,0:T(4,128)S(1)}, f32[130,4,128]{2,1,0:T(4,128)S(1)}, u32[]{:S(2)}, u32[]{:S(2)}) %collective-permute-start.6) | collective-permute-done | bytes 266272 | tf_op jit(solution)/shard_map/ppermute | solution.py:102
  46.9 0.1 copy.11
  47.0 0.1 select_reduce_fusion.2
  47.1 0.1 select_reduce_fusion.1
  47.2 1.0 %gather_fusion.1 = f32[256,4,128]{2,1,0:T(4,128)S(1)} fusion(f32[1040,4,128]{2,1,0:T(4,128)S(1)} %constant_dynamic-update-slice_fusion, s32[1024]{0:T(1024)S(1)} %pad_clamp_fusion.2), kind=kCustom, calls=%fused_computation.1 | custom fusion | bytes 1049600 | tf_op jit(solution)/shard_map/jit(_take)/gather | solution.py:81
  48.3 1.0 %gather_fusion = f32[256,4,128]{2,1,0:T(4,128)S(1)} fusion(f32[1040,4,128]{2,1,0:T(4,128)S(1)} %constant_dynamic-update-slice_fusion, s32[1024]{0:T(1024)S(1)} %pad_clamp_fusion.3), kind=kCustom, calls=%fused_computation | custom fusion | bytes 1049600 | tf_op jit(solution)/shard_map/jit(_take)/gather | solution.py:82
  49.3 0.4 negate_exponential_fusion.1
  49.7 1.1 %add_select_fusion = f32[256,4,128]{2,1,0:T(4,128)} fusion(f32[256,4,128]{2,1,0:T(4,128)S(1)} %gather_fusion, f32[256,4,128]{2,1,0:T(4,128)S(1)} %gather_fusion.1, f32[256,128]{1,0:T(8,128)S(1)} %bitcast.23, f32[256,128]{1,0:T(8,128)S(1)} %bitcast.22, pred[4]{0:T(512)(128)(4,1)S(1)} %iota_compare_fusion), kind=kLoop, calls=%fused_computation.5 | loop fusion | flops 393216 | bytes 1835012 | tf_op jit(solution)/shard_map/jit(_where)/select_n | solution.py:87
  50.8 0.0 collective-permute-start.7
  50.8 0.8 %fusion.9 = pred[256]{0:T(512)(128)(4,1)S(1)} fusion(s32[]{:T(128)S(6)} %axis_index.25, s32[4096]{0:T(1024)} %param.13, s32[]{:T(128)S(6)} %select_n.118), kind=kLoop, calls=%fused_computation.63 | loop fusion | flops 4096 | bytes 1288 | tf_op jit(solution)/shard_map/eq | solution.py:140
  51.5 1.0 %gather_fusion.3 = f32[256,4,128]{2,1,0:T(4,128)S(1)} fusion(f32[1040,4,128]{2,1,0:T(4,128)S(1)} %constant_dynamic-update-slice_fusion, s32[1024]{0:T(1024)S(1)} %pad_clamp_fusion), kind=kCustom, calls=%fused_computation.3 | custom fusion | bytes 1049600 | tf_op jit(solution)/shard_map/jit(_take)/gather | solution.py:81
  52.6 1.0 %gather_fusion.2 = f32[256,4,128]{2,1,0:T(4,128)S(1)} fusion(f32[1040,4,128]{2,1,0:T(4,128)S(1)} %constant_dynamic-update-slice_fusion, s32[1024]{0:T(1024)S(1)} %pad_clamp_fusion.1), kind=kCustom, calls=%fused_computation.2 | custom fusion | bytes 1049600 | tf_op jit(solution)/shard_map/jit(_take)/gather | solution.py:82
  53.6 0.4 negate_exponential_fusion
  54.0 2.6 %select_select_fusion = f32[256,4,128]{2,1,0:T(4,128)} fusion(f32[256,4,128]{2,1,0:T(4,128)} %collective-permute-done.7, f32[256,4,128]{2,1,0:T(4,128)S(1)} %gather_fusion.2, f32[256,4,128]{2,1,0:T(4,128)S(1)} %gather_fusion.3, f32[256,128]{1,0:T(8,128)S(1)} %bitcast.21, f32[256,128]{1,0:T(8,128)S(1)} %bitcast.20, pred[4]{0:T(512)(128)(4,1)S(1)} %iota_compare_fusion, ...), kind=kLoop, calls=%fused_computation.4 | loop fusion | flops 524288 | bytes 2359556 | tf_op jit(solution)/shard_map/jit(_where)/select_n | solution.py:141
  (21 shorter events, 0.4 us)
Async XLA Ops:
  16.6 9.6 %collective-permute-start = (f32[130,4,128]{2,1,0:T(4,128)}, f32[130,4,128]{2,1,0:T(4,128)S(1)}, u32[]{:S(2)}, u32[]{:S(2)}) collective-permute-start(f32[130,4,128]{2,1,0:T(4,128)} %shard_map.73), channel_id=1, source_target_pairs={{0,4},{4,8},{8,12},{12,14},{14,10},{10,6},{6,2},{2,0},{1,5},{5,9},... | collective-permute-start | bytes 798728 | tf_op jit(solution)/shard_map/ppermute | solution.py:102
  19.6 10.2 %collective-permute-start.1 = (f32[130,4,128]{2,1,0:T(4,128)}, f32[130,4,128]{2,1,0:T(4,128)S(1)}, u32[]{:S(2)}, u32[]{:S(2)}) collective-permute-start(f32[130,4,128]{2,1,0:T(4,128)} %shard_map.73), channel_id=1, source_target_pairs={{4,0},{8,4},{12,8},{14,12},{10,14},{6,10},{2,6},{0,2},{5,1},{9,5},... | collective-permute-start | bytes 798728 | tf_op jit(solution)/shard_map/ppermute | solution.py:105
  26.2 7.6 %collective-permute-start.2 = (f32[130,4,128]{2,1,0:T(4,128)S(1)}, f32[130,4,128]{2,1,0:T(4,128)S(1)}, u32[]{:S(2)}, u32[]{:S(2)}) collective-permute-start(f32[130,4,128]{2,1,0:T(4,128)S(1)} %collective-permute-done), channel_id=1, source_target_pairs={{0,4},{4,8},{8,12},{12,14},{14,10},{10,6},{6,2},{2,0},{1,5},{5,9},... | collective-permute-start | bytes 798728 | tf_op jit(solution)/shard_map/ppermute | solution.py:102
  29.8 7.0 %collective-permute-start.3 = (f32[130,4,128]{2,1,0:T(4,128)S(1)}, f32[130,4,128]{2,1,0:T(4,128)S(1)}, u32[]{:S(2)}, u32[]{:S(2)}) collective-permute-start(f32[130,4,128]{2,1,0:T(4,128)S(1)} %collective-permute-done.1), channel_id=1, source_target_pairs={{4,0},{8,4},{12,8},{14,12},{10,14},{6,10},{2,6},{0,2},{5,1},{9,5},... | collective-permute-start | bytes 798728 | tf_op jit(solution)/shard_map/ppermute | solution.py:105
  33.8 6.7 %collective-permute-start.4 = (f32[130,4,128]{2,1,0:T(4,128)S(1)}, f32[130,4,128]{2,1,0:T(4,128)S(1)}, u32[]{:S(2)}, u32[]{:S(2)}) collective-permute-start(f32[130,4,128]{2,1,0:T(4,128)S(1)} %collective-permute-done.2), channel_id=1, source_target_pairs={{0,4},{4,8},{8,12},{12,14},{14,10},{10,6},{6,2},{2,0},{1,5},{5,9},... | collective-permute-start | bytes 798728 | tf_op jit(solution)/shard_map/ppermute | solution.py:102
  36.8 6.4 %collective-permute-start.5 = (f32[130,4,128]{2,1,0:T(4,128)S(1)}, f32[130,4,128]{2,1,0:T(4,128)S(1)}, u32[]{:S(2)}, u32[]{:S(2)}) collective-permute-start(f32[130,4,128]{2,1,0:T(4,128)S(1)} %collective-permute-done.3), channel_id=1, source_target_pairs={{4,0},{8,4},{12,8},{14,12},{10,14},{6,10},{2,6},{0,2},{5,1},{9,5},... | collective-permute-start | bytes 798728 | tf_op jit(solution)/shard_map/ppermute | solution.py:105
  40.4 6.4 %collective-permute-start.6 = (f32[130,4,128]{2,1,0:T(4,128)S(1)}, f32[130,4,128]{2,1,0:T(4,128)S(1)}, u32[]{:S(2)}, u32[]{:S(2)}) collective-permute-start(f32[130,4,128]{2,1,0:T(4,128)S(1)} %collective-permute-done.4), channel_id=1, source_target_pairs={{0,4},{4,8},{8,12},{12,14},{14,10},{10,6},{6,2},{2,0},{1,5},{5,9},... | collective-permute-start | bytes 798728 | tf_op jit(solution)/shard_map/ppermute | solution.py:102
  50.8 3.2 %collective-permute-start.7 = (f32[256,4,128]{2,1,0:T(4,128)}, f32[256,4,128]{2,1,0:T(4,128)}, u32[]{:S(2)}, u32[]{:S(2)}) collective-permute-start(f32[256,4,128]{2,1,0:T(4,128)} %add_select_fusion), channel_id=1, source_target_pairs={{0,1},{1,0},{2,3},{3,2},{4,5},{5,4},{6,7},{7,6},{8,9},{9,8},{10,11... | collective-permute-start | bytes 1572872 | tf_op jit(solution)/shard_map/ppermute | solution.py:137

commit v26 on v24

--- a/solution.py
+++ b/solution.py
@@ -32,7 +32,7 @@
 
     zeros = jnp.zeros((block_rows, pixels), jnp.float32)
     carry = (jnp.full((block_rows, pixels), 0.5, jnp.float32), zeros, zeros, zeros, zeros, zeros)
-    carry = lax.fori_loop(0, sample_count, one_step, carry, unroll=64)
+    carry = lax.fori_loop(0, sample_count, one_step, carry, unroll=128)
     row_ids = pl.program_id(0) * block_rows + lax.broadcasted_iota(jnp.int32, (block_rows, pixels), 0)
     visible = row_ids < shown
     for channel in range(3):

time: 56.6 us -> 57.1 us (level)
  Pallas kernels: 13.8 us -> 14.4 us
where the time goes in v26:
time: 57.1 us; the launch traced here: 56.8 us
  waiting for transfers between devices  18.6 us (33%)
  Pallas kernels  14.4 us (25%)
  starting transfers between devices  8.82 us (15%)
  other arithmetic  6.89 us (12%)
  local copies, waits for them, and re-layouts  6.05 us (11%)
  between operations  2.11 us (4%)
    ppermute x4, waiting for transfers between devices, ring_gather(): ahead = lax.ppermute(ahead, 'depth', forward)  16 us
    pallas_call x1, Pallas kernels, render_layers(): pl.pallas_call(render_kernel, grid=(brick_rows // block_rows,), in_specs=...  14.4 us
    ppermute x4, starting transfers between devices, ring_gather(): ahead = lax.ppermute(ahead, 'depth', forward)  7.99 us
    ppermute x3, waiting for transfers between devices, ring_gather(): behind = lax.ppermute(behind, 'depth', backward)  2.59 us
    select_n x1, other arithmetic, on_device(): return jnp.where(in_my_half[:, None, None], mine, received)  2.58 us
    gather x2, local copies, waits for them, and re-layouts, composite_rows(): front_rows = jnp.take(flat, front_idx, axis=0, mode='clip')  1.99 us
    gather x2, local copies, waits for them, and re-layouts, composite_rows(): back_rows = jnp.take(flat, back_idx, axis=0, mode='clip')  1.99 us
    unnamed x8, local copies, waits for them, and re-layouts  1.27 us
  transfers between devices with their start and end apart: 8, of which 6 were waited for; matrix products, arithmetic and copies ran while one was open for 10% of the time, Pallas kernels for 0%

profile of v26, /device:TPU:0, one launch (start us, length us, event | category | flops | bytes accessed | tf_op | source)
XLA Modules:
  0.0 56.8 jit_solution(7598974096023441126)
XLA Ops:
  1.9 0.1 add_convert_fusion
  2.0 0.7 %dynamic_update_slice.3.slot_ref = f32[130,4,128]{2,1,0:T(4,128)} pad(f32[1,1,3]{2,1,0:T(1,128)S(1)} %add_convert_fusion, f32[]{:T(128)} %constant.61.clone.1), padding=128_1x0_3x0_125 | pad | bytes 266256 | tf_op jit(solution)/shard_map/dynamic_update_slice | solution.py:123
  2.8 14.4 %shard_map.73 = f32[130,4,128]{2,1,0:T(4,128)} custom-call(f32[1]{0:T(128)S(6)} %copy.25.absorb_ref, f32[3]{0:T(128)} %slope_ref.1, f32[3]{0:T(128)} %offset_ref.1, s32[1,1]{1,0:T(1,128)} %copy.24.shown_ref, f32[16384,128]{1,0:T(8,128)} %bitcast.17, f32[130,4,128]{2,1,0:T(4,128)} %dynamic_update_slice.3.slot_ref), custom_call_target="tpu_custom_call", output_to_operand_aliasing={{}: (5, {})} | custom-call | tf_op jit(solution)/shard_map/pallas_call | solution.py:45
  17.2 3.0 %collective-permute-start = (f32[130,4,128]{2,1,0:T(4,128)}, f32[130,4,128]{2,1,0:T(4,128)S(1)}, u32[]{:S(2)}, u32[]{:S(2)}) collective-permute-start(f32[130,4,128]{2,1,0:T(4,128)} %shard_map.73), channel_id=1, source_target_pairs={{0,4},{4,8},{8,12},{12,14},{14,10},{10,6},{6,2},{2,0},{1,5},{5,9},... | collective-permute-start | bytes 798728 | tf_op jit(solution)/shard_map/ppermute | solution.py:101
  20.2 6.5 %collective-permute-done = f32[130,4,128]{2,1,0:T(4,128)S(1)} collective-permute-done((f32[130,4,128]{2,1,0:T(4,128)}, f32[130,4,128]{2,1,0:T(4,128)S(1)}, u32[]{:S(2)}, u32[]{:S(2)}) %collective-permute-start) | collective-permute-done | bytes 266272 | tf_op jit(solution)/shard_map/ppermute | solution.py:101
  26.7 1.8 %collective-permute-start.2 = (f32[130,4,128]{2,1,0:T(4,128)S(1)}, f32[130,4,128]{2,1,0:T(4,128)S(1)}, u32[]{:S(2)}, u32[]{:S(2)}) collective-permute-start(f32[130,4,128]{2,1,0:T(4,128)S(1)} %collective-permute-done), channel_id=1, source_target_pairs={{0,4},{4,8},{8,12},{12,14},{14,10},{10,6},{6,2},{2,0},{1,5},{5,9},... | collective-permute-start | bytes 798728 | tf_op jit(solution)/shard_map/ppermute | solution.py:101
  28.5 0.8 %and_select_fusion.1 = (s32[256]{0:T(256)S(1)}, s32[256]{0:T(256)S(1)}) fusion(s32[4096]{0:T(1024)} %param.13, s32[]{:T(128)S(6)} %select_n.113, s32[]{:T(128)S(6)} %select_n.111), kind=kLoop, calls=%fused_computation.59 | loop fusion | flops 5632 | bytes 4104 | tf_op jit(solution)/shard_map/jit(remainder)/select_n | solution.py:135
  29.4 1.0 %constant_dynamic-update-slice_fusion.7 = f32[1040,4,128]{2,1,0:T(4,128)S(1)} fusion(f32[130,4,128]{2,1,0:T(4,128)} %shard_map.73), kind=kLoop, calls=%fused_computation.33 | loop fusion | bytes 532480
  30.4 0.3 collective-permute-start.3
  30.6 0.8 %fusion.11 = pred[256]{0:T(512)(128)(4,1)S(1)} fusion(s32[]{:T(128)S(6)} %axis_index.25, s32[4096]{0:T(1024)} %param.13, s32[]{:T(128)S(6)} %select_n.111), kind=kLoop, calls=%fused_computation.67 | loop fusion | flops 4096 | bytes 1288 | tf_op jit(solution)/shard_map/eq | solution.py:139
  31.4 2.9 %collective-permute-done.2 = f32[130,4,128]{2,1,0:T(4,128)S(1)} collective-permute-done((f32[130,4,128]{2,1,0:T(4,128)S(1)}, f32[130,4,128]{2,1,0:T(4,128)S(1)}, u32[]{:S(2)}, u32[]{:S(2)}) %collective-permute-start.2) | collective-permute-done | bytes 266272 | tf_op jit(solution)/shard_map/ppermute | solution.py:101
  34.3 1.5 %collective-permute-start.4 = (f32[130,4,128]{2,1,0:T(4,128)S(1)}, f32[130,4,128]{2,1,0:T(4,128)S(1)}, u32[]{:S(2)}, u32[]{:S(2)}) collective-permute-start(f32[130,4,128]{2,1,0:T(4,128)S(1)} %collective-permute-done.2), channel_id=1, source_target_pairs={{0,4},{4,8},{8,12},{12,14},{14,10},{10,6},{6,2},{2,0},{1,5},{5,9},... | collective-permute-start | bytes 798728 | tf_op jit(solution)/shard_map/ppermute | solution.py:101
  35.9 1.5 %collective-permute-done.3 = f32[130,4,128]{2,1,0:T(4,128)S(1)} collective-permute-done((f32[130,4,128]{2,1,0:T(4,128)S(1)}, f32[130,4,128]{2,1,0:T(4,128)S(1)}, u32[]{:S(2)}, u32[]{:S(2)}) %collective-permute-start.3) | collective-permute-done | bytes 266272 | tf_op jit(solution)/shard_map/ppermute | solution.py:104
  37.4 0.5 collective-permute-start.5
  38.0 3.0 %collective-permute-done.4 = f32[130,4,128]{2,1,0:T(4,128)S(1)} collective-permute-done((f32[130,4,128]{2,1,0:T(4,128)S(1)}, f32[130,4,128]{2,1,0:T(4,128)S(1)}, u32[]{:S(2)}, u32[]{:S(2)}) %collective-permute-start.4) | collective-permute-done | bytes 266272 | tf_op jit(solution)/shard_map/ppermute | solution.py:101
  41.0 1.7 %collective-permute-start.6 = (f32[130,4,128]{2,1,0:T(4,128)S(1)}, f32[130,4,128]{2,1,0:T(4,128)S(1)}, u32[]{:S(2)}, u32[]{:S(2)}) collective-permute-start(f32[130,4,128]{2,1,0:T(4,128)S(1)} %collective-permute-done.4), channel_id=1, source_target_pairs={{0,4},{4,8},{8,12},{12,14},{14,10},{10,6},{6,2},{2,0},{1,5},{5,9},... | collective-permute-start | bytes 798728 | tf_op jit(solution)/shard_map/ppermute | solution.py:101
  42.7 1.1 %collective-permute-done.5 = f32[130,4,128]{2,1,0:T(4,128)S(1)} collective-permute-done((f32[130,4,128]{2,1,0:T(4,128)S(1)}, f32[130,4,128]{2,1,0:T(4,128)S(1)}, u32[]{:S(2)}, u32[]{:S(2)}) %collective-permute-start.5) | collective-permute-done | bytes 266272 | tf_op jit(solution)/shard_map/ppermute | solution.py:104
  43.8 3.5 %collective-permute-done.6 = f32[130,4,128]{2,1,0:T(4,128)S(1)} collective-permute-done((f32[130,4,128]{2,1,0:T(4,128)S(1)}, f32[130,4,128]{2,1,0:T(4,128)S(1)}, u32[]{:S(2)}, u32[]{:S(2)}) %collective-permute-start.6) | collective-permute-done | bytes 266272 | tf_op jit(solution)/shard_map/ppermute | solution.py:101
  47.4 0.1 copy.14
  47.5 0.1 select_reduce_fusion.2
  47.6 0.1 fusion.12
  47.7 0.1 select_reduce_fusion.1
  47.9 1.0 %gather_fusion.1 = f32[256,4,128]{2,1,0:T(4,128)S(1)} fusion(f32[1040,4,128]{2,1,0:T(4,128)S(1)} %constant_dynamic-update-slice_fusion, s32[1024]{0:T(1024)S(1)} %pad_clamp_fusion.2), kind=kCustom, calls=%fused_computation.1 | custom fusion | bytes 1049600 | tf_op jit(solution)/shard_map/jit(_take)/gather | solution.py:81
  48.9 1.0 %gather_fusion = f32[256,4,128]{2,1,0:T(4,128)S(1)} fusion(f32[1040,4,128]{2,1,0:T(4,128)S(1)} %constant_dynamic-update-slice_fusion, s32[1024]{0:T(1024)S(1)} %pad_clamp_fusion.3), kind=kCustom, calls=%fused_computation | custom fusion | bytes 1049600 | tf_op jit(solution)/shard_map/jit(_take)/gather | solution.py:82
  49.9 0.4 negate_exponential_fusion.1
  50.4 0.2 fusion.1
  50.5 1.0 %pad_maximum_fusion = f32[256,4,128]{2,1,0:T(4,128)} fusion(f32[256,1,128]{2,1,0:T(1,128)S(1)} %get-tuple-element.27, f32[256,3,128]{2,1,0:T(4,128)S(1)} %fusion.1), kind=kLoop, calls=%fused_computation.8 | loop fusion | flops 131072 | bytes 1048576 | tf_op jit(solution)/shard_map/concatenate | solution.py:86
  51.6 1.0 %gather_fusion.3 = f32[256,4,128]{2,1,0:T(4,128)S(1)} fusion(f32[1040,4,128]{2,1,0:T(4,128)S(1)} %constant_dynamic-update-slice_fusion, s32[1024]{0:T(1024)S(1)} %pad_clamp_fusion), kind=kCustom, calls=%fused_computation.3 | custom fusion | bytes 1049600 | tf_op jit(solution)/shard_map/jit(_take)/gather | solution.py:81
  52.6 1.0 %gather_fusion.2 = f32[256,4,128]{2,1,0:T(4,128)S(1)} fusion(f32[1040,4,128]{2,1,0:T(4,128)S(1)} %constant_dynamic-update-slice_fusion, s32[1024]{0:T(1024)S(1)} %pad_clamp_fusion.1), kind=kCustom, calls=%fused_computation.2 | custom fusion | bytes 1049600 | tf_op jit(solution)/shard_map/jit(_take)/gather | solution.py:82
  53.6 0.4 negate_exponential_fusion
  54.0 0.2 fusion
  54.2 2.6 %maximum_select_fusion = f32[256,4,128]{2,1,0:T(4,128)} fusion(f32[256,4,128]{2,1,0:T(4,128)} %collective-permute-done.7, f32[256,1,128]{2,1,0:T(1,128)S(1)} %get-tuple-element.25, f32[256,3,128]{2,1,0:T(4,128)S(1)} %fusion, pred[256]{0:T(512)(128)(4,1)S(1)} %fusion.11), kind=kLoop, calls=%fused_computation.9 | loop fusion | flops 262144 | bytes 1573120 | tf_op jit(solution)/shard_map/jit(_where)/select_n | solution.py:140
  (23 shorter events, 0.4 us)
Async XLA Ops:
  17.2 9.6 %collective-permute-start = (f32[130,4,128]{2,1,0:T(4,128)}, f32[130,4,128]{2,1,0:T(4,128)S(1)}, u32[]{:S(2)}, u32[]{:S(2)}) collective-permute-start(f32[130,4,128]{2,1,0:T(4,128)} %shard_map.73), channel_id=1, source_target_pairs={{0,4},{4,8},{8,12},{12,14},{14,10},{10,6},{6,2},{2,0},{1,5},{5,9},... | collective-permute-start | bytes 798728 | tf_op jit(solution)/shard_map/ppermute | solution.py:101
  20.2 10.2 %collective-permute-start.1 = (f32[130,4,128]{2,1,0:T(4,128)}, f32[130,4,128]{2,1,0:T(4,128)S(1)}, u32[]{:S(2)}, u32[]{:S(2)}) collective-permute-start(f32[130,4,128]{2,1,0:T(4,128)} %shard_map.73), channel_id=1, source_target_pairs={{4,0},{8,4},{12,8},{14,12},{10,14},{6,10},{2,6},{0,2},{5,1},{9,5},... | collective-permute-start | bytes 798728 | tf_op jit(solution)/shard_map/ppermute | solution.py:104
  26.7 7.6 %collective-permute-start.2 = (f32[130,4,128]{2,1,0:T(4,128)S(1)}, f32[130,4,128]{2,1,0:T(4,128)S(1)}, u32[]{:S(2)}, u32[]{:S(2)}) collective-permute-start(f32[130,4,128]{2,1,0:T(4,128)S(1)} %collective-permute-done), channel_id=1, source_target_pairs={{0,4},{4,8},{8,12},{12,14},{14,10},{10,6},{6,2},{2,0},{1,5},{5,9},... | collective-permute-start | bytes 798728 | tf_op jit(solution)/shard_map/ppermute | solution.py:101
  30.4 7.0 %collective-permute-start.3 = (f32[130,4,128]{2,1,0:T(4,128)S(1)}, f32[130,4,128]{2,1,0:T(4,128)S(1)}, u32[]{:S(2)}, u32[]{:S(2)}) collective-permute-start(f32[130,4,128]{2,1,0:T(4,128)S(1)} %collective-permute-done.1), channel_id=1, source_target_pairs={{4,0},{8,4},{12,8},{14,12},{10,14},{6,10},{2,6},{0,2},{5,1},{9,5},... | collective-permute-start | bytes 798728 | tf_op jit(solution)/shard_map/ppermute | solution.py:104
  34.3 6.7 %collective-permute-start.4 = (f32[130,4,128]{2,1,0:T(4,128)S(1)}, f32[130,4,128]{2,1,0:T(4,128)S(1)}, u32[]{:S(2)}, u32[]{:S(2)}) collective-permute-start(f32[130,4,128]{2,1,0:T(4,128)S(1)} %collective-permute-done.2), channel_id=1, source_target_pairs={{0,4},{4,8},{8,12},{12,14},{14,10},{10,6},{6,2},{2,0},{1,5},{5,9},... | collective-permute-start | bytes 798728 | tf_op jit(solution)/shard_map/ppermute | solution.py:101
  37.4 6.4 %collective-permute-start.5 = (f32[130,4,128]{2,1,0:T(4,128)S(1)}, f32[130,4,128]{2,1,0:T(4,128)S(1)}, u32[]{:S(2)}, u32[]{:S(2)}) collective-permute-start(f32[130,4,128]{2,1,0:T(4,128)S(1)} %collective-permute-done.3), channel_id=1, source_target_pairs={{4,0},{8,4},{12,8},{14,12},{10,14},{6,10},{2,6},{0,2},{5,1},{9,5},... | collective-permute-start | bytes 798728 | tf_op jit(solution)/shard_map/ppermute | solution.py:104
  41.0 6.4 %collective-permute-start.6 = (f32[130,4,128]{2,1,0:T(4,128)S(1)}, f32[130,4,128]{2,1,0:T(4,128)S(1)}, u32[]{:S(2)}, u32[]{:S(2)}) collective-permute-start(f32[130,4,128]{2,1,0:T(4,128)S(1)} %collective-permute-done.4), channel_id=1, source_target_pairs={{0,4},{4,8},{8,12},{12,14},{14,10},{10,6},{6,2},{2,0},{1,5},{5,9},... | collective-permute-start | bytes 798728 | tf_op jit(solution)/shard_map/ppermute | solution.py:101
  51.6 2.7 %collective-permute-start.7 = (f32[256,4,128]{2,1,0:T(4,128)}, f32[256,4,128]{2,1,0:T(4,128)}, u32[]{:S(2)}, u32[]{:S(2)}) collective-permute-start(f32[256,4,128]{2,1,0:T(4,128)} %pad_maximum_fusion), channel_id=1, source_target_pairs={{0,1},{1,0},{2,3},{3,2},{4,5},{5,4},{6,7},{7,6},{8,9},{9,8},{10,11... | collective-permute-start | bytes 1572872 | tf_op jit(solution)/shard_map/ppermute | solution.py:136
